TPU v7x, 32 devices: a whole 2x2x4 slice. The times are simulated.
32 devices in a mesh: groups: 2 (over y), blk: 4 (over z), pool: 4 (over x, core).
Axes of the slice: x: 2, y: 2, z: 4, core: 2. Of those that a mesh axis runs over, the one named last changes fastest.
Arguments:
- q_new: bfloat16 [1024, 8192], P(('groups', 'blk'), 'pool'), parts along dimension 0, may hold values from -64 to 64
- kv_new: bfloat16 [1024, 8, 256], P(('groups', 'blk'), 'pool'), parts along dimension 0, may hold values from -7 to 7
- kv_cache: bfloat16 [256, 8, 128, 256], P(('groups', 'blk'), 'pool'), parts along dimension 0, may hold values from -4.5 to 4.5
- page_table: int32 [16], P('groups'), parts along dimension 0, may hold values from 0 to 127, as said below
- block_offsets: int32 [8], P('groups'), parts along dimension 0, may hold values from 0 to 3, each once
Outputs:
- attended: bfloat16 [1024, 8192], P(('groups', 'blk'), 'pool'), parts along dimension 0
There are 2 independent parts, one for each index of `groups`. A program takes and returns all parts, laid end to end along the dimension named above; each array names one. Nothing has to cross between parts.
Inputs may be any that keep to these rules, and one draw needn't show every extreme that they name: `page_table`: distinct slots; slot s lies on blk index s // 32; at most 4 entries lie on the slots of one blk index, and exactly 4 on some blk index.
All inputs are finite; a program needn't handle non-finite values.
Results may differ from a plain program's by a relative error of at most 0.0045.
Values may be sent and summed in bfloat16 or wider, within the bound.
No kernel may reach another device: no remote copies, remote signals or barrier semaphores. Data moves between devices by JAX's collectives and lax.ppermute only.
A program may use at most 64 MiB of HBM per device.

v0:
```python
import math

import jax
import jax.numpy as jnp
from jax import lax
from jax.sharding import PartitionSpec as P

PG = 2
CAP = 4


def divisor_below(total_count, upper_limit):
    for candidate in range(min(total_count, upper_limit), 0, -1):
        if total_count % candidate == 0:
            return candidate
    return 1


def attend(running, queries, entries, visible, head_size):
    maxima, totals, summed = running
    score_scale = 1.0 / math.sqrt(head_size)
    scores = (
        jnp.einsum(
            "gqd,gkd->gqk", queries, entries[..., :head_size], preferred_element_type=jnp.float32
        )
        * score_scale
    )
    scores = jnp.where(visible[None], scores, -1e30)
    row_top = jnp.maximum(maxima, jnp.max(scores, axis=2))
    factor = jnp.exp(maxima - row_top)
    weights = jnp.where(visible[None], jnp.exp(scores - row_top[..., None]), 0.0)
    totals = totals * factor + jnp.sum(weights, axis=2)
    summed = summed * factor[..., None] + jnp.einsum(
        "gqk,gkd->gqd",
        weights.astype(jnp.bfloat16),
        entries[..., head_size:],
        preferred_element_type=jnp.float32,
    )
    return (row_top, totals, summed)


def local(q_new, kv_new, kv_cache, page_table, block_offsets):
    q_rows = q_new.shape[0]
    kv_heads = kv_new.shape[1]
    head_size = kv_new.shape[2] // 2
    group_size = q_new.shape[1] // (head_size * kv_heads)
    slots_dev = kv_cache.shape[0]
    page_len = kv_cache.shape[2]
    blocks = lax.axis_size("blk")
    myself = lax.axis_index("blk")
    block_ids = jnp.arange(blocks, dtype=jnp.int32)
    my_offset = jnp.sum(jnp.where(block_ids == myself, block_offsets, 0))
    query_pos = jnp.tile(my_offset * q_rows + jnp.arange(q_rows, dtype=jnp.int32), group_size)
    queries = (
        q_new.reshape(q_rows, kv_heads, group_size, head_size)
        .transpose(1, 2, 0, 3)
        .reshape(kv_heads, group_size * q_rows, head_size)
    )
    query_span = group_size * q_rows
    running = (
        jnp.full((kv_heads, query_span), -1e30, jnp.float32),
        jnp.zeros((kv_heads, query_span), jnp.float32),
        jnp.zeros((kv_heads, query_span, head_size), jnp.float32),
    )
    carried = running
    incoming = lax.all_gather(kv_new, "blk", axis=0, tiled=True)
    row_count = incoming.shape[0]
    block_rows = divisor_below(row_count, 512)
    parted = incoming.reshape(
        row_count // block_rows, block_rows, kv_heads, 2 * head_size
    ).transpose(0, 2, 1, 3)
    row_index = jnp.arange(row_count, dtype=jnp.int32).reshape(row_count // block_rows, block_rows)

    def visit_block(state_now, block_pair):
        entries, indices = block_pair
        source = indices // q_rows
        offsets = jnp.sum(
            jnp.where(source[:, None] == block_ids[None, :], block_offsets[None, :], 0), axis=1
        )
        key_pos = offsets * q_rows + indices % q_rows
        visible = key_pos[None, :] <= query_pos[:, None]
        return (attend(state_now, queries, entries, visible, head_size), None)

    carried, unused = lax.scan(visit_block, carried, (parted, row_index))
    running = carried
    page_owner = page_table // slots_dev
    owned = page_owner == myself
    page_rank = jnp.cumsum(owned.astype(jnp.int32)) - 1
    local_slot = page_table % slots_dev
    counts = jnp.sum((page_owner[None, :] == block_ids[:, None]).astype(jnp.int32), axis=1)
    per_peer = (CAP + blocks - 1) // blocks
    starts = jnp.cumsum(counts) - counts
    my_start = jnp.sum(jnp.where(block_ids == myself, starts, 0))
    peer_slots = jnp.arange(per_peer, dtype=jnp.int32)[None, :]
    wanted = (block_ids[:, None] - my_start) % blocks + peer_slots * blocks
    picked = owned[None, None, :] & (page_rank[None, None, :] == wanted[..., None])
    chosen = jnp.sum(jnp.where(picked, local_slot[None, None, :], 0), axis=2).reshape(-1)
    received = lax.all_to_all(kv_cache[chosen], "blk", split_axis=0, concat_axis=0, tiled=True)
    arriving = (myself - starts[:, None]) % blocks + peer_slots * blocks
    present = (arriving < counts[:, None]).reshape(-1)
    order_rank = jnp.cumsum(present.astype(jnp.int32)) - 1
    choose = present[None, :] & (order_rank[None, :] == jnp.arange(PG, dtype=jnp.int32)[:, None])
    positions = jnp.sum(
        jnp.where(choose, jnp.arange(blocks * per_peer, dtype=jnp.int32)[None, :], 0), axis=1
    )
    compact = received[positions]
    valid_all = jnp.ones((blocks * PG,), jnp.bool_)
    carried = running
    incoming = lax.all_gather(compact, "blk", axis=0, tiled=True)
    page_count = incoming.shape[0]
    group_pages = divisor_below(page_count, max(1, 512 // page_len))
    parted = incoming.reshape(
        page_count // group_pages, group_pages, kv_heads, page_len, 2 * head_size
    )
    parted = parted.transpose(0, 2, 1, 3, 4).reshape(
        page_count // group_pages, kv_heads, group_pages * page_len, 2 * head_size
    )
    flags = valid_all.reshape(page_count // group_pages, group_pages)

    def visit_pages(state_now, block_pair):
        entries, present = block_pair
        visible = jnp.repeat(present, page_len)[None, :]
        return (attend(state_now, queries, entries, visible, head_size), None)

    carried, unused = lax.scan(visit_pages, carried, (parted, flags))
    running = carried
    maxima, totals, summed = running
    attended = (summed / totals[..., None]).astype(jnp.bfloat16)
    attended = attended.reshape(kv_heads, group_size, q_rows, head_size).transpose(2, 0, 1, 3)
    return attended.reshape(q_rows, kv_heads * group_size * head_size)


def solution(mesh):
    return jax.shard_map(
        local,
        mesh=mesh,
        in_specs=(
            P(("groups", "blk"), "pool"),
            P(("groups", "blk"), "pool", None),
            P(("groups", "blk"), "pool", None, None),
            P("groups"),
            P("groups"),
        ),
        out_specs=P(("groups", "blk"), "pool"),
        check_vma=False,
    )
```

profile of v0, /device:TPU:0, one launch (start us, length us, event | category | flops | bytes accessed | tf_op | source)
XLA Modules:
  0.0 93.6 jit_solution(7782781215370035208)
XLA Ops:
  6.5 0.7 and_select_fusion.3
  7.2 0.7 convert_bitcast_fusion
  7.9 0.2 reduce-window.21
  8.1 0.1 convert_reduce_fusion
  8.2 0.2 reduce-window.22
  8.3 1.4 %fusion.36 = (s32[]{:T(128)}, s32[]{:T(128)}) fusion(s32[4]{0:T(128)} %param.11, s32[]{:T(128)S(6)} %axis_index.15, s32[4]{0:T(128)S(1)} %convert_reduce_fusion, s32[4,1]{0,1:T(1,128)S(1)} %reduce-window.22), kind=kLoop, calls=%fused_computation.76 | loop fusion | flops 22 | bytes 60 | tf_op jit(solution)/shard_map/reduce_sum | solution.py:52
  9.7 0.7 and_select_fusion.4
  10.4 0.2 select_reduce_fusion.1
  10.6 3.6 %gather_fusion = bf16[4,2,128,256]{3,2,1,0:T(8,128)(2,1)} fusion(bf16[32,2,128,256]{3,2,1,0:T(8,128)(2,1)} %param.9, s32[1024]{0:T(1024)S(1)} %pad_clamp_fusion.1), kind=kCustom, calls=%fused_computation | custom fusion | bytes 1048592 | tf_op jit(solution)/shard_map/gather | solution.py:98
  14.1 6.3 %all-to-all-start = ((bf16[4,2,128,256]{3,2,1,0:T(8,128)(2,1)}), bf16[4,2,128,256]{3,2,1,0:T(8,128)(2,1)S(1)}, u32[]{:S(2)}, u32[]{:S(2)}) async-start(bf16[4,2,128,256]{3,2,1,0:T(8,128)(2,1)} %gather_fusion), calls=%async_computation | async-start | bytes 1048576 | tf_op jit(solution)/shard_map/all_to_all | solution.py:98
  20.5 0.0 all-gather.3.cloned.1.call-start
  20.5 0.2 reduce-window.23
  20.7 0.1 fusion.34
  20.8 0.7 select_reduce_fusion
  21.6 0.9 copy.20
  22.5 22.8 %all_gather.6 = bf16[512,2,256]{2,0,1:T(8,128)(2,1)S(1)} all-gather(bf16[128,2,256]{2,0,1:T(8,128)(2,1)S(1)} %copy.20), channel_id=1, replica_groups=mesh['groups'=2,'blk'=4,'pool'=4] {'blk'}, dimensions={0}, use_global_device_ids=true | all-gather | bytes 655360 | tf_op jit(solution)/shard_map/all_gather | solution.py:66
  45.3 1.1 %copy.26 = bf16[16,8,16,128]{3,2,1,0:T(8,128)(2,1)S(1)} copy(bf16[16,8,16,128]{3,1,2,0:T(8,128)(2,1)} %bitcast.81) | data formatting | bytes 1048576
  46.4 0.1 copy.19
  47.3 0.4 broadcast_compare_fusion
  47.6 0.0 all-to-all-done
  47.7 1.3 %gather_fusion.1 = bf16[2,2,128,256]{3,2,1,0:T(8,128)(2,1)} fusion(bf16[4,2,128,256]{3,2,1,0:T(8,128)(2,1)S(1)} %all-to-all-done, s32[1024]{0:T(1024)S(1)} %pad_clamp_fusion), kind=kCustom, calls=%fused_computation.1 | custom fusion | bytes 524296 | tf_op jit(solution)/shard_map/gather | solution.py:106
  48.9 0.0 all-gather.3.cloned.1.call-update
  48.9 1.0 %fusion.14 = (f32[2,1024]{1,0:T(2,128)S(1)}, f32[2,1024,512]{1,2,0:T(8,128)S(1)}) fusion(pred[1024,512]{0,1:T(8,128)(4,1)S(1)} %broadcast_compare_fusion, bf16[2,1024,128]{2,1,0:T(8,128)(2,1)S(1)} %bitcast.72, bf16[2,512,256]{2,1,0:T(8,128)(2,1)S(1)} %bitcast.79), kind=kOutput, calls=%fused_computation.20 | convolution fusion | flops 271579136 | bytes 5513216 | tf_op jit(solution)/shard_map/while/body/eval_jaxpr/gqd,gkd->gqk/dot_general | solution.py:23
  49.9 1.1 %fusion.16 = f32[2,1024]{1,0:T(2,128)S(1)} fusion(f32[2,1024,512]{1,2,0:T(8,128)S(1)} %get-tuple-element.92, f32[2,1024]{1,0:T(2,128)S(1)} %broadcast_maximum_fusion, pred[1024,512]{0,1:T(8,128)(4,1)S(1)} %broadcast_compare_fusion), kind=kLoop, calls=%fused_computation.22 | loop fusion | flops 5240832 | bytes 4734976 | tf_op jit(solution)/shard_map/while/body/eval_jaxpr/reduce_sum | solution.py:32
  51.1 1.8 %fusion.20 = f32[2,1024,128]{2,1,0:T(8,128)S(1)} fusion(f32[2,1024,512]{1,2,0:T(8,128)S(1)} %get-tuple-element.92, f32[2,1024]{1,0:T(2,128)S(1)} %broadcast_maximum_fusion, pred[1024,512]{0,1:T(8,128)(4,1)S(1)} %broadcast_compare_fusion, f32[2,1024]{1,0:T(2,128)S(1)} %get-tuple-element.89, bf16[2,512,256]{2,1,0:T(8,128)(2,1)S(1)} %bitcast.80), kind=kOutput, calls=%fused_computation.25 | convolution fusion | flops 273940480 | bytes 6045696 | tf_op jit(solution)/shard_map/while/body/eval_jaxpr/gqk,gkd->gqd/dot_general | solution.py:33
  52.9 25.0 %all-gather.3.cloned.1.call-done = bf16[8,2,128,256]{3,2,1,0:T(8,128)(2,1)} async-done(((bf16[2,2,128,256]{3,2,1,0:T(8,128)(2,1)}), bf16[8,2,128,256]{3,2,1,0:T(8,128)(2,1)}) %all-gather.3.cloned.1.call-update) | async-done | bytes 1048592 | tf_op jit(solution)/shard_map/all_gather | solution.py:109
  77.9 1.3 %copy.22 = bf16[2,2,4,128,256]{4,3,2,1,0:T(8,128)(2,1)S(1)} copy(bf16[2,2,4,128,256]{4,3,1,2,0:T(8,128)(2,1)} %bitcast.78) | data formatting | bytes 2097152 | tf_op jit(solution)/shard_map/transpose | solution.py:115
  79.2 5.9 %while.2 = (s32[]{:T(128)}, f32[2,1024]{1,0:T(2,128)S(1)}, f32[2,1024]{1,0:T(2,128)S(1)}, f32[2,1024,128]{2,1,0:T(8,128)S(1)}, bf16[2,2,512,256]{3,2,1,0:T(8,128...) while((s32[]{:T(128)}, f32[2,1024]{1,0:T(2,128)S(1)}, f32[2,1024]{1,0:T(2,128)S(1)}, ...), condition=%wide.region_14.15_spmd, body=%wide.region_11.14_spmd.sunk | while | flops 545787904 | bytes 16908376 | solution.py:125
  79.2 0.7 bitcast_reduce_fusion.2
  80.0 0.7 fusion.57
  80.7 1.4 %fusion.58 = f32[2,1024,128]{2,1,0:T(8,128)S(1)} fusion(f32[2,512,1024]{2,1,0:T(8,128)S(1)} %get-tuple-element.137, f32[2,1024]{1,0:T(2,128)S(1)} %max.21, f32[2,1024,128]{2,1,0:T(8,128)S(1)} %get-tuple-element.150, f32[2,1024]{1,0:T(2,128)S(1)} %get-tuple-element.139, bf16[2,512,256]{2,1,0:T(8,128)(2,1)S(1)} %dynamic-slice_bitcast_fusion.2), kind=kOutput, calls=%fused_computation.10.clone.1 | convolution fusion | flops 272105472 | bytes 6569984 | tf_op jit(solution)/shard_map/while/body/eval_jaxpr/gqk,gkd->gqd/dot_general | solution.py:33
  82.2 0.7 bitcast_reduce_fusion.2
  82.9 0.7 fusion.57
  83.7 1.4 %fusion.58 = f32[2,1024,128]{2,1,0:T(8,128)S(1)} fusion(f32[2,512,1024]{2,1,0:T(8,128)S(1)} %get-tuple-element.137, f32[2,1024]{1,0:T(2,128)S(1)} %max.21, f32[2,1024,128]{2,1,0:T(8,128)S(1)} %get-tuple-element.150, f32[2,1024]{1,0:T(2,128)S(1)} %get-tuple-element.139, bf16[2,512,256]{2,1,0:T(8,128)(2,1)S(1)} %dynamic-slice_bitcast_fusion.2), kind=kOutput, calls=%fused_computation.10.clone.1 | convolution fusion | flops 272105472 | bytes 6569984 | tf_op jit(solution)/shard_map/while/body/eval_jaxpr/gqk,gkd->gqd/dot_general | solution.py:33
  85.1 0.3 divide_convert_fusion
  85.4 0.3 copy.23
  85.8 0.9 copy.29
  (22 shorter events, 0.3 us)
Async XLA Ops:
  14.1 33.5 %all-to-all-start = ((bf16[4,2,128,256]{3,2,1,0:T(8,128)(2,1)}), bf16[4,2,128,256]{3,2,1,0:T(8,128)(2,1)S(1)}, u32[]{:S(2)}, u32[]{:S(2)}) async-start(bf16[4,2,128,256]{3,2,1,0:T(8,128)(2,1)} %gather_fusion), calls=%async_computation | async-start | bytes 1048576 | tf_op jit(solution)/shard_map/all_to_all | solution.py:98
  20.5 57.4 %all-gather.3.cloned.1.call-start = ((), (), s32[]{:S(2)}) async-start(), calls=%async_computation.1 | async-start | bytes 1310720 | tf_op jit(solution)/shard_map/all_gather | solution.py:109
Sparse Core Ops, SparseCore 0:
  49.1 28.7 all-gather.2
where the time goes:
time: 93.9 us; the launch traced here: 93.6 us
  waiting for transfers between devices  25 us (27%)
  blocking collectives  22.8 us (24%)
  between operations  14.2 us (15%)
  local copies, waits for them, and re-layouts  9.7 us (10%)
  other arithmetic  8.44 us (9%)
  matrix products  7.01 us (7%)
  starting transfers between devices  6.32 us (7%)
    all_gather x1, waiting for transfers between devices, local(): incoming = lax.all_gather(compact, 'blk', axis=0, tiled=True)  25 us
    all_gather x1, blocking collectives, local(): incoming = lax.all_gather(kv_new, 'blk', axis=0, tiled=True)  22.8 us
    all_to_all x1, starting transfers between devices, local(): lax.all_to_all(kv_cache[chosen], 'blk', split_axis=0, concat_axis=0, tile...  6.32 us
    dot_general x3, matrix products, attend(): jnp.einsum('gqk,gkd->gqd', weights.astype(jnp.bfloat16), entries[..., hea...  4.59 us
    gather x1, local copies, waits for them, and re-layouts, local(): kv_cache[chosen]  3.56 us
    unnamed x3, local copies, waits for them, and re-layouts  2.99 us
    reduce_sum x3, other arithmetic, attend(): totals = totals * factor + jnp.sum(weights, axis=2)  2.52 us
    dot_general x3, matrix products, attend(): jnp.einsum('gqd,gkd->gqk', queries, entries[..., :head_size], preferred_e...  2.42 us
  transfers between devices with their start and end apart: 2, of which 1 were waited for; matrix products, arithmetic and copies ran while one was open for 8% of the time, Pallas kernels for 0%

commit v1 on v0

v1 whole, which is shorter than its diff:
```python
import math

import jax
import jax.numpy as jnp
from jax import lax
from jax.sharding import PartitionSpec as P

CAP = 4


def attend(running, queries, keys, values, visible, head_size):
    maxima, totals, summed = running
    score_scale = 1.0 / math.sqrt(head_size)
    scores = (
        jnp.einsum("gqd,gkd->gqk", queries, keys, preferred_element_type=jnp.float32)
        * score_scale
    )
    scores = jnp.where(visible, scores, -1e30)
    row_top = jnp.maximum(maxima, jnp.max(scores, axis=2))
    factor = jnp.exp(maxima - row_top)
    weights = jnp.where(visible, jnp.exp(scores - row_top[..., None]), 0.0)
    totals = totals * factor + jnp.sum(weights, axis=2)
    summed = summed * factor[..., None] + jnp.einsum(
        "gqk,gkd->gqd",
        weights.astype(jnp.bfloat16),
        values,
        preferred_element_type=jnp.float32,
    )
    return (row_top, totals, summed)


def local(q_new, kv_new, kv_cache, page_table, block_offsets):
    q_rows = q_new.shape[0]
    kv_heads = kv_new.shape[1]
    head_size = kv_new.shape[2] // 2
    group_size = q_new.shape[1] // (head_size * kv_heads)
    slots_dev = kv_cache.shape[0]
    page_len = kv_cache.shape[2]
    npages = page_table.shape[0]
    blocks = lax.axis_size("blk")
    myself = lax.axis_index("blk")
    pg = -(-npages // blocks)
    block_ids = jnp.arange(blocks, dtype=jnp.int32)
    my_offset = jnp.sum(jnp.where(block_ids == myself, block_offsets, 0))
    query_pos = jnp.tile(my_offset * q_rows + jnp.arange(q_rows, dtype=jnp.int32), group_size)
    queries = (
        q_new.reshape(q_rows, kv_heads, group_size, head_size)
        .transpose(1, 2, 0, 3)
        .reshape(kv_heads, group_size * q_rows, head_size)
    )
    query_span = group_size * q_rows

    page_owner = page_table // slots_dev
    owned = page_owner == myself
    page_rank = jnp.cumsum(owned.astype(jnp.int32)) - 1
    local_slot = page_table % slots_dev
    counts = jnp.sum((page_owner[None, :] == block_ids[:, None]).astype(jnp.int32), axis=1)
    per_peer = (CAP + blocks - 1) // blocks
    starts = jnp.cumsum(counts) - counts
    my_start = jnp.sum(jnp.where(block_ids == myself, starts, 0))
    peer_slots = jnp.arange(per_peer, dtype=jnp.int32)[None, :]
    wanted = (block_ids[:, None] - my_start) % blocks + peer_slots * blocks
    picked = owned[None, None, :] & (page_rank[None, None, :] == wanted[..., None])
    chosen = jnp.sum(jnp.where(picked, local_slot[None, None, :], 0), axis=2).reshape(-1)
    sent_pages = kv_cache[chosen].reshape(blocks, per_peer, kv_heads, page_len, 2 * head_size)
    sent_pages = sent_pages.transpose(0, 2, 1, 3, 4).reshape(
        blocks, kv_heads, per_peer * page_len, 2 * head_size
    )
    own_rows = jnp.broadcast_to(
        kv_new.transpose(1, 0, 2)[None], (blocks, kv_heads, q_rows, 2 * head_size)
    )
    payload = jnp.concatenate([sent_pages, own_rows], axis=2)
    received = lax.all_to_all(payload, "blk", split_axis=0, concat_axis=0, tiled=True)

    page_part = received[:, :, : per_peer * page_len]
    page_part = page_part.reshape(blocks, kv_heads, per_peer, page_len, 2 * head_size)
    page_part = page_part.transpose(0, 2, 1, 3, 4).reshape(
        blocks * per_peer, kv_heads, page_len, 2 * head_size
    )
    arriving = (myself - starts[:, None]) % blocks + peer_slots * blocks
    present = (arriving < counts[:, None]).reshape(-1)
    order_rank = jnp.cumsum(present.astype(jnp.int32)) - 1
    choose = present[None, :] & (order_rank[None, :] == jnp.arange(pg, dtype=jnp.int32)[:, None])
    positions = jnp.sum(
        jnp.where(choose, jnp.arange(blocks * per_peer, dtype=jnp.int32)[None, :], 0), axis=1
    )
    compact = page_part[positions]
    compact_valid = jnp.arange(pg, dtype=jnp.int32) * blocks + myself < npages
    gathered = lax.all_gather(compact, "blk", axis=0, tiled=True)
    gathered_valid = (
        jnp.arange(pg, dtype=jnp.int32)[None, :] * blocks + block_ids[:, None] < npages
    ).reshape(-1)

    new_rows = received[:, :, per_peer * page_len :]
    new_rows = new_rows.transpose(1, 0, 2, 3).reshape(kv_heads, blocks * q_rows, 2 * head_size)
    own_pages = compact.transpose(1, 0, 2, 3).reshape(kv_heads, pg * page_len, 2 * head_size)
    entries_a = jnp.concatenate([new_rows, own_pages], axis=1)
    row_source = jnp.repeat(block_ids, q_rows)
    key_pos = (
        jnp.sum(jnp.where(row_source[:, None] == block_ids[None, :], block_offsets[None, :], 0), axis=1)
        * q_rows
        + jnp.tile(jnp.arange(q_rows, dtype=jnp.int32), blocks)
    )
    visible_new = key_pos[None, :] <= query_pos[:, None]
    visible_own = jnp.broadcast_to(jnp.repeat(compact_valid, page_len)[None, :], (query_span, pg * page_len))
    visible_a = jnp.concatenate([visible_new, visible_own], axis=1)[None]
    running = (
        jnp.full((kv_heads, query_span), -1e30, jnp.float32),
        jnp.zeros((kv_heads, query_span), jnp.float32),
        jnp.zeros((kv_heads, query_span, head_size), jnp.float32),
    )
    running = attend(
        running, queries, entries_a[..., :head_size], entries_a[..., head_size:], visible_a, head_size
    )

    page_block = jnp.repeat(block_ids, pg)
    use_page = gathered_valid & (page_block != myself)
    entries_b = gathered.transpose(1, 0, 2, 3).reshape(
        kv_heads, blocks * pg * page_len, 2 * head_size
    )
    visible_b = jnp.repeat(use_page, page_len)[None, None, :]
    running = attend(
        running, queries, entries_b[..., :head_size], entries_b[..., head_size:], visible_b, head_size
    )
    maxima, totals, summed = running
    attended = (summed / totals[..., None]).astype(jnp.bfloat16)
    attended = attended.reshape(kv_heads, group_size, q_rows, head_size).transpose(2, 0, 1, 3)
    return attended.reshape(q_rows, kv_heads * group_size * head_size)


def solution(mesh):
    return jax.shard_map(
        local,
        mesh=mesh,
        in_specs=(
            P(("groups", "blk"), "pool"),
            P(("groups", "blk"), "pool", None),
            P(("groups", "blk"), "pool", None, None),
            P("groups"),
            P("groups"),
        ),
        out_specs=P(("groups", "blk"), "pool"),
        check_vma=False,
    )
```

time: 93.9 us -> 97.9 us (1.043)
  blocking collectives: 22.8 us -> 0 us
  waiting for transfers between devices: 25 us -> 45.4 us
  matrix products: 7.01 us -> 11.7 us
  other arithmetic: 8.44 us -> 10.6 us
    all_to_all x1, waiting for transfers between devices: 0.01 us -> 24.1 us  [local(): lax.all_to_all(payload, 'blk', split_axis=0, concat_axis=0, tiled=True)]
    all_gather x1 -> x0, blocking collectives: 22.8 us -> none  [local(): incoming = lax.all_gather(kv_new, 'blk', axis=0, tiled=True)]
    dot_general x6 -> x4, matrix products: 7.01 us -> 11.7 us  [the longest x2 5.92 us: attend(): jnp.einsum('gqd,gkd->gqk', queries, keys, preferred_element_type=jnp.floa...]
    all_gather x1, waiting for transfers between devices: 25 us -> 21.3 us  [local(): gathered = lax.all_gather(compact, 'blk', axis=0, tiled=True)]
    transpose x1 -> x6, local copies, waits for them, and re-layouts: 1.31 us -> 3.7 us  [the longest x1 1.29 us: local(): gathered.transpose(1, 0, 2, 3)]
    unnamed x3 -> x10, local copies, waits for them, and re-layouts: 2.99 us -> 1.06 us
    reduce_sum x3 -> x2, other arithmetic: 2.52 us -> 4.16 us  [attend(): totals = totals * factor + jnp.sum(weights, axis=2)]
    concatenate x0 -> x2, other arithmetic: none -> 1.47 us  [the longest x1 1.06 us: local(): payload = jnp.concatenate([sent_pages, own_rows], axis=2)]
  transfers between devices with their start and end apart: 2 -> 2, of which waited for: 1 -> 2; matrix products, arithmetic and copies ran while one was open for 8% -> 7% of each run, Pallas kernels for 0% -> 0%
where the time goes in v1:
time: 97.9 us; the launch traced here: 97.5 us
  waiting for transfers between devices  45.4 us (46%)
  between operations  14.3 us (15%)
  matrix products  11.7 us (12%)
  other arithmetic  10.6 us (11%)
  local copies, waits for them, and re-layouts  9.17 us (9%)
  starting transfers between devices  6.32 us (6%)
    all_to_all x1, waiting for transfers between devices, local(): lax.all_to_all(payload, 'blk', split_axis=0, concat_axis=0, tiled=True)  24.1 us
    all_gather x1, waiting for transfers between devices, local(): gathered = lax.all_gather(compact, 'blk', axis=0, tiled=True)  21.3 us
    all_to_all x1, starting transfers between devices, local(): lax.all_to_all(payload, 'blk', split_axis=0, concat_axis=0, tiled=True)  6.32 us
    dot_general x2, matrix products, attend(): jnp.einsum('gqd,gkd->gqk', queries, keys, preferred_element_type=jnp.floa...  5.92 us
    dot_general x2, matrix products, attend(): jnp.einsum('gqk,gkd->gqd', weights.astype(jnp.bfloat16), values, preferre...  5.81 us
    reduce_sum x2, other arithmetic, attend(): totals = totals * factor + jnp.sum(weights, axis=2)  4.16 us
    gather x1, local copies, waits for them, and re-layouts, local(): kv_cache[chosen]  2.77 us
  transfers between devices with their start and end apart: 2, of which 2 were waited for; matrix products, arithmetic and copies ran while one was open for 7% of the time, Pallas kernels for 0%

profile of v1, /device:TPU:0, one launch (start us, length us, event | category | flops | bytes accessed | tf_op | source)
XLA Modules:
  0.0 97.5 jit_solution(11759745901006424764)
XLA Ops:
  6.5 0.0 copy-start.1
  6.5 0.0 copy-start
  6.5 0.7 and_select_fusion.3
  7.3 0.7 convert_bitcast_fusion
  7.9 0.2 reduce-window.21
  8.1 0.1 convert_reduce_fusion
  8.2 0.2 reduce-window.22
  8.4 1.4 %fusion.35 = (s32[]{:T(128)}, s32[]{:T(128)}) fusion(s32[4]{0:T(128)} %param.9, s32[]{:T(128)S(6)} %axis_index.15, s32[4]{0:T(128)S(1)} %convert_reduce_fusion, s32[4,1]{0,1:T(1,128)S(1)} %reduce-window.22), kind=kLoop, calls=%fused_computation.78 | loop fusion | flops 22 | bytes 60 | tf_op jit(solution)/shard_map/reduce_sum | solution.py:44
  9.8 0.7 and_select_fusion.4
  10.5 0.2 select_reduce_fusion.1
  10.7 0.9 copy.22
  11.6 2.8 %gather_fusion = bf16[4,2,128,256]{3,2,1,0:T(8,128)(2,1)S(1)} fusion(bf16[32,2,128,256]{3,2,1,0:T(8,128)(2,1)} %param.7, s32[1024]{0:T(1024)S(1)} %pad_clamp_fusion.1), kind=kCustom, calls=%fused_computation | custom fusion | bytes 1048592 | tf_op jit(solution)/shard_map/gather | solution.py:65
  14.4 1.1 %pad_maximum_fusion = bf16[4,2,256,256]{3,2,1,0:T(8,128)(2,1)} fusion(bf16[4,2,128,256]{3,2,1,0:T(8,128)(2,1)S(1)} %broadcast_in_dim.150, bf16[4,2,128,256]{3,2,1,0:T(8,128)(2,1)S(1)} %gather_fusion), kind=kLoop, calls=%fused_computation.23 | loop fusion | flops 2097152 | bytes 2097152 | tf_op jit(solution)/shard_map/concatenate | solution.py:72
  15.5 6.3 %all-to-all-start = ((bf16[4,2,256,256]{3,2,1,0:T(8,128)(2,1)}), bf16[4,2,256,256]{3,2,1,0:T(8,128)(2,1)S(1)}, u32[]{:S(2)}, u32[]{:S(2)}) async-start(bf16[4,2,256,256]{3,2,1,0:T(8,128)(2,1)} %pad_maximum_fusion), calls=%async_computation | async-start | bytes 2097152 | tf_op jit(solution)/shard_map/all_to_all | solution.py:73
  21.8 0.0 all-gather.3.cloned.1.call-start
  21.9 0.1 and.99
  21.9 0.2 reduce-window.23
  22.1 0.0 copy-done
  22.1 0.1 copy.32
  22.2 0.1 copy.25
  22.4 0.1 broadcast_bitcast_fusion.2
  23.2 0.1 fusion.33
  23.3 0.0 copy-done.1
  23.3 0.1 select_reduce_fusion
  23.4 24.1 %all-to-all-done = bf16[4,2,256,256]{3,2,1,0:T(8,128)(2,1)S(1)} async-done(((bf16[4,2,256,256]{3,2,1,0:T(8,128)(2,1)}), bf16[4,2,256,256]{3,2,1,0:T(8,128)(2,1)S(1)}, u32[]{:S(2)}, u32[]{:S(2)}) %all-to-all-start) | async-done | bytes 1048608 | tf_op jit(solution)/shard_map/all_to_all | solution.py:73
  47.6 0.1 fusion.51
  47.7 1.3 %gather_fusion.1 = bf16[2,2,128,256]{3,2,1,0:T(8,128)(2,1)} fusion(bf16[4,2,128,256]{3,2,1,0:T(8,128)(2,1)S(1)} %get-tuple-element.10, s32[1024]{0:T(1024)S(1)} %pad_clamp_fusion), kind=kCustom, calls=%fused_computation.1 | custom fusion | bytes 524296 | tf_op jit(solution)/shard_map/gather | solution.py:87
  48.9 0.0 all-gather.3.cloned.1.call-update
  48.9 0.1 broadcast_bitcast_fusion.1
  49.0 0.4 broadcast_compare_fusion
  49.4 0.4 pad_add_fusion
  49.8 1.0 copy.24
  50.8 4.0 %fusion.4 = (f32[2,1024]{1,0:T(2,128)S(1)}, f32[2,768,1024]{2,1,0:T(8,128)}) fusion(pred[1024,768]{0,1:T(8,128)(4,1)S(1)} %pad_add_fusion, bf16[2,1024,128]{2,1,0:T(8,128)(2,1)S(1)} %bitcast.92, bf16[2,512,256]{2,1,0:T(8,128)(2,1)S(1)} %bitcast.98, bf16[2,256,256]{2,1,0:T(8,128)(2,1)S(1)} %bitcast.101), kind=kOutput, calls=%fused_computation.11 | convolution fusion | flops 408156160 | bytes 8396800 | tf_op jit(solution)/shard_map/gqd,gkd->gqk/dot_general | solution.py:15
  54.9 21.3 %all-gather.3.cloned.1.call-done = bf16[8,2,128,256]{3,2,1,0:T(8,128)(2,1)} async-done(((bf16[2,2,128,256]{3,2,1,0:T(8,128)(2,1)}), bf16[8,2,128,256]{3,2,1,0:T(8,128)(2,1)}) %all-gather.3.cloned.1.call-update) | async-done | bytes 1048592 | tf_op jit(solution)/shard_map/all_gather | solution.py:89
  76.1 1.3 %copy.27 = bf16[2,8,128,256]{3,2,1,0:T(8,128)(2,1)S(1)} copy(bf16[2,8,128,256]{3,2,0,1:T(8,128)(2,1)} %bitcast.96) | data formatting | bytes 2097152 | tf_op jit(solution)/shard_map/transpose | solution.py:118
  77.4 0.0 slice-start
  77.4 0.0 slice-start.1
  77.5 1.9 %bitcast_reduce_fusion = (f32[2,1024]{1,0:T(2,128)S(1)}, f32[2,1024,1024]{2,1,0:T(8,128)S(1)}) fusion(pred[1024]{0:T(1024)(128)(4,1)S(1)} %broadcast_bitcast_fusion.1, bf16[2,1024,128]{2,1,0:T(8,128)(2,1)S(1)} %bitcast.93, bf16[2,1024,256]{2,1,0:T(8,128)(2,1)S(1)} %bitcast.89), kind=kOutput, calls=%fused_computation.3 | convolution fusion | flops 543160320 | bytes 9446400 | tf_op jit(solution)/shard_map/gqd,gkd->gqk/dot_general | solution.py:15
  79.4 2.5 %fusion.2 = f32[2,1024]{1,0:T(2,128)S(1)} fusion(f32[2,1024,1024]{2,1,0:T(8,128)S(1)} %get-tuple-element.18, f32[2,1024]{1,0:T(2,128)S(1)} %get-tuple-element.13, pred[1024]{0:T(1024)(128)(4,1)S(1)} %broadcast_bitcast_fusion.1), kind=kLoop, calls=%fused_computation.9 | loop fusion | flops 10483712 | bytes 8406016 | tf_op jit(solution)/shard_map/reduce_sum | solution.py:22
  81.9 0.0 slice-done
  81.9 0.0 slice-done.1
  81.9 1.7 %fusion.5 = f32[2,1024]{1,0:T(2,128)S(1)} fusion(f32[2,768,1024]{2,1,0:T(8,128)S(1)} %bitcast.88, f32[2,1024]{1,0:T(2,128)S(1)} %get-tuple-element.14, pred[1024,768]{0,1:T(8,128)(4,1)S(1)} %pad_add_fusion), kind=kLoop, calls=%fused_computation.12 | loop fusion | flops 7862272 | bytes 7094272 | tf_op jit(solution)/shard_map/reduce_sum | solution.py:22
  83.6 2.8 %fusion.20 = f32[2,1024,128]{2,1,0:T(8,128)S(1)} fusion(f32[2,768,1024]{2,1,0:T(8,128)S(1)} %bitcast.88, f32[2,1024]{1,0:T(2,128)S(1)} %get-tuple-element.14, pred[1024,768]{0,1:T(8,128)(4,1)S(1)} %pad_add_fusion, f32[2,1024]{1,0:T(2,128)S(1)} %get-tuple-element.6, f32[2,1024]{1,0:T(2,128)S(1)} %get-tuple-element.12, ...), kind=kOutput, calls=%fused_computation.22 | convolution fusion | flops 411828224 | bytes 8937472 | tf_op jit(solution)/shard_map/gqk,gkd->gqd/dot_general | solution.py:23
  86.4 3.0 %divide_convert_fusion = bf16[2,1024,128]{2,1,0:T(8,128)(2,1)S(1)} fusion(f32[2,1024,128]{2,1,0:T(8,128)S(1)} %fusion.20, f32[2,1024,1024]{2,1,0:T(8,128)S(1)} %get-tuple-element.18, f32[2,1024]{1,0:T(2,128)S(1)} %get-tuple-element.13, pred[1024]{0:T(1024)(128)(4,1)S(1)} %broadcast_bitcast_fusion.1, bf16[2,1024,256]{2,1,0:T(8,128)(2,1)S(1)} %bitcast.90, ...), kind=kOutput, calls=%fused_computation.24 | convolution fusion | flops 548143104 | bytes 10504192 | tf_op jit(solution)/shard_map/gqk,gkd->gqd/dot_general | solution.py:23
  89.4 0.3 copy.29
  89.8 0.9 copy.35
  (21 shorter events, 0.2 us)
Async XLA Ops:
  6.5 16.8 %copy-start.1 = (s32[4]{0:T(128)S(1)}, s32[4]{0:T(128)}, u32[]{:S(2)}) copy-start(s32[4]{0:T(128)} %param.9) | copy-start | bytes 52
  6.5 15.6 %copy-start = (bf16[128,2048]{1,0:T(8,128)(2,1)S(1)}, bf16[128,2048]{1,0:T(8,128)(2,1)}, u32[]{:S(2)}) copy-start(bf16[128,2048]{1,0:T(8,128)(2,1)} %param.5) | copy-start | bytes 1572868
  15.5 32.0 %all-to-all-start = ((bf16[4,2,256,256]{3,2,1,0:T(8,128)(2,1)}), bf16[4,2,256,256]{3,2,1,0:T(8,128)(2,1)S(1)}, u32[]{:S(2)}, u32[]{:S(2)}) async-start(bf16[4,2,256,256]{3,2,1,0:T(8,128)(2,1)} %pad_maximum_fusion), calls=%async_computation | async-start | bytes 2097152 | tf_op jit(solution)/shard_map/all_to_all | solution.py:73
  21.8 54.3 %all-gather.3.cloned.1.call-start = ((), (), s32[]{:S(2)}) async-start(), calls=%async_computation.1 | async-start | bytes 1310720 | tf_op jit(solution)/shard_map/all_gather | solution.py:89
  77.4 4.5 %slice-start = ((s8[6291456]{0:T(1024)(128)(4,1)}), s8[4194304]{0:T(1024)(128)(4,1)S(1)}, s32[]{:S(2)}) async-start(s8[6291456]{0:T(1024)(128)(4,1)} %bitcast.87), calls=%async_computation.2 | async-start | bytes 8388608
  77.4 4.5 %slice-start.1 = ((s8[6291456]{0:T(1024)(128)(4,1)}), s8[2097152]{0:T(1024)(128)(4,1)S(1)}, s32[]{:S(2)}) async-start(s8[6291456]{0:T(1024)(128)(4,1)} %bitcast.87), calls=%async_computation.3 | async-start | bytes 4194304
Sparse Core Ops, SparseCore 0:
  49.1 27.0 all-gather.2

commit v2 on v1

--- a/solution.py
+++ b/solution.py
@@ -50,6 +50,8 @@
     )
     query_span = group_size * q_rows
 
+    new_all = lax.all_gather(kv_new.transpose(1, 0, 2), "blk", axis=0)
+
     page_owner = page_table // slots_dev
     owned = page_owner == myself
     page_rank = jnp.cumsum(owned.astype(jnp.int32)) - 1
@@ -66,11 +68,7 @@
     sent_pages = sent_pages.transpose(0, 2, 1, 3, 4).reshape(
         blocks, kv_heads, per_peer * page_len, 2 * head_size
     )
-    own_rows = jnp.broadcast_to(
-        kv_new.transpose(1, 0, 2)[None], (blocks, kv_heads, q_rows, 2 * head_size)
-    )
-    payload = jnp.concatenate([sent_pages, own_rows], axis=2)
-    received = lax.all_to_all(payload, "blk", split_axis=0, concat_axis=0, tiled=True)
+    received = lax.all_to_all(sent_pages, "blk", split_axis=0, concat_axis=0, tiled=True)
 
     page_part = received[:, :, : per_peer * page_len]
     page_part = page_part.reshape(blocks, kv_heads, per_peer, page_len, 2 * head_size)
@@ -91,8 +89,7 @@
         jnp.arange(pg, dtype=jnp.int32)[None, :] * blocks + block_ids[:, None] < npages
     ).reshape(-1)
 
-    new_rows = received[:, :, per_peer * page_len :]
-    new_rows = new_rows.transpose(1, 0, 2, 3).reshape(kv_heads, blocks * q_rows, 2 * head_size)
+    new_rows = new_all.transpose(1, 0, 2, 3).reshape(kv_heads, blocks * q_rows, 2 * head_size)
     own_pages = compact.transpose(1, 0, 2, 3).reshape(kv_heads, pg * page_len, 2 * head_size)
     entries_a = jnp.concatenate([new_rows, own_pages], axis=1)
     row_source = jnp.repeat(block_ids, q_rows)

time: 97.9 us -> 99.4 us (1.015)
  blocking collectives: 0 us -> 22.7 us
  waiting for transfers between devices: 45.4 us -> 23.1 us
  local copies, waits for them, and re-layouts: 9.17 us -> 10.9 us
    all_to_all x1, waiting for transfers between devices: 24.1 us -> 0.01 us  [local(): lax.all_to_all(sent_pages, 'blk', split_axis=0, concat_axis=0, tiled=True)]
    all_gather x0 -> x1, blocking collectives: none -> 22.7 us  [local(): new_all = lax.all_gather(kv_new.transpose(1, 0, 2), 'blk', axis=0)]
    unnamed x10 -> x7, local copies, waits for them, and re-layouts: 1.06 us -> 3.01 us
    all_gather x1, waiting for transfers between devices: 21.3 us -> 23 us  [local(): gathered = lax.all_gather(compact, 'blk', axis=0, tiled=True)]
    concatenate x1 -> x0, other arithmetic: 1.06 us -> none  [local(): payload = jnp.concatenate([sent_pages, own_rows], axis=2)]
  transfers between devices with their start and end apart: 2 -> 2, of which waited for: 2 -> 1; matrix products, arithmetic and copies ran while one was open for 7% -> 9% of each run, Pallas kernels for 0% -> 0%
where the time goes in v2:
time: 99.4 us; the launch traced here: 99 us
  waiting for transfers between devices  23.1 us (23%)
  blocking collectives  22.7 us (23%)
  between operations  14.3 us (14%)
  matrix products  11.7 us (12%)
  local copies, waits for them, and re-layouts  10.9 us (11%)
  other arithmetic  10.1 us (10%)
  starting transfers between devices  6.32 us (6%)
    all_gather x1, waiting for transfers between devices, local(): gathered = lax.all_gather(compact, 'blk', axis=0, tiled=True)  23 us
    all_gather x1, blocking collectives, local(): new_all = lax.all_gather(kv_new.transpose(1, 0, 2), 'blk', axis=0)  22.7 us
    all_to_all x1, starting transfers between devices, local(): lax.all_to_all(sent_pages, 'blk', split_axis=0, concat_axis=0, tiled=True)  6.32 us
    dot_general x2, matrix products, attend(): jnp.einsum('gqd,gkd->gqk', queries, keys, preferred_element_type=jnp.floa...  5.92 us
    dot_general x2, matrix products, attend(): jnp.einsum('gqk,gkd->gqd', weights.astype(jnp.bfloat16), values, preferre...  5.77 us
    reduce_sum x2, other arithmetic, attend(): totals = totals * factor + jnp.sum(weights, axis=2)  4.12 us
    gather x1, local copies, waits for them, and re-layouts, local(): kv_cache[chosen]  3.56 us
    unnamed x7, local copies, waits for them, and re-layouts  3.01 us
  transfers between devices with their start and end apart: 2, of which 1 were waited for; matrix products, arithmetic and copies ran while one was open for 9% of the time, Pallas kernels for 0%

profile of v2, /device:TPU:0, one launch (start us, length us, event | category | flops | bytes accessed | tf_op | source)
XLA Modules:
  0.0 99.0 jit_solution(9851125789988168862)
XLA Ops:
  6.5 0.7 and_select_fusion.3
  7.2 0.7 convert_bitcast_fusion
  7.9 0.2 reduce-window.21
  8.1 0.1 convert_reduce_fusion
  8.2 0.2 reduce-window.22
  8.3 1.4 %fusion.35 = (s32[]{:T(128)}, s32[]{:T(128)}) fusion(s32[4]{0:T(128)} %param.9, s32[]{:T(128)S(6)} %axis_index.15, s32[4]{0:T(128)S(1)} %convert_reduce_fusion, s32[4,1]{0,1:T(1,128)S(1)} %reduce-window.22), kind=kLoop, calls=%fused_computation.77 | loop fusion | flops 22 | bytes 60 | tf_op jit(solution)/shard_map/reduce_sum | solution.py:44
  9.7 0.7 and_select_fusion.4
  10.4 0.2 select_reduce_fusion.1
  10.6 3.6 %gather_fusion = bf16[4,2,128,256]{3,2,1,0:T(8,128)(2,1)} fusion(bf16[32,2,128,256]{3,2,1,0:T(8,128)(2,1)} %param.7, s32[1024]{0:T(1024)S(1)} %pad_clamp_fusion.1), kind=kCustom, calls=%fused_computation | custom fusion | bytes 1048592 | tf_op jit(solution)/shard_map/gather | solution.py:67
  14.1 6.3 %all-to-all-start = ((bf16[4,2,128,256]{3,2,1,0:T(8,128)(2,1)}), bf16[4,2,128,256]{3,2,1,0:T(8,128)(2,1)S(1)}, u32[]{:S(2)}, u32[]{:S(2)}) async-start(bf16[4,2,128,256]{3,2,1,0:T(8,128)(2,1)} %gather_fusion), calls=%async_computation | async-start | bytes 1048576 | tf_op jit(solution)/shard_map/all_to_all | solution.py:71
  20.5 0.0 all-gather.4.cloned.1.call-start
  20.5 0.1 broadcast_bitcast_fusion.2
  20.6 0.1 and.99
  21.4 0.2 reduce-window.23
  21.6 0.9 copy.36
  22.5 22.7 %all-gather = bf16[8,128,256]{2,1,0:T(8,128)(2,1)S(1)} all-gather(bf16[2,128,256]{2,1,0:T(8,128)(2,1)S(1)} %bitcast.101), channel_id=2, replica_groups=mesh['groups'=2,'blk'=4,'pool'=4] {'blk'}, dimensions={0}, use_global_device_ids=true | all-gather | bytes 655360 | tf_op jit(solution)/shard_map/all_gather | solution.py:53
  45.3 1.1 %copy.31 = bf16[16,8,16,128]{3,2,1,0:T(8,128)(2,1)S(1)} copy(bf16[16,8,16,128]{3,1,2,0:T(8,128)(2,1)} %bitcast.102) | data formatting | bytes 1048576
  46.4 0.1 copy.24
  46.6 0.1 fusion.33
  46.8 0.7 select_reduce_fusion
  47.5 0.0 all-to-all-done
  47.5 1.3 %gather_fusion.1 = bf16[2,2,128,256]{3,2,1,0:T(8,128)(2,1)} fusion(bf16[4,2,128,256]{3,2,1,0:T(8,128)(2,1)S(1)} %all-to-all-done, s32[1024]{0:T(1024)S(1)} %pad_clamp_fusion), kind=kCustom, calls=%fused_computation.1 | custom fusion | bytes 524296 | tf_op jit(solution)/shard_map/gather | solution.py:85
  48.8 0.0 all-gather.4.cloned.1.call-update
  48.8 0.1 broadcast_bitcast_fusion.1
  48.9 0.4 broadcast_compare_fusion
  49.2 0.4 pad_add_fusion
  49.7 1.0 copy.23
  50.6 4.0 %fusion.4 = (f32[2,1024]{1,0:T(2,128)S(1)}, f32[2,768,1024]{2,1,0:T(8,128)}) fusion(pred[1024,768]{0,1:T(8,128)(4,1)S(1)} %pad_add_fusion, bf16[2,1024,128]{2,1,0:T(8,128)(2,1)S(1)} %bitcast.95, bf16[2,512,256]{2,1,0:T(8,128)(2,1)S(1)} %bitcast.103, bf16[2,256,256]{2,1,0:T(8,128)(2,1)S(1)} %bitcast.106), kind=kOutput, calls=%fused_computation.11 | convolution fusion | flops 408156160 | bytes 8396800 | tf_op jit(solution)/shard_map/gqd,gkd->gqk/dot_general | solution.py:15
  54.7 23.0 %all-gather.4.cloned.1.call-done = bf16[8,2,128,256]{3,2,1,0:T(8,128)(2,1)} async-done(((bf16[2,2,128,256]{3,2,1,0:T(8,128)(2,1)}), bf16[8,2,128,256]{3,2,1,0:T(8,128)(2,1)}) %all-gather.4.cloned.1.call-update) | async-done | bytes 1048592 | tf_op jit(solution)/shard_map/all_gather | solution.py:87
  77.7 1.3 %copy.26 = bf16[2,8,128,256]{3,2,1,0:T(8,128)(2,1)S(1)} copy(bf16[2,8,128,256]{3,2,0,1:T(8,128)(2,1)} %bitcast.100) | data formatting | bytes 2097152 | tf_op jit(solution)/shard_map/transpose | solution.py:115
  79.0 0.0 slice-start
  79.0 0.0 slice-start.1
  79.0 1.9 %bitcast_reduce_fusion = (f32[2,1024]{1,0:T(2,128)S(1)}, f32[2,1024,1024]{2,1,0:T(8,128)S(1)}) fusion(pred[1024]{0:T(1024)(128)(4,1)S(1)} %broadcast_bitcast_fusion.1, bf16[2,1024,128]{2,1,0:T(8,128)(2,1)S(1)} %bitcast.96, bf16[2,1024,256]{2,1,0:T(8,128)(2,1)S(1)} %bitcast.92), kind=kOutput, calls=%fused_computation.3 | convolution fusion | flops 543160320 | bytes 9446400 | tf_op jit(solution)/shard_map/gqd,gkd->gqk/dot_general | solution.py:15
  80.9 2.5 %fusion.2 = f32[2,1024]{1,0:T(2,128)S(1)} fusion(f32[2,1024,1024]{2,1,0:T(8,128)S(1)} %get-tuple-element.16, f32[2,1024]{1,0:T(2,128)S(1)} %get-tuple-element.11, pred[1024]{0:T(1024)(128)(4,1)S(1)} %broadcast_bitcast_fusion.1), kind=kLoop, calls=%fused_computation.9 | loop fusion | flops 10483712 | bytes 8406016 | tf_op jit(solution)/shard_map/reduce_sum | solution.py:22
  83.4 0.0 slice-done
  83.4 0.0 slice-done.1
  83.5 1.7 %fusion.5 = f32[2,1024]{1,0:T(2,128)S(1)} fusion(f32[2,768,1024]{2,1,0:T(8,128)S(1)} %bitcast.91, f32[2,1024]{1,0:T(2,128)S(1)} %get-tuple-element.12, pred[1024,768]{0,1:T(8,128)(4,1)S(1)} %pad_add_fusion), kind=kLoop, calls=%fused_computation.12 | loop fusion | flops 7862272 | bytes 7094272 | tf_op jit(solution)/shard_map/reduce_sum | solution.py:22
  85.1 2.8 %fusion.20 = f32[2,1024,128]{2,1,0:T(8,128)S(1)} fusion(f32[2,768,1024]{2,1,0:T(8,128)S(1)} %bitcast.91, f32[2,1024]{1,0:T(2,128)S(1)} %get-tuple-element.12, pred[1024,768]{0,1:T(8,128)(4,1)S(1)} %pad_add_fusion, f32[2,1024]{1,0:T(2,128)S(1)} %get-tuple-element.6, f32[2,1024]{1,0:T(2,128)S(1)} %get-tuple-element.10, ...), kind=kOutput, calls=%fused_computation.22 | convolution fusion | flops 411828224 | bytes 8937472 | tf_op jit(solution)/shard_map/gqk,gkd->gqd/dot_general | solution.py:23
  88.0 3.0 %divide_convert_fusion = bf16[2,1024,128]{2,1,0:T(8,128)(2,1)S(1)} fusion(f32[2,1024,128]{2,1,0:T(8,128)S(1)} %fusion.20, f32[2,1024,1024]{2,1,0:T(8,128)S(1)} %get-tuple-element.16, f32[2,1024]{1,0:T(2,128)S(1)} %get-tuple-element.11, pred[1024]{0:T(1024)(128)(4,1)S(1)} %broadcast_bitcast_fusion.1, bf16[2,1024,256]{2,1,0:T(8,128)(2,1)S(1)} %bitcast.93, ...), kind=kOutput, calls=%fused_computation.23 | convolution fusion | flops 548143104 | bytes 10504192 | tf_op jit(solution)/shard_map/gqk,gkd->gqd/dot_general | solution.py:23
  90.9 0.3 copy.28
  91.3 0.9 copy.35
  (20 shorter events, 0.2 us)
Async XLA Ops:
  14.1 33.4 %all-to-all-start = ((bf16[4,2,128,256]{3,2,1,0:T(8,128)(2,1)}), bf16[4,2,128,256]{3,2,1,0:T(8,128)(2,1)S(1)}, u32[]{:S(2)}, u32[]{:S(2)}) async-start(bf16[4,2,128,256]{3,2,1,0:T(8,128)(2,1)} %gather_fusion), calls=%async_computation | async-start | bytes 1048576 | tf_op jit(solution)/shard_map/all_to_all | solution.py:71
  20.5 57.2 %all-gather.4.cloned.1.call-start = ((), (), s32[]{:S(2)}) async-start(), calls=%async_computation.1 | async-start | bytes 1310720 | tf_op jit(solution)/shard_map/all_gather | solution.py:87
  79.0 4.4 %slice-start = ((s8[6291456]{0:T(1024)(128)(4,1)}), s8[4194304]{0:T(1024)(128)(4,1)S(1)}, s32[]{:S(2)}) async-start(s8[6291456]{0:T(1024)(128)(4,1)} %bitcast.90), calls=%async_computation.2 | async-start | bytes 8388608
  79.0 4.4 %slice-start.1 = ((s8[6291456]{0:T(1024)(128)(4,1)}), s8[2097152]{0:T(1024)(128)(4,1)S(1)}, s32[]{:S(2)}) async-start(s8[6291456]{0:T(1024)(128)(4,1)} %bitcast.90), calls=%async_computation.3 | async-start | bytes 4194304
Sparse Core Ops, SparseCore 0:
  48.9 28.7 all-gather.3

commit v3 on v2

v3 whole, which is shorter than its diff:
```python
import functools
import math

import jax
import jax.numpy as jnp
from jax import lax
from jax.experimental import pallas as pl
from jax.experimental.pallas import tpu as pltpu
from jax.sharding import PartitionSpec as P

CAP = 4


def attention_kernel(
    new_mode, page_mode, q_ref, new_ref, page_ref, o_ref, qs_ref, m_ref, l_ref, acc_ref,
    *, group_size, q_rows, head_size,
):
    scale = 1.0 / math.sqrt(head_size)
    for h in range(group_size):
        qs_ref[h * q_rows : (h + 1) * q_rows, :] = q_ref[:, h * head_size : (h + 1) * head_size]
    m_ref[...] = jnp.full(m_ref.shape, -1e30, jnp.float32)
    l_ref[...] = jnp.zeros(l_ref.shape, jnp.float32)
    acc_ref[...] = jnp.zeros(acc_ref.shape, jnp.float32)

    def update(kv, causal):
        keys = kv[:, :head_size]
        values = kv[:, head_size:]
        scores = lax.dot_general(
            qs_ref[...], keys, (((1,), (1,)), ((), ())), preferred_element_type=jnp.float32
        ) * scale
        if causal:
            row = lax.broadcasted_iota(jnp.int32, scores.shape, 0) % q_rows
            col = lax.broadcasted_iota(jnp.int32, scores.shape, 1)
            visible = col <= row
            scores = jnp.where(visible, scores, -1e30)
        m_prev = m_ref[...]
        m_new = jnp.maximum(m_prev, jnp.max(scores, axis=1, keepdims=True))
        alpha = jnp.exp(m_prev - m_new)
        weights = jnp.exp(scores - m_new)
        if causal:
            weights = jnp.where(visible, weights, 0.0)
        l_ref[...] = alpha * l_ref[...] + jnp.sum(weights, axis=1, keepdims=True)
        acc_ref[...] = alpha * acc_ref[...] + lax.dot_general(
            weights.astype(jnp.bfloat16), values, (((1,), (0,)), ((), ())),
            preferred_element_type=jnp.float32,
        )
        m_ref[...] = m_new

    def new_step(c, carry):
        mode = new_mode[c]

        @pl.when(mode == 1)
        def _():
            update(new_ref[c, 0], False)

        @pl.when(mode == 2)
        def _():
            update(new_ref[c, 0], True)

        return carry

    def page_step(c, carry):
        @pl.when(page_mode[c] == 1)
        def _():
            update(page_ref[c, 0], False)

        return carry

    lax.fori_loop(0, new_ref.shape[0], new_step, 0)
    lax.fori_loop(0, page_ref.shape[0], page_step, 0)
    result = (acc_ref[...] / l_ref[...]).astype(o_ref.dtype)
    for h in range(group_size):
        o_ref[:, h * head_size : (h + 1) * head_size] = result[h * q_rows : (h + 1) * q_rows, :]


def attention(new_mode, page_mode, q_new, new_all, pages, group_size, head_size):
    q_rows = q_new.shape[0]
    blocks, kv_heads, new_len, width = new_all.shape
    npage, _, page_len, _ = pages.shape
    rows = group_size * q_rows
    kernel = functools.partial(
        attention_kernel, group_size=group_size, q_rows=q_rows, head_size=head_size
    )
    return pl.pallas_call(
        kernel,
        out_shape=jax.ShapeDtypeStruct(q_new.shape, q_new.dtype),
        grid_spec=pltpu.PrefetchScalarGridSpec(
            num_scalar_prefetch=2,
            grid=(kv_heads,),
            in_specs=[
                pl.BlockSpec((q_rows, group_size * head_size), lambda g, a, b: (0, g)),
                pl.BlockSpec((blocks, 1, new_len, width), lambda g, a, b: (0, g, 0, 0)),
                pl.BlockSpec((npage, 1, page_len, width), lambda g, a, b: (0, g, 0, 0)),
            ],
            out_specs=pl.BlockSpec((q_rows, group_size * head_size), lambda g, a, b: (0, g)),
            scratch_shapes=[
                pltpu.VMEM((rows, head_size), jnp.bfloat16),
                pltpu.VMEM((rows, 1), jnp.float32),
                pltpu.VMEM((rows, 1), jnp.float32),
                pltpu.VMEM((rows, head_size), jnp.float32),
            ],
        ),
    )(new_mode, page_mode, q_new, new_all, pages)


def local(q_new, kv_new, kv_cache, page_table, block_offsets):
    kv_heads = kv_new.shape[1]
    head_size = kv_new.shape[2] // 2
    group_size = q_new.shape[1] // (head_size * kv_heads)
    slots_dev = kv_cache.shape[0]
    npages = page_table.shape[0]
    blocks = lax.axis_size("blk")
    myself = lax.axis_index("blk")
    pg = -(-npages // blocks)
    block_ids = jnp.arange(blocks, dtype=jnp.int32)
    my_offset = jnp.sum(jnp.where(block_ids == myself, block_offsets, 0))

    new_all = lax.all_gather(kv_new.transpose(1, 0, 2), "blk", axis=0)

    page_owner = page_table // slots_dev
    owned = page_owner == myself
    page_rank = jnp.cumsum(owned.astype(jnp.int32)) - 1
    local_slot = page_table % slots_dev
    counts = jnp.sum((page_owner[None, :] == block_ids[:, None]).astype(jnp.int32), axis=1)
    per_peer = (CAP + blocks - 1) // blocks
    starts = jnp.cumsum(counts) - counts
    my_start = jnp.sum(jnp.where(block_ids == myself, starts, 0))
    peer_slots = jnp.arange(per_peer, dtype=jnp.int32)[None, :]
    wanted = (block_ids[:, None] - my_start) % blocks + peer_slots * blocks
    picked = owned[None, None, :] & (page_rank[None, None, :] == wanted[..., None])
    chosen = jnp.sum(jnp.where(picked, local_slot[None, None, :], 0), axis=2).reshape(-1)
    received = lax.all_to_all(kv_cache[chosen], "blk", split_axis=0, concat_axis=0, tiled=True)
    arriving = (myself - starts[:, None]) % blocks + peer_slots * blocks
    present = (arriving < counts[:, None]).reshape(-1)
    order_rank = jnp.cumsum(present.astype(jnp.int32)) - 1
    choose = present[None, :] & (order_rank[None, :] == jnp.arange(pg, dtype=jnp.int32)[:, None])
    positions = jnp.sum(
        jnp.where(choose, jnp.arange(blocks * per_peer, dtype=jnp.int32)[None, :], 0), axis=1
    )
    gathered = lax.all_gather(received[positions], "blk", axis=0, tiled=True)

    new_mode = jnp.where(
        block_offsets < my_offset, 1, jnp.where(block_offsets == my_offset, 2, 0)
    ).astype(jnp.int32)
    page_mode = (
        jnp.arange(pg, dtype=jnp.int32)[None, :] * blocks + block_ids[:, None] < npages
    ).reshape(-1).astype(jnp.int32)
    return attention(new_mode, page_mode, q_new, new_all, gathered, group_size, head_size)


def solution(mesh):
    return jax.shard_map(
        local,
        mesh=mesh,
        in_specs=(
            P(("groups", "blk"), "pool"),
            P(("groups", "blk"), "pool", None),
            P(("groups", "blk"), "pool", None, None),
            P("groups"),
            P("groups"),
        ),
        out_specs=P(("groups", "blk"), "pool"),
        check_vma=False,
    )
```

time: 99.4 us -> 114 us (1.15); the launches traced: 99 us -> 115 us
  Pallas kernels: 0 us -> 40 us
  matrix products: 11.7 us -> 0 us
  local copies, waits for them, and re-layouts: 10.9 us -> 6.37 us
  other arithmetic: 10.1 us -> 6.85 us
  blocking collectives: 22.7 us -> 20 us
  waiting for transfers between devices: 23.1 us -> 21.9 us
    pallas_call x0 -> x1, Pallas kernels: none -> 40 us  [attention(): pl.pallas_call(kernel, out_shape=jax.ShapeDtypeStruct(q_new.shape, q_new....]
    all_gather x1, waiting for transfers between devices: 23 us -> 7.75 us  [local(): gathered = lax.all_gather(received[positions], 'blk', axis=0, tiled=True)]
    all_to_all x1, waiting for transfers between devices: 0.01 us -> 14.1 us  [local(): lax.all_to_all(kv_cache[chosen], 'blk', split_axis=0, concat_axis=0, tile...]
    dot_general x4 -> x0, matrix products: 11.7 us -> none  [the longest x2 5.92 us: attend(): jnp.einsum('gqd,gkd->gqk', queries, keys, preferred_element_type=jnp.floa...]
    reduce_sum x3 -> x1, other arithmetic: 4.87 us -> 0.64 us  [local(): my_start = jnp.sum(jnp.where(block_ids == myself, starts, 0))]
    transpose x4 -> x0, local copies, waits for them, and re-layouts: 2.74 us -> none  [the longest x1 1.29 us: local(): gathered.transpose(1, 0, 2, 3)]
    all_gather x1, blocking collectives: 22.7 us -> 20 us  [local(): new_all = lax.all_gather(kv_new.transpose(1, 0, 2), 'blk', axis=0)]
    unnamed x7 -> x1, local copies, waits for them, and re-layouts: 3.01 us -> 0.92 us
  transfers between devices with their start and end apart: 2 -> 2, of which waited for: 1 -> 2; matrix products, arithmetic and copies ran while one was open for 9% -> 4% of each run, Pallas kernels for 0% -> 0%
where the time goes in v3:
time: 114 us; the launch traced here: 115 us
  Pallas kernels  40 us (35%)
  waiting for transfers between devices  21.9 us (19%)
  blocking collectives  20 us (18%)
  between operations  13.4 us (12%)
  other arithmetic  6.85 us (6%)
  local copies, waits for them, and re-layouts  6.37 us (6%)
  starting transfers between devices  6.32 us (6%)
    pallas_call x1, Pallas kernels, attention(): pl.pallas_call(kernel, out_shape=jax.ShapeDtypeStruct(q_new.shape, q_new....  40 us
    all_gather x1, blocking collectives, local(): new_all = lax.all_gather(kv_new.transpose(1, 0, 2), 'blk', axis=0)  20 us
    all_to_all x1, waiting for transfers between devices, local(): lax.all_to_all(kv_cache[chosen], 'blk', split_axis=0, concat_axis=0, tile...  14.1 us
    all_gather x1, waiting for transfers between devices, local(): gathered = lax.all_gather(received[positions], 'blk', axis=0, tiled=True)  7.75 us
    all_to_all x1, starting transfers between devices, local(): lax.all_to_all(kv_cache[chosen], 'blk', split_axis=0, concat_axis=0, tile...  6.32 us
    gather x1, local copies, waits for them, and re-layouts, local(): kv_cache[chosen]  3.56 us
  transfers between devices with their start and end apart: 2, of which 2 were waited for; matrix products, arithmetic and copies ran while one was open for 4% of the time, Pallas kernels for 0%

profile of v3, /device:TPU:0, one launch (start us, length us, event | category | flops | bytes accessed | tf_op | source)
XLA Modules:
  0.0 114.9 jit_solution(13940887736073317027)
XLA Ops:
  6.5 0.7 and_select_fusion.3
  7.2 0.7 convert_bitcast_fusion
  7.9 0.2 reduce-window.21
  8.1 0.1 convert_reduce_fusion
  8.2 0.2 reduce-window.22
  8.3 0.6 fusion.4
  9.0 0.7 and_select_fusion.4
  9.6 0.2 select_reduce_fusion
  9.8 3.6 %gather_fusion = bf16[4,2,128,256]{3,2,1,0:T(8,128)(2,1)} fusion(bf16[32,2,128,256]{3,2,1,0:T(8,128)(2,1)} %param.7, s32[1024]{0:T(1024)S(1)} %pad_clamp_fusion.1), kind=kCustom, calls=%fused_computation | custom fusion | bytes 1048592 | tf_op jit(solution)/shard_map/gather | solution.py:132
  13.4 6.3 %all-to-all-start = ((bf16[4,2,128,256]{3,2,1,0:T(8,128)(2,1)}), bf16[4,2,128,256]{3,2,1,0:T(8,128)(2,1)S(1)}, u32[]{:S(2)}, u32[]{:S(2)}) async-start(bf16[4,2,128,256]{3,2,1,0:T(8,128)(2,1)} %gather_fusion), calls=%async_computation | async-start | bytes 1048576 | tf_op jit(solution)/shard_map/all_to_all | solution.py:132
  19.7 0.0 all-gather.4.cloned.1.call-start
  19.7 0.2 reduce-window.23
  19.9 0.1 fusion.1
  20.1 14.1 %all-to-all-done = bf16[4,2,128,256]{3,2,1,0:T(8,128)(2,1)S(1)} async-done(((bf16[4,2,128,256]{3,2,1,0:T(8,128)(2,1)}), bf16[4,2,128,256]{3,2,1,0:T(8,128)(2,1)S(1)}, u32[]{:S(2)}, u32[]{:S(2)}) %all-to-all-start) | async-done | bytes 524320 | tf_op jit(solution)/shard_map/all_to_all | solution.py:132
  34.2 1.3 %gather_fusion.1 = bf16[2,2,128,256]{3,2,1,0:T(8,128)(2,1)} fusion(bf16[4,2,128,256]{3,2,1,0:T(8,128)(2,1)S(1)} %all-to-all-done, s32[1024]{0:T(1024)S(1)} %pad_clamp_fusion), kind=kCustom, calls=%fused_computation.1 | custom fusion | bytes 524296 | tf_op jit(solution)/shard_map/gather | solution.py:140
  35.5 0.0 all-gather.4.cloned.1.call-update
  35.5 0.6 reshape.303.page_mode
  36.2 0.9 copy.11
  37.1 1.3 %fusion.3 = s32[]{:T(128)} fusion(s32[4]{0:T(128)} %param.9, s32[]{:T(128)S(6)} %axis_index.15), kind=kLoop, calls=%fused_computation.34 | loop fusion | flops 11 | bytes 24 | tf_op jit(solution)/shard_map/reduce_sum | solution.py:116
  38.4 20.0 %all-gather = bf16[8,128,256]{2,1,0:T(8,128)(2,1)} all-gather(bf16[2,128,256]{2,1,0:T(8,128)(2,1)S(1)} %bitcast.27), channel_id=2, replica_groups=mesh['groups'=2,'blk'=4,'pool'=4] {'blk'}, dimensions={0}, use_global_device_ids=true | all-gather | bytes 655360 | tf_op jit(solution)/shard_map/all_gather | solution.py:118
  58.4 1.9 %compare_select_fusion.9.new_mode = s32[4]{0:T(128)} fusion(s32[4]{0:T(128)} %param.9, s32[]{:T(128)} %fusion.3), kind=kLoop, calls=%fused_computation.26 | loop fusion | flops 16 | bytes 36 | tf_op jit(solution)/shard_map/jit(_where)/select_n | solution.py:142
  60.3 7.8 %all-gather.4.cloned.1.call-done.page_ref = bf16[8,2,128,256]{3,2,1,0:T(8,128)(2,1)} async-done(((bf16[2,2,128,256]{3,2,1,0:T(8,128)(2,1)}), bf16[8,2,128,256]{3,2,1,0:T(8,128)(2,1)}) %all-gather.4.cloned.1.call-update) | async-done | bytes 1048592 | tf_op jit(solution)/shard_map/all_gather | solution.py:140
  68.1 40.0 %shard_map.55 = bf16[128,2048]{1,0:T(8,128)(2,1)} custom-call(s32[4]{0:T(128)} %compare_select_fusion.9.new_mode, s32[8]{0:T(128)} %reshape.303.page_mode, bf16[128,2048]{1,0:T(8,128)(2,1)} %q_ref.1, bf16[4,2,128,256]{3,2,1,0:T(8,128)(2,1)} %bitcast.26, bf16[8,2,128,256]{3,2,1,0:T(8,128)(2,1)} %all-gather.4.cloned.1.call-done.page_ref), custom_call_target="tpu_custom_call" | custom-call | tf_op jit(solution)/shard_map/pallas_call | solution.py:84
  (10 shorter events, 0.1 us)
Async XLA Ops:
  13.4 20.8 %all-to-all-start = ((bf16[4,2,128,256]{3,2,1,0:T(8,128)(2,1)}), bf16[4,2,128,256]{3,2,1,0:T(8,128)(2,1)S(1)}, u32[]{:S(2)}, u32[]{:S(2)}) async-start(bf16[4,2,128,256]{3,2,1,0:T(8,128)(2,1)} %gather_fusion), calls=%async_computation | async-start | bytes 1048576 | tf_op jit(solution)/shard_map/all_to_all | solution.py:132
  19.7 48.3 %all-gather.4.cloned.1.call-start = ((), (), s32[]{:S(2)}) async-start(), calls=%async_computation.1 | async-start | bytes 1310720 | tf_op jit(solution)/shard_map/all_gather | solution.py:140
Sparse Core Ops, SparseCore 0:
  35.6 32.3 all-gather.3

commit v4 on v3

v4 whole, which is shorter than its diff:
```python
import functools
import math

import jax
import jax.numpy as jnp
from jax import lax
from jax.experimental import pallas as pl
from jax.experimental.pallas import tpu as pltpu
from jax.sharding import PartitionSpec as P

CAP = 4


def attention_kernel(
    query_start, q_ref, new_ref, page_ref, key_pos_ref, page_ok_ref, o_ref, *, head_size
):
    scale = 1.0 / math.sqrt(head_size)
    queries = q_ref[...]
    new_kv = new_ref[:, 0].reshape(-1, new_ref.shape[-1])
    page_kv = page_ref[:, 0].reshape(-1, page_ref.shape[-1])
    dims = (((1,), (1,)), ((), ()))
    new_scores = lax.dot_general(
        queries, new_kv[:, :head_size], dims, preferred_element_type=jnp.float32
    ) * scale
    page_scores = lax.dot_general(
        queries, page_kv[:, :head_size], dims, preferred_element_type=jnp.float32
    ) * scale
    row_pos = query_start[0] + lax.broadcasted_iota(jnp.int32, new_scores.shape, 0)
    new_visible = key_pos_ref[...] <= row_pos
    page_visible = page_ok_ref[...] > 0
    new_scores = jnp.where(new_visible, new_scores, -1e30)
    page_scores = jnp.where(page_visible, page_scores, -1e30)
    row_top = jnp.maximum(
        jnp.max(new_scores, axis=1, keepdims=True), jnp.max(page_scores, axis=1, keepdims=True)
    )
    new_weights = jnp.where(new_visible, jnp.exp(new_scores - row_top), 0.0)
    page_weights = jnp.where(page_visible, jnp.exp(page_scores - row_top), 0.0)
    row_total = jnp.sum(new_weights, axis=1, keepdims=True) + jnp.sum(
        page_weights, axis=1, keepdims=True
    )
    pv = (((1,), (0,)), ((), ()))
    summed = lax.dot_general(
        new_weights.astype(jnp.bfloat16), new_kv[:, head_size:], pv,
        preferred_element_type=jnp.float32,
    ) + lax.dot_general(
        page_weights.astype(jnp.bfloat16), page_kv[:, head_size:], pv,
        preferred_element_type=jnp.float32,
    )
    o_ref[...] = (summed / row_total).astype(o_ref.dtype)


def attention(query_start, key_pos, page_ok, q_new, new_all, pages, group_size, head_size):
    q_rows = q_new.shape[0]
    blocks, kv_heads, new_len, width = new_all.shape
    npage, _, page_len, _ = pages.shape
    kernel = functools.partial(attention_kernel, head_size=head_size)
    return pl.pallas_call(
        kernel,
        out_shape=jax.ShapeDtypeStruct(q_new.shape, q_new.dtype),
        grid_spec=pltpu.PrefetchScalarGridSpec(
            num_scalar_prefetch=1,
            grid=(kv_heads, group_size),
            in_specs=[
                pl.BlockSpec((q_rows, head_size), lambda g, h, s: (0, g * group_size + h)),
                pl.BlockSpec((blocks, 1, new_len, width), lambda g, h, s: (0, g, 0, 0)),
                pl.BlockSpec((npage, 1, page_len, width), lambda g, h, s: (0, g, 0, 0)),
                pl.BlockSpec((1, blocks * new_len), lambda g, h, s: (0, 0)),
                pl.BlockSpec((1, npage * page_len), lambda g, h, s: (0, 0)),
            ],
            out_specs=pl.BlockSpec((q_rows, head_size), lambda g, h, s: (0, g * group_size + h)),
        ),
    )(query_start, q_new, new_all, pages, key_pos, page_ok)


def local(q_new, kv_new, kv_cache, page_table, block_offsets):
    kv_heads = kv_new.shape[1]
    head_size = kv_new.shape[2] // 2
    group_size = q_new.shape[1] // (head_size * kv_heads)
    slots_dev = kv_cache.shape[0]
    npages = page_table.shape[0]
    blocks = lax.axis_size("blk")
    myself = lax.axis_index("blk")
    pg = -(-npages // blocks)
    block_ids = jnp.arange(blocks, dtype=jnp.int32)
    my_offset = jnp.sum(jnp.where(block_ids == myself, block_offsets, 0))

    new_all = lax.all_gather(kv_new.transpose(1, 0, 2), "blk", axis=0)

    page_owner = page_table // slots_dev
    owned = page_owner == myself
    page_rank = jnp.cumsum(owned.astype(jnp.int32)) - 1
    local_slot = page_table % slots_dev
    counts = jnp.sum((page_owner[None, :] == block_ids[:, None]).astype(jnp.int32), axis=1)
    per_peer = (CAP + blocks - 1) // blocks
    starts = jnp.cumsum(counts) - counts
    my_start = jnp.sum(jnp.where(block_ids == myself, starts, 0))
    peer_slots = jnp.arange(per_peer, dtype=jnp.int32)[None, :]
    wanted = (block_ids[:, None] - my_start) % blocks + peer_slots * blocks
    picked = owned[None, None, :] & (page_rank[None, None, :] == wanted[..., None])
    chosen = jnp.sum(jnp.where(picked, local_slot[None, None, :], 0), axis=2).reshape(-1)
    received = lax.all_to_all(kv_cache[chosen], "blk", split_axis=0, concat_axis=0, tiled=True)
    arriving = (myself - starts[:, None]) % blocks + peer_slots * blocks
    present = (arriving < counts[:, None]).reshape(-1)
    order_rank = jnp.cumsum(present.astype(jnp.int32)) - 1
    choose = present[None, :] & (order_rank[None, :] == jnp.arange(pg, dtype=jnp.int32)[:, None])
    positions = jnp.sum(
        jnp.where(choose, jnp.arange(blocks * per_peer, dtype=jnp.int32)[None, :], 0), axis=1
    )
    gathered = lax.all_gather(received[positions], "blk", axis=0, tiled=True)

    q_rows = q_new.shape[0]
    page_len = kv_cache.shape[2]
    query_start = (my_offset * q_rows).reshape(1).astype(jnp.int32)
    key_pos = (
        jnp.repeat(block_offsets, q_rows) * q_rows
        + jnp.tile(jnp.arange(q_rows, dtype=jnp.int32), blocks)
    ).reshape(1, -1).astype(jnp.int32)
    page_ok = (
        jnp.arange(pg, dtype=jnp.int32)[None, :] * blocks + block_ids[:, None] < npages
    ).reshape(-1)
    page_ok = jnp.repeat(page_ok.astype(jnp.int32), page_len).reshape(1, -1)
    return attention(
        query_start, key_pos, page_ok, q_new, new_all, gathered, group_size, head_size
    )


def solution(mesh):
    return jax.shard_map(
        local,
        mesh=mesh,
        in_specs=(
            P(("groups", "blk"), "pool"),
            P(("groups", "blk"), "pool", None),
            P(("groups", "blk"), "pool", None, None),
            P("groups"),
            P("groups"),
        ),
        out_specs=P(("groups", "blk"), "pool"),
        check_vma=False,
    )
```

time: 114 us -> 90.2 us (0.79); the launches traced: 115 us -> 88.9 us
  Pallas kernels: 40 us -> 13.7 us
  other arithmetic: 6.85 us -> 5.05 us
  waiting for transfers between devices: 21.9 us -> 23.1 us
    pallas_call x1, Pallas kernels: 40 us -> 13.7 us  [attention(): pl.pallas_call(kernel, out_shape=jax.ShapeDtypeStruct(q_new.shape, q_new....]
    reduce_sum x2 -> x0, other arithmetic: 1.95 us -> none  [the longest x1 1.32 us: local(): my_offset = jnp.sum(jnp.where(block_ids == myself, block_offsets, 0))]
    select_n x1 -> x0, other arithmetic: 1.87 us -> none  [local(): jnp.where(block_offsets < my_offset, 1, jnp.where(block_offsets == my_off...]
    mul x0 -> x1, other arithmetic: none -> 1.37 us  [local(): jnp.repeat(block_offsets, q_rows) * q_rows]
    all_gather x1, waiting for transfers between devices: 7.75 us -> 8.97 us  [local(): gathered = lax.all_gather(received[positions], 'blk', axis=0, tiled=True)]
  transfers between devices with their start and end apart: 2 -> 2, of which waited for: 2 -> 2; matrix products, arithmetic and copies ran while one was open for 4% -> 2% of each run, Pallas kernels for 0% -> 0%
where the time goes in v4:
time: 90.2 us; the launch traced here: 88.9 us
  waiting for transfers between devices  23.1 us (26%)
  blocking collectives  20.1 us (22%)
  between operations  14.1 us (16%)
  Pallas kernels  13.7 us (15%)
  local copies, waits for them, and re-layouts  6.49 us (7%)
  starting transfers between devices  6.32 us (7%)
  other arithmetic  5.05 us (6%)
    all_gather x1, blocking collectives, local(): new_all = lax.all_gather(kv_new.transpose(1, 0, 2), 'blk', axis=0)  20.1 us
    all_to_all x1, waiting for transfers between devices, local(): lax.all_to_all(kv_cache[chosen], 'blk', split_axis=0, concat_axis=0, tile...  14.1 us
    pallas_call x1, Pallas kernels, attention(): pl.pallas_call(kernel, out_shape=jax.ShapeDtypeStruct(q_new.shape, q_new....  13.7 us
    all_gather x1, waiting for transfers between devices, local(): gathered = lax.all_gather(received[positions], 'blk', axis=0, tiled=True)  8.97 us
    all_to_all x1, starting transfers between devices, local(): lax.all_to_all(kv_cache[chosen], 'blk', split_axis=0, concat_axis=0, tile...  6.32 us
    gather x1, local copies, waits for them, and re-layouts, local(): kv_cache[chosen]  3.56 us
  transfers between devices with their start and end apart: 2, of which 2 were waited for; matrix products, arithmetic and copies ran while one was open for 2% of the time, Pallas kernels for 0%

profile of v4, /device:TPU:0, one launch (start us, length us, event | category | flops | bytes accessed | tf_op | source)
XLA Modules:
  0.0 88.9 jit_solution(5372364631292451424)
XLA Ops:
  6.5 0.7 and_select_fusion.3
  7.2 0.7 convert_bitcast_fusion
  7.9 0.2 reduce-window.21
  8.1 0.1 convert_reduce_fusion
  8.2 0.2 reduce-window.22
  8.3 1.4 %broadcast_multiply_fusion = (s32[4]{0:T(128)S(1)}, s32[]{:T(128)}, s32[]{:T(128)}) fusion(s32[4]{0:T(128)} %param.9, s32[]{:T(128)S(6)} %axis_index.15, s32[4]{0:T(128)S(1)} %convert_reduce_fusion, s32[4,1]{0,1:T(1,128)S(1)} %reduce-window.22), kind=kLoop, calls=%fused_computation.45 | loop fusion | flops 26 | bytes 76 | tf_op jit(solution)/shard_map/mul | solution.py:115
  9.7 0.7 and_select_fusion.4
  10.4 0.2 select_reduce_fusion
  10.6 3.6 %gather_fusion = bf16[4,2,128,256]{3,2,1,0:T(8,128)(2,1)} fusion(bf16[32,2,128,256]{3,2,1,0:T(8,128)(2,1)} %param.7, s32[1024]{0:T(1024)S(1)} %pad_clamp_fusion.1), kind=kCustom, calls=%fused_computation | custom fusion | bytes 1048592 | tf_op jit(solution)/shard_map/gather | solution.py:101
  14.1 6.3 %all-to-all-start = ((bf16[4,2,128,256]{3,2,1,0:T(8,128)(2,1)}), bf16[4,2,128,256]{3,2,1,0:T(8,128)(2,1)S(1)}, u32[]{:S(2)}, u32[]{:S(2)}) async-start(bf16[4,2,128,256]{3,2,1,0:T(8,128)(2,1)} %gather_fusion), calls=%async_computation | async-start | bytes 1048576 | tf_op jit(solution)/shard_map/all_to_all | solution.py:101
  20.5 0.0 all-gather.4.cloned.1.call-start
  20.5 0.2 reduce-window.23
  20.7 0.1 fusion.1
  20.8 14.1 %all-to-all-done = bf16[4,2,128,256]{3,2,1,0:T(8,128)(2,1)S(1)} async-done(((bf16[4,2,128,256]{3,2,1,0:T(8,128)(2,1)}), bf16[4,2,128,256]{3,2,1,0:T(8,128)(2,1)S(1)}, u32[]{:S(2)}, u32[]{:S(2)}) %all-to-all-start) | async-done | bytes 524320 | tf_op jit(solution)/shard_map/all_to_all | solution.py:101
  35.0 1.3 %gather_fusion.1 = bf16[2,2,128,256]{3,2,1,0:T(8,128)(2,1)} fusion(bf16[4,2,128,256]{3,2,1,0:T(8,128)(2,1)S(1)} %all-to-all-done, s32[1024]{0:T(1024)S(1)} %pad_clamp_fusion), kind=kCustom, calls=%fused_computation.1 | custom fusion | bytes 524296 | tf_op jit(solution)/shard_map/gather | solution.py:109
  36.2 0.0 all-gather.4.cloned.1.call-update
  36.3 0.1 reshape.333
  36.4 0.9 %copy.11 = bf16[128,2,256]{2,0,1:T(8,128)(2,1)S(1)} copy(bf16[128,2,256]{2,1,0:T(2,128)(2,1)} %param.6) | data formatting | bytes 262144 | tf_op args[1]
  38.0 20.1 %all-gather = bf16[8,128,256]{2,1,0:T(8,128)(2,1)} all-gather(bf16[2,128,256]{2,1,0:T(8,128)(2,1)S(1)} %bitcast.30), channel_id=2, replica_groups=mesh['groups'=2,'blk'=4,'pool'=4] {'blk'}, dimensions={0}, use_global_device_ids=true | all-gather | bytes 655360 | tf_op jit(solution)/shard_map/all_gather | solution.py:87
  58.0 0.6 iota_add_fusion
  58.7 9.0 %all-gather.4.cloned.1.call-done.page_ref = bf16[8,2,128,256]{3,2,1,0:T(8,128)(2,1)} async-done(((bf16[2,2,128,256]{3,2,1,0:T(8,128)(2,1)}), bf16[8,2,128,256]{3,2,1,0:T(8,128)(2,1)}) %all-gather.4.cloned.1.call-update) | async-done | bytes 1048592 | tf_op jit(solution)/shard_map/all_gather | solution.py:109
  67.7 0.7 broadcast_in_dim.60
  68.3 13.7 %shard_map.55 = bf16[128,2048]{1,0:T(8,128)(2,1)} custom-call(s32[1]{0:T(128)} %bitcast.query_start, bf16[128,2048]{1,0:T(8,128)(2,1)} %q_ref.1, bf16[4,2,128,256]{3,2,1,0:T(8,128)(2,1)} %bitcast.29, bf16[8,2,128,256]{3,2,1,0:T(8,128)(2,1)} %all-gather.4.cloned.1.call-done.page_ref, s32[1,512]{1,0:T(1,128)} %bitcast.32, s32[1,1024]{1,0:T(1,128)} %bitcast.31), custom_call_target="tpu_custom_call" | custom-call | tf_op jit(solution)/shard_map/pallas_call | solution.py:57
  (10 shorter events, 0.1 us)
Async XLA Ops:
  14.1 20.8 %all-to-all-start = ((bf16[4,2,128,256]{3,2,1,0:T(8,128)(2,1)}), bf16[4,2,128,256]{3,2,1,0:T(8,128)(2,1)S(1)}, u32[]{:S(2)}, u32[]{:S(2)}) async-start(bf16[4,2,128,256]{3,2,1,0:T(8,128)(2,1)} %gather_fusion), calls=%async_computation | async-start | bytes 1048576 | tf_op jit(solution)/shard_map/all_to_all | solution.py:101
  20.5 47.2 %all-gather.4.cloned.1.call-start = ((), (), s32[]{:S(2)}) async-start(), calls=%async_computation.1 | async-start | bytes 1310720 | tf_op jit(solution)/shard_map/all_gather | solution.py:109
Sparse Core Ops, SparseCore 0:
  36.4 31.2 all-gather.3

commit v5 on v4

--- a/solution.py
+++ b/solution.py
@@ -12,62 +12,75 @@
 
 
 def attention_kernel(
-    query_start, q_ref, new_ref, page_ref, key_pos_ref, page_ok_ref, o_ref, *, head_size
+    query_start, q_ref, new_ref, page_ref, key_pos_ref, page_ok_ref, o_ref,
+    *, head_size, group_size, mask_pages,
 ):
     scale = 1.0 / math.sqrt(head_size)
-    queries = q_ref[...]
+    q_rows = q_ref.shape[0]
     new_kv = new_ref[:, 0].reshape(-1, new_ref.shape[-1])
     page_kv = page_ref[:, 0].reshape(-1, page_ref.shape[-1])
-    dims = (((1,), (1,)), ((), ()))
-    new_scores = lax.dot_general(
-        queries, new_kv[:, :head_size], dims, preferred_element_type=jnp.float32
-    ) * scale
-    page_scores = lax.dot_general(
-        queries, page_kv[:, :head_size], dims, preferred_element_type=jnp.float32
-    ) * scale
-    row_pos = query_start[0] + lax.broadcasted_iota(jnp.int32, new_scores.shape, 0)
+    new_keys = new_kv[:, :head_size]
+    new_values = new_kv[:, head_size:]
+    page_keys = page_kv[:, :head_size]
+    page_values = page_kv[:, head_size:]
+    row_pos = query_start[0] + lax.broadcasted_iota(jnp.int32, (q_rows, new_kv.shape[0]), 0)
     new_visible = key_pos_ref[...] <= row_pos
     page_visible = page_ok_ref[...] > 0
-    new_scores = jnp.where(new_visible, new_scores, -1e30)
-    page_scores = jnp.where(page_visible, page_scores, -1e30)
-    row_top = jnp.maximum(
-        jnp.max(new_scores, axis=1, keepdims=True), jnp.max(page_scores, axis=1, keepdims=True)
-    )
-    new_weights = jnp.where(new_visible, jnp.exp(new_scores - row_top), 0.0)
-    page_weights = jnp.where(page_visible, jnp.exp(page_scores - row_top), 0.0)
-    row_total = jnp.sum(new_weights, axis=1, keepdims=True) + jnp.sum(
-        page_weights, axis=1, keepdims=True
-    )
+    dims = (((1,), (1,)), ((), ()))
     pv = (((1,), (0,)), ((), ()))
-    summed = lax.dot_general(
-        new_weights.astype(jnp.bfloat16), new_kv[:, head_size:], pv,
-        preferred_element_type=jnp.float32,
-    ) + lax.dot_general(
-        page_weights.astype(jnp.bfloat16), page_kv[:, head_size:], pv,
-        preferred_element_type=jnp.float32,
-    )
-    o_ref[...] = (summed / row_total).astype(o_ref.dtype)
+    for h in range(group_size):
+        queries = q_ref[:, h * head_size : (h + 1) * head_size]
+        new_scores = lax.dot_general(
+            queries, new_keys, dims, preferred_element_type=jnp.float32
+        ) * scale
+        page_scores = lax.dot_general(
+            queries, page_keys, dims, preferred_element_type=jnp.float32
+        ) * scale
+        new_scores = jnp.where(new_visible, new_scores, -1e30)
+        if mask_pages:
+            page_scores = jnp.where(page_visible, page_scores, -1e30)
+        row_top = jnp.maximum(
+            jnp.max(new_scores, axis=1, keepdims=True),
+            jnp.max(page_scores, axis=1, keepdims=True),
+        )
+        new_weights = jnp.exp(new_scores - row_top)
+        page_weights = jnp.exp(page_scores - row_top)
+        row_total = jnp.sum(new_weights, axis=1, keepdims=True) + jnp.sum(
+            page_weights, axis=1, keepdims=True
+        )
+        summed = lax.dot_general(
+            new_weights.astype(jnp.bfloat16), new_values, pv,
+            preferred_element_type=jnp.float32,
+        ) + lax.dot_general(
+            page_weights.astype(jnp.bfloat16), page_values, pv,
+            preferred_element_type=jnp.float32,
+        )
+        o_ref[:, h * head_size : (h + 1) * head_size] = (summed / row_total).astype(o_ref.dtype)
 
 
-def attention(query_start, key_pos, page_ok, q_new, new_all, pages, group_size, head_size):
+def attention(query_start, key_pos, page_ok, q_new, new_all, pages, group_size, head_size,
+              mask_pages):
     q_rows = q_new.shape[0]
     blocks, kv_heads, new_len, width = new_all.shape
     npage, _, page_len, _ = pages.shape
-    kernel = functools.partial(attention_kernel, head_size=head_size)
+    kernel = functools.partial(
+        attention_kernel, head_size=head_size, group_size=group_size, mask_pages=mask_pages
+    )
+    span = group_size * head_size
     return pl.pallas_call(
         kernel,
         out_shape=jax.ShapeDtypeStruct(q_new.shape, q_new.dtype),
         grid_spec=pltpu.PrefetchScalarGridSpec(
             num_scalar_prefetch=1,
-            grid=(kv_heads, group_size),
+            grid=(kv_heads,),
             in_specs=[
-                pl.BlockSpec((q_rows, head_size), lambda g, h, s: (0, g * group_size + h)),
-                pl.BlockSpec((blocks, 1, new_len, width), lambda g, h, s: (0, g, 0, 0)),
-                pl.BlockSpec((npage, 1, page_len, width), lambda g, h, s: (0, g, 0, 0)),
-                pl.BlockSpec((1, blocks * new_len), lambda g, h, s: (0, 0)),
-                pl.BlockSpec((1, npage * page_len), lambda g, h, s: (0, 0)),
+                pl.BlockSpec((q_rows, span), lambda g, s: (0, g)),
+                pl.BlockSpec((blocks, 1, new_len, width), lambda g, s: (0, g, 0, 0)),
+                pl.BlockSpec((npage, 1, page_len, width), lambda g, s: (0, g, 0, 0)),
+                pl.BlockSpec((1, blocks * new_len), lambda g, s: (0, 0)),
+                pl.BlockSpec((1, npage * page_len), lambda g, s: (0, 0)),
             ],
-            out_specs=pl.BlockSpec((q_rows, head_size), lambda g, h, s: (0, g * group_size + h)),
+            out_specs=pl.BlockSpec((q_rows, span), lambda g, s: (0, g)),
         ),
     )(query_start, q_new, new_all, pages, key_pos, page_ok)
 
@@ -120,7 +133,8 @@
     ).reshape(-1)
     page_ok = jnp.repeat(page_ok.astype(jnp.int32), page_len).reshape(1, -1)
     return attention(
-        query_start, key_pos, page_ok, q_new, new_all, gathered, group_size, head_size
+        query_start, key_pos, page_ok, q_new, new_all, gathered, group_size, head_size,
+        npages % blocks != 0,
     )
 
 

time: 90.2 us -> 84.7 us (0.939); the launches traced: 88.9 us -> 84.4 us
  Pallas kernels: 13.7 us -> 9.23 us
    pallas_call x1, Pallas kernels: 13.7 us -> 9.23 us  [attention(): pl.pallas_call(kernel, out_shape=jax.ShapeDtypeStruct(q_new.shape, q_new....]
where the time goes in v5:
time: 84.7 us; the launch traced here: 84.4 us
  waiting for transfers between devices  23.1 us (27%)
  blocking collectives  20.1 us (24%)
  between operations  14.1 us (17%)
  Pallas kernels  9.23 us (11%)
  local copies, waits for them, and re-layouts  6.49 us (8%)
  starting transfers between devices  6.32 us (7%)
  other arithmetic  5.05 us (6%)
    all_gather x1, blocking collectives, local(): new_all = lax.all_gather(kv_new.transpose(1, 0, 2), 'blk', axis=0)  20.1 us
    all_to_all x1, waiting for transfers between devices, local(): lax.all_to_all(kv_cache[chosen], 'blk', split_axis=0, concat_axis=0, tile...  14.1 us
    pallas_call x1, Pallas kernels, attention(): pl.pallas_call(kernel, out_shape=jax.ShapeDtypeStruct(q_new.shape, q_new....  9.23 us
    all_gather x1, waiting for transfers between devices, local(): gathered = lax.all_gather(received[positions], 'blk', axis=0, tiled=True)  8.97 us
    all_to_all x1, starting transfers between devices, local(): lax.all_to_all(kv_cache[chosen], 'blk', split_axis=0, concat_axis=0, tile...  6.32 us
    gather x1, local copies, waits for them, and re-layouts, local(): kv_cache[chosen]  3.56 us
  transfers between devices with their start and end apart: 2, of which 2 were waited for; matrix products, arithmetic and copies ran while one was open for 2% of the time, Pallas kernels for 0%

profile of v5, /device:TPU:0, one launch (start us, length us, event | category | flops | bytes accessed | tf_op | source)
XLA Modules:
  0.0 84.4 jit_solution(6337054532260188997)
XLA Ops:
  6.5 0.7 and_select_fusion.3
  7.2 0.7 convert_bitcast_fusion
  7.9 0.2 reduce-window.21
  8.1 0.1 convert_reduce_fusion
  8.2 0.2 reduce-window.22
  8.3 1.4 %broadcast_multiply_fusion = (s32[4]{0:T(128)S(1)}, s32[]{:T(128)}, s32[]{:T(128)}) fusion(s32[4]{0:T(128)} %param.9, s32[]{:T(128)S(6)} %axis_index.15, s32[4]{0:T(128)S(1)} %convert_reduce_fusion, s32[4,1]{0,1:T(1,128)S(1)} %reduce-window.22), kind=kLoop, calls=%fused_computation.45 | loop fusion | flops 26 | bytes 76 | tf_op jit(solution)/shard_map/mul | solution.py:128
  9.7 0.7 and_select_fusion.4
  10.4 0.2 select_reduce_fusion
  10.6 3.6 %gather_fusion = bf16[4,2,128,256]{3,2,1,0:T(8,128)(2,1)} fusion(bf16[32,2,128,256]{3,2,1,0:T(8,128)(2,1)} %param.7, s32[1024]{0:T(1024)S(1)} %pad_clamp_fusion.1), kind=kCustom, calls=%fused_computation | custom fusion | bytes 1048592 | tf_op jit(solution)/shard_map/gather | solution.py:114
  14.1 6.3 %all-to-all-start = ((bf16[4,2,128,256]{3,2,1,0:T(8,128)(2,1)}), bf16[4,2,128,256]{3,2,1,0:T(8,128)(2,1)S(1)}, u32[]{:S(2)}, u32[]{:S(2)}) async-start(bf16[4,2,128,256]{3,2,1,0:T(8,128)(2,1)} %gather_fusion), calls=%async_computation | async-start | bytes 1048576 | tf_op jit(solution)/shard_map/all_to_all | solution.py:114
  20.5 0.0 all-gather.4.cloned.1.call-start
  20.5 0.2 reduce-window.23
  20.7 0.1 fusion.1
  20.8 14.1 %all-to-all-done = bf16[4,2,128,256]{3,2,1,0:T(8,128)(2,1)S(1)} async-done(((bf16[4,2,128,256]{3,2,1,0:T(8,128)(2,1)}), bf16[4,2,128,256]{3,2,1,0:T(8,128)(2,1)S(1)}, u32[]{:S(2)}, u32[]{:S(2)}) %all-to-all-start) | async-done | bytes 524320 | tf_op jit(solution)/shard_map/all_to_all | solution.py:114
  35.0 1.3 %gather_fusion.1 = bf16[2,2,128,256]{3,2,1,0:T(8,128)(2,1)} fusion(bf16[4,2,128,256]{3,2,1,0:T(8,128)(2,1)S(1)} %all-to-all-done, s32[1024]{0:T(1024)S(1)} %pad_clamp_fusion), kind=kCustom, calls=%fused_computation.1 | custom fusion | bytes 524296 | tf_op jit(solution)/shard_map/gather | solution.py:122
  36.2 0.0 all-gather.4.cloned.1.call-update
  36.3 0.1 reshape.333
  36.4 0.9 %copy.11 = bf16[128,2,256]{2,0,1:T(8,128)(2,1)S(1)} copy(bf16[128,2,256]{2,1,0:T(2,128)(2,1)} %param.6) | data formatting | bytes 262144 | tf_op args[1]
  38.0 20.1 %all-gather = bf16[8,128,256]{2,1,0:T(8,128)(2,1)} all-gather(bf16[2,128,256]{2,1,0:T(8,128)(2,1)S(1)} %bitcast.30), channel_id=2, replica_groups=mesh['groups'=2,'blk'=4,'pool'=4] {'blk'}, dimensions={0}, use_global_device_ids=true | all-gather | bytes 655360 | tf_op jit(solution)/shard_map/all_gather | solution.py:100
  58.0 0.6 iota_add_fusion
  58.7 9.0 %all-gather.4.cloned.1.call-done.page_ref = bf16[8,2,128,256]{3,2,1,0:T(8,128)(2,1)} async-done(((bf16[2,2,128,256]{3,2,1,0:T(8,128)(2,1)}), bf16[8,2,128,256]{3,2,1,0:T(8,128)(2,1)}) %all-gather.4.cloned.1.call-update) | async-done | bytes 1048592 | tf_op jit(solution)/shard_map/all_gather | solution.py:122
  67.7 0.7 broadcast_in_dim.60
  68.3 9.2 %shard_map.55 = bf16[128,2048]{1,0:T(8,128)(2,1)} custom-call(s32[1]{0:T(128)} %bitcast.query_start, bf16[128,2048]{1,0:T(8,128)(2,1)} %q_ref.1, bf16[4,2,128,256]{3,2,1,0:T(8,128)(2,1)} %bitcast.29, bf16[8,2,128,256]{3,2,1,0:T(8,128)(2,1)} %all-gather.4.cloned.1.call-done.page_ref, s32[1,512]{1,0:T(1,128)} %bitcast.32, s32[1,1024]{1,0:T(1,128)} %bitcast.31), custom_call_target="tpu_custom_call" | custom-call | tf_op jit(solution)/shard_map/pallas_call | solution.py:70
  (10 shorter events, 0.1 us)
Async XLA Ops:
  14.1 20.8 %all-to-all-start = ((bf16[4,2,128,256]{3,2,1,0:T(8,128)(2,1)}), bf16[4,2,128,256]{3,2,1,0:T(8,128)(2,1)S(1)}, u32[]{:S(2)}, u32[]{:S(2)}) async-start(bf16[4,2,128,256]{3,2,1,0:T(8,128)(2,1)} %gather_fusion), calls=%async_computation | async-start | bytes 1048576 | tf_op jit(solution)/shard_map/all_to_all | solution.py:114
  20.5 47.2 %all-gather.4.cloned.1.call-start = ((), (), s32[]{:S(2)}) async-start(), calls=%async_computation.1 | async-start | bytes 1310720 | tf_op jit(solution)/shard_map/all_gather | solution.py:122
Sparse Core Ops, SparseCore 0:
  36.4 31.2 all-gather.3

commit v6 on v5

v6 whole, which is shorter than its diff:
```python
import functools
import math

import jax
import jax.numpy as jnp
from jax import lax
from jax.experimental import pallas as pl
from jax.experimental.pallas import tpu as pltpu
from jax.sharding import PartitionSpec as P

CAP = 4


def new_turn_kernel(
    query_start, q_ref, new_ref, own_ref, key_pos_ref, own_ok_ref, acc_ref, top_ref, total_ref,
    *, head_size, group_size, mask_own,
):
    scale = 1.0 / math.sqrt(head_size)
    q_rows = q_ref.shape[0]
    new_kv = new_ref[:, 0].reshape(-1, new_ref.shape[-1])
    own_kv = own_ref[:, 0].reshape(-1, own_ref.shape[-1])
    row_pos = query_start[0] + lax.broadcasted_iota(jnp.int32, (q_rows, new_kv.shape[0]), 0)
    new_visible = key_pos_ref[...] <= row_pos
    own_visible = own_ok_ref[...] > 0
    dims = (((1,), (1,)), ((), ()))
    pv = (((1,), (0,)), ((), ()))
    for h in range(group_size):
        cols = slice(h * head_size, (h + 1) * head_size)
        queries = q_ref[:, cols]
        new_scores = lax.dot_general(
            queries, new_kv[:, :head_size], dims, preferred_element_type=jnp.float32
        ) * scale
        own_scores = lax.dot_general(
            queries, own_kv[:, :head_size], dims, preferred_element_type=jnp.float32
        ) * scale
        new_scores = jnp.where(new_visible, new_scores, -1e30)
        if mask_own:
            own_scores = jnp.where(own_visible, own_scores, -1e30)
        row_top = jnp.maximum(
            jnp.max(new_scores, axis=1, keepdims=True),
            jnp.max(own_scores, axis=1, keepdims=True),
        )
        new_weights = jnp.exp(new_scores - row_top)
        own_weights = jnp.exp(own_scores - row_top)
        row_total = jnp.sum(new_weights, axis=1, keepdims=True) + jnp.sum(
            own_weights, axis=1, keepdims=True
        )
        acc_ref[:, cols] = lax.dot_general(
            new_weights.astype(jnp.bfloat16), new_kv[:, head_size:], pv,
            preferred_element_type=jnp.float32,
        ) + lax.dot_general(
            own_weights.astype(jnp.bfloat16), own_kv[:, head_size:], pv,
            preferred_element_type=jnp.float32,
        )
        top_ref[:, cols] = jnp.broadcast_to(row_top, (q_rows, head_size))
        total_ref[:, cols] = jnp.broadcast_to(row_total, (q_rows, head_size))


def prefix_kernel(
    q_ref, page_ref, page_ok_ref, acc_ref, top_ref, total_ref, o_ref, *, head_size, group_size
):
    scale = 1.0 / math.sqrt(head_size)
    page_kv = page_ref[:, 0].reshape(-1, page_ref.shape[-1])
    page_visible = page_ok_ref[...] > 0
    dims = (((1,), (1,)), ((), ()))
    pv = (((1,), (0,)), ((), ()))
    for h in range(group_size):
        cols = slice(h * head_size, (h + 1) * head_size)
        scores = lax.dot_general(
            q_ref[:, cols], page_kv[:, :head_size], dims, preferred_element_type=jnp.float32
        ) * scale
        scores = jnp.where(page_visible, scores, -1e30)
        top_prev = top_ref[:, cols][:, :1]
        row_top = jnp.maximum(top_prev, jnp.max(scores, axis=1, keepdims=True))
        factor = jnp.exp(top_prev - row_top)
        weights = jnp.exp(scores - row_top)
        row_total = total_ref[:, cols][:, :1] * factor + jnp.sum(weights, axis=1, keepdims=True)
        summed = acc_ref[:, cols] * factor + lax.dot_general(
            weights.astype(jnp.bfloat16), page_kv[:, head_size:], pv,
            preferred_element_type=jnp.float32,
        )
        o_ref[:, cols] = (summed / row_total).astype(o_ref.dtype)


def new_turn_part(query_start, key_pos, own_ok, q_new, new_all, own, group_size, head_size,
                  mask_own):
    q_rows = q_new.shape[0]
    blocks, kv_heads, new_len, width = new_all.shape
    npage, _, page_len, _ = own.shape
    kernel = functools.partial(
        new_turn_kernel, head_size=head_size, group_size=group_size, mask_own=mask_own
    )
    span = group_size * head_size
    state = jax.ShapeDtypeStruct(q_new.shape, jnp.float32)
    state_spec = pl.BlockSpec((q_rows, span), lambda g, s: (0, g))
    return pl.pallas_call(
        kernel,
        out_shape=(state, state, state),
        grid_spec=pltpu.PrefetchScalarGridSpec(
            num_scalar_prefetch=1,
            grid=(kv_heads,),
            in_specs=[
                pl.BlockSpec((q_rows, span), lambda g, s: (0, g)),
                pl.BlockSpec((blocks, 1, new_len, width), lambda g, s: (0, g, 0, 0)),
                pl.BlockSpec((npage, 1, page_len, width), lambda g, s: (0, g, 0, 0)),
                pl.BlockSpec((1, blocks * new_len), lambda g, s: (0, 0)),
                pl.BlockSpec((1, npage * page_len), lambda g, s: (0, 0)),
            ],
            out_specs=(state_spec, state_spec, state_spec),
        ),
    )(query_start, q_new, new_all, own, key_pos, own_ok)


def prefix_part(page_ok, q_new, pages, acc, top, total, group_size, head_size):
    q_rows = q_new.shape[0]
    npage, kv_heads, page_len, width = pages.shape
    kernel = functools.partial(prefix_kernel, head_size=head_size, group_size=group_size)
    span = group_size * head_size
    block = pl.BlockSpec((q_rows, span), lambda g: (0, g))
    return pl.pallas_call(
        kernel,
        out_shape=jax.ShapeDtypeStruct(q_new.shape, q_new.dtype),
        grid=(kv_heads,),
        in_specs=[
            block,
            pl.BlockSpec((npage, 1, page_len, width), lambda g: (0, g, 0, 0)),
            pl.BlockSpec((1, npage * page_len), lambda g: (0, 0)),
            block,
            block,
            block,
        ],
        out_specs=block,
    )(q_new, pages, page_ok, acc, top, total)


def local(q_new, kv_new, kv_cache, page_table, block_offsets):
    kv_heads = kv_new.shape[1]
    head_size = kv_new.shape[2] // 2
    group_size = q_new.shape[1] // (head_size * kv_heads)
    slots_dev = kv_cache.shape[0]
    npages = page_table.shape[0]
    blocks = lax.axis_size("blk")
    myself = lax.axis_index("blk")
    pg = -(-npages // blocks)
    block_ids = jnp.arange(blocks, dtype=jnp.int32)
    my_offset = jnp.sum(jnp.where(block_ids == myself, block_offsets, 0))

    new_all = lax.all_gather(kv_new.transpose(1, 0, 2), "blk", axis=0)

    page_owner = page_table // slots_dev
    owned = page_owner == myself
    page_rank = jnp.cumsum(owned.astype(jnp.int32)) - 1
    local_slot = page_table % slots_dev
    counts = jnp.sum((page_owner[None, :] == block_ids[:, None]).astype(jnp.int32), axis=1)
    per_peer = (CAP + blocks - 1) // blocks
    starts = jnp.cumsum(counts) - counts
    my_start = jnp.sum(jnp.where(block_ids == myself, starts, 0))
    peer_slots = jnp.arange(per_peer, dtype=jnp.int32)[None, :]
    wanted = (block_ids[:, None] - my_start) % blocks + peer_slots * blocks
    picked = owned[None, None, :] & (page_rank[None, None, :] == wanted[..., None])
    chosen = jnp.sum(jnp.where(picked, local_slot[None, None, :], 0), axis=2).reshape(-1)
    received = lax.all_to_all(kv_cache[chosen], "blk", split_axis=0, concat_axis=0, tiled=True)
    received, new_all = lax.optimization_barrier((received, new_all))
    arriving = (myself - starts[:, None]) % blocks + peer_slots * blocks
    present = (arriving < counts[:, None]).reshape(-1)
    order_rank = jnp.cumsum(present.astype(jnp.int32)) - 1
    choose = present[None, :] & (order_rank[None, :] == jnp.arange(pg, dtype=jnp.int32)[:, None])
    positions = jnp.sum(
        jnp.where(choose, jnp.arange(blocks * per_peer, dtype=jnp.int32)[None, :], 0), axis=1
    )
    own = received[positions]
    gathered = lax.all_gather(own, "blk", axis=0, tiled=True)

    q_rows = q_new.shape[0]
    page_len = kv_cache.shape[2]
    query_start = (my_offset * q_rows).reshape(1).astype(jnp.int32)
    key_pos = (
        jnp.repeat(block_offsets, q_rows) * q_rows
        + jnp.tile(jnp.arange(q_rows, dtype=jnp.int32), blocks)
    ).reshape(1, -1).astype(jnp.int32)
    slot_ids = jnp.arange(pg, dtype=jnp.int32)
    own_ok = slot_ids * blocks + myself < npages
    own_ok = jnp.repeat(own_ok.astype(jnp.int32), page_len).reshape(1, -1)
    page_ok = (
        (slot_ids[None, :] * blocks + block_ids[:, None] < npages)
        & (block_ids[:, None] != myself)
    ).reshape(-1)
    page_ok = jnp.repeat(page_ok.astype(jnp.int32), page_len).reshape(1, -1)
    acc, top, total = new_turn_part(
        query_start, key_pos, own_ok, q_new, new_all, own, group_size, head_size,
        npages % blocks != 0,
    )
    return prefix_part(page_ok, q_new, gathered, acc, top, total, group_size, head_size)


def solution(mesh):
    return jax.shard_map(
        local,
        mesh=mesh,
        in_specs=(
            P(("groups", "blk"), "pool"),
            P(("groups", "blk"), "pool", None),
            P(("groups", "blk"), "pool", None, None),
            P("groups"),
            P("groups"),
        ),
        out_specs=P(("groups", "blk"), "pool"),
        check_vma=False,
    )
```

time: 84.7 us -> 93.3 us (1.10)
  Pallas kernels: 9.23 us -> 16.9 us
  blocking collectives: 20.1 us -> 24.1 us
  waiting for transfers between devices: 23.1 us -> 19.5 us
    all_to_all x1, waiting for transfers between devices: 14.1 us -> 0.01 us  [local(): lax.all_to_all(kv_cache[chosen], 'blk', split_axis=0, concat_axis=0, tile...]
    all_gather x1, waiting for transfers between devices: 8.97 us -> 19.5 us  [local(): gathered = lax.all_gather(own, 'blk', axis=0, tiled=True)]
    pallas_call x1 -> x2, Pallas kernels: 9.23 us -> 16.9 us  [the longest x1 9.47 us: prefix_part(): pl.pallas_call(kernel, out_shape=jax.ShapeDtypeStruct(q_new.shape, q_new....]
    all_gather x1, blocking collectives: 20.1 us -> 24.1 us  [local(): new_all = lax.all_gather(kv_new.transpose(1, 0, 2), 'blk', axis=0)]
  transfers between devices with their start and end apart: 2 -> 2, of which waited for: 2 -> 1; matrix products, arithmetic and copies ran while one was open for 2% -> 3% of each run, Pallas kernels for 0% -> 8%
where the time goes in v6:
time: 93.3 us; the launch traced here: 93 us
  blocking collectives  24.1 us (26%)
  waiting for transfers between devices  19.5 us (21%)
  Pallas kernels  16.9 us (18%)
  between operations  14 us (15%)
  local copies, waits for them, and re-layouts  7.14 us (8%)
  starting transfers between devices  6.32 us (7%)
  other arithmetic  5.02 us (5%)
    all_gather x1, blocking collectives, local(): new_all = lax.all_gather(kv_new.transpose(1, 0, 2), 'blk', axis=0)  24.1 us
    all_gather x1, waiting for transfers between devices, local(): gathered = lax.all_gather(own, 'blk', axis=0, tiled=True)  19.5 us
    pallas_call x1, Pallas kernels, prefix_part(): pl.pallas_call(kernel, out_shape=jax.ShapeDtypeStruct(q_new.shape, q_new....  9.47 us
    pallas_call x1, Pallas kernels, new_turn_part(): pl.pallas_call(kernel, out_shape=(state, state, state), grid_spec=pltpu.P...  7.43 us
    all_to_all x1, starting transfers between devices, local(): lax.all_to_all(kv_cache[chosen], 'blk', split_axis=0, concat_axis=0, tile...  6.32 us
    gather x1, local copies, waits for them, and re-layouts, local(): kv_cache[chosen]  3.56 us
  transfers between devices with their start and end apart: 2, of which 1 were waited for; matrix products, arithmetic and copies ran while one was open for 3% of the time, Pallas kernels for 8%

profile of v6, /device:TPU:0, one launch (start us, length us, event | category | flops | bytes accessed | tf_op | source)
XLA Modules:
  0.0 93.0 jit_solution(15678020128047879810)
XLA Ops:
  6.5 0.7 and_select_fusion.3
  7.2 0.7 convert_bitcast_fusion
  7.9 0.1 convert_reduce_fusion
  8.0 0.2 reduce-window.22
  8.2 1.3 %broadcast_multiply_fusion = (s32[4]{0:T(128)S(1)}, s32[]{:T(128)}, s32[]{:T(128)}) fusion(s32[4]{0:T(128)} %param.9, s32[]{:T(128)S(6)} %axis_index.15, s32[4]{0:T(128)S(1)} %convert_reduce_fusion, s32[4,1]{0,1:T(1,128)S(1)} %reduce-window.22), kind=kLoop, calls=%fused_computation.48 | loop fusion | flops 26 | bytes 76 | tf_op jit(solution)/shard_map/mul | solution.py:178
  9.5 0.7 and_select_fusion.4
  10.1 0.2 reduce-window.21
  10.3 0.2 select_reduce_fusion
  10.5 3.6 %gather_fusion = bf16[4,2,128,256]{3,2,1,0:T(8,128)(2,1)} fusion(bf16[32,2,128,256]{3,2,1,0:T(8,128)(2,1)} %param.7, s32[1024]{0:T(1024)S(1)} %pad_clamp_fusion.1), kind=kCustom, calls=%fused_computation | custom fusion | bytes 1048592 | tf_op jit(solution)/shard_map/gather | solution.py:162
  14.1 6.3 %all-to-all-start = ((bf16[4,2,128,256]{3,2,1,0:T(8,128)(2,1)}), bf16[4,2,128,256]{3,2,1,0:T(8,128)(2,1)S(1)}, u32[]{:S(2)}, u32[]{:S(2)}) async-start(bf16[4,2,128,256]{3,2,1,0:T(8,128)(2,1)} %gather_fusion), calls=%async_computation | async-start | bytes 1048576 | tf_op jit(solution)/shard_map/all_to_all | solution.py:162
  20.4 0.0 all-gather.4.cloned.1.call-start
  20.4 0.2 reduce-window.23
  20.6 0.9 copy.11
  21.5 0.1 fusion.2
  21.7 24.1 %all-gather = bf16[8,128,256]{2,1,0:T(8,128)(2,1)} all-gather(bf16[2,128,256]{2,1,0:T(8,128)(2,1)S(1)} %bitcast.31), channel_id=2, replica_groups=mesh['groups'=2,'blk'=4,'pool'=4] {'blk'}, dimensions={0}, use_global_device_ids=true | all-gather | bytes 655360 | tf_op jit(solution)/shard_map/all_gather | solution.py:148
  45.8 0.0 all-to-all-done
  45.8 1.3 %gather_fusion.1 = bf16[2,2,128,256]{3,2,1,0:T(8,128)(2,1)} fusion(bf16[4,2,128,256]{3,2,1,0:T(8,128)(2,1)S(1)} %all-to-all-done, s32[1024]{0:T(1024)S(1)} %pad_clamp_fusion), kind=kCustom, calls=%fused_computation.1 | custom fusion | bytes 524296 | tf_op jit(solution)/shard_map/gather | solution.py:171
  47.1 0.0 all-gather.4.cloned.1.call-update
  47.1 0.1 fusion.1
  47.2 0.1 reshape.340
  47.8 0.6 iota_add_fusion
  48.5 0.6 broadcast_in_dim.65
  49.1 7.4 %shard_map.55 = (f32[128,2048]{1,0:T(8,128)}, f32[128,2048]{1,0:T(8,128)}, f32[128,2048]{1,0:T(8,128)}) custom-call(s32[1]{0:T(128)} %bitcast.12.query_start, bf16[128,2048]{1,0:T(8,128)(2,1)} %q_ref.3, bf16[4,2,128,256]{3,2,1,0:T(8,128)(2,1)} %bitcast.30, bf16[2,2,128,256]{3,2,1,0:T(8,128)(2,1)} %gather_fusion.1, s32[1,512]{1,0:T(1,128)} %bitcast.33, ...), custom_call_target="tpu_custom_call" | custom-call | tf_op jit(solution)/shard_map/pallas_call | solution.py:96
  56.5 19.5 %all-gather.4.cloned.1.call-done.page_ref = bf16[8,2,128,256]{3,2,1,0:T(8,128)(2,1)} async-done(((bf16[2,2,128,256]{3,2,1,0:T(8,128)(2,1)}), bf16[8,2,128,256]{3,2,1,0:T(8,128)(2,1)}) %all-gather.4.cloned.1.call-update) | async-done | bytes 1048592 | tf_op jit(solution)/shard_map/all_gather | solution.py:172
  76.1 0.7 broadcast_in_dim.63
  76.7 9.5 %shard_map.56 = bf16[128,2048]{1,0:T(8,128)(2,1)} custom-call(bf16[128,2048]{1,0:T(8,128)(2,1)} %q_ref.3, bf16[8,2,128,256]{3,2,1,0:T(8,128)(2,1)} %all-gather.4.cloned.1.call-done.page_ref, s32[1,1024]{1,0:T(1,128)} %bitcast.32, f32[128,2048]{1,0:T(8,128)} %get-tuple-element.12.acc_ref, f32[128,2048]{1,0:T(8,128)} %get-tuple-element.13.top_ref, ...), custom_call_target="tpu_custom_call" | custom-call | tf_op jit(solution)/shard_map/pallas_call | solution.py:120
  (10 shorter events, 0.1 us)
Async XLA Ops:
  14.1 31.7 %all-to-all-start = ((bf16[4,2,128,256]{3,2,1,0:T(8,128)(2,1)}), bf16[4,2,128,256]{3,2,1,0:T(8,128)(2,1)S(1)}, u32[]{:S(2)}, u32[]{:S(2)}) async-start(bf16[4,2,128,256]{3,2,1,0:T(8,128)(2,1)} %gather_fusion), calls=%async_computation | async-start | bytes 1048576 | tf_op jit(solution)/shard_map/all_to_all | solution.py:162
  20.4 55.7 %all-gather.4.cloned.1.call-start = ((), (), s32[]{:S(2)}) async-start(), calls=%async_computation.1 | async-start | bytes 1310720 | tf_op jit(solution)/shard_map/all_gather | solution.py:172
Sparse Core Ops, SparseCore 0:
  47.2 28.7 all-gather.3

commit v7 on v6

--- a/solution.py
+++ b/solution.py
@@ -52,8 +52,8 @@
             own_weights.astype(jnp.bfloat16), own_kv[:, head_size:], pv,
             preferred_element_type=jnp.float32,
         )
-        top_ref[:, cols] = jnp.broadcast_to(row_top, (q_rows, head_size))
-        total_ref[:, cols] = jnp.broadcast_to(row_total, (q_rows, head_size))
+        top_ref[0, :, h : h + 1] = row_top
+        total_ref[0, :, h : h + 1] = row_total
 
 
 def prefix_kernel(
@@ -70,11 +70,11 @@
             q_ref[:, cols], page_kv[:, :head_size], dims, preferred_element_type=jnp.float32
         ) * scale
         scores = jnp.where(page_visible, scores, -1e30)
-        top_prev = top_ref[:, cols][:, :1]
+        top_prev = top_ref[0, :, h : h + 1]
         row_top = jnp.maximum(top_prev, jnp.max(scores, axis=1, keepdims=True))
         factor = jnp.exp(top_prev - row_top)
         weights = jnp.exp(scores - row_top)
-        row_total = total_ref[:, cols][:, :1] * factor + jnp.sum(weights, axis=1, keepdims=True)
+        row_total = total_ref[0, :, h : h + 1] * factor + jnp.sum(weights, axis=1, keepdims=True)
         summed = acc_ref[:, cols] * factor + lax.dot_general(
             weights.astype(jnp.bfloat16), page_kv[:, head_size:], pv,
             preferred_element_type=jnp.float32,
@@ -93,9 +93,11 @@
     span = group_size * head_size
     state = jax.ShapeDtypeStruct(q_new.shape, jnp.float32)
     state_spec = pl.BlockSpec((q_rows, span), lambda g, s: (0, g))
+    stat = jax.ShapeDtypeStruct((kv_heads, q_rows, group_size), jnp.float32)
+    stat_spec = pl.BlockSpec((1, q_rows, group_size), lambda g, s: (g, 0, 0))
     return pl.pallas_call(
         kernel,
-        out_shape=(state, state, state),
+        out_shape=(state, stat, stat),
         grid_spec=pltpu.PrefetchScalarGridSpec(
             num_scalar_prefetch=1,
             grid=(kv_heads,),
@@ -106,7 +108,7 @@
                 pl.BlockSpec((1, blocks * new_len), lambda g, s: (0, 0)),
                 pl.BlockSpec((1, npage * page_len), lambda g, s: (0, 0)),
             ],
-            out_specs=(state_spec, state_spec, state_spec),
+            out_specs=(state_spec, stat_spec, stat_spec),
         ),
     )(query_start, q_new, new_all, own, key_pos, own_ok)
 
@@ -117,6 +119,7 @@
     kernel = functools.partial(prefix_kernel, head_size=head_size, group_size=group_size)
     span = group_size * head_size
     block = pl.BlockSpec((q_rows, span), lambda g: (0, g))
+    stat_spec = pl.BlockSpec((1, q_rows, group_size), lambda g: (g, 0, 0))
     return pl.pallas_call(
         kernel,
         out_shape=jax.ShapeDtypeStruct(q_new.shape, q_new.dtype),
@@ -126,8 +129,8 @@
             pl.BlockSpec((npage, 1, page_len, width), lambda g: (0, g, 0, 0)),
             pl.BlockSpec((1, npage * page_len), lambda g: (0, 0)),
             block,
-            block,
-            block,
+            stat_spec,
+            stat_spec,
         ],
         out_specs=block,
     )(q_new, pages, page_ok, acc, top, total)
@@ -145,7 +148,6 @@
     block_ids = jnp.arange(blocks, dtype=jnp.int32)
     my_offset = jnp.sum(jnp.where(block_ids == myself, block_offsets, 0))
 
-    new_all = lax.all_gather(kv_new.transpose(1, 0, 2), "blk", axis=0)
 
     page_owner = page_table // slots_dev
     owned = page_owner == myself
@@ -160,7 +162,6 @@
     picked = owned[None, None, :] & (page_rank[None, None, :] == wanted[..., None])
     chosen = jnp.sum(jnp.where(picked, local_slot[None, None, :], 0), axis=2).reshape(-1)
     received = lax.all_to_all(kv_cache[chosen], "blk", split_axis=0, concat_axis=0, tiled=True)
-    received, new_all = lax.optimization_barrier((received, new_all))
     arriving = (myself - starts[:, None]) % blocks + peer_slots * blocks
     present = (arriving < counts[:, None]).reshape(-1)
     order_rank = jnp.cumsum(present.astype(jnp.int32)) - 1
@@ -170,6 +171,8 @@
     )
     own = received[positions]
     gathered = lax.all_gather(own, "blk", axis=0, tiled=True)
+    own, new_rows = lax.optimization_barrier((own, kv_new.transpose(1, 0, 2)))
+    new_all = lax.all_gather(new_rows, "blk", axis=0)
 
     q_rows = q_new.shape[0]
     page_len = kv_cache.shape[2]

time: 93.3 us -> 85.7 us (0.919)
  blocking collectives: 24.1 us -> 20 us
  waiting for transfers between devices: 19.5 us -> 15.8 us
    all_gather x1, waiting for transfers between devices: 19.5 us -> 1.66 us  [local(): gathered = lax.all_gather(own, 'blk', axis=0, tiled=True)]
    all_to_all x1, waiting for transfers between devices: 0.01 us -> 14.1 us  [local(): lax.all_to_all(kv_cache[chosen], 'blk', split_axis=0, concat_axis=0, tile...]
    all_gather x1, blocking collectives: 24.1 us -> 20 us  [local(): new_all = lax.all_gather(new_rows, 'blk', axis=0)]
  transfers between devices with their start and end apart: 2 -> 2, of which waited for: 1 -> 2; matrix products, arithmetic and copies ran while one was open for 3% -> 3% of each run, Pallas kernels for 8% -> 9%
where the time goes in v7:
time: 85.7 us; the launch traced here: 85.4 us
  blocking collectives  20 us (23%)
  Pallas kernels  16.8 us (20%)
  waiting for transfers between devices  15.8 us (18%)
  between operations  14.1 us (16%)
  local copies, waits for them, and re-layouts  7.15 us (8%)
  starting transfers between devices  6.32 us (7%)
  other arithmetic  5.11 us (6%)
    all_gather x1, blocking collectives, local(): new_all = lax.all_gather(new_rows, 'blk', axis=0)  20 us
    all_to_all x1, waiting for transfers between devices, local(): lax.all_to_all(kv_cache[chosen], 'blk', split_axis=0, concat_axis=0, tile...  14.1 us
    pallas_call x1, Pallas kernels, prefix_part(): pl.pallas_call(kernel, out_shape=jax.ShapeDtypeStruct(q_new.shape, q_new....  9.53 us
    pallas_call x1, Pallas kernels, new_turn_part(): pl.pallas_call(kernel, out_shape=(state, stat, stat), grid_spec=pltpu.Pre...  7.3 us
    all_to_all x1, starting transfers between devices, local(): lax.all_to_all(kv_cache[chosen], 'blk', split_axis=0, concat_axis=0, tile...  6.32 us
    gather x1, local copies, waits for them, and re-layouts, local(): kv_cache[chosen]  3.56 us
  transfers between devices with their start and end apart: 2, of which 2 were waited for; matrix products, arithmetic and copies ran while one was open for 3% of the time, Pallas kernels for 9%

profile of v7, /device:TPU:0, one launch (start us, length us, event | category | flops | bytes accessed | tf_op | source)
XLA Modules:
  0.0 85.4 jit_solution(12167252356428896828)
XLA Ops:
  6.5 0.7 and_select_fusion.3
  7.2 0.7 convert_bitcast_fusion
  7.9 0.1 convert_reduce_fusion
  8.0 0.2 reduce-window.22
  8.2 1.4 %broadcast_multiply_fusion = (s32[4]{0:T(128)S(1)}, s32[]{:T(128)}, s32[]{:T(128)}) fusion(s32[4]{0:T(128)} %param.9, s32[]{:T(128)S(6)} %axis_index.15, s32[4]{0:T(128)S(1)} %convert_reduce_fusion, s32[4,1]{0,1:T(1,128)S(1)} %reduce-window.22), kind=kLoop, calls=%fused_computation.48 | loop fusion | flops 26 | bytes 76 | tf_op jit(solution)/shard_map/mul | solution.py:181
  9.5 0.7 and_select_fusion.4
  10.2 0.2 reduce-window.21
  10.4 0.2 select_reduce_fusion
  10.6 3.6 %gather_fusion = bf16[4,2,128,256]{3,2,1,0:T(8,128)(2,1)} fusion(bf16[32,2,128,256]{3,2,1,0:T(8,128)(2,1)} %param.7, s32[1024]{0:T(1024)S(1)} %pad_clamp_fusion.1), kind=kCustom, calls=%fused_computation | custom fusion | bytes 1048592 | tf_op jit(solution)/shard_map/gather | solution.py:164
  14.1 6.3 %all-to-all-start = ((bf16[4,2,128,256]{3,2,1,0:T(8,128)(2,1)}), bf16[4,2,128,256]{3,2,1,0:T(8,128)(2,1)S(1)}, u32[]{:S(2)}, u32[]{:S(2)}) async-start(bf16[4,2,128,256]{3,2,1,0:T(8,128)(2,1)} %gather_fusion), calls=%async_computation | async-start | bytes 1048576 | tf_op jit(solution)/shard_map/all_to_all | solution.py:164
  20.5 0.0 all-gather.4.cloned.1.call-start
  20.5 0.2 reduce-window.23
  20.7 0.1 fusion.2
  20.8 14.1 %all-to-all-done = bf16[4,2,128,256]{3,2,1,0:T(8,128)(2,1)S(1)} async-done(((bf16[4,2,128,256]{3,2,1,0:T(8,128)(2,1)}), bf16[4,2,128,256]{3,2,1,0:T(8,128)(2,1)S(1)}, u32[]{:S(2)}, u32[]{:S(2)}) %all-to-all-start) | async-done | bytes 524320 | tf_op jit(solution)/shard_map/all_to_all | solution.py:164
  35.0 1.3 %gather_fusion.1 = bf16[2,2,128,256]{3,2,1,0:T(8,128)(2,1)} fusion(bf16[4,2,128,256]{3,2,1,0:T(8,128)(2,1)S(1)} %all-to-all-done, s32[1024]{0:T(1024)S(1)} %pad_clamp_fusion), kind=kCustom, calls=%fused_computation.1 | custom fusion | bytes 524296 | tf_op jit(solution)/shard_map/gather | solution.py:172
  36.2 0.0 all-gather.4.cloned.1.call-update
  36.2 0.9 %copy.11 = bf16[128,2,256]{2,0,1:T(8,128)(2,1)S(1)} copy(bf16[128,2,256]{2,1,0:T(2,128)(2,1)} %param.6) | data formatting | bytes 262144 | tf_op args[1]
  37.2 0.1 fusion.1
  37.3 0.1 reshape.340
  38.0 0.6 iota_add_fusion
  38.7 20.0 %all-gather.1 = bf16[8,128,256]{2,1,0:T(8,128)(2,1)} all-gather(bf16[2,128,256]{2,1,0:T(8,128)(2,1)S(1)} %bitcast.31), channel_id=3, replica_groups=mesh['groups'=2,'blk'=4,'pool'=4] {'blk'}, dimensions={0}, use_global_device_ids=true | all-gather | bytes 655360 | tf_op jit(solution)/shard_map/all_gather | solution.py:175
  58.7 0.7 broadcast_in_dim.65
  59.4 7.3 %shard_map.55 = (f32[128,2048]{1,0:T(8,128)}, f32[2,128,8]{2,1,0:T(8,128)}, f32[2,128,8]{2,1,0:T(8,128)}) custom-call(s32[1]{0:T(128)} %bitcast.10.query_start, bf16[128,2048]{1,0:T(8,128)(2,1)} %q_ref.3, bf16[4,2,128,256]{3,2,1,0:T(8,128)(2,1)} %bitcast.30, bf16[2,2,128,256]{3,2,1,0:T(8,128)(2,1)} %gather_fusion.1, s32[1,512]{1,0:T(1,128)} %bitcast.33, ...), custom_call_target="tpu_custom_call" | custom-call | tf_op jit(solution)/shard_map/pallas_call | solution.py:98
  66.7 1.7 %all-gather.4.cloned.1.call-done.page_ref = bf16[8,2,128,256]{3,2,1,0:T(8,128)(2,1)} async-done(((bf16[2,2,128,256]{3,2,1,0:T(8,128)(2,1)}), bf16[8,2,128,256]{3,2,1,0:T(8,128)(2,1)}) %all-gather.4.cloned.1.call-update) | async-done | bytes 1048592 | tf_op jit(solution)/shard_map/all_gather | solution.py:173
  68.3 0.7 broadcast_in_dim.63
  69.0 9.5 %shard_map.56 = bf16[128,2048]{1,0:T(8,128)(2,1)} custom-call(bf16[128,2048]{1,0:T(8,128)(2,1)} %q_ref.3, bf16[8,2,128,256]{3,2,1,0:T(8,128)(2,1)} %all-gather.4.cloned.1.call-done.page_ref, s32[1,1024]{1,0:T(1,128)} %bitcast.32, f32[128,2048]{1,0:T(8,128)} %get-tuple-element.12.acc_ref, f32[2,128,8]{2,1,0:T(8,128)} %get-tuple-element.13.top_ref, ...), custom_call_target="tpu_custom_call" | custom-call | tf_op jit(solution)/shard_map/pallas_call | solution.py:123
  (10 shorter events, 0.1 us)
Async XLA Ops:
  14.1 20.8 %all-to-all-start = ((bf16[4,2,128,256]{3,2,1,0:T(8,128)(2,1)}), bf16[4,2,128,256]{3,2,1,0:T(8,128)(2,1)S(1)}, u32[]{:S(2)}, u32[]{:S(2)}) async-start(bf16[4,2,128,256]{3,2,1,0:T(8,128)(2,1)} %gather_fusion), calls=%async_computation | async-start | bytes 1048576 | tf_op jit(solution)/shard_map/all_to_all | solution.py:164
  20.5 47.9 %all-gather.4.cloned.1.call-start = ((), (), s32[]{:S(2)}) async-start(), calls=%async_computation.1 | async-start | bytes 1310720 | tf_op jit(solution)/shard_map/all_gather | solution.py:173
Sparse Core Ops, SparseCore 0:
  36.4 31.9 all-gather.3

commit v8 on v7

--- a/solution.py
+++ b/solution.py
@@ -136,6 +136,75 @@
     )(q_new, pages, page_ok, acc, top, total)
 
 
+def send_kernel(table_ref, cache_ref, out_ref, sem, *, blocks, per_peer, slots_dev):
+    me = lax.axis_index("blk")
+    npages = table_ref.shape[0]
+
+    def count_before(j, acc):
+        return acc + (table_ref[j] // slots_dev < me).astype(jnp.int32)
+
+    my_start = lax.fori_loop(0, npages, count_before, jnp.int32(0))
+
+    def issue(j, rank):
+        slot = table_ref[j]
+        mine = slot // slots_dev == me
+        dest = ((rank % blocks + my_start) % blocks) * per_peer + rank // blocks
+
+        @pl.when(mine)
+        def _():
+            copy = pltpu.make_async_copy(cache_ref.at[slot % slots_dev], out_ref.at[dest], sem.at[0])
+            copy.start()
+            copy.wait()
+
+        return rank + mine.astype(jnp.int32)
+
+    lax.fori_loop(0, npages, issue, jnp.int32(0))
+
+
+def compact_kernel(table_ref, recv_ref, out_ref, sem, *, blocks, per_peer, slots_dev):
+    me = lax.axis_index("blk")
+    npages = table_ref.shape[0]
+    pg = out_ref.shape[0]
+
+    def source(j, filled):
+        def tally(i, acc):
+            owner = table_ref[i] // slots_dev
+            return (acc[0] + (owner == j).astype(jnp.int32), acc[1] + (owner < j).astype(jnp.int32))
+
+        count, start = lax.fori_loop(0, npages, tally, (jnp.int32(0), jnp.int32(0)))
+        for s in range(per_peer):
+            arriving = (me - start) % blocks + s * blocks
+            present = (arriving < count) & (filled < pg)
+
+            @pl.when(present)
+            def _():
+                copy = pltpu.make_async_copy(
+                    recv_ref.at[j * per_peer + s], out_ref.at[filled], sem.at[0]
+                )
+                copy.start()
+                copy.wait()
+
+            filled = filled + present.astype(jnp.int32)
+        return filled
+
+    lax.fori_loop(0, blocks, source, jnp.int32(0))
+
+
+def pick_pages(kernel, page_table, source, count, blocks, per_peer, slots_dev):
+    body = functools.partial(kernel, blocks=blocks, per_peer=per_peer, slots_dev=slots_dev)
+    return pl.pallas_call(
+        body,
+        out_shape=jax.ShapeDtypeStruct((count,) + source.shape[1:], source.dtype),
+        grid_spec=pltpu.PrefetchScalarGridSpec(
+            num_scalar_prefetch=1,
+            grid=(1,),
+            in_specs=[pl.BlockSpec(memory_space=pl.ANY)],
+            out_specs=pl.BlockSpec(memory_space=pl.ANY),
+            scratch_shapes=[pltpu.SemaphoreType.DMA((1,))],
+        ),
+    )(page_table, source)
+
+
 def local(q_new, kv_new, kv_cache, page_table, block_offsets):
     kv_heads = kv_new.shape[1]
     head_size = kv_new.shape[2] // 2
@@ -149,27 +218,39 @@
     my_offset = jnp.sum(jnp.where(block_ids == myself, block_offsets, 0))
 
 
-    page_owner = page_table // slots_dev
-    owned = page_owner == myself
-    page_rank = jnp.cumsum(owned.astype(jnp.int32)) - 1
-    local_slot = page_table % slots_dev
-    counts = jnp.sum((page_owner[None, :] == block_ids[:, None]).astype(jnp.int32), axis=1)
     per_peer = (CAP + blocks - 1) // blocks
-    starts = jnp.cumsum(counts) - counts
-    my_start = jnp.sum(jnp.where(block_ids == myself, starts, 0))
-    peer_slots = jnp.arange(per_peer, dtype=jnp.int32)[None, :]
-    wanted = (block_ids[:, None] - my_start) % blocks + peer_slots * blocks
-    picked = owned[None, None, :] & (page_rank[None, None, :] == wanted[..., None])
-    chosen = jnp.sum(jnp.where(picked, local_slot[None, None, :], 0), axis=2).reshape(-1)
-    received = lax.all_to_all(kv_cache[chosen], "blk", split_axis=0, concat_axis=0, tiled=True)
-    arriving = (myself - starts[:, None]) % blocks + peer_slots * blocks
-    present = (arriving < counts[:, None]).reshape(-1)
-    order_rank = jnp.cumsum(present.astype(jnp.int32)) - 1
-    choose = present[None, :] & (order_rank[None, :] == jnp.arange(pg, dtype=jnp.int32)[:, None])
-    positions = jnp.sum(
-        jnp.where(choose, jnp.arange(blocks * per_peer, dtype=jnp.int32)[None, :], 0), axis=1
-    )
-    own = received[positions]
+    if npages % blocks == 0:
+        sent = pick_pages(
+            send_kernel, page_table, kv_cache, blocks * per_peer, blocks, per_peer, slots_dev
+        )
+        received = lax.all_to_all(sent, "blk", split_axis=0, concat_axis=0, tiled=True)
+        own = pick_pages(compact_kernel, page_table, received, pg, blocks, per_peer, slots_dev)
+    else:
+        page_owner = page_table // slots_dev
+        owned = page_owner == myself
+        page_rank = jnp.cumsum(owned.astype(jnp.int32)) - 1
+        local_slot = page_table % slots_dev
+        counts = jnp.sum((page_owner[None, :] == block_ids[:, None]).astype(jnp.int32), axis=1)
+        starts = jnp.cumsum(counts) - counts
+        my_start = jnp.sum(jnp.where(block_ids == myself, starts, 0))
+        peer_slots = jnp.arange(per_peer, dtype=jnp.int32)[None, :]
+        wanted = (block_ids[:, None] - my_start) % blocks + peer_slots * blocks
+        picked = owned[None, None, :] & (page_rank[None, None, :] == wanted[..., None])
+        chosen = jnp.sum(jnp.where(picked, local_slot[None, None, :], 0), axis=2).reshape(-1)
+        received = lax.all_to_all(
+            kv_cache[chosen], "blk", split_axis=0, concat_axis=0, tiled=True
+        )
+        arriving = (myself - starts[:, None]) % blocks + peer_slots * blocks
+        present = (arriving < counts[:, None]).reshape(-1)
+        order_rank = jnp.cumsum(present.astype(jnp.int32)) - 1
+        choose = present[None, :] & (
+            order_rank[None, :] == jnp.arange(pg, dtype=jnp.int32)[:, None]
+        )
+        positions = jnp.sum(
+            jnp.where(choose, jnp.arange(blocks * per_peer, dtype=jnp.int32)[None, :], 0),
+            axis=1,
+        )
+        own = received[positions]
     gathered = lax.all_gather(own, "blk", axis=0, tiled=True)
     own, new_rows = lax.optimization_barrier((own, kv_new.transpose(1, 0, 2)))
     new_all = lax.all_gather(new_rows, "blk", axis=0)

time: 85.7 us -> 108 us (1.26)
  blocking collectives: 20 us -> 54.1 us
  Pallas kernels: 16.8 us -> 33.8 us
  waiting for transfers between devices: 15.8 us -> 2.75 us
  starting transfers between devices: 6.32 us -> 0.01 us
  local copies, waits for them, and re-layouts: 7.15 us -> 1.36 us
  other arithmetic: 5.11 us -> 1.43 us
    all_to_all x0 -> x1, blocking collectives: none -> 34.1 us  [local(): lax.all_to_all(sent, 'blk', split_axis=0, concat_axis=0, tiled=True)]
    pallas_call x0 -> x2, Pallas kernels: none -> 17 us  [pick_pages(): pl.pallas_call(body, out_shape=jax.ShapeDtypeStruct((count,) + source.sha...]
    all_to_all x1 -> x0, waiting for transfers between devices: 14.1 us -> none  [local(): lax.all_to_all(kv_cache[chosen], 'blk', split_axis=0, concat_axis=0, tile...]
    all_to_all x1 -> x0, starting transfers between devices: 6.32 us -> none  [local(): lax.all_to_all(kv_cache[chosen], 'blk', split_axis=0, concat_axis=0, tile...]
    gather x2 -> x0, local copies, waits for them, and re-layouts: 4.83 us -> none  [the longest x1 3.56 us: local(): kv_cache[chosen]]
    select_n x4 -> x0, other arithmetic: 1.33 us -> none  [the longest x1 0.66 us: local(): local_slot = page_table % slots_dev]
    another operation x4 -> x0, other arithmetic: 1.21 us -> none
  transfers between devices with their start and end apart: 2 -> 1, of which waited for: 2 -> 1; matrix products, arithmetic and copies ran while one was open for 3% -> 2% of each run, Pallas kernels for 9% -> 7%
where the time goes in v8:
time: 108 us
  blocking collectives  54.1 us (50%)
  Pallas kernels  33.8 us (31%)
  between operations  14.1 us (13%)
  waiting for transfers between devices  2.75 us (3%)
  other arithmetic  1.43 us (1%)
  local copies, waits for them, and re-layouts  1.36 us (1%)
    all_to_all x1, blocking collectives, local(): lax.all_to_all(sent, 'blk', split_axis=0, concat_axis=0, tiled=True)  34.1 us
    all_gather x1, blocking collectives, local(): new_all = lax.all_gather(new_rows, 'blk', axis=0)  20 us
    pallas_call x2, Pallas kernels, pick_pages(): pl.pallas_call(body, out_shape=jax.ShapeDtypeStruct((count,) + source.sha...  17 us
    pallas_call x1, Pallas kernels, prefix_part(): pl.pallas_call(kernel, out_shape=jax.ShapeDtypeStruct(q_new.shape, q_new....  9.53 us
    pallas_call x1, Pallas kernels, new_turn_part(): pl.pallas_call(kernel, out_shape=(state, stat, stat), grid_spec=pltpu.Pre...  7.31 us
    all_gather x1, waiting for transfers between devices, local(): gathered = lax.all_gather(own, 'blk', axis=0, tiled=True)  2.73 us
  transfers between devices with their start and end apart: 1, of which 1 were waited for; matrix products, arithmetic and copies ran while one was open for 2% of the time, Pallas kernels for 7%

profile of v8, /device:TPU:0, one launch (start us, length us, event | category | flops | bytes accessed | tf_op | source)
XLA Modules:
  0.0 107.5 jit_solution(16425764858513540049)
XLA Ops:
  6.5 0.0 copy-start
  6.5 0.0 copy-start.1
  6.5 0.0 all-gather.3.cloned.1.call-start
  6.5 6.0 %shard_map.55 = bf16[4,2,128,256]{3,2,1,0:T(8,128)(2,1)} custom-call(s32[8]{0:T(128)} %table_ref.3, bf16[32,2,128,256]{3,2,1,0:T(8,128)(2,1)} %cache_ref.1), custom_call_target="tpu_custom_call" | custom-call | tf_op jit(solution)/shard_map/pallas_call | solution.py:195
  12.6 34.1 %all_to_all.5.recv_ref = bf16[4,2,128,256]{3,2,1,0:T(8,128)(2,1)} all-to-all(bf16[4,2,128,256]{3,2,1,0:T(8,128)(2,1)} %shard_map.55), channel_id=1, replica_groups=mesh['groups'=2,'blk'=4,'pool'=4] {'blk'}, dimensions={0} | all-to-all | bytes 1048576 | tf_op jit(solution)/shard_map/all_to_all | solution.py:226
  46.7 10.9 %shard_map.56.own_ref = bf16[2,2,128,256]{3,2,1,0:T(8,128)(2,1)} custom-call(s32[8]{0:T(128)} %table_ref.3, bf16[4,2,128,256]{3,2,1,0:T(8,128)(2,1)} %all_to_all.5.recv_ref), custom_call_target="tpu_custom_call" | custom-call | tf_op jit(solution)/shard_map/pallas_call | solution.py:195
  57.6 0.0 all-gather.3.cloned.1.call-update
  57.6 0.0 copy-done
  57.7 0.1 fusion.1
  57.8 0.1 reshape.49
  57.8 0.0 copy-done.1
  57.8 0.7 broadcast_multiply_fusion
  59.2 0.6 iota_add_fusion
  59.9 20.0 %all-gather = bf16[8,128,256]{2,1,0:T(8,128)(2,1)} all-gather(bf16[2,128,256]{2,1,0:T(8,128)(2,1)S(1)} %bitcast.9), channel_id=2, replica_groups=mesh['groups'=2,'blk'=4,'pool'=4] {'blk'}, dimensions={0}, use_global_device_ids=true | all-gather | bytes 655360 | tf_op jit(solution)/shard_map/all_gather | solution.py:256
  79.9 0.6 broadcast_in_dim.19
  80.5 7.3 %shard_map.57 = (f32[128,2048]{1,0:T(8,128)}, f32[2,128,8]{2,1,0:T(8,128)}, f32[2,128,8]{2,1,0:T(8,128)}) custom-call(s32[1]{0:T(128)} %bitcast.1.query_start, bf16[128,2048]{1,0:T(8,128)(2,1)} %q_ref.3, bf16[4,2,128,256]{3,2,1,0:T(8,128)(2,1)} %bitcast.8, bf16[2,2,128,256]{3,2,1,0:T(8,128)(2,1)} %shard_map.56.own_ref, s32[1,512]{1,0:T(1,128)} %bitcast.11, ...), custom_call_target="tpu_custom_call" | custom-call | tf_op jit(solution)/shard_map/pallas_call | solution.py:98
  87.8 2.7 %all-gather.3.cloned.1.call-done.page_ref = bf16[8,2,128,256]{3,2,1,0:T(8,128)(2,1)} async-done(((bf16[2,2,128,256]{3,2,1,0:T(8,128)(2,1)}), bf16[8,2,128,256]{3,2,1,0:T(8,128)(2,1)}) %all-gather.3.cloned.1.call-update) | async-done | bytes 1048592 | tf_op jit(solution)/shard_map/all_gather | solution.py:254
  90.5 0.7 broadcast_in_dim.16
  91.2 9.5 %shard_map.58 = bf16[128,2048]{1,0:T(8,128)(2,1)} custom-call(bf16[128,2048]{1,0:T(8,128)(2,1)} %q_ref.3, bf16[8,2,128,256]{3,2,1,0:T(8,128)(2,1)} %all-gather.3.cloned.1.call-done.page_ref, s32[1,1024]{1,0:T(1,128)} %bitcast.10, f32[128,2048]{1,0:T(8,128)} %get-tuple-element.12.acc_ref, f32[2,128,8]{2,1,0:T(8,128)} %get-tuple-element.13.top_ref, ...), custom_call_target="tpu_custom_call" | custom-call | tf_op jit(solution)/shard_map/pallas_call | solution.py:123
  (4 shorter events, 0.0 us)
Async XLA Ops:
  6.5 51.1 %copy-start = (bf16[128,2,256]{2,1,0:T(2,128)(2,1)S(1)}, bf16[128,2,256]{2,1,0:T(2,128)(2,1)}, u32[]{:S(2)}) copy-start(bf16[128,2,256]{2,1,0:T(2,128)(2,1)} %param.6) | copy-start | bytes 393220
  6.5 51.3 %copy-start.1 = (s32[4]{0:T(128)S(1)}, s32[4]{0:T(128)}, u32[]{:S(2)}) copy-start(s32[4]{0:T(128)} %param.9) | copy-start | bytes 52
  6.5 84.0 %all-gather.3.cloned.1.call-start = ((), (), s32[]{:S(2)}) async-start(), calls=%async_computation.1 | async-start | bytes 1310720 | tf_op jit(solution)/shard_map/all_gather | solution.py:254
Sparse Core Ops, SparseCore 0:
  57.7 32.7 all-gather.2

commit v9 on v5

--- a/solution.py
+++ b/solution.py
@@ -111,9 +111,16 @@
     wanted = (block_ids[:, None] - my_start) % blocks + peer_slots * blocks
     picked = owned[None, None, :] & (page_rank[None, None, :] == wanted[..., None])
     chosen = jnp.sum(jnp.where(picked, local_slot[None, None, :], 0), axis=2).reshape(-1)
-    received = lax.all_to_all(kv_cache[chosen], "blk", split_axis=0, concat_axis=0, tiled=True)
+    by_shift = chosen.reshape(blocks, per_peer)[(myself + block_ids) % blocks].reshape(-1)
+    sent = kv_cache[by_shift].reshape((blocks, per_peer) + kv_cache.shape[1:])
+    arrived = [sent[0]]
+    for k in range(1, blocks):
+        arrived.append(
+            lax.ppermute(sent[k], "blk", [(i, (i + k) % blocks) for i in range(blocks)])
+        )
+    received = jnp.stack(arrived).reshape((blocks * per_peer,) + kv_cache.shape[1:])
     arriving = (myself - starts[:, None]) % blocks + peer_slots * blocks
-    present = (arriving < counts[:, None]).reshape(-1)
+    present = (arriving < counts[:, None])[(myself - block_ids) % blocks].reshape(-1)
     order_rank = jnp.cumsum(present.astype(jnp.int32)) - 1
     choose = present[None, :] & (order_rank[None, :] == jnp.arange(pg, dtype=jnp.int32)[:, None])
     positions = jnp.sum(

time: 84.7 us -> 79.7 us (0.941)
  waiting for transfers between devices: 23.1 us -> 15.6 us
  starting transfers between devices: 6.32 us -> 7.93 us
  blocking collectives: 20.1 us -> 21.3 us
    all_to_all x1 -> x0, waiting for transfers between devices: 14.1 us -> none  [local(): lax.all_to_all(kv_cache[chosen], 'blk', split_axis=0, concat_axis=0, tile...]
    ppermute x0 -> x3, starting transfers between devices: none -> 7.93 us  [local(): lax.ppermute(sent[k], 'blk', [(i, (i + k) % blocks) for i in range(blocks)])]
    all_to_all x1 -> x0, starting transfers between devices: 6.32 us -> none  [local(): lax.all_to_all(kv_cache[chosen], 'blk', split_axis=0, concat_axis=0, tile...]
    ppermute x0 -> x3, waiting for transfers between devices: none -> 5.88 us  [local(): lax.ppermute(sent[k], 'blk', [(i, (i + k) % blocks) for i in range(blocks)])]
    all_gather x1, blocking collectives: 20.1 us -> 21.3 us  [local(): new_all = lax.all_gather(kv_new.transpose(1, 0, 2), 'blk', axis=0)]
    unnamed x1 -> x3, local copies, waits for them, and re-layouts: 0.92 us -> 0.02 us
    gather x1 -> x3, local copies, waits for them, and re-layouts: 3.56 us -> 4.05 us  [the longest x1 2.77 us: local(): sent = kv_cache[by_shift].reshape((blocks, per_peer) + kv_cache.shape[1:])]
  transfers between devices with their start and end apart: 2 -> 4, of which waited for: 2 -> 3; matrix products, arithmetic and copies ran while one was open for 2% -> 2% of each run, Pallas kernels for 0% -> 0%
where the time goes in v9:
time: 79.7 us; the launch traced here: 79.5 us
  blocking collectives  21.3 us (27%)
  waiting for transfers between devices  15.6 us (20%)
  between operations  14.2 us (18%)
  Pallas kernels  9.22 us (12%)
  starting transfers between devices  7.93 us (10%)
  local copies, waits for them, and re-layouts  6.11 us (8%)
  other arithmetic  5.17 us (6%)
    all_gather x1, blocking collectives, local(): new_all = lax.all_gather(kv_new.transpose(1, 0, 2), 'blk', axis=0)  21.3 us
    all_gather x1, waiting for transfers between devices, local(): gathered = lax.all_gather(received[positions], 'blk', axis=0, tiled=True)  9.69 us
    pallas_call x1, Pallas kernels, attention(): pl.pallas_call(kernel, out_shape=jax.ShapeDtypeStruct(q_new.shape, q_new....  9.22 us
    ppermute x3, starting transfers between devices, local(): lax.ppermute(sent[k], 'blk', [(i, (i + k) % blocks) for i in range(blocks)])  7.93 us
    ppermute x3, waiting for transfers between devices, local(): lax.ppermute(sent[k], 'blk', [(i, (i + k) % blocks) for i in range(blocks)])  5.88 us
    gather x1, local copies, waits for them, and re-layouts, local(): sent = kv_cache[by_shift].reshape((blocks, per_peer) + kv_cache.shape[1:])  2.77 us
  transfers between devices with their start and end apart: 4, of which 3 were waited for; matrix products, arithmetic and copies ran while one was open for 2% of the time, Pallas kernels for 0%

profile of v9, /device:TPU:0, one launch (start us, length us, event | category | flops | bytes accessed | tf_op | source)
XLA Modules:
  0.0 79.5 jit_solution(2181726337888063362)
XLA Ops:
  6.5 0.0 copy-start
  6.5 0.0 all-gather.4.cloned.1.call-start
  6.5 0.7 and_select_fusion.4
  7.3 0.7 convert_bitcast_fusion.1
  7.9 0.2 reduce-window.21
  8.1 0.1 convert_reduce_fusion
  8.2 0.2 reduce-window.22
  8.4 1.4 %broadcast_multiply_fusion = (s32[4]{0:T(128)S(1)}, s32[]{:T(128)}, s32[]{:T(128)}) fusion(s32[4]{0:T(128)} %param.9, s32[]{:T(128)S(6)} %axis_index.15, s32[4]{0:T(128)S(1)} %convert_reduce_fusion, s32[4,1]{0,1:T(1,128)S(1)} %reduce-window.22), kind=kLoop, calls=%fused_computation.59 | loop fusion | flops 26 | bytes 76 | tf_op jit(solution)/shard_map/mul | solution.py:135
  9.8 0.7 and_select_fusion.5
  10.5 0.2 select_reduce_fusion
  10.6 0.6 gather_fusion
  11.3 2.8 %gather_fusion.1 = bf16[4,2,128,256]{3,2,1,0:T(8,128)(2,1)S(1)} fusion(bf16[32,2,128,256]{3,2,1,0:T(8,128)(2,1)} %param.7, s32[1024]{0:T(1024)S(1)} %pad_clamp_fusion.2), kind=kCustom, calls=%fused_computation.1 | custom fusion | bytes 1048592 | tf_op jit(solution)/shard_map/gather | solution.py:115
  14.1 4.1 %collective-permute-start.1 = (bf16[1,2,128,256]{3,2,1,0:T(8,128)(2,1)S(1)}, bf16[1,2,128,256]{3,2,1,0:T(8,128)(2,1)S(1)}, u32[]{:S(2)}, u32[]{:S(2)}) collective-permute-start(bf16[1,2,128,256]{3,2,1,0:T(8,128)(2,1)S(1)} %get-tuple-element.9), channel_id=1, source_target_pairs={{0,8},{4,12},{8,0},{12,4},{1,9},{5,13},{9,1},{13,5},{2,10},{6,14},... | collective-permute-start | bytes 393224 | tf_op jit(solution)/shard_map/ppermute | solution.py:119
  18.2 1.6 %collective-permute-start = (bf16[1,2,128,256]{3,2,1,0:T(8,128)(2,1)S(1)}, bf16[1,2,128,256]{3,2,1,0:T(8,128)(2,1)S(1)}, u32[]{:S(2)}, u32[]{:S(2)}) collective-permute-start(bf16[1,2,128,256]{3,2,1,0:T(8,128)(2,1)S(1)} %get-tuple-element.10), channel_id=1, source_target_pairs={{0,4},{4,8},{8,12},{12,0},{1,5},{5,9},{9,13},{13,1},{2,6},{6,10},{... | collective-permute-start | bytes 393224 | tf_op jit(solution)/shard_map/ppermute | solution.py:119
  19.8 2.2 %collective-permute-start.2 = (bf16[1,2,128,256]{3,2,1,0:T(8,128)(2,1)S(1)}, bf16[1,2,128,256]{3,2,1,0:T(8,128)(2,1)S(1)}, u32[]{:S(2)}, u32[]{:S(2)}) collective-permute-start(bf16[1,2,128,256]{3,2,1,0:T(8,128)(2,1)S(1)} %get-tuple-element.11), channel_id=1, source_target_pairs={{0,12},{4,0},{8,4},{12,8},{1,13},{5,1},{9,5},{13,9},{2,14},{6,2},{... | collective-permute-start | bytes 393224 | tf_op jit(solution)/shard_map/ppermute | solution.py:119
  22.1 0.6 gather_fusion.2
  22.7 0.2 reduce-window.23
  22.9 0.1 fusion.1
  23.0 5.2 %collective-permute-done.1 = bf16[1,2,128,256]{3,2,1,0:T(8,128)(2,1)S(1)} collective-permute-done((bf16[1,2,128,256]{3,2,1,0:T(8,128)(2,1)S(1)}, bf16[1,2,128,256]{3,2,1,0:T(8,128)(2,1)S(1)}, u32[]{:S(2)}, u32[]{:S(2)}) %collective-permute-start.1) | collective-permute-done | bytes 131104 | tf_op jit(solution)/shard_map/ppermute | solution.py:119
  28.2 0.0 collective-permute-done
  28.2 0.7 collective-permute-done.2
  28.9 0.1 maximum_bitcast_fusion
  29.0 1.3 %gather_fusion.3 = bf16[2,2,128,256]{3,2,1,0:T(8,128)(2,1)} fusion(bf16[4,2,128,256]{3,2,1,0:T(8,128)(2,1)S(1)} %maximum_bitcast_fusion, s32[1024]{0:T(1024)S(1)} %pad_clamp_fusion), kind=kCustom, calls=%fused_computation.3 | custom fusion | bytes 524296 | tf_op jit(solution)/shard_map/gather | solution.py:129
  30.3 0.0 all-gather.4.cloned.1.call-update
  30.3 0.1 reshape.429
  30.4 0.0 copy-done
  31.1 21.3 %all-gather = bf16[8,128,256]{2,1,0:T(8,128)(2,1)} all-gather(bf16[2,128,256]{2,1,0:T(8,128)(2,1)S(1)} %bitcast.43), channel_id=2, replica_groups=mesh['groups'=2,'blk'=4,'pool'=4] {'blk'}, dimensions={0}, use_global_device_ids=true | all-gather | bytes 655360 | tf_op jit(solution)/shard_map/all_gather | solution.py:100
  52.4 0.6 iota_add_fusion
  53.1 9.7 %all-gather.4.cloned.1.call-done.page_ref = bf16[8,2,128,256]{3,2,1,0:T(8,128)(2,1)} async-done(((bf16[2,2,128,256]{3,2,1,0:T(8,128)(2,1)}), bf16[8,2,128,256]{3,2,1,0:T(8,128)(2,1)}) %all-gather.4.cloned.1.call-update) | async-done | bytes 1048592 | tf_op jit(solution)/shard_map/all_gather | solution.py:129
  62.7 0.7 broadcast_in_dim.59
  63.4 9.2 %shard_map.55 = bf16[128,2048]{1,0:T(8,128)(2,1)} custom-call(s32[1]{0:T(128)} %bitcast.query_start, bf16[128,2048]{1,0:T(8,128)(2,1)} %q_ref.1, bf16[4,2,128,256]{3,2,1,0:T(8,128)(2,1)} %bitcast.42, bf16[8,2,128,256]{3,2,1,0:T(8,128)(2,1)} %all-gather.4.cloned.1.call-done.page_ref, s32[1,512]{1,0:T(1,128)} %bitcast.48, s32[1,1024]{1,0:T(1,128)} %bitcast.47), custom_call_target="tpu_custom_call" | custom-call | tf_op jit(solution)/shard_map/pallas_call | solution.py:70
  (15 shorter events, 0.1 us)
Async XLA Ops:
  6.5 23.9 %copy-start = (bf16[128,2,256]{2,1,0:T(2,128)(2,1)S(1)}, bf16[128,2,256]{2,1,0:T(2,128)(2,1)}, u32[]{:S(2)}) copy-start(bf16[128,2,256]{2,1,0:T(2,128)(2,1)} %param.6) | copy-start | bytes 393220
  6.5 56.2 %all-gather.4.cloned.1.call-start = ((), (), s32[]{:S(2)}) async-start(), calls=%async_computation | async-start | bytes 1310720 | tf_op jit(solution)/shard_map/all_gather | solution.py:129
  14.1 14.1 %collective-permute-start.1 = (bf16[1,2,128,256]{3,2,1,0:T(8,128)(2,1)S(1)}, bf16[1,2,128,256]{3,2,1,0:T(8,128)(2,1)S(1)}, u32[]{:S(2)}, u32[]{:S(2)}) collective-permute-start(bf16[1,2,128,256]{3,2,1,0:T(8,128)(2,1)S(1)} %get-tuple-element.9), channel_id=1, source_target_pairs={{0,8},{4,12},{8,0},{12,4},{1,9},{5,13},{9,1},{13,5},{2,10},{6,14},... | collective-permute-start | bytes 393224 | tf_op jit(solution)/shard_map/ppermute | solution.py:119
  18.2 10.0 %collective-permute-start = (bf16[1,2,128,256]{3,2,1,0:T(8,128)(2,1)S(1)}, bf16[1,2,128,256]{3,2,1,0:T(8,128)(2,1)S(1)}, u32[]{:S(2)}, u32[]{:S(2)}) collective-permute-start(bf16[1,2,128,256]{3,2,1,0:T(8,128)(2,1)S(1)} %get-tuple-element.10), channel_id=1, source_target_pairs={{0,4},{4,8},{8,12},{12,0},{1,5},{5,9},{9,13},{13,1},{2,6},{6,10},{... | collective-permute-start | bytes 393224 | tf_op jit(solution)/shard_map/ppermute | solution.py:119
  19.8 9.1 %collective-permute-start.2 = (bf16[1,2,128,256]{3,2,1,0:T(8,128)(2,1)S(1)}, bf16[1,2,128,256]{3,2,1,0:T(8,128)(2,1)S(1)}, u32[]{:S(2)}, u32[]{:S(2)}) collective-permute-start(bf16[1,2,128,256]{3,2,1,0:T(8,128)(2,1)S(1)} %get-tuple-element.11), channel_id=1, source_target_pairs={{0,12},{4,0},{8,4},{12,8},{1,13},{5,1},{9,5},{13,9},{2,14},{6,2},{... | collective-permute-start | bytes 393224 | tf_op jit(solution)/shard_map/ppermute | solution.py:119
Sparse Core Ops, SparseCore 0:
  30.4 32.2 all-gather.3

commit v10 on v9

--- a/solution.py
+++ b/solution.py
@@ -97,7 +97,14 @@
     block_ids = jnp.arange(blocks, dtype=jnp.int32)
     my_offset = jnp.sum(jnp.where(block_ids == myself, block_offsets, 0))
 
-    new_all = lax.all_gather(kv_new.transpose(1, 0, 2), "blk", axis=0)
+    own_rows = kv_new.transpose(1, 0, 2)
+    new_all = [own_rows]
+    for k in range(1, blocks):
+        new_all.append(
+            lax.ppermute(own_rows, "blk", [(i, (i + k) % blocks) for i in range(blocks)])
+        )
+    new_all = jnp.stack(new_all)
+    shifted_offsets = block_offsets[(myself - block_ids) % blocks]
 
     page_owner = page_table // slots_dev
     owned = page_owner == myself
@@ -113,6 +120,7 @@
     chosen = jnp.sum(jnp.where(picked, local_slot[None, None, :], 0), axis=2).reshape(-1)
     by_shift = chosen.reshape(blocks, per_peer)[(myself + block_ids) % blocks].reshape(-1)
     sent = kv_cache[by_shift].reshape((blocks, per_peer) + kv_cache.shape[1:])
+    sent, new_all = lax.optimization_barrier((sent, new_all))
     arrived = [sent[0]]
     for k in range(1, blocks):
         arrived.append(
@@ -132,7 +140,7 @@
     page_len = kv_cache.shape[2]
     query_start = (my_offset * q_rows).reshape(1).astype(jnp.int32)
     key_pos = (
-        jnp.repeat(block_offsets, q_rows) * q_rows
+        jnp.repeat(shifted_offsets, q_rows) * q_rows
         + jnp.tile(jnp.arange(q_rows, dtype=jnp.int32), blocks)
     ).reshape(1, -1).astype(jnp.int32)
     page_ok = (

time: 79.7 us -> 85 us (1.066)
  waiting for transfers between devices: 15.6 us -> 39.3 us
  blocking collectives: 21.3 us -> 0 us
  local copies, waits for them, and re-layouts: 6.11 us -> 7.67 us
    all_gather x1 -> x0, blocking collectives: 21.3 us -> none  [local(): new_all = lax.all_gather(kv_new.transpose(1, 0, 2), 'blk', axis=0)]
    all_gather x1, waiting for transfers between devices: 9.69 us -> 26.2 us  [local(): gathered = lax.all_gather(received[positions], 'blk', axis=0, tiled=True)]
    ppermute x0 -> x3, starting transfers between devices: none -> 6.11 us  [local(): lax.ppermute(own_rows, 'blk', [(i, (i + k) % blocks) for i in range(block...]
    ppermute x3, starting transfers between devices: 7.93 us -> 2.32 us  [local(): lax.ppermute(sent[k], 'blk', [(i, (i + k) % blocks) for i in range(blocks)])]
    ppermute x3, waiting for transfers between devices: 5.88 us -> 10.6 us  [local(): lax.ppermute(sent[k], 'blk', [(i, (i + k) % blocks) for i in range(blocks)])]
    ppermute x0 -> x3, waiting for transfers between devices: none -> 2.48 us  [local(): lax.ppermute(own_rows, 'blk', [(i, (i + k) % blocks) for i in range(block...]
    mul x1, other arithmetic: 1.37 us -> 0.01 us  [local(): jnp.repeat(shifted_offsets, q_rows) * q_rows]
    reduce_sum x0 -> x1, other arithmetic: none -> 1.32 us  [local(): my_offset = jnp.sum(jnp.where(block_ids == myself, block_offsets, 0))]
  transfers between devices with their start and end apart: 4 -> 7, of which waited for: 3 -> 4; matrix products, arithmetic and copies ran while one was open for 2% -> 12% of each run, Pallas kernels for 0% -> 0%
where the time goes in v10:
time: 85 us; the launch traced here: 84.7 us
  waiting for transfers between devices  39.3 us (46%)
  between operations  14.1 us (17%)
  Pallas kernels  9.23 us (11%)
  starting transfers between devices  8.44 us (10%)
  local copies, waits for them, and re-layouts  7.67 us (9%)
  other arithmetic  5.97 us (7%)
    all_gather x1, waiting for transfers between devices, local(): gathered = lax.all_gather(received[positions], 'blk', axis=0, tiled=True)  26.2 us
    ppermute x3, waiting for transfers between devices, local(): lax.ppermute(sent[k], 'blk', [(i, (i + k) % blocks) for i in range(blocks)])  10.6 us
    pallas_call x1, Pallas kernels, attention(): pl.pallas_call(kernel, out_shape=jax.ShapeDtypeStruct(q_new.shape, q_new....  9.23 us
    ppermute x3, starting transfers between devices, local(): lax.ppermute(own_rows, 'blk', [(i, (i + k) % blocks) for i in range(block...  6.11 us
    gather x1, local copies, waits for them, and re-layouts, local(): sent = kv_cache[by_shift].reshape((blocks, per_peer) + kv_cache.shape[1:])  2.77 us
    ppermute x3, waiting for transfers between devices, local(): lax.ppermute(own_rows, 'blk', [(i, (i + k) % blocks) for i in range(block...  2.48 us
    ppermute x3, starting transfers between devices, local(): lax.ppermute(sent[k], 'blk', [(i, (i + k) % blocks) for i in range(blocks)])  2.32 us
  transfers between devices with their start and end apart: 7, of which 4 were waited for; matrix products, arithmetic and copies ran while one was open for 12% of the time, Pallas kernels for 0%

profile of v10, /device:TPU:0, one launch (start us, length us, event | category | flops | bytes accessed | tf_op | source)
XLA Modules:
  0.0 84.7 jit_solution(4326612615026014522)
XLA Ops:
  6.5 0.0 copy-start
  6.5 0.0 all-gather.3.cloned.1.call-start
  6.5 0.9 %copy.24 = bf16[128,2,256]{2,0,1:T(8,128)(2,1)S(1)} copy(bf16[128,2,256]{2,1,0:T(2,128)(2,1)} %param.6) | data formatting | bytes 262144 | tf_op args[1]
  7.5 3.1 %collective-permute-start = (bf16[2,128,256]{2,1,0:T(8,128)(2,1)S(1)}, bf16[2,128,256]{2,1,0:T(8,128)(2,1)S(1)}, u32[]{:S(2)}, u32[]{:S(2)}) collective-permute-start(bf16[2,128,256]{2,1,0:T(8,128)(2,1)S(1)} %bitcast.55), channel_id=1, source_target_pairs={{0,4},{4,8},{8,12},{12,0},{1,5},{5,9},{9,13},{13,1},{2,6},{6,10},{... | collective-permute-start | bytes 393224 | tf_op jit(solution)/shard_map/ppermute | solution.py:104
  10.5 2.1 %collective-permute-start.2 = (bf16[2,128,256]{2,1,0:T(8,128)(2,1)S(1)}, bf16[2,128,256]{2,1,0:T(8,128)(2,1)S(1)}, u32[]{:S(2)}, u32[]{:S(2)}) collective-permute-start(bf16[2,128,256]{2,1,0:T(8,128)(2,1)S(1)} %bitcast.56), channel_id=1, source_target_pairs={{0,12},{4,0},{8,4},{12,8},{1,13},{5,1},{9,5},{13,9},{2,14},{6,2},{... | collective-permute-start | bytes 393224 | tf_op jit(solution)/shard_map/ppermute | solution.py:104
  12.6 0.9 %collective-permute-start.1 = (bf16[2,128,256]{2,1,0:T(8,128)(2,1)S(1)}, bf16[2,128,256]{2,1,0:T(8,128)(2,1)S(1)}, u32[]{:S(2)}, u32[]{:S(2)}) collective-permute-start(bf16[2,128,256]{2,1,0:T(8,128)(2,1)S(1)} %bitcast.57), channel_id=1, source_target_pairs={{0,8},{4,12},{8,0},{12,4},{1,9},{5,13},{9,1},{13,5},{2,10},{6,14},... | collective-permute-start | bytes 393224 | tf_op jit(solution)/shard_map/ppermute | solution.py:104
  13.6 0.7 and_select_fusion.4
  14.3 0.7 convert_bitcast_fusion.1
  14.9 0.2 reduce-window.21
  15.1 0.1 convert_reduce_fusion
  15.2 0.2 reduce-window.22
  15.4 1.3 %fusion.2 = (s32[]{:T(128)}, s32[]{:T(128)}) fusion(s32[4]{0:T(128)} %param.9, s32[]{:T(128)S(6)} %axis_index.15, s32[4]{0:T(128)S(1)} %convert_reduce_fusion, s32[4,1]{0,1:T(1,128)S(1)} %reduce-window.22), kind=kLoop, calls=%fused_computation.48 | loop fusion | flops 22 | bytes 60 | tf_op jit(solution)/shard_map/reduce_sum | solution.py:98
  16.8 0.7 and_select_fusion.5
  17.4 0.2 select_reduce_fusion
  17.6 0.6 gather_fusion
  18.3 0.6 gather_fusion.2
  18.9 0.2 reduce-window.23
  19.1 2.8 %gather_fusion.1 = bf16[4,2,128,256]{3,2,1,0:T(8,128)(2,1)S(1)} fusion(bf16[32,2,128,256]{3,2,1,0:T(8,128)(2,1)} %param.7, s32[1024]{0:T(1024)S(1)} %pad_clamp_fusion.2), kind=kCustom, calls=%fused_computation.1 | custom fusion | bytes 1048592 | tf_op jit(solution)/shard_map/gather | solution.py:122
  21.9 0.1 fusion.1
  22.0 0.0 collective-permute-done
  22.0 0.0 collective-permute-done.2
  22.0 2.5 %collective-permute-done.1 = bf16[2,128,256]{2,1,0:T(8,128)(2,1)S(1)} collective-permute-done((bf16[2,128,256]{2,1,0:T(8,128)(2,1)S(1)}, bf16[2,128,256]{2,1,0:T(8,128)(2,1)S(1)}, u32[]{:S(2)}, u32[]{:S(2)}) %collective-permute-start.1) | collective-permute-done | bytes 131104 | tf_op jit(solution)/shard_map/ppermute | solution.py:104
  24.5 0.9 %pad_maximum_fusion.new_ref = bf16[4,2,128,256]{3,2,1,0:T(8,128)(2,1)} fusion(bf16[1,2,128,256]{3,2,1,0:T(8,128)(2,1)S(1)} %bitcast.60, bf16[1,2,128,256]{3,2,1,0:T(8,128)(2,1)S(1)} %bitcast.61, bf16[1,2,128,256]{3,2,1,0:T(8,128)(2,1)S(1)} %bitcast.59, bf16[1,2,128,256]{3,2,1,0:T(8,128)(2,1)S(1)} %bitcast.58), kind=kLoop, calls=%fused_computation.5 | loop fusion | flops 786432 | bytes 1048576 | tf_op jit(solution)/shard_map/stack | solution.py:106
  25.4 1.7 %collective-permute-start.5 = (bf16[1,2,128,256]{3,2,1,0:T(8,128)(2,1)S(1)}, bf16[1,2,128,256]{3,2,1,0:T(8,128)(2,1)S(1)}, u32[]{:S(2)}, u32[]{:S(2)}) collective-permute-start(bf16[1,2,128,256]{3,2,1,0:T(8,128)(2,1)S(1)} %slice_bitcast_fusion.2), channel_id=1, source_target_pairs={{0,12},{4,0},{8,4},{12,8},{1,13},{5,1},{9,5},{13,9},{2,14},{6,2},{... | collective-permute-start | bytes 393224 | tf_op jit(solution)/shard_map/ppermute | solution.py:127
  27.1 0.1 collective-permute-start.4
  27.2 0.6 collective-permute-start.3
  27.8 3.6 %collective-permute-done.5 = bf16[1,2,128,256]{3,2,1,0:T(8,128)(2,1)S(1)} collective-permute-done((bf16[1,2,128,256]{3,2,1,0:T(8,128)(2,1)S(1)}, bf16[1,2,128,256]{3,2,1,0:T(8,128)(2,1)S(1)}, u32[]{:S(2)}, u32[]{:S(2)}) %collective-permute-start.5) | collective-permute-done | bytes 131104 | tf_op jit(solution)/shard_map/ppermute | solution.py:127
  31.3 7.1 %collective-permute-done.4 = bf16[1,2,128,256]{3,2,1,0:T(8,128)(2,1)S(1)} collective-permute-done((bf16[1,2,128,256]{3,2,1,0:T(8,128)(2,1)S(1)}, bf16[1,2,128,256]{3,2,1,0:T(8,128)(2,1)S(1)}, u32[]{:S(2)}, u32[]{:S(2)}) %collective-permute-start.4) | collective-permute-done | bytes 131104 | tf_op jit(solution)/shard_map/ppermute | solution.py:127
  38.4 0.0 collective-permute-done.3
  38.4 0.1 maximum_bitcast_fusion
  38.5 1.3 %gather_fusion.3 = bf16[2,2,128,256]{3,2,1,0:T(8,128)(2,1)} fusion(bf16[4,2,128,256]{3,2,1,0:T(8,128)(2,1)S(1)} %maximum_bitcast_fusion, s32[1024]{0:T(1024)S(1)} %pad_clamp_fusion), kind=kCustom, calls=%fused_computation.3 | custom fusion | bytes 524296 | tf_op jit(solution)/shard_map/gather | solution.py:137
  39.7 0.0 all-gather.3.cloned.1.call-update
  39.7 0.0 copy-done
  39.8 0.6 gather_fusion.4
  40.4 0.1 reshape.425
  41.1 0.6 iota_add_fusion
  41.8 26.2 %all-gather.3.cloned.1.call-done.page_ref = bf16[8,2,128,256]{3,2,1,0:T(8,128)(2,1)} async-done(((bf16[2,2,128,256]{3,2,1,0:T(8,128)(2,1)}), bf16[8,2,128,256]{3,2,1,0:T(8,128)(2,1)}) %all-gather.3.cloned.1.call-update) | async-done | bytes 1048592 | tf_op jit(solution)/shard_map/all_gather | solution.py:137
  68.0 0.7 broadcast_in_dim.60
  68.7 9.2 %shard_map.55 = bf16[128,2048]{1,0:T(8,128)(2,1)} custom-call(s32[1]{0:T(128)} %bitcast.query_start, bf16[128,2048]{1,0:T(8,128)(2,1)} %q_ref.1, bf16[4,2,128,256]{3,2,1,0:T(8,128)(2,1)} %pad_maximum_fusion.new_ref, bf16[8,2,128,256]{3,2,1,0:T(8,128)(2,1)} %all-gather.3.cloned.1.call-done.page_ref, s32[1,512]{1,0:T(1,128)} %bitcast.66, s32[1,1024]{1,0:T(1,128)} %bitcast.65), custom_call_target="tpu_custom_call" | custom-call | tf_op jit(solution)/shard_map/pallas_call | solution.py:70
  (16 shorter events, 0.1 us)
Async XLA Ops:
  6.5 33.2 %copy-start = (s32[4]{0:T(128)S(1)}, s32[4]{0:T(128)}, u32[]{:S(2)}) copy-start(s32[4]{0:T(128)} %param.9) | copy-start | bytes 52
  6.5 61.5 %all-gather.3.cloned.1.call-start = ((), (), s32[]{:S(2)}) async-start(), calls=%async_computation | async-start | bytes 1310720 | tf_op jit(solution)/shard_map/all_gather | solution.py:137
  7.5 14.5 %collective-permute-start = (bf16[2,128,256]{2,1,0:T(8,128)(2,1)S(1)}, bf16[2,128,256]{2,1,0:T(8,128)(2,1)S(1)}, u32[]{:S(2)}, u32[]{:S(2)}) collective-permute-start(bf16[2,128,256]{2,1,0:T(8,128)(2,1)S(1)} %bitcast.55), channel_id=1, source_target_pairs={{0,4},{4,8},{8,12},{12,0},{1,5},{5,9},{9,13},{13,1},{2,6},{6,10},{... | collective-permute-start | bytes 393224 | tf_op jit(solution)/shard_map/ppermute | solution.py:104
  10.5 11.5 %collective-permute-start.2 = (bf16[2,128,256]{2,1,0:T(8,128)(2,1)S(1)}, bf16[2,128,256]{2,1,0:T(8,128)(2,1)S(1)}, u32[]{:S(2)}, u32[]{:S(2)}) collective-permute-start(bf16[2,128,256]{2,1,0:T(8,128)(2,1)S(1)} %bitcast.56), channel_id=1, source_target_pairs={{0,12},{4,0},{8,4},{12,8},{1,13},{5,1},{9,5},{13,9},{2,14},{6,2},{... | collective-permute-start | bytes 393224 | tf_op jit(solution)/shard_map/ppermute | solution.py:104
  12.6 11.9 %collective-permute-start.1 = (bf16[2,128,256]{2,1,0:T(8,128)(2,1)S(1)}, bf16[2,128,256]{2,1,0:T(8,128)(2,1)S(1)}, u32[]{:S(2)}, u32[]{:S(2)}) collective-permute-start(bf16[2,128,256]{2,1,0:T(8,128)(2,1)S(1)} %bitcast.57), channel_id=1, source_target_pairs={{0,8},{4,12},{8,0},{12,4},{1,9},{5,13},{9,1},{13,5},{2,10},{6,14},... | collective-permute-start | bytes 393224 | tf_op jit(solution)/shard_map/ppermute | solution.py:104
  25.4 5.9 %collective-permute-start.5 = (bf16[1,2,128,256]{3,2,1,0:T(8,128)(2,1)S(1)}, bf16[1,2,128,256]{3,2,1,0:T(8,128)(2,1)S(1)}, u32[]{:S(2)}, u32[]{:S(2)}) collective-permute-start(bf16[1,2,128,256]{3,2,1,0:T(8,128)(2,1)S(1)} %slice_bitcast_fusion.2), channel_id=1, source_target_pairs={{0,12},{4,0},{8,4},{12,8},{1,13},{5,1},{9,5},{13,9},{2,14},{6,2},{... | collective-permute-start | bytes 393224 | tf_op jit(solution)/shard_map/ppermute | solution.py:127
  27.1 11.3 %collective-permute-start.4 = (bf16[1,2,128,256]{3,2,1,0:T(8,128)(2,1)S(1)}, bf16[1,2,128,256]{3,2,1,0:T(8,128)(2,1)S(1)}, u32[]{:S(2)}, u32[]{:S(2)}) collective-permute-start(bf16[1,2,128,256]{3,2,1,0:T(8,128)(2,1)S(1)} %get-tuple-element.13), channel_id=1, source_target_pairs={{0,8},{4,12},{8,0},{12,4},{1,9},{5,13},{9,1},{13,5},{2,10},{6,14},... | collective-permute-start | bytes 393224 | tf_op jit(solution)/shard_map/ppermute | solution.py:127
  27.2 11.2 %collective-permute-start.3 = (bf16[1,2,128,256]{3,2,1,0:T(8,128)(2,1)S(1)}, bf16[1,2,128,256]{3,2,1,0:T(8,128)(2,1)S(1)}, u32[]{:S(2)}, u32[]{:S(2)}) collective-permute-start(bf16[1,2,128,256]{3,2,1,0:T(8,128)(2,1)S(1)} %get-tuple-element.14), channel_id=1, source_target_pairs={{0,4},{4,8},{8,12},{12,0},{1,5},{5,9},{9,13},{13,1},{2,6},{6,10},{... | collective-permute-start | bytes 393224 | tf_op jit(solution)/shard_map/ppermute | solution.py:127
Sparse Core Ops, SparseCore 0:
  39.9 28.0 all-gather.2

commit v11 on v10

--- a/solution.py
+++ b/solution.py
@@ -134,7 +134,13 @@
     positions = jnp.sum(
         jnp.where(choose, jnp.arange(blocks * per_peer, dtype=jnp.int32)[None, :], 0), axis=1
     )
-    gathered = lax.all_gather(received[positions], "blk", axis=0, tiled=True)
+    own = received[positions]
+    gathered = [own]
+    for k in range(1, blocks):
+        gathered.append(
+            lax.ppermute(own, "blk", [(i, (i + k) % blocks) for i in range(blocks)])
+        )
+    gathered = jnp.concatenate(gathered)
 
     q_rows = q_new.shape[0]
     page_len = kv_cache.shape[2]
@@ -144,7 +150,8 @@
         + jnp.tile(jnp.arange(q_rows, dtype=jnp.int32), blocks)
     ).reshape(1, -1).astype(jnp.int32)
     page_ok = (
-        jnp.arange(pg, dtype=jnp.int32)[None, :] * blocks + block_ids[:, None] < npages
+        jnp.arange(pg, dtype=jnp.int32)[None, :] * blocks + ((myself - block_ids) % blocks)[:, None]
+        < npages
     ).reshape(-1)
     page_ok = jnp.repeat(page_ok.astype(jnp.int32), page_len).reshape(1, -1)
     return attention(

time: 85 us -> 66.5 us (0.78)
  the two profiles are of different devices: /device:TPU:0 before, /device:TPU:9 now
where the time goes in v11:
time: 66.5 us; the launch traced here: 66.3 us
  waiting for transfers between devices  33.9 us (51%)
  Pallas kernels  9.23 us (14%)
  other arithmetic  7.76 us (12%)
  starting transfers between devices  7.64 us (11%)
  local copies, waits for them, and re-layouts  6.96 us (10%)
  between operations  0.75 us (1%)
    ppermute x3, waiting for transfers between devices, local(): lax.ppermute(own, 'blk', [(i, (i + k) % blocks) for i in range(blocks)])  20.8 us
    ppermute x3, waiting for transfers between devices, local(): lax.ppermute(sent[k], 'blk', [(i, (i + k) % blocks) for i in range(blocks)])  11.3 us
    pallas_call x1, Pallas kernels, attention(): pl.pallas_call(kernel, out_shape=jax.ShapeDtypeStruct(q_new.shape, q_new....  9.23 us
    ppermute x3, starting transfers between devices, local(): lax.ppermute(own_rows, 'blk', [(i, (i + k) % blocks) for i in range(block...  3.83 us
    gather x1, local copies, waits for them, and re-layouts, local(): sent = kv_cache[by_shift].reshape((blocks, per_peer) + kv_cache.shape[1:])  2.77 us
    ppermute x3, starting transfers between devices, local(): lax.ppermute(own, 'blk', [(i, (i + k) % blocks) for i in range(blocks)])  2 us
    ppermute x3, waiting for transfers between devices, local(): lax.ppermute(own_rows, 'blk', [(i, (i + k) % blocks) for i in range(block...  1.81 us
    ppermute x3, starting transfers between devices, local(): lax.ppermute(sent[k], 'blk', [(i, (i + k) % blocks) for i in range(blocks)])  1.81 us
  transfers between devices with their start and end apart: 9, of which 7 were waited for; matrix products, arithmetic and copies ran while one was open for 16% of the time, Pallas kernels for 0%

profile of v11, /device:TPU:9, one launch (start us, length us, event | category | flops | bytes accessed | tf_op | source)
XLA Modules:
  0.0 66.3 jit_solution(10694650318880414035)
XLA Ops:
  0.0 0.0 copy-start
  0.0 0.9 %copy.20 = bf16[128,2,256]{2,0,1:T(8,128)(2,1)S(1)} copy(bf16[128,2,256]{2,1,0:T(2,128)(2,1)} %param.6) | data formatting | bytes 262144 | tf_op args[1]
  0.9 1.3 %collective-permute-start = (bf16[2,128,256]{2,1,0:T(8,128)(2,1)S(1)}, bf16[2,128,256]{2,1,0:T(8,128)(2,1)S(1)}, u32[]{:S(2)}, u32[]{:S(2)}) collective-permute-start(bf16[2,128,256]{2,1,0:T(8,128)(2,1)S(1)} %bitcast.55), channel_id=1, source_target_pairs={{0,4},{4,8},{8,12},{12,0},{1,5},{5,9},{9,13},{13,1},{2,6},{6,10},{... | collective-permute-start | bytes 393224 | tf_op jit(solution)/shard_map/ppermute | solution.py:104
  2.3 1.1 %collective-permute-start.1 = (bf16[2,128,256]{2,1,0:T(8,128)(2,1)S(1)}, bf16[2,128,256]{2,1,0:T(8,128)(2,1)S(1)}, u32[]{:S(2)}, u32[]{:S(2)}) collective-permute-start(bf16[2,128,256]{2,1,0:T(8,128)(2,1)S(1)} %bitcast.56), channel_id=1, source_target_pairs={{0,8},{4,12},{8,0},{12,4},{1,9},{5,13},{9,1},{13,5},{2,10},{6,14},... | collective-permute-start | bytes 393224 | tf_op jit(solution)/shard_map/ppermute | solution.py:104
  3.4 1.4 %collective-permute-start.2 = (bf16[2,128,256]{2,1,0:T(8,128)(2,1)S(1)}, bf16[2,128,256]{2,1,0:T(8,128)(2,1)S(1)}, u32[]{:S(2)}, u32[]{:S(2)}) collective-permute-start(bf16[2,128,256]{2,1,0:T(8,128)(2,1)S(1)} %bitcast.57), channel_id=1, source_target_pairs={{0,12},{4,0},{8,4},{12,8},{1,13},{5,1},{9,5},{13,9},{2,14},{6,2},{... | collective-permute-start | bytes 393224 | tf_op jit(solution)/shard_map/ppermute | solution.py:104
  4.8 0.7 and_select_fusion.5
  5.4 0.7 %convert_bitcast_fusion.1 = (s32[8,1]{0,1:T(1,128)S(1)}, pred[8]{0:T(512)(128)(4,1)S(1)}, s32[8]{0:T(128)S(1)}) fusion(s32[]{:T(128)S(6)} %axis_index.15, s32[8]{0:T(128)} %param.8), kind=kLoop, calls=%fused_computation.65 | loop fusion | flops 136 | bytes 108 | tf_op jit(solution)/shard_map/convert
  6.1 0.1 convert_reduce_fusion
  6.2 0.2 reduce-window.22
  6.4 0.6 fusion.3
  7.1 0.7 and_select_fusion.6
  7.7 0.2 reduce-window.21
  7.9 0.2 select_reduce_fusion
  8.1 0.6 gather_fusion
  8.8 0.6 gather_fusion.2
  9.4 0.2 reduce-window.23
  9.6 1.3 %and_select_fusion = (s32[4]{0:T(128)S(1)}, s32[]{:T(128)}) fusion(s32[]{:T(128)S(6)} %axis_index.15, s32[4]{0:T(128)} %param.9), kind=kLoop, calls=%fused_computation.37 | loop fusion | flops 59 | bytes 40 | tf_op jit(solution)/shard_map/jit(remainder)/select_n | solution.py:131
  10.9 0.1 fusion
  11.0 2.8 %gather_fusion.1 = bf16[4,2,128,256]{3,2,1,0:T(8,128)(2,1)S(1)} fusion(bf16[32,2,128,256]{3,2,1,0:T(8,128)(2,1)} %param.7, s32[1024]{0:T(1024)S(1)} %pad_clamp_fusion.2), kind=kCustom, calls=%fused_computation.1 | custom fusion | bytes 1048592 | tf_op jit(solution)/shard_map/gather | solution.py:122
  13.7 0.1 fusion.1
  13.9 0.0 collective-permute-done
  13.9 0.0 collective-permute-done.1
  13.9 1.8 %collective-permute-done.2 = bf16[2,128,256]{2,1,0:T(8,128)(2,1)S(1)} collective-permute-done((bf16[2,128,256]{2,1,0:T(8,128)(2,1)S(1)}, bf16[2,128,256]{2,1,0:T(8,128)(2,1)S(1)}, u32[]{:S(2)}, u32[]{:S(2)}) %collective-permute-start.2) | collective-permute-done | bytes 131104 | tf_op jit(solution)/shard_map/ppermute | solution.py:104
  15.7 0.9 %pad_maximum_fusion.1.new_ref = bf16[4,2,128,256]{3,2,1,0:T(8,128)(2,1)} fusion(bf16[1,2,128,256]{3,2,1,0:T(8,128)(2,1)S(1)} %bitcast.61, bf16[1,2,128,256]{3,2,1,0:T(8,128)(2,1)S(1)} %bitcast.60, bf16[1,2,128,256]{3,2,1,0:T(8,128)(2,1)S(1)} %bitcast.59, bf16[1,2,128,256]{3,2,1,0:T(8,128)(2,1)S(1)} %bitcast.58), kind=kLoop, calls=%fused_computation.6 | loop fusion | flops 786432 | bytes 1048576 | tf_op jit(solution)/shard_map/stack | solution.py:106
  16.6 0.1 collective-permute-start.3
  16.7 1.3 %collective-permute-start.4 = (bf16[1,2,128,256]{3,2,1,0:T(8,128)(2,1)S(1)}, bf16[1,2,128,256]{3,2,1,0:T(8,128)(2,1)S(1)}, u32[]{:S(2)}, u32[]{:S(2)}) collective-permute-start(bf16[1,2,128,256]{3,2,1,0:T(8,128)(2,1)S(1)} %get-tuple-element.13), channel_id=1, source_target_pairs={{0,8},{4,12},{8,0},{12,4},{1,9},{5,13},{9,1},{13,5},{2,10},{6,14},... | collective-permute-start | bytes 393224 | tf_op jit(solution)/shard_map/ppermute | solution.py:127
  18.0 0.4 collective-permute-start.5
  18.4 0.0 copy-done
  18.4 0.6 gather_fusion.4
  19.1 2.2 %collective-permute-done.3 = bf16[1,2,128,256]{3,2,1,0:T(8,128)(2,1)S(1)} collective-permute-done((bf16[1,2,128,256]{3,2,1,0:T(8,128)(2,1)S(1)}, bf16[1,2,128,256]{3,2,1,0:T(8,128)(2,1)S(1)}, u32[]{:S(2)}, u32[]{:S(2)}) %collective-permute-start.3) | collective-permute-done | bytes 131104 | tf_op jit(solution)/shard_map/ppermute | solution.py:127
  21.2 6.5 %collective-permute-done.4 = bf16[1,2,128,256]{3,2,1,0:T(8,128)(2,1)S(1)} collective-permute-done((bf16[1,2,128,256]{3,2,1,0:T(8,128)(2,1)S(1)}, bf16[1,2,128,256]{3,2,1,0:T(8,128)(2,1)S(1)}, u32[]{:S(2)}, u32[]{:S(2)}) %collective-permute-start.4) | collective-permute-done | bytes 131104 | tf_op jit(solution)/shard_map/ppermute | solution.py:127
  27.8 2.6 %collective-permute-done.5 = bf16[1,2,128,256]{3,2,1,0:T(8,128)(2,1)S(1)} collective-permute-done((bf16[1,2,128,256]{3,2,1,0:T(8,128)(2,1)S(1)}, bf16[1,2,128,256]{3,2,1,0:T(8,128)(2,1)S(1)}, u32[]{:S(2)}, u32[]{:S(2)}) %collective-permute-start.5) | collective-permute-done | bytes 131104 | tf_op jit(solution)/shard_map/ppermute | solution.py:127
  30.4 0.1 maximum_bitcast_fusion
  30.5 0.6 gather_fusion.3
  31.1 0.1 collective-permute-start.6
  31.1 0.6 collective-permute-start.7
  31.7 1.4 %collective-permute-start.8 = (bf16[2,2,128,256]{3,2,1,0:T(8,128)(2,1)S(1)}, bf16[2,2,128,256]{3,2,1,0:T(8,128)(2,1)S(1)}, u32[]{:S(2)}, u32[]{:S(2)}) collective-permute-start(bf16[2,2,128,256]{3,2,1,0:T(8,128)(2,1)S(1)} %gather_fusion.3), channel_id=1, source_target_pairs={{0,12},{4,0},{8,4},{12,8},{1,13},{5,1},{9,5},{13,9},{2,14},{6,2},{... | collective-permute-start | bytes 786440 | tf_op jit(solution)/shard_map/ppermute | solution.py:141
  33.1 0.1 reshape.427
  33.8 0.6 iota_add_fusion
  34.5 4.0 %collective-permute-done.6 = bf16[2,2,128,256]{3,2,1,0:T(8,128)(2,1)S(1)} collective-permute-done((bf16[2,2,128,256]{3,2,1,0:T(8,128)(2,1)S(1)}, bf16[2,2,128,256]{3,2,1,0:T(8,128)(2,1)S(1)}, u32[]{:S(2)}, u32[]{:S(2)}) %collective-permute-start.6) | collective-permute-done | bytes 262176 | tf_op jit(solution)/shard_map/ppermute | solution.py:141
  38.5 15.0 %collective-permute-done.7 = bf16[2,2,128,256]{3,2,1,0:T(8,128)(2,1)S(1)} collective-permute-done((bf16[2,2,128,256]{3,2,1,0:T(8,128)(2,1)S(1)}, bf16[2,2,128,256]{3,2,1,0:T(8,128)(2,1)S(1)}, u32[]{:S(2)}, u32[]{:S(2)}) %collective-permute-start.7) | collective-permute-done | bytes 262176 | tf_op jit(solution)/shard_map/ppermute | solution.py:141
  53.5 1.8 %collective-permute-done.8 = bf16[2,2,128,256]{3,2,1,0:T(8,128)(2,1)S(1)} collective-permute-done((bf16[2,2,128,256]{3,2,1,0:T(8,128)(2,1)S(1)}, bf16[2,2,128,256]{3,2,1,0:T(8,128)(2,1)S(1)}, u32[]{:S(2)}, u32[]{:S(2)}) %collective-permute-start.8) | collective-permute-done | bytes 262176 | tf_op jit(solution)/shard_map/ppermute | solution.py:141
  55.3 1.1 %pad_maximum_fusion.page_ref = bf16[8,2,128,256]{3,2,1,0:T(8,128)(2,1)} fusion(bf16[2,2,128,256]{3,2,1,0:T(8,128)(2,1)S(1)} %collective-permute-done.8, bf16[2,2,128,256]{3,2,1,0:T(8,128)(2,1)S(1)} %collective-permute-done.7, bf16[2,2,128,256]{3,2,1,0:T(8,128)(2,1)S(1)} %collective-permute-done.6, bf16[2,2,128,256]{3,2,1,0:T(8,128)(2,1)S(1)} %gather_fusion.3), kind=kLoop, calls=%fused_computation.5 | loop fusion | flops 1572864 | bytes 2097152 | tf_op jit(solution)/shard_map/concatenate | solution.py:143
  56.4 0.7 broadcast_in_dim.60
  57.0 9.2 %shard_map.55 = bf16[128,2048]{1,0:T(8,128)(2,1)} custom-call(s32[1]{0:T(128)} %bitcast.query_start, bf16[128,2048]{1,0:T(8,128)(2,1)} %q_ref.1, bf16[4,2,128,256]{3,2,1,0:T(8,128)(2,1)} %pad_maximum_fusion.1.new_ref, bf16[8,2,128,256]{3,2,1,0:T(8,128)(2,1)} %pad_maximum_fusion.page_ref, s32[1,512]{1,0:T(1,128)} %bitcast.66, s32[1,1024]{1,0:T(1,128)} %bitcast.65), custom_call_target="tpu_custom_call" | custom-call | tf_op jit(solution)/shard_map/pallas_call | solution.py:70
  (15 shorter events, 0.1 us)
Async XLA Ops:
  0.0 18.4 %copy-start = (s32[4]{0:T(128)S(1)}, s32[4]{0:T(128)}, u32[]{:S(2)}) copy-start(s32[4]{0:T(128)} %param.9) | copy-start | bytes 52
  0.9 12.9 %collective-permute-start = (bf16[2,128,256]{2,1,0:T(8,128)(2,1)S(1)}, bf16[2,128,256]{2,1,0:T(8,128)(2,1)S(1)}, u32[]{:S(2)}, u32[]{:S(2)}) collective-permute-start(bf16[2,128,256]{2,1,0:T(8,128)(2,1)S(1)} %bitcast.55), channel_id=1, source_target_pairs={{0,4},{4,8},{8,12},{12,0},{1,5},{5,9},{9,13},{13,1},{2,6},{6,10},{... | collective-permute-start | bytes 393224 | tf_op jit(solution)/shard_map/ppermute | solution.py:104
  2.3 11.6 %collective-permute-start.1 = (bf16[2,128,256]{2,1,0:T(8,128)(2,1)S(1)}, bf16[2,128,256]{2,1,0:T(8,128)(2,1)S(1)}, u32[]{:S(2)}, u32[]{:S(2)}) collective-permute-start(bf16[2,128,256]{2,1,0:T(8,128)(2,1)S(1)} %bitcast.56), channel_id=1, source_target_pairs={{0,8},{4,12},{8,0},{12,4},{1,9},{5,13},{9,1},{13,5},{2,10},{6,14},... | collective-permute-start | bytes 393224 | tf_op jit(solution)/shard_map/ppermute | solution.py:104
  3.4 12.3 %collective-permute-start.2 = (bf16[2,128,256]{2,1,0:T(8,128)(2,1)S(1)}, bf16[2,128,256]{2,1,0:T(8,128)(2,1)S(1)}, u32[]{:S(2)}, u32[]{:S(2)}) collective-permute-start(bf16[2,128,256]{2,1,0:T(8,128)(2,1)S(1)} %bitcast.57), channel_id=1, source_target_pairs={{0,12},{4,0},{8,4},{12,8},{1,13},{5,1},{9,5},{13,9},{2,14},{6,2},{... | collective-permute-start | bytes 393224 | tf_op jit(solution)/shard_map/ppermute | solution.py:104
  16.6 4.6 %collective-permute-start.3 = (bf16[1,2,128,256]{3,2,1,0:T(8,128)(2,1)S(1)}, bf16[1,2,128,256]{3,2,1,0:T(8,128)(2,1)S(1)}, u32[]{:S(2)}, u32[]{:S(2)}) collective-permute-start(bf16[1,2,128,256]{3,2,1,0:T(8,128)(2,1)S(1)} %get-tuple-element.14), channel_id=1, source_target_pairs={{0,4},{4,8},{8,12},{12,0},{1,5},{5,9},{9,13},{13,1},{2,6},{6,10},{... | collective-permute-start | bytes 393224 | tf_op jit(solution)/shard_map/ppermute | solution.py:127
  16.7 11.1 %collective-permute-start.4 = (bf16[1,2,128,256]{3,2,1,0:T(8,128)(2,1)S(1)}, bf16[1,2,128,256]{3,2,1,0:T(8,128)(2,1)S(1)}, u32[]{:S(2)}, u32[]{:S(2)}) collective-permute-start(bf16[1,2,128,256]{3,2,1,0:T(8,128)(2,1)S(1)} %get-tuple-element.13), channel_id=1, source_target_pairs={{0,8},{4,12},{8,0},{12,4},{1,9},{5,13},{9,1},{13,5},{2,10},{6,14},... | collective-permute-start | bytes 393224 | tf_op jit(solution)/shard_map/ppermute | solution.py:127
  18.0 12.4 %collective-permute-start.5 = (bf16[1,2,128,256]{3,2,1,0:T(8,128)(2,1)S(1)}, bf16[1,2,128,256]{3,2,1,0:T(8,128)(2,1)S(1)}, u32[]{:S(2)}, u32[]{:S(2)}) collective-permute-start(bf16[1,2,128,256]{3,2,1,0:T(8,128)(2,1)S(1)} %slice_bitcast_fusion.2), channel_id=1, source_target_pairs={{0,12},{4,0},{8,4},{12,8},{1,13},{5,1},{9,5},{13,9},{2,14},{6,2},{... | collective-permute-start | bytes 393224 | tf_op jit(solution)/shard_map/ppermute | solution.py:127
  31.1 7.4 %collective-permute-start.6 = (bf16[2,2,128,256]{3,2,1,0:T(8,128)(2,1)S(1)}, bf16[2,2,128,256]{3,2,1,0:T(8,128)(2,1)S(1)}, u32[]{:S(2)}, u32[]{:S(2)}) collective-permute-start(bf16[2,2,128,256]{3,2,1,0:T(8,128)(2,1)S(1)} %gather_fusion.3), channel_id=1, source_target_pairs={{0,4},{4,8},{8,12},{12,0},{1,5},{5,9},{9,13},{13,1},{2,6},{6,10},{... | collective-permute-start | bytes 786440 | tf_op jit(solution)/shard_map/ppermute | solution.py:141
  31.1 22.3 %collective-permute-start.7 = (bf16[2,2,128,256]{3,2,1,0:T(8,128)(2,1)S(1)}, bf16[2,2,128,256]{3,2,1,0:T(8,128)(2,1)S(1)}, u32[]{:S(2)}, u32[]{:S(2)}) collective-permute-start(bf16[2,2,128,256]{3,2,1,0:T(8,128)(2,1)S(1)} %gather_fusion.3), channel_id=1, source_target_pairs={{0,8},{4,12},{8,0},{12,4},{1,9},{5,13},{9,1},{13,5},{2,10},{6,14},... | collective-permute-start | bytes 786440 | tf_op jit(solution)/shard_map/ppermute | solution.py:141
  31.7 23.6 %collective-permute-start.8 = (bf16[2,2,128,256]{3,2,1,0:T(8,128)(2,1)S(1)}, bf16[2,2,128,256]{3,2,1,0:T(8,128)(2,1)S(1)}, u32[]{:S(2)}, u32[]{:S(2)}) collective-permute-start(bf16[2,2,128,256]{3,2,1,0:T(8,128)(2,1)S(1)} %gather_fusion.3), channel_id=1, source_target_pairs={{0,12},{4,0},{8,4},{12,8},{1,13},{5,1},{9,5},{13,9},{2,14},{6,2},{... | collective-permute-start | bytes 786440 | tf_op jit(solution)/shard_map/ppermute | solution.py:141

commit v12 on v11

--- a/solution.py
+++ b/solution.py
@@ -28,8 +28,13 @@
     page_visible = page_ok_ref[...] > 0
     dims = (((1,), (1,)), ((), ()))
     pv = (((1,), (0,)), ((), ()))
-    for h in range(group_size):
-        queries = q_ref[:, h * head_size : (h + 1) * head_size]
+    stack = 2 if group_size % 2 == 0 else 1
+    new_visible = jnp.concatenate([new_visible] * stack, axis=0)
+    for c in range(group_size // stack):
+        heads = range(c * stack, (c + 1) * stack)
+        queries = jnp.concatenate(
+            [q_ref[:, h * head_size : (h + 1) * head_size] for h in heads], axis=0
+        )
         new_scores = lax.dot_general(
             queries, new_keys, dims, preferred_element_type=jnp.float32
         ) * scale
@@ -55,7 +60,9 @@
             page_weights.astype(jnp.bfloat16), page_values, pv,
             preferred_element_type=jnp.float32,
         )
-        o_ref[:, h * head_size : (h + 1) * head_size] = (summed / row_total).astype(o_ref.dtype)
+        result = (summed / row_total).astype(o_ref.dtype)
+        for j, h in enumerate(heads):
+            o_ref[:, h * head_size : (h + 1) * head_size] = result[j * q_rows : (j + 1) * q_rows]
 
 
 def attention(query_start, key_pos, page_ok, q_new, new_all, pages, group_size, head_size,

time: 66.5 us -> 65.1 us (0.979)
  Pallas kernels: 9.23 us -> 7.82 us
    pallas_call x1, Pallas kernels: 9.23 us -> 7.82 us  [attention(): pl.pallas_call(kernel, out_shape=jax.ShapeDtypeStruct(q_new.shape, q_new....]
where the time goes in v12:
time: 65.1 us; the launch traced here: 64.9 us
  waiting for transfers between devices  33.9 us (52%)
  Pallas kernels  7.82 us (12%)
  other arithmetic  7.76 us (12%)
  starting transfers between devices  7.64 us (12%)
  local copies, waits for them, and re-layouts  6.96 us (11%)
  between operations  0.75 us (1%)
    ppermute x3, waiting for transfers between devices, local(): lax.ppermute(own, 'blk', [(i, (i + k) % blocks) for i in range(blocks)])  20.8 us
    ppermute x3, waiting for transfers between devices, local(): lax.ppermute(sent[k], 'blk', [(i, (i + k) % blocks) for i in range(blocks)])  11.3 us
    pallas_call x1, Pallas kernels, attention(): pl.pallas_call(kernel, out_shape=jax.ShapeDtypeStruct(q_new.shape, q_new....  7.82 us
    ppermute x3, starting transfers between devices, local(): lax.ppermute(own_rows, 'blk', [(i, (i + k) % blocks) for i in range(block...  3.83 us
    gather x1, local copies, waits for them, and re-layouts, local(): sent = kv_cache[by_shift].reshape((blocks, per_peer) + kv_cache.shape[1:])  2.77 us
    ppermute x3, starting transfers between devices, local(): lax.ppermute(own, 'blk', [(i, (i + k) % blocks) for i in range(blocks)])  2 us
    ppermute x3, waiting for transfers between devices, local(): lax.ppermute(own_rows, 'blk', [(i, (i + k) % blocks) for i in range(block...  1.81 us
    ppermute x3, starting transfers between devices, local(): lax.ppermute(sent[k], 'blk', [(i, (i + k) % blocks) for i in range(blocks)])  1.81 us
  transfers between devices with their start and end apart: 9, of which 7 were waited for; matrix products, arithmetic and copies ran while one was open for 16% of the time, Pallas kernels for 0%

profile of v12, /device:TPU:9, one launch (start us, length us, event | category | flops | bytes accessed | tf_op | source)
XLA Modules:
  0.0 64.9 jit_solution(5868741382651291081)
XLA Ops:
  0.0 0.0 copy-start
  0.0 0.9 %copy.20 = bf16[128,2,256]{2,0,1:T(8,128)(2,1)S(1)} copy(bf16[128,2,256]{2,1,0:T(2,128)(2,1)} %param.6) | data formatting | bytes 262144 | tf_op args[1]
  0.9 1.3 %collective-permute-start = (bf16[2,128,256]{2,1,0:T(8,128)(2,1)S(1)}, bf16[2,128,256]{2,1,0:T(8,128)(2,1)S(1)}, u32[]{:S(2)}, u32[]{:S(2)}) collective-permute-start(bf16[2,128,256]{2,1,0:T(8,128)(2,1)S(1)} %bitcast.55), channel_id=1, source_target_pairs={{0,4},{4,8},{8,12},{12,0},{1,5},{5,9},{9,13},{13,1},{2,6},{6,10},{... | collective-permute-start | bytes 393224 | tf_op jit(solution)/shard_map/ppermute | solution.py:111
  2.3 1.1 %collective-permute-start.1 = (bf16[2,128,256]{2,1,0:T(8,128)(2,1)S(1)}, bf16[2,128,256]{2,1,0:T(8,128)(2,1)S(1)}, u32[]{:S(2)}, u32[]{:S(2)}) collective-permute-start(bf16[2,128,256]{2,1,0:T(8,128)(2,1)S(1)} %bitcast.56), channel_id=1, source_target_pairs={{0,8},{4,12},{8,0},{12,4},{1,9},{5,13},{9,1},{13,5},{2,10},{6,14},... | collective-permute-start | bytes 393224 | tf_op jit(solution)/shard_map/ppermute | solution.py:111
  3.4 1.4 %collective-permute-start.2 = (bf16[2,128,256]{2,1,0:T(8,128)(2,1)S(1)}, bf16[2,128,256]{2,1,0:T(8,128)(2,1)S(1)}, u32[]{:S(2)}, u32[]{:S(2)}) collective-permute-start(bf16[2,128,256]{2,1,0:T(8,128)(2,1)S(1)} %bitcast.57), channel_id=1, source_target_pairs={{0,12},{4,0},{8,4},{12,8},{1,13},{5,1},{9,5},{13,9},{2,14},{6,2},{... | collective-permute-start | bytes 393224 | tf_op jit(solution)/shard_map/ppermute | solution.py:111
  4.8 0.7 %and_select_fusion.5 = s32[8]{0:T(128)S(1)} fusion(s32[8]{0:T(128)} %param.8), kind=kLoop, calls=%fused_computation.43 | loop fusion | flops 88 | bytes 64 | tf_op jit(solution)/shard_map/jit(remainder)/select_n | solution.py:119
  5.4 0.7 %convert_bitcast_fusion.1 = (s32[8,1]{0,1:T(1,128)S(1)}, pred[8]{0:T(512)(128)(4,1)S(1)}, s32[8]{0:T(128)S(1)}) fusion(s32[]{:T(128)S(6)} %axis_index.15, s32[8]{0:T(128)} %param.8), kind=kLoop, calls=%fused_computation.65 | loop fusion | flops 136 | bytes 108 | tf_op jit(solution)/shard_map/convert
  6.1 0.1 convert_reduce_fusion
  6.2 0.2 reduce-window.22
  6.4 0.6 fusion.3
  7.1 0.7 %and_select_fusion.6 = s32[4]{0:T(128)S(1)} fusion(s32[]{:T(128)} %fusion.3), kind=kLoop, calls=%fused_computation.44 | loop fusion | flops 48 | bytes 20 | tf_op jit(solution)/shard_map/jit(remainder)/select_n | solution.py:125
  7.7 0.2 reduce-window.21
  7.9 0.2 select_reduce_fusion
  8.1 0.6 gather_fusion
  8.8 0.6 gather_fusion.2
  9.4 0.2 reduce-window.23
  9.6 1.3 %and_select_fusion = (s32[4]{0:T(128)S(1)}, s32[]{:T(128)}) fusion(s32[]{:T(128)S(6)} %axis_index.15, s32[4]{0:T(128)} %param.9), kind=kLoop, calls=%fused_computation.37 | loop fusion | flops 59 | bytes 40 | tf_op jit(solution)/shard_map/jit(remainder)/select_n | solution.py:138
  10.9 0.1 fusion
  11.0 2.8 %gather_fusion.1 = bf16[4,2,128,256]{3,2,1,0:T(8,128)(2,1)S(1)} fusion(bf16[32,2,128,256]{3,2,1,0:T(8,128)(2,1)} %param.7, s32[1024]{0:T(1024)S(1)} %pad_clamp_fusion.2), kind=kCustom, calls=%fused_computation.1 | custom fusion | bytes 1048592 | tf_op jit(solution)/shard_map/gather | solution.py:129
  13.7 0.1 fusion.1
  13.9 0.0 collective-permute-done
  13.9 0.0 collective-permute-done.1
  13.9 1.8 %collective-permute-done.2 = bf16[2,128,256]{2,1,0:T(8,128)(2,1)S(1)} collective-permute-done((bf16[2,128,256]{2,1,0:T(8,128)(2,1)S(1)}, bf16[2,128,256]{2,1,0:T(8,128)(2,1)S(1)}, u32[]{:S(2)}, u32[]{:S(2)}) %collective-permute-start.2) | collective-permute-done | bytes 131104 | tf_op jit(solution)/shard_map/ppermute | solution.py:111
  15.7 0.9 %pad_maximum_fusion.1.new_ref = bf16[4,2,128,256]{3,2,1,0:T(8,128)(2,1)} fusion(bf16[1,2,128,256]{3,2,1,0:T(8,128)(2,1)S(1)} %bitcast.61, bf16[1,2,128,256]{3,2,1,0:T(8,128)(2,1)S(1)} %bitcast.60, bf16[1,2,128,256]{3,2,1,0:T(8,128)(2,1)S(1)} %bitcast.59, bf16[1,2,128,256]{3,2,1,0:T(8,128)(2,1)S(1)} %bitcast.58), kind=kLoop, calls=%fused_computation.6 | loop fusion | flops 786432 | bytes 1048576 | tf_op jit(solution)/shard_map/stack | solution.py:113
  16.6 0.1 collective-permute-start.3
  16.7 1.3 %collective-permute-start.4 = (bf16[1,2,128,256]{3,2,1,0:T(8,128)(2,1)S(1)}, bf16[1,2,128,256]{3,2,1,0:T(8,128)(2,1)S(1)}, u32[]{:S(2)}, u32[]{:S(2)}) collective-permute-start(bf16[1,2,128,256]{3,2,1,0:T(8,128)(2,1)S(1)} %get-tuple-element.13), channel_id=1, source_target_pairs={{0,8},{4,12},{8,0},{12,4},{1,9},{5,13},{9,1},{13,5},{2,10},{6,14},... | collective-permute-start | bytes 393224 | tf_op jit(solution)/shard_map/ppermute | solution.py:134
  18.0 0.4 collective-permute-start.5
  18.4 0.0 copy-done
  18.4 0.6 gather_fusion.4
  19.1 2.2 %collective-permute-done.3 = bf16[1,2,128,256]{3,2,1,0:T(8,128)(2,1)S(1)} collective-permute-done((bf16[1,2,128,256]{3,2,1,0:T(8,128)(2,1)S(1)}, bf16[1,2,128,256]{3,2,1,0:T(8,128)(2,1)S(1)}, u32[]{:S(2)}, u32[]{:S(2)}) %collective-permute-start.3) | collective-permute-done | bytes 131104 | tf_op jit(solution)/shard_map/ppermute | solution.py:134
  21.2 6.5 %collective-permute-done.4 = bf16[1,2,128,256]{3,2,1,0:T(8,128)(2,1)S(1)} collective-permute-done((bf16[1,2,128,256]{3,2,1,0:T(8,128)(2,1)S(1)}, bf16[1,2,128,256]{3,2,1,0:T(8,128)(2,1)S(1)}, u32[]{:S(2)}, u32[]{:S(2)}) %collective-permute-start.4) | collective-permute-done | bytes 131104 | tf_op jit(solution)/shard_map/ppermute | solution.py:134
  27.8 2.6 %collective-permute-done.5 = bf16[1,2,128,256]{3,2,1,0:T(8,128)(2,1)S(1)} collective-permute-done((bf16[1,2,128,256]{3,2,1,0:T(8,128)(2,1)S(1)}, bf16[1,2,128,256]{3,2,1,0:T(8,128)(2,1)S(1)}, u32[]{:S(2)}, u32[]{:S(2)}) %collective-permute-start.5) | collective-permute-done | bytes 131104 | tf_op jit(solution)/shard_map/ppermute | solution.py:134
  30.4 0.1 maximum_bitcast_fusion
  30.5 0.6 gather_fusion.3
  31.1 0.1 collective-permute-start.6
  31.1 0.6 collective-permute-start.7
  31.7 1.4 %collective-permute-start.8 = (bf16[2,2,128,256]{3,2,1,0:T(8,128)(2,1)S(1)}, bf16[2,2,128,256]{3,2,1,0:T(8,128)(2,1)S(1)}, u32[]{:S(2)}, u32[]{:S(2)}) collective-permute-start(bf16[2,2,128,256]{3,2,1,0:T(8,128)(2,1)S(1)} %gather_fusion.3), channel_id=1, source_target_pairs={{0,12},{4,0},{8,4},{12,8},{1,13},{5,1},{9,5},{13,9},{2,14},{6,2},{... | collective-permute-start | bytes 786440 | tf_op jit(solution)/shard_map/ppermute | solution.py:148
  33.1 0.1 reshape.427
  33.8 0.6 %iota_add_fusion = s32[4,128]{1,0:T(4,128)} fusion(s32[4]{0:T(128)S(1)} %broadcast_multiply_fusion), kind=kLoop, calls=%fused_computation.32 | loop fusion | flops 512 | bytes 2064 | tf_op jit(solution)/shard_map/add | solution.py:156
  34.5 4.0 %collective-permute-done.6 = bf16[2,2,128,256]{3,2,1,0:T(8,128)(2,1)S(1)} collective-permute-done((bf16[2,2,128,256]{3,2,1,0:T(8,128)(2,1)S(1)}, bf16[2,2,128,256]{3,2,1,0:T(8,128)(2,1)S(1)}, u32[]{:S(2)}, u32[]{:S(2)}) %collective-permute-start.6) | collective-permute-done | bytes 262176 | tf_op jit(solution)/shard_map/ppermute | solution.py:148
  38.5 15.0 %collective-permute-done.7 = bf16[2,2,128,256]{3,2,1,0:T(8,128)(2,1)S(1)} collective-permute-done((bf16[2,2,128,256]{3,2,1,0:T(8,128)(2,1)S(1)}, bf16[2,2,128,256]{3,2,1,0:T(8,128)(2,1)S(1)}, u32[]{:S(2)}, u32[]{:S(2)}) %collective-permute-start.7) | collective-permute-done | bytes 262176 | tf_op jit(solution)/shard_map/ppermute | solution.py:148
  53.5 1.8 %collective-permute-done.8 = bf16[2,2,128,256]{3,2,1,0:T(8,128)(2,1)S(1)} collective-permute-done((bf16[2,2,128,256]{3,2,1,0:T(8,128)(2,1)S(1)}, bf16[2,2,128,256]{3,2,1,0:T(8,128)(2,1)S(1)}, u32[]{:S(2)}, u32[]{:S(2)}) %collective-permute-start.8) | collective-permute-done | bytes 262176 | tf_op jit(solution)/shard_map/ppermute | solution.py:148
  55.3 1.1 %pad_maximum_fusion.page_ref = bf16[8,2,128,256]{3,2,1,0:T(8,128)(2,1)} fusion(bf16[2,2,128,256]{3,2,1,0:T(8,128)(2,1)S(1)} %collective-permute-done.8, bf16[2,2,128,256]{3,2,1,0:T(8,128)(2,1)S(1)} %collective-permute-done.7, bf16[2,2,128,256]{3,2,1,0:T(8,128)(2,1)S(1)} %collective-permute-done.6, bf16[2,2,128,256]{3,2,1,0:T(8,128)(2,1)S(1)} %gather_fusion.3), kind=kLoop, calls=%fused_computation.5 | loop fusion | flops 1572864 | bytes 2097152 | tf_op jit(solution)/shard_map/concatenate | solution.py:150
  56.4 0.7 %broadcast_in_dim.60 = s32[8,128]{1,0:T(8,128)} broadcast(s32[8]{0:T(128)S(1)} %reshape.427), dimensions={0} | broadcast | bytes 4128 | tf_op jit(solution)/shard_map/broadcast_in_dim | solution.py:163
  57.0 7.8 %shard_map.55 = bf16[128,2048]{1,0:T(8,128)(2,1)} custom-call(s32[1]{0:T(128)} %bitcast.query_start, bf16[128,2048]{1,0:T(8,128)(2,1)} %q_ref.1, bf16[4,2,128,256]{3,2,1,0:T(8,128)(2,1)} %pad_maximum_fusion.1.new_ref, bf16[8,2,128,256]{3,2,1,0:T(8,128)(2,1)} %pad_maximum_fusion.page_ref, s32[1,512]{1,0:T(1,128)} %bitcast.66, s32[1,1024]{1,0:T(1,128)} %bitcast.65), custom_call_target="tpu_custom_call" | custom-call | tf_op jit(solution)/shard_map/pallas_call | solution.py:77
  (15 shorter events, 0.1 us)
Async XLA Ops:
  0.0 18.4 %copy-start = (s32[4]{0:T(128)S(1)}, s32[4]{0:T(128)}, u32[]{:S(2)}) copy-start(s32[4]{0:T(128)} %param.9) | copy-start | bytes 52
  0.9 12.9 %collective-permute-start = (bf16[2,128,256]{2,1,0:T(8,128)(2,1)S(1)}, bf16[2,128,256]{2,1,0:T(8,128)(2,1)S(1)}, u32[]{:S(2)}, u32[]{:S(2)}) collective-permute-start(bf16[2,128,256]{2,1,0:T(8,128)(2,1)S(1)} %bitcast.55), channel_id=1, source_target_pairs={{0,4},{4,8},{8,12},{12,0},{1,5},{5,9},{9,13},{13,1},{2,6},{6,10},{... | collective-permute-start | bytes 393224 | tf_op jit(solution)/shard_map/ppermute | solution.py:111
  2.3 11.6 %collective-permute-start.1 = (bf16[2,128,256]{2,1,0:T(8,128)(2,1)S(1)}, bf16[2,128,256]{2,1,0:T(8,128)(2,1)S(1)}, u32[]{:S(2)}, u32[]{:S(2)}) collective-permute-start(bf16[2,128,256]{2,1,0:T(8,128)(2,1)S(1)} %bitcast.56), channel_id=1, source_target_pairs={{0,8},{4,12},{8,0},{12,4},{1,9},{5,13},{9,1},{13,5},{2,10},{6,14},... | collective-permute-start | bytes 393224 | tf_op jit(solution)/shard_map/ppermute | solution.py:111
  3.4 12.3 %collective-permute-start.2 = (bf16[2,128,256]{2,1,0:T(8,128)(2,1)S(1)}, bf16[2,128,256]{2,1,0:T(8,128)(2,1)S(1)}, u32[]{:S(2)}, u32[]{:S(2)}) collective-permute-start(bf16[2,128,256]{2,1,0:T(8,128)(2,1)S(1)} %bitcast.57), channel_id=1, source_target_pairs={{0,12},{4,0},{8,4},{12,8},{1,13},{5,1},{9,5},{13,9},{2,14},{6,2},{... | collective-permute-start | bytes 393224 | tf_op jit(solution)/shard_map/ppermute | solution.py:111
  16.6 4.6 %collective-permute-start.3 = (bf16[1,2,128,256]{3,2,1,0:T(8,128)(2,1)S(1)}, bf16[1,2,128,256]{3,2,1,0:T(8,128)(2,1)S(1)}, u32[]{:S(2)}, u32[]{:S(2)}) collective-permute-start(bf16[1,2,128,256]{3,2,1,0:T(8,128)(2,1)S(1)} %get-tuple-element.14), channel_id=1, source_target_pairs={{0,4},{4,8},{8,12},{12,0},{1,5},{5,9},{9,13},{13,1},{2,6},{6,10},{... | collective-permute-start | bytes 393224 | tf_op jit(solution)/shard_map/ppermute | solution.py:134
  16.7 11.1 %collective-permute-start.4 = (bf16[1,2,128,256]{3,2,1,0:T(8,128)(2,1)S(1)}, bf16[1,2,128,256]{3,2,1,0:T(8,128)(2,1)S(1)}, u32[]{:S(2)}, u32[]{:S(2)}) collective-permute-start(bf16[1,2,128,256]{3,2,1,0:T(8,128)(2,1)S(1)} %get-tuple-element.13), channel_id=1, source_target_pairs={{0,8},{4,12},{8,0},{12,4},{1,9},{5,13},{9,1},{13,5},{2,10},{6,14},... | collective-permute-start | bytes 393224 | tf_op jit(solution)/shard_map/ppermute | solution.py:134
  18.0 12.4 %collective-permute-start.5 = (bf16[1,2,128,256]{3,2,1,0:T(8,128)(2,1)S(1)}, bf16[1,2,128,256]{3,2,1,0:T(8,128)(2,1)S(1)}, u32[]{:S(2)}, u32[]{:S(2)}) collective-permute-start(bf16[1,2,128,256]{3,2,1,0:T(8,128)(2,1)S(1)} %slice_bitcast_fusion.2), channel_id=1, source_target_pairs={{0,12},{4,0},{8,4},{12,8},{1,13},{5,1},{9,5},{13,9},{2,14},{6,2},{... | collective-permute-start | bytes 393224 | tf_op jit(solution)/shard_map/ppermute | solution.py:134
  31.1 7.4 %collective-permute-start.6 = (bf16[2,2,128,256]{3,2,1,0:T(8,128)(2,1)S(1)}, bf16[2,2,128,256]{3,2,1,0:T(8,128)(2,1)S(1)}, u32[]{:S(2)}, u32[]{:S(2)}) collective-permute-start(bf16[2,2,128,256]{3,2,1,0:T(8,128)(2,1)S(1)} %gather_fusion.3), channel_id=1, source_target_pairs={{0,4},{4,8},{8,12},{12,0},{1,5},{5,9},{9,13},{13,1},{2,6},{6,10},{... | collective-permute-start | bytes 786440 | tf_op jit(solution)/shard_map/ppermute | solution.py:148
  31.1 22.3 %collective-permute-start.7 = (bf16[2,2,128,256]{3,2,1,0:T(8,128)(2,1)S(1)}, bf16[2,2,128,256]{3,2,1,0:T(8,128)(2,1)S(1)}, u32[]{:S(2)}, u32[]{:S(2)}) collective-permute-start(bf16[2,2,128,256]{3,2,1,0:T(8,128)(2,1)S(1)} %gather_fusion.3), channel_id=1, source_target_pairs={{0,8},{4,12},{8,0},{12,4},{1,9},{5,13},{9,1},{13,5},{2,10},{6,14},... | collective-permute-start | bytes 786440 | tf_op jit(solution)/shard_map/ppermute | solution.py:148
  31.7 23.6 %collective-permute-start.8 = (bf16[2,2,128,256]{3,2,1,0:T(8,128)(2,1)S(1)}, bf16[2,2,128,256]{3,2,1,0:T(8,128)(2,1)S(1)}, u32[]{:S(2)}, u32[]{:S(2)}) collective-permute-start(bf16[2,2,128,256]{3,2,1,0:T(8,128)(2,1)S(1)} %gather_fusion.3), channel_id=1, source_target_pairs={{0,12},{4,0},{8,4},{12,8},{1,13},{5,1},{9,5},{13,9},{2,14},{6,2},{... | collective-permute-start | bytes 786440 | tf_op jit(solution)/shard_map/ppermute | solution.py:148

commit v13 on v12

--- a/solution.py
+++ b/solution.py
@@ -11,14 +11,16 @@
 CAP = 4
 
 
-def attention_kernel(
-    query_start, q_ref, new_ref, page_ref, key_pos_ref, page_ok_ref, o_ref,
-    *, head_size, group_size, mask_pages,
-):
+def attention_kernel(query_start, q_ref, *refs, head_size, group_size, mask_pages, chunks):
+    new_refs = refs[:chunks]
+    page_refs = refs[chunks : 2 * chunks]
+    key_pos_ref, page_ok_ref, o_ref = refs[2 * chunks :]
     scale = 1.0 / math.sqrt(head_size)
     q_rows = q_ref.shape[0]
-    new_kv = new_ref[:, 0].reshape(-1, new_ref.shape[-1])
-    page_kv = page_ref[:, 0].reshape(-1, page_ref.shape[-1])
+    new_kv = jnp.concatenate([r[0] for r in new_refs], axis=0)
+    page_kv = jnp.concatenate(
+        [r[:, 0].reshape(-1, r.shape[-1]) for r in page_refs], axis=0
+    )
     new_keys = new_kv[:, :head_size]
     new_values = new_kv[:, head_size:]
     page_keys = page_kv[:, :head_size]
@@ -28,7 +30,7 @@
     page_visible = page_ok_ref[...] > 0
     dims = (((1,), (1,)), ((), ()))
     pv = (((1,), (0,)), ((), ()))
-    stack = 2 if group_size % 2 == 0 else 1
+    stack = math.gcd(group_size, 4)
     new_visible = jnp.concatenate([new_visible] * stack, axis=0)
     for c in range(group_size // stack):
         heads = range(c * stack, (c + 1) * stack)
@@ -65,13 +67,16 @@
             o_ref[:, h * head_size : (h + 1) * head_size] = result[j * q_rows : (j + 1) * q_rows]
 
 
-def attention(query_start, key_pos, page_ok, q_new, new_all, pages, group_size, head_size,
+def attention(query_start, key_pos, page_ok, q_new, new_list, page_list, group_size, head_size,
               mask_pages):
     q_rows = q_new.shape[0]
-    blocks, kv_heads, new_len, width = new_all.shape
-    npage, _, page_len, _ = pages.shape
+    blocks = len(new_list)
+    kv_heads, new_len, width = new_list[0].shape
+    pg, _, page_len, _ = page_list[0].shape
+    npage = blocks * pg
     kernel = functools.partial(
-        attention_kernel, head_size=head_size, group_size=group_size, mask_pages=mask_pages
+        attention_kernel, head_size=head_size, group_size=group_size, mask_pages=mask_pages,
+        chunks=blocks,
     )
     span = group_size * head_size
     return pl.pallas_call(
@@ -82,14 +87,14 @@
             grid=(kv_heads,),
             in_specs=[
                 pl.BlockSpec((q_rows, span), lambda g, s: (0, g)),
-                pl.BlockSpec((blocks, 1, new_len, width), lambda g, s: (0, g, 0, 0)),
-                pl.BlockSpec((npage, 1, page_len, width), lambda g, s: (0, g, 0, 0)),
+                *[pl.BlockSpec((1, new_len, width), lambda g, s: (g, 0, 0))] * blocks,
+                *[pl.BlockSpec((pg, 1, page_len, width), lambda g, s: (0, g, 0, 0))] * blocks,
                 pl.BlockSpec((1, blocks * new_len), lambda g, s: (0, 0)),
                 pl.BlockSpec((1, npage * page_len), lambda g, s: (0, 0)),
             ],
             out_specs=pl.BlockSpec((q_rows, span), lambda g, s: (0, g)),
         ),
-    )(query_start, q_new, new_all, pages, key_pos, page_ok)
+    )(query_start, q_new, *new_list, *page_list, key_pos, page_ok)
 
 
 def local(q_new, kv_new, kv_cache, page_table, block_offsets):
@@ -110,7 +115,6 @@
         new_all.append(
             lax.ppermute(own_rows, "blk", [(i, (i + k) % blocks) for i in range(blocks)])
         )
-    new_all = jnp.stack(new_all)
     shifted_offsets = block_offsets[(myself - block_ids) % blocks]
 
     page_owner = page_table // slots_dev
@@ -128,6 +132,7 @@
     by_shift = chosen.reshape(blocks, per_peer)[(myself + block_ids) % blocks].reshape(-1)
     sent = kv_cache[by_shift].reshape((blocks, per_peer) + kv_cache.shape[1:])
     sent, new_all = lax.optimization_barrier((sent, new_all))
+    new_all = list(new_all)
     arrived = [sent[0]]
     for k in range(1, blocks):
         arrived.append(
@@ -147,7 +152,6 @@
         gathered.append(
             lax.ppermute(own, "blk", [(i, (i + k) % blocks) for i in range(blocks)])
         )
-    gathered = jnp.concatenate(gathered)
 
     q_rows = q_new.shape[0]
     page_len = kv_cache.shape[2]

time: 65.1 us -> 67 us (1.029)
  the two profiles are of different devices: /device:TPU:9 before, /device:TPU:0 now
where the time goes in v13:
time: 67 us; the launch traced here: 66.7 us
  waiting for transfers between devices  29.1 us (43%)
  starting transfers between devices  14.5 us (22%)
  Pallas kernels  8.69 us (13%)
  local copies, waits for them, and re-layouts  7.71 us (12%)
  other arithmetic  5.87 us (9%)
  between operations  0.8 us (1%)
    ppermute x3, waiting for transfers between devices, local(): lax.ppermute(own, 'blk', [(i, (i + k) % blocks) for i in range(blocks)])  19.9 us
    pallas_call x1, Pallas kernels, attention(): pl.pallas_call(kernel, out_shape=jax.ShapeDtypeStruct(q_new.shape, q_new....  8.69 us
    ppermute x3, waiting for transfers between devices, local(): lax.ppermute(sent[k], 'blk', [(i, (i + k) % blocks) for i in range(blocks)])  8.26 us
    ppermute x3, starting transfers between devices, local(): lax.ppermute(own_rows, 'blk', [(i, (i + k) % blocks) for i in range(block...  6.11 us
    ppermute x3, starting transfers between devices, local(): lax.ppermute(sent[k], 'blk', [(i, (i + k) % blocks) for i in range(blocks)])  4.77 us
    ppermute x3, starting transfers between devices, local(): lax.ppermute(own, 'blk', [(i, (i + k) % blocks) for i in range(blocks)])  3.66 us
    gather x1, local copies, waits for them, and re-layouts, local(): sent = kv_cache[by_shift].reshape((blocks, per_peer) + kv_cache.shape[1:])  2.77 us
  transfers between devices with their start and end apart: 9, of which 4 were waited for; matrix products, arithmetic and copies ran while one was open for 17% of the time, Pallas kernels for 0%

profile of v13, /device:TPU:0, one launch (start us, length us, event | category | flops | bytes accessed | tf_op | source)
XLA Modules:
  0.0 66.7 jit_solution(3561558366584829580)
XLA Ops:
  0.0 0.9 %copy.19 = bf16[128,2,256]{2,0,1:T(8,128)(2,1)S(1)} copy(bf16[128,2,256]{2,1,0:T(2,128)(2,1)} %param.6) | data formatting | bytes 262144 | tf_op args[1]
  0.9 0.0 copy-start.1
  0.9 5.1 %collective-permute-start.2 = (bf16[2,128,256]{2,1,0:T(8,128)(2,1)S(1)}, bf16[2,128,256]{2,1,0:T(8,128)(2,1)S(1)}, u32[]{:S(2)}, u32[]{:S(2)}) collective-permute-start(bf16[2,128,256]{2,1,0:T(8,128)(2,1)S(1)} %bitcast.49), channel_id=1, source_target_pairs={{0,12},{4,0},{8,4},{12,8},{1,13},{5,1},{9,5},{13,9},{2,14},{6,2},{... | collective-permute-start | bytes 393224 | tf_op jit(solution)/shard_map/ppermute | solution.py:116
  6.0 0.0 collective-permute-start.1
  6.0 1.0 %collective-permute-start = (bf16[2,128,256]{2,1,0:T(8,128)(2,1)S(1)}, bf16[2,128,256]{2,1,0:T(8,128)(2,1)S(1)}, u32[]{:S(2)}, u32[]{:S(2)}) collective-permute-start(bf16[2,128,256]{2,1,0:T(8,128)(2,1)S(1)} %bitcast.51), channel_id=1, source_target_pairs={{0,4},{4,8},{8,12},{12,0},{1,5},{5,9},{9,13},{13,1},{2,6},{6,10},{... | collective-permute-start | bytes 393224 | tf_op jit(solution)/shard_map/ppermute | solution.py:116
  7.1 0.7 and_select_fusion.5
  7.7 0.7 %convert_bitcast_fusion.1 = (s32[8,1]{0,1:T(1,128)S(1)}, pred[8]{0:T(512)(128)(4,1)S(1)}, s32[8]{0:T(128)S(1)}) fusion(s32[]{:T(128)S(6)} %axis_index.15, s32[8]{0:T(128)} %param.8), kind=kLoop, calls=%fused_computation.62 | loop fusion | flops 136 | bytes 108 | tf_op jit(solution)/shard_map/convert
  8.4 0.1 convert_reduce_fusion
  8.5 0.2 reduce-window.22
  8.7 0.7 %fusion.3 = s32[]{:T(128)} fusion(s32[4]{0:T(128)S(1)} %convert_reduce_fusion, s32[4,1]{0,1:T(1,128)S(1)} %reduce-window.22, s32[]{:T(128)S(6)} %axis_index.15), kind=kLoop, calls=%fused_computation.50 | loop fusion | flops 15 | bytes 40 | tf_op jit(solution)/shard_map/reduce_sum | solution.py:127
  9.4 1.3 %and_select_fusion = (s32[4]{0:T(128)S(1)}, s32[]{:T(128)}) fusion(s32[]{:T(128)S(6)} %axis_index.15, s32[4]{0:T(128)} %param.9), kind=kLoop, calls=%fused_computation.34 | loop fusion | flops 59 | bytes 40 | tf_op jit(solution)/shard_map/jit(remainder)/select_n | solution.py:143
  10.7 0.2 reduce-window.21
  10.9 0.7 %and_select_fusion.6 = s32[4]{0:T(128)S(1)} fusion(s32[]{:T(128)} %fusion.3), kind=kLoop, calls=%fused_computation.41 | loop fusion | flops 48 | bytes 20 | tf_op jit(solution)/shard_map/jit(remainder)/select_n | solution.py:129
  11.6 0.2 select_reduce_fusion
  11.8 0.6 gather_fusion
  12.5 0.6 gather_fusion.2
  13.1 0.2 reduce-window.23
  13.3 0.1 fusion
  13.4 2.8 %gather_fusion.1 = bf16[4,2,128,256]{3,2,1,0:T(8,128)(2,1)S(1)} fusion(bf16[32,2,128,256]{3,2,1,0:T(8,128)(2,1)} %param.7, s32[1024]{0:T(1024)S(1)} %pad_clamp_fusion.2), kind=kCustom, calls=%fused_computation.1 | custom fusion | bytes 1048592 | tf_op jit(solution)/shard_map/gather | solution.py:133
  16.2 0.1 fusion.1
  16.3 0.0 collective-permute-done.2.refs_3_
  16.3 0.0 copy-start.5
  16.3 0.9 %collective-permute-done.1.refs_2_ = bf16[2,128,256]{2,1,0:T(8,128)(2,1)S(1)} collective-permute-done((bf16[2,128,256]{2,1,0:T(8,128)(2,1)S(1)}, bf16[2,128,256]{2,1,0:T(8,128)(2,1)S(1)}, u32[]{:S(2)}, u32[]{:S(2)}) %collective-permute-start.1) | collective-permute-done | bytes 131104 | tf_op jit(solution)/shard_map/ppermute | solution.py:116
  17.2 0.0 copy-start.6
  17.2 0.0 collective-permute-done.refs_1_
  17.2 0.0 copy-start.7
  17.3 2.0 %collective-permute-start.5 = (bf16[1,2,128,256]{3,2,1,0:T(8,128)(2,1)S(1)}, bf16[1,2,128,256]{3,2,1,0:T(8,128)(2,1)S(1)}, u32[]{:S(2)}, u32[]{:S(2)}) collective-permute-start(bf16[1,2,128,256]{3,2,1,0:T(8,128)(2,1)S(1)} %slice_bitcast_fusion.2), channel_id=1, source_target_pairs={{0,12},{4,0},{8,4},{12,8},{1,13},{5,1},{9,5},{13,9},{2,14},{6,2},{... | collective-permute-start | bytes 393224 | tf_op jit(solution)/shard_map/ppermute | solution.py:139
  19.2 1.2 %collective-permute-start.4 = (bf16[1,2,128,256]{3,2,1,0:T(8,128)(2,1)S(1)}, bf16[1,2,128,256]{3,2,1,0:T(8,128)(2,1)S(1)}, u32[]{:S(2)}, u32[]{:S(2)}) collective-permute-start(bf16[1,2,128,256]{3,2,1,0:T(8,128)(2,1)S(1)} %get-tuple-element.19), channel_id=1, source_target_pairs={{0,8},{4,12},{8,0},{12,4},{1,9},{5,13},{9,1},{13,5},{2,10},{6,14},... | collective-permute-start | bytes 393224 | tf_op jit(solution)/shard_map/ppermute | solution.py:139
  20.4 1.6 %collective-permute-start.3 = (bf16[1,2,128,256]{3,2,1,0:T(8,128)(2,1)S(1)}, bf16[1,2,128,256]{3,2,1,0:T(8,128)(2,1)S(1)}, u32[]{:S(2)}, u32[]{:S(2)}) collective-permute-start(bf16[1,2,128,256]{3,2,1,0:T(8,128)(2,1)S(1)} %get-tuple-element.20), channel_id=1, source_target_pairs={{0,4},{4,8},{8,12},{12,0},{1,5},{5,9},{9,13},{13,1},{2,6},{6,10},{... | collective-permute-start | bytes 393224 | tf_op jit(solution)/shard_map/ppermute | solution.py:139
  22.1 1.3 %gather_fusion.4 = s32[4]{0:T(128)S(1)} fusion(s32[4]{0:T(128)} %param.9, s32[1024]{0:T(1024)S(1)} %pad_clamp_fusion.1), kind=kCustom, calls=%fused_computation.4 | custom fusion | bytes 48 | tf_op jit(solution)/shard_map/gather | solution.py:118
  23.4 0.0 collective-permute-done.5
  23.4 8.3 %collective-permute-done.4 = bf16[1,2,128,256]{3,2,1,0:T(8,128)(2,1)S(1)} collective-permute-done((bf16[1,2,128,256]{3,2,1,0:T(8,128)(2,1)S(1)}, bf16[1,2,128,256]{3,2,1,0:T(8,128)(2,1)S(1)}, u32[]{:S(2)}, u32[]{:S(2)}) %collective-permute-start.4) | collective-permute-done | bytes 131104 | tf_op jit(solution)/shard_map/ppermute | solution.py:139
  31.6 0.0 collective-permute-done.3
  31.6 0.1 maximum_bitcast_fusion
  31.7 0.6 gather_fusion.3
  32.3 0.0 copy-start
  32.3 0.1 collective-permute-start.8
  32.4 1.7 %collective-permute-start.7 = (bf16[2,2,128,256]{3,2,1,0:T(8,128)(2,1)S(1)}, bf16[2,2,128,256]{3,2,1,0:T(8,128)(2,1)S(1)}, u32[]{:S(2)}, u32[]{:S(2)}) collective-permute-start(bf16[2,2,128,256]{3,2,1,0:T(8,128)(2,1)S(1)} %gather_fusion.3), channel_id=1, source_target_pairs={{0,8},{4,12},{8,0},{12,4},{1,9},{5,13},{9,1},{13,5},{2,10},{6,14},... | collective-permute-start | bytes 786440 | tf_op jit(solution)/shard_map/ppermute | solution.py:153
  34.0 1.9 %collective-permute-start.6 = (bf16[2,2,128,256]{3,2,1,0:T(8,128)(2,1)S(1)}, bf16[2,2,128,256]{3,2,1,0:T(8,128)(2,1)S(1)}, u32[]{:S(2)}, u32[]{:S(2)}) collective-permute-start(bf16[2,2,128,256]{3,2,1,0:T(8,128)(2,1)S(1)} %gather_fusion.3), channel_id=1, source_target_pairs={{0,4},{4,8},{8,12},{12,0},{1,5},{5,9},{9,13},{13,1},{2,6},{6,10},{... | collective-permute-start | bytes 786440 | tf_op jit(solution)/shard_map/ppermute | solution.py:153
  36.0 0.1 reshape.427
  36.7 0.6 iota_add_fusion
  37.3 1.8 %collective-permute-done.8.refs_7_ = bf16[2,2,128,256]{3,2,1,0:T(8,128)(2,1)S(1)} collective-permute-done((bf16[2,2,128,256]{3,2,1,0:T(8,128)(2,1)S(1)}, bf16[2,2,128,256]{3,2,1,0:T(8,128)(2,1)S(1)}, u32[]{:S(2)}, u32[]{:S(2)}) %collective-permute-start.8) | collective-permute-done | bytes 262176 | tf_op jit(solution)/shard_map/ppermute | solution.py:153
  39.2 0.0 copy-start.2
  39.2 18.1 %collective-permute-done.7.refs_6_ = bf16[2,2,128,256]{3,2,1,0:T(8,128)(2,1)S(1)} collective-permute-done((bf16[2,2,128,256]{3,2,1,0:T(8,128)(2,1)S(1)}, bf16[2,2,128,256]{3,2,1,0:T(8,128)(2,1)S(1)}, u32[]{:S(2)}, u32[]{:S(2)}) %collective-permute-start.7) | collective-permute-done | bytes 262176 | tf_op jit(solution)/shard_map/ppermute | solution.py:153
  57.3 0.0 copy-start.3
  57.3 0.0 collective-permute-done.6.refs_5_
  57.3 0.0 copy-start.4
  57.3 0.7 %broadcast_in_dim.60 = s32[8,128]{1,0:T(8,128)} broadcast(s32[8]{0:T(128)S(1)} %reshape.427), dimensions={0} | broadcast | bytes 4128 | tf_op jit(solution)/shard_map/broadcast_in_dim | solution.py:167
  58.0 0.0 copy-done.1
  58.0 0.0 copy-done.5
  58.0 0.0 copy-done.6
  58.0 0.0 copy-done.7
  58.0 0.0 copy-done
  58.0 0.0 copy-done.2
  58.0 0.0 copy-done.3
  58.1 0.0 copy-done.4
  58.1 8.7 %shard_map.55 = bf16[128,2048]{1,0:T(8,128)(2,1)} custom-call(s32[1]{0:T(128)} %bitcast.query_start, bf16[128,2048]{1,0:T(8,128)(2,1)} %q_ref.1, bf16[2,128,256]{2,1,0:T(8,128)(2,1)} %bitcast.52, bf16[2,128,256]{2,1,0:T(8,128)(2,1)} %copy-done.7, bf16[2,128,256]{2,1,0:T(8,128)(2,1)} %copy-done.6, bf16[2,128,256]{2,1,0:T(8,128)(2,1)} %copy-done.5, ...), custom_call_target="tpu_custom_call" | custom-call | tf_op jit(solution)/shard_map/pallas_call | solution.py:82
  (15 shorter events, 0.1 us)
Async XLA Ops:
  0.9 57.1 %copy-start.1 = (bf16[128,2,256]{2,0,1:T(8,128)(2,1)}, bf16[128,2,256]{2,0,1:T(8,128)(2,1)S(1)}, u32[]{:S(2)}) copy-start(bf16[128,2,256]{2,0,1:T(8,128)(2,1)S(1)} %copy.19) | copy-start | bytes 393220
  0.9 15.3 %collective-permute-start.2 = (bf16[2,128,256]{2,1,0:T(8,128)(2,1)S(1)}, bf16[2,128,256]{2,1,0:T(8,128)(2,1)S(1)}, u32[]{:S(2)}, u32[]{:S(2)}) collective-permute-start(bf16[2,128,256]{2,1,0:T(8,128)(2,1)S(1)} %bitcast.49), channel_id=1, source_target_pairs={{0,12},{4,0},{8,4},{12,8},{1,13},{5,1},{9,5},{13,9},{2,14},{6,2},{... | collective-permute-start | bytes 393224 | tf_op jit(solution)/shard_map/ppermute | solution.py:116
  6.0 11.2 %collective-permute-start.1 = (bf16[2,128,256]{2,1,0:T(8,128)(2,1)S(1)}, bf16[2,128,256]{2,1,0:T(8,128)(2,1)S(1)}, u32[]{:S(2)}, u32[]{:S(2)}) collective-permute-start(bf16[2,128,256]{2,1,0:T(8,128)(2,1)S(1)} %bitcast.50), channel_id=1, source_target_pairs={{0,8},{4,12},{8,0},{12,4},{1,9},{5,13},{9,1},{13,5},{2,10},{6,14},... | collective-permute-start | bytes 393224 | tf_op jit(solution)/shard_map/ppermute | solution.py:116
  6.0 11.2 %collective-permute-start = (bf16[2,128,256]{2,1,0:T(8,128)(2,1)S(1)}, bf16[2,128,256]{2,1,0:T(8,128)(2,1)S(1)}, u32[]{:S(2)}, u32[]{:S(2)}) collective-permute-start(bf16[2,128,256]{2,1,0:T(8,128)(2,1)S(1)} %bitcast.51), channel_id=1, source_target_pairs={{0,4},{4,8},{8,12},{12,0},{1,5},{5,9},{9,13},{13,1},{2,6},{6,10},{... | collective-permute-start | bytes 393224 | tf_op jit(solution)/shard_map/ppermute | solution.py:116
  16.3 41.7 %copy-start.5 = (bf16[2,128,256]{2,1,0:T(8,128)(2,1)}, bf16[2,128,256]{2,1,0:T(8,128)(2,1)S(1)}, u32[]{:S(2)}) copy-start(bf16[2,128,256]{2,1,0:T(8,128)(2,1)S(1)} %collective-permute-done.2.refs_3_) | copy-start | bytes 393220
  17.2 40.8 %copy-start.6 = (bf16[2,128,256]{2,1,0:T(8,128)(2,1)}, bf16[2,128,256]{2,1,0:T(8,128)(2,1)S(1)}, u32[]{:S(2)}) copy-start(bf16[2,128,256]{2,1,0:T(8,128)(2,1)S(1)} %collective-permute-done.1.refs_2_) | copy-start | bytes 393220
  17.2 40.8 %copy-start.7 = (bf16[2,128,256]{2,1,0:T(8,128)(2,1)}, bf16[2,128,256]{2,1,0:T(8,128)(2,1)S(1)}, u32[]{:S(2)}) copy-start(bf16[2,128,256]{2,1,0:T(8,128)(2,1)S(1)} %collective-permute-done.refs_1_) | copy-start | bytes 393220
  17.3 6.1 %collective-permute-start.5 = (bf16[1,2,128,256]{3,2,1,0:T(8,128)(2,1)S(1)}, bf16[1,2,128,256]{3,2,1,0:T(8,128)(2,1)S(1)}, u32[]{:S(2)}, u32[]{:S(2)}) collective-permute-start(bf16[1,2,128,256]{3,2,1,0:T(8,128)(2,1)S(1)} %slice_bitcast_fusion.2), channel_id=1, source_target_pairs={{0,12},{4,0},{8,4},{12,8},{1,13},{5,1},{9,5},{13,9},{2,14},{6,2},{... | collective-permute-start | bytes 393224 | tf_op jit(solution)/shard_map/ppermute | solution.py:139
  19.2 12.4 %collective-permute-start.4 = (bf16[1,2,128,256]{3,2,1,0:T(8,128)(2,1)S(1)}, bf16[1,2,128,256]{3,2,1,0:T(8,128)(2,1)S(1)}, u32[]{:S(2)}, u32[]{:S(2)}) collective-permute-start(bf16[1,2,128,256]{3,2,1,0:T(8,128)(2,1)S(1)} %get-tuple-element.19), channel_id=1, source_target_pairs={{0,8},{4,12},{8,0},{12,4},{1,9},{5,13},{9,1},{13,5},{2,10},{6,14},... | collective-permute-start | bytes 393224 | tf_op jit(solution)/shard_map/ppermute | solution.py:139
  20.4 11.2 %collective-permute-start.3 = (bf16[1,2,128,256]{3,2,1,0:T(8,128)(2,1)S(1)}, bf16[1,2,128,256]{3,2,1,0:T(8,128)(2,1)S(1)}, u32[]{:S(2)}, u32[]{:S(2)}) collective-permute-start(bf16[1,2,128,256]{3,2,1,0:T(8,128)(2,1)S(1)} %get-tuple-element.20), channel_id=1, source_target_pairs={{0,4},{4,8},{8,12},{12,0},{1,5},{5,9},{9,13},{13,1},{2,6},{6,10},{... | collective-permute-start | bytes 393224 | tf_op jit(solution)/shard_map/ppermute | solution.py:139
  32.3 25.7 %copy-start = (bf16[2,2,128,256]{3,2,1,0:T(8,128)(2,1)}, bf16[2,2,128,256]{3,2,1,0:T(8,128)(2,1)S(1)}, u32[]{:S(2)}) copy-start(bf16[2,2,128,256]{3,2,1,0:T(8,128)(2,1)S(1)} %gather_fusion.3) | copy-start | bytes 786436
  32.3 6.9 %collective-permute-start.8 = (bf16[2,2,128,256]{3,2,1,0:T(8,128)(2,1)S(1)}, bf16[2,2,128,256]{3,2,1,0:T(8,128)(2,1)S(1)}, u32[]{:S(2)}, u32[]{:S(2)}) collective-permute-start(bf16[2,2,128,256]{3,2,1,0:T(8,128)(2,1)S(1)} %gather_fusion.3), channel_id=1, source_target_pairs={{0,12},{4,0},{8,4},{12,8},{1,13},{5,1},{9,5},{13,9},{2,14},{6,2},{... | collective-permute-start | bytes 786440 | tf_op jit(solution)/shard_map/ppermute | solution.py:153
  32.4 24.9 %collective-permute-start.7 = (bf16[2,2,128,256]{3,2,1,0:T(8,128)(2,1)S(1)}, bf16[2,2,128,256]{3,2,1,0:T(8,128)(2,1)S(1)}, u32[]{:S(2)}, u32[]{:S(2)}) collective-permute-start(bf16[2,2,128,256]{3,2,1,0:T(8,128)(2,1)S(1)} %gather_fusion.3), channel_id=1, source_target_pairs={{0,8},{4,12},{8,0},{12,4},{1,9},{5,13},{9,1},{13,5},{2,10},{6,14},... | collective-permute-start | bytes 786440 | tf_op jit(solution)/shard_map/ppermute | solution.py:153
  34.0 23.3 %collective-permute-start.6 = (bf16[2,2,128,256]{3,2,1,0:T(8,128)(2,1)S(1)}, bf16[2,2,128,256]{3,2,1,0:T(8,128)(2,1)S(1)}, u32[]{:S(2)}, u32[]{:S(2)}) collective-permute-start(bf16[2,2,128,256]{3,2,1,0:T(8,128)(2,1)S(1)} %gather_fusion.3), channel_id=1, source_target_pairs={{0,4},{4,8},{8,12},{12,0},{1,5},{5,9},{9,13},{13,1},{2,6},{6,10},{... | collective-permute-start | bytes 786440 | tf_op jit(solution)/shard_map/ppermute | solution.py:153
  39.2 18.9 %copy-start.2 = (bf16[2,2,128,256]{3,2,1,0:T(8,128)(2,1)}, bf16[2,2,128,256]{3,2,1,0:T(8,128)(2,1)S(1)}, u32[]{:S(2)}) copy-start(bf16[2,2,128,256]{3,2,1,0:T(8,128)(2,1)S(1)} %collective-permute-done.8.refs_7_) | copy-start | bytes 786436
  57.3 0.8 %copy-start.3 = (bf16[2,2,128,256]{3,2,1,0:T(8,128)(2,1)}, bf16[2,2,128,256]{3,2,1,0:T(8,128)(2,1)S(1)}, u32[]{:S(2)}) copy-start(bf16[2,2,128,256]{3,2,1,0:T(8,128)(2,1)S(1)} %collective-permute-done.7.refs_6_) | copy-start | bytes 786436
  57.3 0.8 %copy-start.4 = (bf16[2,2,128,256]{3,2,1,0:T(8,128)(2,1)}, bf16[2,2,128,256]{3,2,1,0:T(8,128)(2,1)S(1)}, u32[]{:S(2)}) copy-start(bf16[2,2,128,256]{3,2,1,0:T(8,128)(2,1)S(1)} %collective-permute-done.6.refs_5_) | copy-start | bytes 786436

commit v14 on v12

--- a/solution.py
+++ b/solution.py
@@ -12,7 +12,7 @@
 
 
 def attention_kernel(
-    query_start, q_ref, new_ref, page_ref, key_pos_ref, page_ok_ref, o_ref,
+    query_start, q_ref, new_ref, page_ref, key_pos_ref, page_ok_ref, acc_ref, top_ref, total_ref,
     *, head_size, group_size, mask_pages,
 ):
     scale = 1.0 / math.sqrt(head_size)
@@ -60,9 +60,76 @@
             page_weights.astype(jnp.bfloat16), page_values, pv,
             preferred_element_type=jnp.float32,
         )
+        for j, h in enumerate(heads):
+            rows = slice(j * q_rows, (j + 1) * q_rows)
+            acc_ref[:, h * head_size : (h + 1) * head_size] = summed[rows]
+            top_ref[0, :, h : h + 1] = row_top[rows]
+            total_ref[0, :, h : h + 1] = row_total[rows]
+
+
+def prefix_kernel(
+    q_ref, page_ref, page_ok_ref, acc_ref, top_ref, total_ref, o_ref,
+    *, head_size, group_size, mask_pages,
+):
+    scale = 1.0 / math.sqrt(head_size)
+    q_rows = q_ref.shape[0]
+    page_kv = page_ref[:, 0].reshape(-1, page_ref.shape[-1])
+    page_keys = page_kv[:, :head_size]
+    page_values = page_kv[:, head_size:]
+    page_visible = page_ok_ref[...] > 0
+    dims = (((1,), (1,)), ((), ()))
+    pv = (((1,), (0,)), ((), ()))
+    stack = 2 if group_size % 2 == 0 else 1
+    for c in range(group_size // stack):
+        heads = range(c * stack, (c + 1) * stack)
+        queries = jnp.concatenate(
+            [q_ref[:, h * head_size : (h + 1) * head_size] for h in heads], axis=0
+        )
+        top_prev = jnp.concatenate([top_ref[0, :, h : h + 1] for h in heads], axis=0)
+        total_prev = jnp.concatenate([total_ref[0, :, h : h + 1] for h in heads], axis=0)
+        acc_prev = jnp.concatenate(
+            [acc_ref[:, h * head_size : (h + 1) * head_size] for h in heads], axis=0
+        )
+        scores = lax.dot_general(
+            queries, page_keys, dims, preferred_element_type=jnp.float32
+        ) * scale
+        if mask_pages:
+            scores = jnp.where(page_visible, scores, -1e30)
+        row_top = jnp.maximum(top_prev, jnp.max(scores, axis=1, keepdims=True))
+        factor = jnp.exp(top_prev - row_top)
+        weights = jnp.exp(scores - row_top)
+        row_total = total_prev * factor + jnp.sum(weights, axis=1, keepdims=True)
+        summed = acc_prev * factor + lax.dot_general(
+            weights.astype(jnp.bfloat16), page_values, pv, preferred_element_type=jnp.float32
+        )
         result = (summed / row_total).astype(o_ref.dtype)
         for j, h in enumerate(heads):
             o_ref[:, h * head_size : (h + 1) * head_size] = result[j * q_rows : (j + 1) * q_rows]
+
+
+def prefix_part(page_ok, q_new, pages, acc, top, total, group_size, head_size, mask_pages):
+    q_rows = q_new.shape[0]
+    npage, kv_heads, page_len, width = pages.shape
+    kernel = functools.partial(
+        prefix_kernel, head_size=head_size, group_size=group_size, mask_pages=mask_pages
+    )
+    span = group_size * head_size
+    block = pl.BlockSpec((q_rows, span), lambda g: (0, g))
+    stat_spec = pl.BlockSpec((1, q_rows, group_size), lambda g: (g, 0, 0))
+    return pl.pallas_call(
+        kernel,
+        out_shape=jax.ShapeDtypeStruct(q_new.shape, q_new.dtype),
+        grid=(kv_heads,),
+        in_specs=[
+            block,
+            pl.BlockSpec((npage, 1, page_len, width), lambda g: (0, g, 0, 0)),
+            pl.BlockSpec((1, npage * page_len), lambda g: (0, 0)),
+            block,
+            stat_spec,
+            stat_spec,
+        ],
+        out_specs=block,
+    )(q_new, pages, page_ok, acc, top, total)
 
 
 def attention(query_start, key_pos, page_ok, q_new, new_all, pages, group_size, head_size,
@@ -74,9 +141,11 @@
         attention_kernel, head_size=head_size, group_size=group_size, mask_pages=mask_pages
     )
     span = group_size * head_size
+    stat = jax.ShapeDtypeStruct((kv_heads, q_rows, group_size), jnp.float32)
+    stat_spec = pl.BlockSpec((1, q_rows, group_size), lambda g, s: (g, 0, 0))
     return pl.pallas_call(
         kernel,
-        out_shape=jax.ShapeDtypeStruct(q_new.shape, q_new.dtype),
+        out_shape=(jax.ShapeDtypeStruct(q_new.shape, jnp.float32), stat, stat),
         grid_spec=pltpu.PrefetchScalarGridSpec(
             num_scalar_prefetch=1,
             grid=(kv_heads,),
@@ -87,7 +156,7 @@
                 pl.BlockSpec((1, blocks * new_len), lambda g, s: (0, 0)),
                 pl.BlockSpec((1, npage * page_len), lambda g, s: (0, 0)),
             ],
-            out_specs=pl.BlockSpec((q_rows, span), lambda g, s: (0, g)),
+            out_specs=(pl.BlockSpec((q_rows, span), lambda g, s: (0, g)), stat_spec, stat_spec),
         ),
     )(query_start, q_new, new_all, pages, key_pos, page_ok)
 
@@ -110,7 +179,6 @@
         new_all.append(
             lax.ppermute(own_rows, "blk", [(i, (i + k) % blocks) for i in range(blocks)])
         )
-    new_all = jnp.stack(new_all)
     shifted_offsets = block_offsets[(myself - block_ids) % blocks]
 
     page_owner = page_table // slots_dev
@@ -128,6 +196,7 @@
     by_shift = chosen.reshape(blocks, per_peer)[(myself + block_ids) % blocks].reshape(-1)
     sent = kv_cache[by_shift].reshape((blocks, per_peer) + kv_cache.shape[1:])
     sent, new_all = lax.optimization_barrier((sent, new_all))
+    new_all = jnp.stack(new_all)
     arrived = [sent[0]]
     for k in range(1, blocks):
         arrived.append(
@@ -147,7 +216,7 @@
         gathered.append(
             lax.ppermute(own, "blk", [(i, (i + k) % blocks) for i in range(blocks)])
         )
-    gathered = jnp.concatenate(gathered)
+    others = jnp.concatenate(gathered[1:])
 
     q_rows = q_new.shape[0]
     page_len = kv_cache.shape[2]
@@ -156,15 +225,16 @@
         jnp.repeat(shifted_offsets, q_rows) * q_rows
         + jnp.tile(jnp.arange(q_rows, dtype=jnp.int32), blocks)
     ).reshape(1, -1).astype(jnp.int32)
-    page_ok = (
-        jnp.arange(pg, dtype=jnp.int32)[None, :] * blocks + ((myself - block_ids) % blocks)[:, None]
-        < npages
-    ).reshape(-1)
-    page_ok = jnp.repeat(page_ok.astype(jnp.int32), page_len).reshape(1, -1)
-    return attention(
-        query_start, key_pos, page_ok, q_new, new_all, gathered, group_size, head_size,
-        npages % blocks != 0,
-    )
+    slot_ids = jnp.arange(pg, dtype=jnp.int32)
+    page_ok = slot_ids[None, :] * blocks + ((myself - block_ids) % blocks)[:, None] < npages
+    page_ok = jnp.repeat(page_ok.astype(jnp.int32).reshape(-1), page_len).reshape(1, -1)
+    own_ok = page_ok[:, : pg * page_len]
+    others_ok = page_ok[:, pg * page_len :]
+    ragged = npages % blocks != 0
+    acc, top, total = attention(
+        query_start, key_pos, own_ok, q_new, new_all, own, group_size, head_size, ragged
+    )
+    return prefix_part(others_ok, q_new, others, acc, top, total, group_size, head_size, ragged)
 
 
 def solution(mesh):

time: 65.1 us -> 62.5 us (0.960)
  waiting for transfers between devices: 33.9 us -> 25.7 us
  Pallas kernels: 7.82 us -> 12.4 us
  local copies, waits for them, and re-layouts: 6.96 us -> 8.17 us
    ppermute x3, waiting for transfers between devices: 20.8 us -> 15.1 us  [local(): lax.ppermute(own, 'blk', [(i, (i + k) % blocks) for i in range(blocks)])]
    pallas_call x1 -> x2, Pallas kernels: 7.82 us -> 12.4 us  [the longest x1 6.89 us: prefix_part(): pl.pallas_call(kernel, out_shape=jax.ShapeDtypeStruct(q_new.shape, q_new....]
    ppermute x3, waiting for transfers between devices: 11.3 us -> 8.73 us  [local(): lax.ppermute(sent[k], 'blk', [(i, (i + k) % blocks) for i in range(blocks)])]
    slice x0 -> x2, local copies, waits for them, and re-layouts: none -> 1.14 us  [the longest x1 0.6 us: local(): others_ok = page_ok[:, pg * page_len:]]
    gather x1, local copies, waits for them, and re-layouts: 0.64 us -> 1.3 us  [local(): shifted_offsets = block_offsets[(myself - block_ids) % blocks]]
    select_n x1, other arithmetic: 1.29 us -> 0.64 us  [local(): (myself - block_ids) % blocks]
    reduce_sum x1, other arithmetic: 0.64 us -> 1.29 us  [local(): my_offset = jnp.sum(jnp.where(block_ids == myself, block_offsets, 0))]
  transfers between devices with their start and end apart: 9 -> 9, of which waited for: 7 -> 5; matrix products, arithmetic and copies ran while one was open for 16% -> 21% of each run, Pallas kernels for 0% -> 9%
where the time goes in v14:
time: 62.5 us; the launch traced here: 62.3 us
  waiting for transfers between devices  25.7 us (41%)
  Pallas kernels  12.4 us (20%)
  local copies, waits for them, and re-layouts  8.17 us (13%)
  other arithmetic  7.62 us (12%)
  starting transfers between devices  7.61 us (12%)
  between operations  0.77 us (1%)
    ppermute x3, waiting for transfers between devices, local(): lax.ppermute(own, 'blk', [(i, (i + k) % blocks) for i in range(blocks)])  15.1 us
    ppermute x3, waiting for transfers between devices, local(): lax.ppermute(sent[k], 'blk', [(i, (i + k) % blocks) for i in range(blocks)])  8.73 us
    pallas_call x1, Pallas kernels, prefix_part(): pl.pallas_call(kernel, out_shape=jax.ShapeDtypeStruct(q_new.shape, q_new....  6.89 us
    pallas_call x1, Pallas kernels, attention(): pl.pallas_call(kernel, out_shape=(jax.ShapeDtypeStruct(q_new.shape, jnp.f...  5.54 us
    ppermute x3, starting transfers between devices, local(): lax.ppermute(own_rows, 'blk', [(i, (i + k) % blocks) for i in range(block...  3.83 us
    gather x1, local copies, waits for them, and re-layouts, local(): sent = kv_cache[by_shift].reshape((blocks, per_peer) + kv_cache.shape[1:])  2.77 us
    ppermute x3, starting transfers between devices, local(): lax.ppermute(own, 'blk', [(i, (i + k) % blocks) for i in range(blocks)])  1.98 us
    ppermute x3, starting transfers between devices, local(): lax.ppermute(sent[k], 'blk', [(i, (i + k) % blocks) for i in range(blocks)])  1.81 us
  transfers between devices with their start and end apart: 9, of which 5 were waited for; matrix products, arithmetic and copies ran while one was open for 21% of the time, Pallas kernels for 9%

profile of v14, /device:TPU:9, one launch (start us, length us, event | category | flops | bytes accessed | tf_op | source)
XLA Modules:
  0.0 62.3 jit_solution(3741193078038002018)
XLA Ops:
  0.0 0.9 %copy.19 = bf16[128,2,256]{2,0,1:T(8,128)(2,1)S(1)} copy(bf16[128,2,256]{2,1,0:T(2,128)(2,1)} %param.6) | data formatting | bytes 262144 | tf_op args[1]
  0.9 1.3 %collective-permute-start = (bf16[2,128,256]{2,1,0:T(8,128)(2,1)S(1)}, bf16[2,128,256]{2,1,0:T(8,128)(2,1)S(1)}, u32[]{:S(2)}, u32[]{:S(2)}) collective-permute-start(bf16[2,128,256]{2,1,0:T(8,128)(2,1)S(1)} %bitcast.53), channel_id=1, source_target_pairs={{0,4},{4,8},{8,12},{12,0},{1,5},{5,9},{9,13},{13,1},{2,6},{6,10},{... | collective-permute-start | bytes 393224 | tf_op jit(solution)/shard_map/ppermute | solution.py:180
  2.3 1.1 %collective-permute-start.1 = (bf16[2,128,256]{2,1,0:T(8,128)(2,1)S(1)}, bf16[2,128,256]{2,1,0:T(8,128)(2,1)S(1)}, u32[]{:S(2)}, u32[]{:S(2)}) collective-permute-start(bf16[2,128,256]{2,1,0:T(8,128)(2,1)S(1)} %bitcast.54), channel_id=1, source_target_pairs={{0,8},{4,12},{8,0},{12,4},{1,9},{5,13},{9,1},{13,5},{2,10},{6,14},... | collective-permute-start | bytes 393224 | tf_op jit(solution)/shard_map/ppermute | solution.py:180
  3.4 1.4 %collective-permute-start.2 = (bf16[2,128,256]{2,1,0:T(8,128)(2,1)S(1)}, bf16[2,128,256]{2,1,0:T(8,128)(2,1)S(1)}, u32[]{:S(2)}, u32[]{:S(2)}) collective-permute-start(bf16[2,128,256]{2,1,0:T(8,128)(2,1)S(1)} %bitcast.55), channel_id=1, source_target_pairs={{0,12},{4,0},{8,4},{12,8},{1,13},{5,1},{9,5},{13,9},{2,14},{6,2},{... | collective-permute-start | bytes 393224 | tf_op jit(solution)/shard_map/ppermute | solution.py:180
  4.8 0.7 %and_select_fusion.5 = s32[8]{0:T(128)S(1)} fusion(s32[8]{0:T(128)} %param.8), kind=kLoop, calls=%fused_computation.42 | loop fusion | flops 88 | bytes 64 | tf_op jit(solution)/shard_map/jit(remainder)/select_n | solution.py:187
  5.4 0.7 %convert_bitcast_fusion.1 = (s32[8,1]{0,1:T(1,128)S(1)}, pred[8]{0:T(512)(128)(4,1)S(1)}, s32[8]{0:T(128)S(1)}) fusion(s32[]{:T(128)S(6)} %axis_index.15, s32[8]{0:T(128)} %param.8), kind=kLoop, calls=%fused_computation.64 | loop fusion | flops 136 | bytes 108 | tf_op jit(solution)/shard_map/convert
  6.1 0.1 convert_reduce_fusion
  6.2 0.2 reduce-window.22
  6.4 0.6 %and_select_fusion = (s32[4]{0:T(128)S(1)}, s32[]{:T(128)}) fusion(s32[]{:T(128)S(6)} %axis_index.15, s32[4]{0:T(128)S(1)} %convert_reduce_fusion, s32[4,1]{0,1:T(1,128)S(1)} %reduce-window.22), kind=kLoop, calls=%fused_computation.36 | loop fusion | flops 63 | bytes 56 | tf_op jit(solution)/shard_map/jit(remainder)/select_n | solution.py:207
  7.1 0.7 %and_select_fusion.6 = s32[4]{0:T(128)S(1)} fusion(s32[]{:T(128)} %get-tuple-element.28), kind=kLoop, calls=%fused_computation.43 | loop fusion | flops 48 | bytes 20 | tf_op jit(solution)/shard_map/jit(remainder)/select_n | solution.py:193
  7.7 0.2 reduce-window.21
  7.9 0.2 select_reduce_fusion
  8.1 0.6 %gather_fusion = s32[4]{0:T(128)S(1)} fusion(s32[4]{0:T(128)S(1)} %select_reduce_fusion, s32[1024]{0:T(1024)S(1)} %pad_clamp_fusion.3), kind=kCustom, calls=%fused_computation | custom fusion | bytes 48 | tf_op jit(solution)/shard_map/gather | solution.py:196
  8.8 0.6 %gather_fusion.2 = pred[4]{0:T(512)(128)(4,1)S(1)} fusion(pred[4]{0:T(512)(128)(4,1)S(1)} %compare_bitcast_fusion, s32[1024]{0:T(1024)S(1)} %pad_clamp_fusion.1), kind=kCustom, calls=%fused_computation.2 | custom fusion | bytes 24 | tf_op jit(solution)/shard_map/gather | solution.py:207
  9.4 0.2 reduce-window.23
  9.6 0.1 fusion.1
  9.7 1.3 %gather_fusion.4 = s32[4]{0:T(128)S(1)} fusion(s32[4]{0:T(128)} %param.9, s32[1024]{0:T(1024)S(1)} %pad_clamp_fusion.1), kind=kCustom, calls=%fused_computation.4 | custom fusion | bytes 48 | tf_op jit(solution)/shard_map/gather | solution.py:182
  11.0 2.8 %gather_fusion.1 = bf16[4,2,128,256]{3,2,1,0:T(8,128)(2,1)S(1)} fusion(bf16[32,2,128,256]{3,2,1,0:T(8,128)(2,1)} %param.7, s32[1024]{0:T(1024)S(1)} %pad_clamp_fusion.2), kind=kCustom, calls=%fused_computation.1 | custom fusion | bytes 1048592 | tf_op jit(solution)/shard_map/gather | solution.py:197
  13.8 0.1 fusion
  13.9 0.0 collective-permute-done
  13.9 0.0 collective-permute-done.1
  13.9 1.8 %collective-permute-done.2 = bf16[2,128,256]{2,1,0:T(8,128)(2,1)S(1)} collective-permute-done((bf16[2,128,256]{2,1,0:T(8,128)(2,1)S(1)}, bf16[2,128,256]{2,1,0:T(8,128)(2,1)S(1)}, u32[]{:S(2)}, u32[]{:S(2)}) %collective-permute-start.2) | collective-permute-done | bytes 131104 | tf_op jit(solution)/shard_map/ppermute | solution.py:180
  15.7 0.1 collective-permute-start.3
  15.8 1.4 %collective-permute-start.4 = (bf16[1,2,128,256]{3,2,1,0:T(8,128)(2,1)S(1)}, bf16[1,2,128,256]{3,2,1,0:T(8,128)(2,1)S(1)}, u32[]{:S(2)}, u32[]{:S(2)}) collective-permute-start(bf16[1,2,128,256]{3,2,1,0:T(8,128)(2,1)S(1)} %get-tuple-element.25), channel_id=1, source_target_pairs={{0,8},{4,12},{8,0},{12,4},{1,9},{5,13},{9,1},{13,5},{2,10},{6,14},... | collective-permute-start | bytes 393224 | tf_op jit(solution)/shard_map/ppermute | solution.py:203
  17.2 0.4 collective-permute-start.5
  17.5 1.3 %fusion.3 = s32[]{:T(128)} fusion(s32[4]{0:T(128)} %param.9, s32[]{:T(128)S(6)} %axis_index.15), kind=kLoop, calls=%fused_computation.52 | loop fusion | flops 11 | bytes 24 | tf_op jit(solution)/shard_map/reduce_sum | solution.py:174
  18.8 0.1 reshape.427
  18.9 0.1 broadcast_in_dim.38
  19.0 0.5 slice.38.page_ok_ref
  19.5 0.6 slice.37.page_ok_ref
  20.8 0.0 collective-permute-done.3
  20.8 6.1 %collective-permute-done.4 = bf16[1,2,128,256]{3,2,1,0:T(8,128)(2,1)S(1)} collective-permute-done((bf16[1,2,128,256]{3,2,1,0:T(8,128)(2,1)S(1)}, bf16[1,2,128,256]{3,2,1,0:T(8,128)(2,1)S(1)}, u32[]{:S(2)}, u32[]{:S(2)}) %collective-permute-start.4) | collective-permute-done | bytes 131104 | tf_op jit(solution)/shard_map/ppermute | solution.py:203
  26.9 2.6 %collective-permute-done.5 = bf16[1,2,128,256]{3,2,1,0:T(8,128)(2,1)S(1)} collective-permute-done((bf16[1,2,128,256]{3,2,1,0:T(8,128)(2,1)S(1)}, bf16[1,2,128,256]{3,2,1,0:T(8,128)(2,1)S(1)}, u32[]{:S(2)}, u32[]{:S(2)}) %collective-permute-start.5) | collective-permute-done | bytes 131104 | tf_op jit(solution)/shard_map/ppermute | solution.py:203
  29.5 0.1 maximum_bitcast_fusion
  29.6 0.6 gather_fusion.3
  30.2 0.0 copy-start
  30.2 0.1 collective-permute-start.6
  30.3 0.5 collective-permute-start.7
  30.8 1.4 %collective-permute-start.8 = (bf16[2,2,128,256]{3,2,1,0:T(8,128)(2,1)S(1)}, bf16[2,2,128,256]{3,2,1,0:T(8,128)(2,1)S(1)}, u32[]{:S(2)}, u32[]{:S(2)}) collective-permute-start(bf16[2,2,128,256]{3,2,1,0:T(8,128)(2,1)S(1)} %gather_fusion.3), channel_id=1, source_target_pairs={{0,12},{4,0},{8,4},{12,8},{1,13},{5,1},{9,5},{13,9},{2,14},{6,2},{... | collective-permute-start | bytes 786440 | tf_op jit(solution)/shard_map/ppermute | solution.py:217
  32.2 0.6 %iota_add_fusion = s32[4,128]{1,0:T(4,128)} fusion(s32[4]{0:T(128)S(1)} %broadcast_multiply_fusion), kind=kLoop, calls=%fused_computation.30 | loop fusion | flops 512 | bytes 2064 | tf_op jit(solution)/shard_map/add | solution.py:225
  32.8 0.9 %pad_maximum_fusion.1.new_ref = bf16[4,2,128,256]{3,2,1,0:T(8,128)(2,1)} fusion(bf16[1,2,128,256]{3,2,1,0:T(8,128)(2,1)S(1)} %bitcast.59, bf16[1,2,128,256]{3,2,1,0:T(8,128)(2,1)S(1)} %bitcast.58, bf16[1,2,128,256]{3,2,1,0:T(8,128)(2,1)S(1)} %bitcast.57, bf16[1,2,128,256]{3,2,1,0:T(8,128)(2,1)S(1)} %bitcast.56), kind=kLoop, calls=%fused_computation.7 | loop fusion | flops 786432 | bytes 1048576 | tf_op jit(solution)/shard_map/stack | solution.py:199
  33.7 0.0 copy-done
  33.7 5.5 %shard_map.55 = (f32[128,2048]{1,0:T(8,128)}, f32[2,128,8]{2,1,0:T(8,128)}, f32[2,128,8]{2,1,0:T(8,128)}) custom-call(s32[1]{0:T(128)} %bitcast.24.query_start, bf16[128,2048]{1,0:T(8,128)(2,1)} %q_ref.3, bf16[4,2,128,256]{3,2,1,0:T(8,128)(2,1)} %pad_maximum_fusion.1.new_ref, bf16[2,2,128,256]{3,2,1,0:T(8,128)(2,1)} %copy-done, s32[1,512]{1,0:T(1,128)} %bitcast.65, ...), custom_call_target="tpu_custom_call" | custom-call | tf_op jit(solution)/shard_map/pallas_call | solution.py:146
  39.2 0.0 collective-permute-done.6
  39.2 13.4 %collective-permute-done.7 = bf16[2,2,128,256]{3,2,1,0:T(8,128)(2,1)S(1)} collective-permute-done((bf16[2,2,128,256]{3,2,1,0:T(8,128)(2,1)S(1)}, bf16[2,2,128,256]{3,2,1,0:T(8,128)(2,1)S(1)}, u32[]{:S(2)}, u32[]{:S(2)}) %collective-permute-start.7) | collective-permute-done | bytes 262176 | tf_op jit(solution)/shard_map/ppermute | solution.py:217
  52.6 1.8 %collective-permute-done.8 = bf16[2,2,128,256]{3,2,1,0:T(8,128)(2,1)S(1)} collective-permute-done((bf16[2,2,128,256]{3,2,1,0:T(8,128)(2,1)S(1)}, bf16[2,2,128,256]{3,2,1,0:T(8,128)(2,1)S(1)}, u32[]{:S(2)}, u32[]{:S(2)}) %collective-permute-start.8) | collective-permute-done | bytes 262176 | tf_op jit(solution)/shard_map/ppermute | solution.py:217
  54.4 1.0 %pad_maximum_fusion.page_ref = bf16[6,2,128,256]{3,2,1,0:T(8,128)(2,1)} fusion(bf16[2,2,128,256]{3,2,1,0:T(8,128)(2,1)S(1)} %collective-permute-done.8, bf16[2,2,128,256]{3,2,1,0:T(8,128)(2,1)S(1)} %collective-permute-done.7, bf16[2,2,128,256]{3,2,1,0:T(8,128)(2,1)S(1)} %collective-permute-done.6), kind=kLoop, calls=%fused_computation.5 | loop fusion | flops 786432 | bytes 1572864 | tf_op jit(solution)/shard_map/concatenate | solution.py:219
  55.4 6.9 %shard_map.56 = bf16[128,2048]{1,0:T(8,128)(2,1)} custom-call(bf16[128,2048]{1,0:T(8,128)(2,1)} %q_ref.3, bf16[6,2,128,256]{3,2,1,0:T(8,128)(2,1)} %pad_maximum_fusion.page_ref, s32[1,768]{1,0:T(1,128)} %slice.37.page_ok_ref, f32[128,2048]{1,0:T(8,128)} %get-tuple-element.18.acc_ref, f32[2,128,8]{2,1,0:T(8,128)} %get-tuple-element.19.top_ref, ...), custom_call_target="tpu_custom_call" | custom-call | tf_op jit(solution)/shard_map/pallas_call | solution.py:119
  (15 shorter events, 0.1 us)
Async XLA Ops:
  0.9 13.0 %collective-permute-start = (bf16[2,128,256]{2,1,0:T(8,128)(2,1)S(1)}, bf16[2,128,256]{2,1,0:T(8,128)(2,1)S(1)}, u32[]{:S(2)}, u32[]{:S(2)}) collective-permute-start(bf16[2,128,256]{2,1,0:T(8,128)(2,1)S(1)} %bitcast.53), channel_id=1, source_target_pairs={{0,4},{4,8},{8,12},{12,0},{1,5},{5,9},{9,13},{13,1},{2,6},{6,10},{... | collective-permute-start | bytes 393224 | tf_op jit(solution)/shard_map/ppermute | solution.py:180
  2.3 11.6 %collective-permute-start.1 = (bf16[2,128,256]{2,1,0:T(8,128)(2,1)S(1)}, bf16[2,128,256]{2,1,0:T(8,128)(2,1)S(1)}, u32[]{:S(2)}, u32[]{:S(2)}) collective-permute-start(bf16[2,128,256]{2,1,0:T(8,128)(2,1)S(1)} %bitcast.54), channel_id=1, source_target_pairs={{0,8},{4,12},{8,0},{12,4},{1,9},{5,13},{9,1},{13,5},{2,10},{6,14},... | collective-permute-start | bytes 393224 | tf_op jit(solution)/shard_map/ppermute | solution.py:180
  3.4 12.3 %collective-permute-start.2 = (bf16[2,128,256]{2,1,0:T(8,128)(2,1)S(1)}, bf16[2,128,256]{2,1,0:T(8,128)(2,1)S(1)}, u32[]{:S(2)}, u32[]{:S(2)}) collective-permute-start(bf16[2,128,256]{2,1,0:T(8,128)(2,1)S(1)} %bitcast.55), channel_id=1, source_target_pairs={{0,12},{4,0},{8,4},{12,8},{1,13},{5,1},{9,5},{13,9},{2,14},{6,2},{... | collective-permute-start | bytes 393224 | tf_op jit(solution)/shard_map/ppermute | solution.py:180
  15.7 5.1 %collective-permute-start.3 = (bf16[1,2,128,256]{3,2,1,0:T(8,128)(2,1)S(1)}, bf16[1,2,128,256]{3,2,1,0:T(8,128)(2,1)S(1)}, u32[]{:S(2)}, u32[]{:S(2)}) collective-permute-start(bf16[1,2,128,256]{3,2,1,0:T(8,128)(2,1)S(1)} %get-tuple-element.26), channel_id=1, source_target_pairs={{0,4},{4,8},{8,12},{12,0},{1,5},{5,9},{9,13},{13,1},{2,6},{6,10},{... | collective-permute-start | bytes 393224 | tf_op jit(solution)/shard_map/ppermute | solution.py:203
  15.8 11.1 %collective-permute-start.4 = (bf16[1,2,128,256]{3,2,1,0:T(8,128)(2,1)S(1)}, bf16[1,2,128,256]{3,2,1,0:T(8,128)(2,1)S(1)}, u32[]{:S(2)}, u32[]{:S(2)}) collective-permute-start(bf16[1,2,128,256]{3,2,1,0:T(8,128)(2,1)S(1)} %get-tuple-element.25), channel_id=1, source_target_pairs={{0,8},{4,12},{8,0},{12,4},{1,9},{5,13},{9,1},{13,5},{2,10},{6,14},... | collective-permute-start | bytes 393224 | tf_op jit(solution)/shard_map/ppermute | solution.py:203
  17.2 12.4 %collective-permute-start.5 = (bf16[1,2,128,256]{3,2,1,0:T(8,128)(2,1)S(1)}, bf16[1,2,128,256]{3,2,1,0:T(8,128)(2,1)S(1)}, u32[]{:S(2)}, u32[]{:S(2)}) collective-permute-start(bf16[1,2,128,256]{3,2,1,0:T(8,128)(2,1)S(1)} %slice_bitcast_fusion.2), channel_id=1, source_target_pairs={{0,12},{4,0},{8,4},{12,8},{1,13},{5,1},{9,5},{13,9},{2,14},{6,2},{... | collective-permute-start | bytes 393224 | tf_op jit(solution)/shard_map/ppermute | solution.py:203
  30.2 3.5 %copy-start = (bf16[2,2,128,256]{3,2,1,0:T(8,128)(2,1)}, bf16[2,2,128,256]{3,2,1,0:T(8,128)(2,1)S(1)}, u32[]{:S(2)}) copy-start(bf16[2,2,128,256]{3,2,1,0:T(8,128)(2,1)S(1)} %gather_fusion.3) | copy-start | bytes 786436
  30.2 9.0 %collective-permute-start.6 = (bf16[2,2,128,256]{3,2,1,0:T(8,128)(2,1)S(1)}, bf16[2,2,128,256]{3,2,1,0:T(8,128)(2,1)S(1)}, u32[]{:S(2)}, u32[]{:S(2)}) collective-permute-start(bf16[2,2,128,256]{3,2,1,0:T(8,128)(2,1)S(1)} %gather_fusion.3), channel_id=1, source_target_pairs={{0,4},{4,8},{8,12},{12,0},{1,5},{5,9},{9,13},{13,1},{2,6},{6,10},{... | collective-permute-start | bytes 786440 | tf_op jit(solution)/shard_map/ppermute | solution.py:217
  30.3 22.3 %collective-permute-start.7 = (bf16[2,2,128,256]{3,2,1,0:T(8,128)(2,1)S(1)}, bf16[2,2,128,256]{3,2,1,0:T(8,128)(2,1)S(1)}, u32[]{:S(2)}, u32[]{:S(2)}) collective-permute-start(bf16[2,2,128,256]{3,2,1,0:T(8,128)(2,1)S(1)} %gather_fusion.3), channel_id=1, source_target_pairs={{0,8},{4,12},{8,0},{12,4},{1,9},{5,13},{9,1},{13,5},{2,10},{6,14},... | collective-permute-start | bytes 786440 | tf_op jit(solution)/shard_map/ppermute | solution.py:217
  30.8 23.6 %collective-permute-start.8 = (bf16[2,2,128,256]{3,2,1,0:T(8,128)(2,1)S(1)}, bf16[2,2,128,256]{3,2,1,0:T(8,128)(2,1)S(1)}, u32[]{:S(2)}, u32[]{:S(2)}) collective-permute-start(bf16[2,2,128,256]{3,2,1,0:T(8,128)(2,1)S(1)} %gather_fusion.3), channel_id=1, source_target_pairs={{0,12},{4,0},{8,4},{12,8},{1,13},{5,1},{9,5},{13,9},{2,14},{6,2},{... | collective-permute-start | bytes 786440 | tf_op jit(solution)/shard_map/ppermute | solution.py:217

commit v15 on v14

--- a/solution.py
+++ b/solution.py
@@ -68,8 +68,8 @@
 
 
 def prefix_kernel(
-    q_ref, page_ref, page_ok_ref, acc_ref, top_ref, total_ref, o_ref,
-    *, head_size, group_size, mask_pages,
+    q_ref, page_ref, page_ok_ref, acc_ref, top_ref, total_ref, *out_refs,
+    head_size, group_size, mask_pages, final,
 ):
     scale = 1.0 / math.sqrt(head_size)
     q_rows = q_ref.shape[0]
@@ -102,23 +102,46 @@
         summed = acc_prev * factor + lax.dot_general(
             weights.astype(jnp.bfloat16), page_values, pv, preferred_element_type=jnp.float32
         )
-        result = (summed / row_total).astype(o_ref.dtype)
         for j, h in enumerate(heads):
-            o_ref[:, h * head_size : (h + 1) * head_size] = result[j * q_rows : (j + 1) * q_rows]
-
-
-def prefix_part(page_ok, q_new, pages, acc, top, total, group_size, head_size, mask_pages):
+            rows = slice(j * q_rows, (j + 1) * q_rows)
+            cols = slice(h * head_size, (h + 1) * head_size)
+            if final:
+                out_refs[0][:, cols] = (summed[rows] / row_total[rows]).astype(out_refs[0].dtype)
+            else:
+                out_refs[0][:, cols] = summed[rows]
+                out_refs[1][0, :, h : h + 1] = row_top[rows]
+                out_refs[2][0, :, h : h + 1] = row_total[rows]
+
+
+def prefix_part(page_ok, q_new, pages, acc, top, total, group_size, head_size, mask_pages,
+                final=True):
     q_rows = q_new.shape[0]
     npage, kv_heads, page_len, width = pages.shape
     kernel = functools.partial(
-        prefix_kernel, head_size=head_size, group_size=group_size, mask_pages=mask_pages
+        prefix_kernel, head_size=head_size, group_size=group_size, mask_pages=mask_pages,
+        final=final,
     )
     span = group_size * head_size
     block = pl.BlockSpec((q_rows, span), lambda g: (0, g))
     stat_spec = pl.BlockSpec((1, q_rows, group_size), lambda g: (g, 0, 0))
+    if final:
+        out_shape = jax.ShapeDtypeStruct(q_new.shape, q_new.dtype)
+        out_specs = block
+    else:
+        stat = jax.ShapeDtypeStruct(top.shape, jnp.float32)
+        out_shape = (jax.ShapeDtypeStruct(q_new.shape, jnp.float32), stat, stat)
+        out_specs = (block, stat_spec, stat_spec)
+    rows = q_new.shape[0] * q_new.shape[1] // head_size
+    keys = npage * page_len
+    cost = pl.CostEstimate(
+        flops=4 * rows * keys * head_size,
+        transcendentals=rows * keys,
+        bytes_accessed=q_new.size * 2 + pages.size * 2 + acc.size * 8,
+    )
     return pl.pallas_call(
         kernel,
-        out_shape=jax.ShapeDtypeStruct(q_new.shape, q_new.dtype),
+        out_shape=out_shape,
+        cost_estimate=cost,
         grid=(kv_heads,),
         in_specs=[
             block,
@@ -128,7 +151,7 @@
             stat_spec,
             stat_spec,
         ],
-        out_specs=block,
+        out_specs=out_specs,
     )(q_new, pages, page_ok, acc, top, total)
 
 
@@ -216,7 +239,7 @@
         gathered.append(
             lax.ppermute(own, "blk", [(i, (i + k) % blocks) for i in range(blocks)])
         )
-    others = jnp.concatenate(gathered[1:])
+    later = blocks > 2
 
     q_rows = q_new.shape[0]
     page_len = kv_cache.shape[2]
@@ -229,12 +252,22 @@
     page_ok = slot_ids[None, :] * blocks + ((myself - block_ids) % blocks)[:, None] < npages
     page_ok = jnp.repeat(page_ok.astype(jnp.int32).reshape(-1), page_len).reshape(1, -1)
     own_ok = page_ok[:, : pg * page_len]
-    others_ok = page_ok[:, pg * page_len :]
+    first_ok = page_ok[:, pg * page_len : 2 * pg * page_len]
+    later_ok = page_ok[:, 2 * pg * page_len :]
     ragged = npages % blocks != 0
     acc, top, total = attention(
         query_start, key_pos, own_ok, q_new, new_all, own, group_size, head_size, ragged
     )
-    return prefix_part(others_ok, q_new, others, acc, top, total, group_size, head_size, ragged)
+    if not later:
+        return prefix_part(
+            first_ok, q_new, gathered[1], acc, top, total, group_size, head_size, ragged
+        )
+    acc, top, total = prefix_part(
+        first_ok, q_new, gathered[1], acc, top, total, group_size, head_size, ragged, False
+    )
+    acc, top, total, farther = lax.optimization_barrier((acc, top, total, gathered[2:]))
+    later = jnp.concatenate(farther)
+    return prefix_part(later_ok, q_new, later, acc, top, total, group_size, head_size, ragged)
 
 
 def solution(mesh):

time: 62.5 us -> 61.9 us (level)
  the two profiles are of different devices: /device:TPU:9 before, /device:TPU:13 now
where the time goes in v15:
time: 61.9 us; the launch traced here: 61.6 us
  waiting for transfers between devices  19.2 us (31%)
  Pallas kernels  18.4 us (30%)
  local copies, waits for them, and re-layouts  8.92 us (14%)
  starting transfers between devices  7.53 us (12%)
  other arithmetic  6.8 us (11%)
  between operations  0.79 us (1%)
    pallas_call x2, Pallas kernels, prefix_part(): pl.pallas_call(kernel, out_shape=out_shape, cost_estimate=cost, grid=(kv_...  12.9 us
    ppermute x3, waiting for transfers between devices, local(): lax.ppermute(sent[k], 'blk', [(i, (i + k) % blocks) for i in range(blocks)])  12.4 us
    ppermute x3, waiting for transfers between devices, local(): lax.ppermute(own, 'blk', [(i, (i + k) % blocks) for i in range(blocks)])  5.76 us
    pallas_call x1, Pallas kernels, attention(): pl.pallas_call(kernel, out_shape=(jax.ShapeDtypeStruct(q_new.shape, jnp.f...  5.55 us
    ppermute x3, starting transfers between devices, local(): lax.ppermute(own_rows, 'blk', [(i, (i + k) % blocks) for i in range(block...  3.83 us
    gather x1, local copies, waits for them, and re-layouts, local(): sent = kv_cache[by_shift].reshape((blocks, per_peer) + kv_cache.shape[1:])  2.77 us
    ppermute x3, starting transfers between devices, local(): lax.ppermute(sent[k], 'blk', [(i, (i + k) % blocks) for i in range(blocks)])  2.2 us
    unnamed x7, local copies, waits for them, and re-layouts  1.64 us
  transfers between devices with their start and end apart: 9, of which 6 were waited for; matrix products, arithmetic and copies ran while one was open for 20% of the time, Pallas kernels for 21%

profile of v15, /device:TPU:13, one launch (start us, length us, event | category | flops | bytes accessed | tf_op | source)
XLA Modules:
  0.0 61.6 jit_solution(7392490424195821390)
XLA Ops:
  0.0 0.0 copy-start
  0.0 0.9 %copy.19 = bf16[128,2,256]{2,0,1:T(8,128)(2,1)S(1)} copy(bf16[128,2,256]{2,1,0:T(2,128)(2,1)} %param.6) | data formatting | bytes 262144 | tf_op args[1]
  0.9 1.3 %collective-permute-start = (bf16[2,128,256]{2,1,0:T(8,128)(2,1)S(1)}, bf16[2,128,256]{2,1,0:T(8,128)(2,1)S(1)}, u32[]{:S(2)}, u32[]{:S(2)}) collective-permute-start(bf16[2,128,256]{2,1,0:T(8,128)(2,1)S(1)} %bitcast.53), channel_id=1, source_target_pairs={{0,4},{4,8},{8,12},{12,0},{1,5},{5,9},{9,13},{13,1},{2,6},{6,10},{... | collective-permute-start | bytes 393224 | tf_op jit(solution)/shard_map/ppermute | solution.py:203
  2.3 1.1 %collective-permute-start.1 = (bf16[2,128,256]{2,1,0:T(8,128)(2,1)S(1)}, bf16[2,128,256]{2,1,0:T(8,128)(2,1)S(1)}, u32[]{:S(2)}, u32[]{:S(2)}) collective-permute-start(bf16[2,128,256]{2,1,0:T(8,128)(2,1)S(1)} %bitcast.54), channel_id=1, source_target_pairs={{0,8},{4,12},{8,0},{12,4},{1,9},{5,13},{9,1},{13,5},{2,10},{6,14},... | collective-permute-start | bytes 393224 | tf_op jit(solution)/shard_map/ppermute | solution.py:203
  3.4 1.4 %collective-permute-start.2 = (bf16[2,128,256]{2,1,0:T(8,128)(2,1)S(1)}, bf16[2,128,256]{2,1,0:T(8,128)(2,1)S(1)}, u32[]{:S(2)}, u32[]{:S(2)}) collective-permute-start(bf16[2,128,256]{2,1,0:T(8,128)(2,1)S(1)} %bitcast.55), channel_id=1, source_target_pairs={{0,12},{4,0},{8,4},{12,8},{1,13},{5,1},{9,5},{13,9},{2,14},{6,2},{... | collective-permute-start | bytes 393224 | tf_op jit(solution)/shard_map/ppermute | solution.py:203
  4.8 0.7 %and_select_fusion.5 = s32[8]{0:T(128)S(1)} fusion(s32[8]{0:T(128)} %param.8), kind=kLoop, calls=%fused_computation.42 | loop fusion | flops 88 | bytes 64 | tf_op jit(solution)/shard_map/jit(remainder)/select_n | solution.py:210
  5.4 0.7 %convert_bitcast_fusion.1 = (s32[8,1]{0,1:T(1,128)S(1)}, pred[8]{0:T(512)(128)(4,1)S(1)}, s32[8]{0:T(128)S(1)}) fusion(s32[]{:T(128)S(6)} %axis_index.15, s32[8]{0:T(128)} %param.8), kind=kLoop, calls=%fused_computation.64 | loop fusion | flops 136 | bytes 108 | tf_op jit(solution)/shard_map/convert
  6.1 0.1 convert_reduce_fusion
  6.2 0.2 reduce-window.22
  6.4 0.6 %and_select_fusion = (s32[4]{0:T(128)S(1)}, s32[]{:T(128)}) fusion(s32[]{:T(128)S(6)} %axis_index.15, s32[4]{0:T(128)S(1)} %convert_reduce_fusion, s32[4,1]{0,1:T(1,128)S(1)} %reduce-window.22), kind=kLoop, calls=%fused_computation.36 | loop fusion | flops 63 | bytes 56 | tf_op jit(solution)/shard_map/jit(remainder)/select_n | solution.py:230
  7.1 0.7 %and_select_fusion.6 = s32[4]{0:T(128)S(1)} fusion(s32[]{:T(128)} %get-tuple-element.46), kind=kLoop, calls=%fused_computation.43 | loop fusion | flops 48 | bytes 20 | tf_op jit(solution)/shard_map/jit(remainder)/select_n | solution.py:216
  7.7 0.2 reduce-window.21
  7.9 0.2 select_reduce_fusion
  8.1 0.6 %gather_fusion = s32[4]{0:T(128)S(1)} fusion(s32[4]{0:T(128)S(1)} %select_reduce_fusion, s32[1024]{0:T(1024)S(1)} %pad_clamp_fusion.3), kind=kCustom, calls=%fused_computation | custom fusion | bytes 48 | tf_op jit(solution)/shard_map/gather | solution.py:219
  8.8 0.6 %gather_fusion.2 = pred[4]{0:T(512)(128)(4,1)S(1)} fusion(pred[4]{0:T(512)(128)(4,1)S(1)} %compare_bitcast_fusion, s32[1024]{0:T(1024)S(1)} %pad_clamp_fusion.1), kind=kCustom, calls=%fused_computation.2 | custom fusion | bytes 24 | tf_op jit(solution)/shard_map/gather | solution.py:230
  9.4 0.2 reduce-window.23
  9.6 0.1 fusion.1
  9.7 0.1 fusion
  9.8 0.1 reshape.427
  9.9 0.1 broadcast_in_dim.38
  10.0 0.6 fusion.14
  10.6 1.3 %gather_fusion.4 = s32[4]{0:T(128)S(1)} fusion(s32[4]{0:T(128)} %param.9, s32[1024]{0:T(1024)S(1)} %pad_clamp_fusion.1), kind=kCustom, calls=%fused_computation.4 | custom fusion | bytes 48 | tf_op jit(solution)/shard_map/gather | solution.py:205
  11.9 2.8 %gather_fusion.1 = bf16[4,2,128,256]{3,2,1,0:T(8,128)(2,1)S(1)} fusion(bf16[32,2,128,256]{3,2,1,0:T(8,128)(2,1)} %param.7, s32[1024]{0:T(1024)S(1)} %pad_clamp_fusion.2), kind=kCustom, calls=%fused_computation.1 | custom fusion | bytes 1048592 | tf_op jit(solution)/shard_map/gather | solution.py:220
  14.6 0.0 collective-permute-done
  14.7 0.0 collective-permute-done.1
  14.7 1.0 %collective-permute-done.2 = bf16[2,128,256]{2,1,0:T(8,128)(2,1)S(1)} collective-permute-done((bf16[2,128,256]{2,1,0:T(8,128)(2,1)S(1)}, bf16[2,128,256]{2,1,0:T(8,128)(2,1)S(1)}, u32[]{:S(2)}, u32[]{:S(2)}) %collective-permute-start.2) | collective-permute-done | bytes 131104 | tf_op jit(solution)/shard_map/ppermute | solution.py:203
  15.7 0.1 collective-permute-start.3
  15.8 2.1 %collective-permute-start.4 = (bf16[1,2,128,256]{3,2,1,0:T(8,128)(2,1)S(1)}, bf16[1,2,128,256]{3,2,1,0:T(8,128)(2,1)S(1)}, u32[]{:S(2)}, u32[]{:S(2)}) collective-permute-start(bf16[1,2,128,256]{3,2,1,0:T(8,128)(2,1)S(1)} %get-tuple-element.41), channel_id=1, source_target_pairs={{0,8},{4,12},{8,0},{12,4},{1,9},{5,13},{9,1},{13,5},{2,10},{6,14},... | collective-permute-start | bytes 393224 | tf_op jit(solution)/shard_map/ppermute | solution.py:226
  17.9 0.0 collective-permute-start.5
  18.0 2.4 %collective-permute-done.3 = bf16[1,2,128,256]{3,2,1,0:T(8,128)(2,1)S(1)} collective-permute-done((bf16[1,2,128,256]{3,2,1,0:T(8,128)(2,1)S(1)}, bf16[1,2,128,256]{3,2,1,0:T(8,128)(2,1)S(1)}, u32[]{:S(2)}, u32[]{:S(2)}) %collective-permute-start.3) | collective-permute-done | bytes 131104 | tf_op jit(solution)/shard_map/ppermute | solution.py:226
  20.3 6.1 %collective-permute-done.4 = bf16[1,2,128,256]{3,2,1,0:T(8,128)(2,1)S(1)} collective-permute-done((bf16[1,2,128,256]{3,2,1,0:T(8,128)(2,1)S(1)}, bf16[1,2,128,256]{3,2,1,0:T(8,128)(2,1)S(1)}, u32[]{:S(2)}, u32[]{:S(2)}) %collective-permute-start.4) | collective-permute-done | bytes 131104 | tf_op jit(solution)/shard_map/ppermute | solution.py:226
  26.4 3.9 %collective-permute-done.5 = bf16[1,2,128,256]{3,2,1,0:T(8,128)(2,1)S(1)} collective-permute-done((bf16[1,2,128,256]{3,2,1,0:T(8,128)(2,1)S(1)}, bf16[1,2,128,256]{3,2,1,0:T(8,128)(2,1)S(1)}, u32[]{:S(2)}, u32[]{:S(2)}) %collective-permute-start.5) | collective-permute-done | bytes 131104 | tf_op jit(solution)/shard_map/ppermute | solution.py:226
  30.4 0.1 maximum_bitcast_fusion
  30.4 0.6 gather_fusion.3
  31.0 0.0 copy-start.1
  31.0 0.1 collective-permute-start.6
  31.1 0.7 %iota_add_fusion = s32[4,128]{1,0:T(4,128)} fusion(s32[4]{0:T(128)S(1)} %broadcast_multiply_fusion), kind=kLoop, calls=%fused_computation.30 | loop fusion | flops 512 | bytes 2064 | tf_op jit(solution)/shard_map/add | solution.py:248
  31.7 0.6 slice.43.page_ok_ref
  32.3 0.4 collective-permute-start.7
  32.8 1.0 %collective-permute-start.8 = (bf16[2,2,128,256]{3,2,1,0:T(8,128)(2,1)S(1)}, bf16[2,2,128,256]{3,2,1,0:T(8,128)(2,1)S(1)}, u32[]{:S(2)}, u32[]{:S(2)}) collective-permute-start(bf16[2,2,128,256]{3,2,1,0:T(8,128)(2,1)S(1)} %gather_fusion.3), channel_id=1, source_target_pairs={{0,12},{4,0},{8,4},{12,8},{1,13},{5,1},{9,5},{13,9},{2,14},{6,2},{... | collective-permute-start | bytes 786440 | tf_op jit(solution)/shard_map/ppermute | solution.py:240
  33.8 0.0 copy-done
  33.8 0.6 %fusion.3 = s32[]{:T(128)} fusion(s32[4]{0:T(128)S(1)} %copy-done, s32[]{:T(128)S(6)} %axis_index.15), kind=kLoop, calls=%fused_computation.52 | loop fusion | flops 11 | bytes 24 | tf_op jit(solution)/shard_map/reduce_sum | solution.py:197
  35.1 0.9 %pad_maximum_fusion.new_ref = bf16[4,2,128,256]{3,2,1,0:T(8,128)(2,1)} fusion(bf16[1,2,128,256]{3,2,1,0:T(8,128)(2,1)S(1)} %bitcast.59, bf16[1,2,128,256]{3,2,1,0:T(8,128)(2,1)S(1)} %bitcast.58, bf16[1,2,128,256]{3,2,1,0:T(8,128)(2,1)S(1)} %bitcast.57, bf16[1,2,128,256]{3,2,1,0:T(8,128)(2,1)S(1)} %bitcast.56), kind=kLoop, calls=%fused_computation.6 | loop fusion | flops 786432 | bytes 1048576 | tf_op jit(solution)/shard_map/stack | solution.py:222
  35.9 0.0 copy-done.1
  35.9 5.5 %shard_map.55 = (f32[128,2048]{1,0:T(8,128)}, f32[2,128,8]{2,1,0:T(8,128)}, f32[2,128,8]{2,1,0:T(8,128)}) custom-call(s32[1]{0:T(128)} %bitcast.24.query_start, bf16[128,2048]{1,0:T(8,128)(2,1)} %q_ref.5, bf16[4,2,128,256]{3,2,1,0:T(8,128)(2,1)} %pad_maximum_fusion.new_ref, bf16[2,2,128,256]{3,2,1,0:T(8,128)(2,1)} %copy-done.1, s32[1,512]{1,0:T(1,128)} %bitcast.65, ...), custom_call_target="tpu_custom_call" | custom-call | tf_op jit(solution)/shard_map/pallas_call | solution.py:169
  41.5 0.0 collective-permute-done.6.page_ref
  41.5 0.0 copy-start.2
  41.5 0.7 %copy-done.2 = bf16[2,2,128,256]{3,2,1,0:T(8,128)(2,1)} copy-done((bf16[2,2,128,256]{3,2,1,0:T(8,128)(2,1)}, bf16[2,2,128,256]{3,2,1,0:T(8,128)(2,1)S(1)}, u32[]{:S(2)}) %copy-start.2) | copy-done | bytes 262168
  42.2 7.2 %shard_map.56 = (f32[128,2048]{1,0:T(8,128)}, f32[2,128,8]{2,1,0:T(8,128)}, f32[2,128,8]{2,1,0:T(8,128)}) custom-call(bf16[128,2048]{1,0:T(8,128)(2,1)} %q_ref.5, bf16[2,2,128,256]{3,2,1,0:T(8,128)(2,1)} %copy-done.2, s32[1,256]{1,0:T(1,128)} %get-tuple-element.44.page_ok_ref, f32[128,2048]{1,0:T(8,128)} %get-tuple-element.26.acc_ref, ...), custom_call_target="tpu_custom_call" | custom-call | flops 268435456 | bytes 2883584 | tf_op jit(solution)/shard_map/pallas_call | solution.py:141
  49.4 4.0 %collective-permute-done.7 = bf16[2,2,128,256]{3,2,1,0:T(8,128)(2,1)S(1)} collective-permute-done((bf16[2,2,128,256]{3,2,1,0:T(8,128)(2,1)S(1)}, bf16[2,2,128,256]{3,2,1,0:T(8,128)(2,1)S(1)}, u32[]{:S(2)}, u32[]{:S(2)}) %collective-permute-start.7) | collective-permute-done | bytes 262176 | tf_op jit(solution)/shard_map/ppermute | solution.py:240
  53.4 1.8 %collective-permute-done.8 = bf16[2,2,128,256]{3,2,1,0:T(8,128)(2,1)S(1)} collective-permute-done((bf16[2,2,128,256]{3,2,1,0:T(8,128)(2,1)S(1)}, bf16[2,2,128,256]{3,2,1,0:T(8,128)(2,1)S(1)}, u32[]{:S(2)}, u32[]{:S(2)}) %collective-permute-start.8) | collective-permute-done | bytes 262176 | tf_op jit(solution)/shard_map/ppermute | solution.py:240
  55.2 0.8 %pad_maximum_fusion.1.page_ref = bf16[4,2,128,256]{3,2,1,0:T(8,128)(2,1)} fusion(bf16[2,2,128,256]{3,2,1,0:T(8,128)(2,1)S(1)} %collective-permute-done.8, bf16[2,2,128,256]{3,2,1,0:T(8,128)(2,1)S(1)} %collective-permute-done.7), kind=kLoop, calls=%fused_computation.7 | loop fusion | flops 262144 | bytes 1048576 | tf_op jit(solution)/shard_map/concatenate | solution.py:269
  56.0 5.6 %shard_map.57 = bf16[128,2048]{1,0:T(8,128)(2,1)} custom-call(bf16[128,2048]{1,0:T(8,128)(2,1)} %q_ref.5, bf16[4,2,128,256]{3,2,1,0:T(8,128)(2,1)} %pad_maximum_fusion.1.page_ref, s32[1,512]{1,0:T(1,128)} %slice.43.page_ok_ref, f32[128,2048]{1,0:T(8,128)} %get-tuple-element.34.acc_ref, f32[2,128,8]{2,1,0:T(8,128)} %get-tuple-element.35.top_ref, ...), custom_call_target="tpu_custom_call" | custom-call | flops 536870912 | bytes 3145728 | tf_op jit(solution)/shard_map/pallas_call | solution.py:141
  (15 shorter events, 0.1 us)
Async XLA Ops:
  0.0 33.8 %copy-start = (s32[4]{0:T(128)S(1)}, s32[4]{0:T(128)}, u32[]{:S(2)}) copy-start(s32[4]{0:T(128)} %param.9) | copy-start | bytes 52
  0.9 13.7 %collective-permute-start = (bf16[2,128,256]{2,1,0:T(8,128)(2,1)S(1)}, bf16[2,128,256]{2,1,0:T(8,128)(2,1)S(1)}, u32[]{:S(2)}, u32[]{:S(2)}) collective-permute-start(bf16[2,128,256]{2,1,0:T(8,128)(2,1)S(1)} %bitcast.53), channel_id=1, source_target_pairs={{0,4},{4,8},{8,12},{12,0},{1,5},{5,9},{9,13},{13,1},{2,6},{6,10},{... | collective-permute-start | bytes 393224 | tf_op jit(solution)/shard_map/ppermute | solution.py:203
  2.3 12.4 %collective-permute-start.1 = (bf16[2,128,256]{2,1,0:T(8,128)(2,1)S(1)}, bf16[2,128,256]{2,1,0:T(8,128)(2,1)S(1)}, u32[]{:S(2)}, u32[]{:S(2)}) collective-permute-start(bf16[2,128,256]{2,1,0:T(8,128)(2,1)S(1)} %bitcast.54), channel_id=1, source_target_pairs={{0,8},{4,12},{8,0},{12,4},{1,9},{5,13},{9,1},{13,5},{2,10},{6,14},... | collective-permute-start | bytes 393224 | tf_op jit(solution)/shard_map/ppermute | solution.py:203
  3.4 12.3 %collective-permute-start.2 = (bf16[2,128,256]{2,1,0:T(8,128)(2,1)S(1)}, bf16[2,128,256]{2,1,0:T(8,128)(2,1)S(1)}, u32[]{:S(2)}, u32[]{:S(2)}) collective-permute-start(bf16[2,128,256]{2,1,0:T(8,128)(2,1)S(1)} %bitcast.55), channel_id=1, source_target_pairs={{0,12},{4,0},{8,4},{12,8},{1,13},{5,1},{9,5},{13,9},{2,14},{6,2},{... | collective-permute-start | bytes 393224 | tf_op jit(solution)/shard_map/ppermute | solution.py:203
  15.7 4.6 %collective-permute-start.3 = (bf16[1,2,128,256]{3,2,1,0:T(8,128)(2,1)S(1)}, bf16[1,2,128,256]{3,2,1,0:T(8,128)(2,1)S(1)}, u32[]{:S(2)}, u32[]{:S(2)}) collective-permute-start(bf16[1,2,128,256]{3,2,1,0:T(8,128)(2,1)S(1)} %get-tuple-element.42), channel_id=1, source_target_pairs={{0,4},{4,8},{8,12},{12,0},{1,5},{5,9},{9,13},{13,1},{2,6},{6,10},{... | collective-permute-start | bytes 393224 | tf_op jit(solution)/shard_map/ppermute | solution.py:226
  15.8 10.6 %collective-permute-start.4 = (bf16[1,2,128,256]{3,2,1,0:T(8,128)(2,1)S(1)}, bf16[1,2,128,256]{3,2,1,0:T(8,128)(2,1)S(1)}, u32[]{:S(2)}, u32[]{:S(2)}) collective-permute-start(bf16[1,2,128,256]{3,2,1,0:T(8,128)(2,1)S(1)} %get-tuple-element.41), channel_id=1, source_target_pairs={{0,8},{4,12},{8,0},{12,4},{1,9},{5,13},{9,1},{13,5},{2,10},{6,14},... | collective-permute-start | bytes 393224 | tf_op jit(solution)/shard_map/ppermute | solution.py:226
  17.9 12.4 %collective-permute-start.5 = (bf16[1,2,128,256]{3,2,1,0:T(8,128)(2,1)S(1)}, bf16[1,2,128,256]{3,2,1,0:T(8,128)(2,1)S(1)}, u32[]{:S(2)}, u32[]{:S(2)}) collective-permute-start(bf16[1,2,128,256]{3,2,1,0:T(8,128)(2,1)S(1)} %slice_bitcast_fusion.2), channel_id=1, source_target_pairs={{0,12},{4,0},{8,4},{12,8},{1,13},{5,1},{9,5},{13,9},{2,14},{6,2},{... | collective-permute-start | bytes 393224 | tf_op jit(solution)/shard_map/ppermute | solution.py:226
  31.0 4.9 %copy-start.1 = (bf16[2,2,128,256]{3,2,1,0:T(8,128)(2,1)}, bf16[2,2,128,256]{3,2,1,0:T(8,128)(2,1)S(1)}, u32[]{:S(2)}) copy-start(bf16[2,2,128,256]{3,2,1,0:T(8,128)(2,1)S(1)} %gather_fusion.3) | copy-start | bytes 786436
  31.0 10.5 %collective-permute-start.6 = (bf16[2,2,128,256]{3,2,1,0:T(8,128)(2,1)S(1)}, bf16[2,2,128,256]{3,2,1,0:T(8,128)(2,1)S(1)}, u32[]{:S(2)}, u32[]{:S(2)}) collective-permute-start(bf16[2,2,128,256]{3,2,1,0:T(8,128)(2,1)S(1)} %gather_fusion.3), channel_id=1, source_target_pairs={{0,4},{4,8},{8,12},{12,0},{1,5},{5,9},{9,13},{13,1},{2,6},{6,10},{... | collective-permute-start | bytes 786440 | tf_op jit(solution)/shard_map/ppermute | solution.py:240
  32.3 21.1 %collective-permute-start.7 = (bf16[2,2,128,256]{3,2,1,0:T(8,128)(2,1)S(1)}, bf16[2,2,128,256]{3,2,1,0:T(8,128)(2,1)S(1)}, u32[]{:S(2)}, u32[]{:S(2)}) collective-permute-start(bf16[2,2,128,256]{3,2,1,0:T(8,128)(2,1)S(1)} %gather_fusion.3), channel_id=1, source_target_pairs={{0,8},{4,12},{8,0},{12,4},{1,9},{5,13},{9,1},{13,5},{2,10},{6,14},... | collective-permute-start | bytes 786440 | tf_op jit(solution)/shard_map/ppermute | solution.py:240
  32.8 22.4 %collective-permute-start.8 = (bf16[2,2,128,256]{3,2,1,0:T(8,128)(2,1)S(1)}, bf16[2,2,128,256]{3,2,1,0:T(8,128)(2,1)S(1)}, u32[]{:S(2)}, u32[]{:S(2)}) collective-permute-start(bf16[2,2,128,256]{3,2,1,0:T(8,128)(2,1)S(1)} %gather_fusion.3), channel_id=1, source_target_pairs={{0,12},{4,0},{8,4},{12,8},{1,13},{5,1},{9,5},{13,9},{2,14},{6,2},{... | collective-permute-start | bytes 786440 | tf_op jit(solution)/shard_map/ppermute | solution.py:240
  41.5 0.7 %copy-start.2 = (bf16[2,2,128,256]{3,2,1,0:T(8,128)(2,1)}, bf16[2,2,128,256]{3,2,1,0:T(8,128)(2,1)S(1)}, u32[]{:S(2)}) copy-start(bf16[2,2,128,256]{3,2,1,0:T(8,128)(2,1)S(1)} %collective-permute-done.6.page_ref) | copy-start | bytes 786436

commit v16 on v15

--- a/solution.py
+++ b/solution.py
@@ -206,18 +206,21 @@
 
     page_owner = page_table // slots_dev
     owned = page_owner == myself
-    page_rank = jnp.cumsum(owned.astype(jnp.int32)) - 1
     local_slot = page_table % slots_dev
-    counts = jnp.sum((page_owner[None, :] == block_ids[:, None]).astype(jnp.int32), axis=1)
     per_peer = (CAP + blocks - 1) // blocks
-    starts = jnp.cumsum(counts) - counts
-    my_start = jnp.sum(jnp.where(block_ids == myself, starts, 0))
+    page_ids = jnp.arange(npages, dtype=jnp.int32)
+    page_rank = jnp.sum(
+        ((page_ids[None, :] < page_ids[:, None]) & owned[None, :]).astype(jnp.int32), axis=1
+    )
+    my_start = jnp.sum((page_owner < myself).astype(jnp.int32))
     peer_slots = jnp.arange(per_peer, dtype=jnp.int32)[None, :]
-    wanted = (block_ids[:, None] - my_start) % blocks + peer_slots * blocks
+    wanted = (myself + block_ids[:, None] - my_start) % blocks + peer_slots * blocks
     picked = owned[None, None, :] & (page_rank[None, None, :] == wanted[..., None])
-    chosen = jnp.sum(jnp.where(picked, local_slot[None, None, :], 0), axis=2).reshape(-1)
-    by_shift = chosen.reshape(blocks, per_peer)[(myself + block_ids) % blocks].reshape(-1)
-    sent = kv_cache[by_shift].reshape((blocks, per_peer) + kv_cache.shape[1:])
+    by_shift = jnp.sum(jnp.where(picked, local_slot[None, None, :], 0), axis=2).reshape(-1)
+    sent = jnp.stack(
+        [lax.dynamic_index_in_dim(kv_cache, by_shift[i], keepdims=False)
+         for i in range(blocks * per_peer)]
+    ).reshape((blocks, per_peer) + kv_cache.shape[1:])
     sent, new_all = lax.optimization_barrier((sent, new_all))
     new_all = jnp.stack(new_all)
     arrived = [sent[0]]
@@ -226,14 +229,20 @@
             lax.ppermute(sent[k], "blk", [(i, (i + k) % blocks) for i in range(blocks)])
         )
     received = jnp.stack(arrived).reshape((blocks * per_peer,) + kv_cache.shape[1:])
+    source = (myself - block_ids) % blocks
+    counts = jnp.sum((page_owner[None, :] == source[:, None]).astype(jnp.int32), axis=1)
+    starts = jnp.sum((page_owner[None, :] < source[:, None]).astype(jnp.int32), axis=1)
     arriving = (myself - starts[:, None]) % blocks + peer_slots * blocks
-    present = (arriving < counts[:, None])[(myself - block_ids) % blocks].reshape(-1)
-    order_rank = jnp.cumsum(present.astype(jnp.int32)) - 1
+    present = (arriving < counts[:, None]).reshape(-1)
+    chunk_ids = jnp.arange(blocks * per_peer, dtype=jnp.int32)
+    order_rank = jnp.sum(
+        ((chunk_ids[None, :] < chunk_ids[:, None]) & present[None, :]).astype(jnp.int32), axis=1
+    )
     choose = present[None, :] & (order_rank[None, :] == jnp.arange(pg, dtype=jnp.int32)[:, None])
-    positions = jnp.sum(
-        jnp.where(choose, jnp.arange(blocks * per_peer, dtype=jnp.int32)[None, :], 0), axis=1
-    )
-    own = received[positions]
+    positions = jnp.sum(jnp.where(choose, chunk_ids[None, :], 0), axis=1)
+    own = jnp.stack(
+        [lax.dynamic_index_in_dim(received, positions[i], keepdims=False) for i in range(pg)]
+    )
     gathered = [own]
     for k in range(1, blocks):
         gathered.append(

time: 61.9 us -> 69.3 us (1.12)
  between operations: 0.79 us -> 12.1 us
  local copies, waits for them, and re-layouts: 8.92 us -> 6.79 us
  waiting for transfers between devices: 19.2 us -> 18 us
  other arithmetic: 6.8 us -> 5.96 us
    gather x4 -> x0, local copies, waits for them, and re-layouts: 4.61 us -> none  [the longest x1 2.77 us: local(): sent = kv_cache[by_shift].reshape((blocks, per_peer) + kv_cache.shape[1:])]
    reduce_sum x2 -> x5, other arithmetic: 0.24 us -> 1.84 us  [the longest x1 1.3 us: local(): my_start = jnp.sum((page_owner < myself).astype(jnp.int32))]
    slice x0 -> x2, local copies, waits for them, and re-layouts: none -> 1.32 us  [the longest x1 0.67 us: local(): by_shift[i]]
    select_n x6 -> x2, other arithmetic: 1.98 us -> 0.67 us  [the longest x1 0.66 us: local(): source = (myself - block_ids) % blocks]
    dynamic_slice x0 -> x2, local copies, waits for them, and re-layouts: none -> 1.17 us  [the longest x1 1.14 us: local(): lax.dynamic_index_in_dim(kv_cache, by_shift[i], keepdims=False)]
    another operation x4 -> x2, other arithmetic: 1.21 us -> 0.1 us  [the longest x1 0.07 us: local(): jnp.stack(arrived).reshape((blocks * per_peer,) + kv_cache.shape[1:])]
    ppermute x3, waiting for transfers between devices: 1.02 us -> 0.01 us  [local(): lax.ppermute(own_rows, 'blk', [(i, (i + k) % blocks) for i in range(block...]
  transfers between devices with their start and end apart: 9 -> 9, of which waited for: 6 -> 5; matrix products, arithmetic and copies ran while one was open for 20% -> 15% of each run, Pallas kernels for 21% -> 19%
where the time goes in v16:
time: 69.3 us; the launch traced here: 68.9 us
  Pallas kernels  18.4 us (27%)
  waiting for transfers between devices  18 us (26%)
  between operations  12.1 us (17%)
  starting transfers between devices  7.66 us (11%)
  local copies, waits for them, and re-layouts  6.79 us (10%)
  other arithmetic  5.96 us (9%)
    pallas_call x2, Pallas kernels, prefix_part(): pl.pallas_call(kernel, out_shape=out_shape, cost_estimate=cost, grid=(kv_...  12.9 us
    ppermute x3, waiting for transfers between devices, local(): lax.ppermute(sent[k], 'blk', [(i, (i + k) % blocks) for i in range(blocks)])  12.3 us
    ppermute x3, waiting for transfers between devices, local(): lax.ppermute(own, 'blk', [(i, (i + k) % blocks) for i in range(blocks)])  5.76 us
    pallas_call x1, Pallas kernels, attention(): pl.pallas_call(kernel, out_shape=(jax.ShapeDtypeStruct(q_new.shape, jnp.f...  5.54 us
    ppermute x3, starting transfers between devices, local(): lax.ppermute(own_rows, 'blk', [(i, (i + k) % blocks) for i in range(block...  3.83 us
    ppermute x3, starting transfers between devices, local(): lax.ppermute(sent[k], 'blk', [(i, (i + k) % blocks) for i in range(blocks)])  2.32 us
    unnamed x7, local copies, waits for them, and re-layouts  1.64 us
    ppermute x3, starting transfers between devices, local(): lax.ppermute(own, 'blk', [(i, (i + k) % blocks) for i in range(blocks)])  1.51 us
  transfers between devices with their start and end apart: 9, of which 5 were waited for; matrix products, arithmetic and copies ran while one was open for 15% of the time, Pallas kernels for 19%

profile of v16, /device:TPU:13, one launch (start us, length us, event | category | flops | bytes accessed | tf_op | source)
XLA Modules:
  0.0 68.9 jit_solution(15270851852850759179)
XLA Ops:
  0.0 0.0 copy-start
  0.0 0.9 %copy.19 = bf16[128,2,256]{2,0,1:T(8,128)(2,1)S(1)} copy(bf16[128,2,256]{2,1,0:T(2,128)(2,1)} %param.6) | data formatting | bytes 262144 | tf_op args[1]
  0.9 1.3 %collective-permute-start = (bf16[2,128,256]{2,1,0:T(8,128)(2,1)S(1)}, bf16[2,128,256]{2,1,0:T(8,128)(2,1)S(1)}, u32[]{:S(2)}, u32[]{:S(2)}) collective-permute-start(bf16[2,128,256]{2,1,0:T(8,128)(2,1)S(1)} %bitcast.35), channel_id=1, source_target_pairs={{0,4},{4,8},{8,12},{12,0},{1,5},{5,9},{9,13},{13,1},{2,6},{6,10},{... | collective-permute-start | bytes 393224 | tf_op jit(solution)/shard_map/ppermute | solution.py:203
  2.3 1.1 %collective-permute-start.1 = (bf16[2,128,256]{2,1,0:T(8,128)(2,1)S(1)}, bf16[2,128,256]{2,1,0:T(8,128)(2,1)S(1)}, u32[]{:S(2)}, u32[]{:S(2)}) collective-permute-start(bf16[2,128,256]{2,1,0:T(8,128)(2,1)S(1)} %bitcast.36), channel_id=1, source_target_pairs={{0,8},{4,12},{8,0},{12,4},{1,9},{5,13},{9,1},{13,5},{2,10},{6,14},... | collective-permute-start | bytes 393224 | tf_op jit(solution)/shard_map/ppermute | solution.py:203
  3.4 1.4 %collective-permute-start.2 = (bf16[2,128,256]{2,1,0:T(8,128)(2,1)S(1)}, bf16[2,128,256]{2,1,0:T(8,128)(2,1)S(1)}, u32[]{:S(2)}, u32[]{:S(2)}) collective-permute-start(bf16[2,128,256]{2,1,0:T(8,128)(2,1)S(1)} %bitcast.37), channel_id=1, source_target_pairs={{0,12},{4,0},{8,4},{12,8},{1,13},{5,1},{9,5},{13,9},{2,14},{6,2},{... | collective-permute-start | bytes 393224 | tf_op jit(solution)/shard_map/ppermute | solution.py:203
  4.8 1.3 %fusion.5 = (s32[]{:T(128)}, s32[8]{0:T(128)S(1)}, s32[8]{0:T(128)S(1)}) fusion(s32[]{:T(128)S(6)} %axis_index.15, s32[8]{0:T(128)} %param.8), kind=kLoop, calls=%fused_computation.52 | loop fusion | flops 175 | bytes 104 | tf_op jit(solution)/shard_map/reduce_sum | solution.py:215
  6.1 0.1 convert_reduce_fusion
  6.2 0.7 and_select_fusion.3
  6.9 0.2 select_reduce_fusion
  7.0 0.7 fusion.15
  12.9 0.2 convert_reduce_fusion.3
  13.1 0.1 convert_reduce_fusion.1
  13.2 0.1 fusion.3
  13.3 0.7 fusion.14
  14.0 0.1 fusion.1
  14.0 0.1 reshape.266
  14.1 0.1 broadcast_in_dim.30
  14.2 0.6 fusion.13
  17.4 1.1 %constant_dynamic-slice_fusion.3 = (bf16[1,2,128,256]{3,2,1,0:T(8,128)(2,1)S(1)}, bf16[1,2,128,256]{3,2,1,0:T(8,128)(2,1)S(1)}, bf16[1,2,128,256]{3,2,1,0:T(8,128)(2,1)S(1)}, bf16[1,2,128,256]{3,2,1,0:T(8,128)(2,1)S(1)}) fusion(bf16[32,2,128,256]{3,2,1,0:T(8,128)(2,1)} %param.7, s32[]{:T(128)S(6)} %select_n.110, s32[]{:T(128)S(6)} %select_n.111, ...), kind=kLoop, calls=%fused_computation.46 | loop fusion | bytes 1048592 | tf_op jit(solution)/shard_map/jit(dynamic_index_in_dim)/dynamic_slice | solution.py:221
  22.1 1.3 %gather_fusion = s32[4]{0:T(128)S(1)} fusion(s32[4]{0:T(128)} %param.9, s32[1024]{0:T(1024)S(1)} %pad_clamp_fusion), kind=kCustom, calls=%fused_computation | custom fusion | bytes 48 | tf_op jit(solution)/shard_map/gather | solution.py:205
  23.4 0.1 maximum_bitcast_fusion
  23.5 0.0 collective-permute-done
  23.5 0.0 collective-permute-done.1
  23.5 0.0 collective-permute-done.2
  23.5 0.1 collective-permute-start.4
  23.7 2.2 %collective-permute-start.3 = (bf16[1,2,128,256]{3,2,1,0:T(8,128)(2,1)S(1)}, bf16[1,2,128,256]{3,2,1,0:T(8,128)(2,1)S(1)}, u32[]{:S(2)}, u32[]{:S(2)}) collective-permute-start(bf16[1,2,128,256]{3,2,1,0:T(8,128)(2,1)S(1)} %get-tuple-element.49), channel_id=1, source_target_pairs={{0,4},{4,8},{8,12},{12,0},{1,5},{5,9},{9,13},{13,1},{2,6},{6,10},{... | collective-permute-start | bytes 393224 | tf_op jit(solution)/shard_map/ppermute | solution.py:229
  25.9 0.0 collective-permute-start.5
  25.9 2.6 %collective-permute-done.4 = bf16[1,2,128,256]{3,2,1,0:T(8,128)(2,1)S(1)} collective-permute-done((bf16[1,2,128,256]{3,2,1,0:T(8,128)(2,1)S(1)}, bf16[1,2,128,256]{3,2,1,0:T(8,128)(2,1)S(1)}, u32[]{:S(2)}, u32[]{:S(2)}) %collective-permute-start.4) | collective-permute-done | bytes 131104 | tf_op jit(solution)/shard_map/ppermute | solution.py:229
  28.4 5.8 %collective-permute-done.3 = bf16[1,2,128,256]{3,2,1,0:T(8,128)(2,1)S(1)} collective-permute-done((bf16[1,2,128,256]{3,2,1,0:T(8,128)(2,1)S(1)}, bf16[1,2,128,256]{3,2,1,0:T(8,128)(2,1)S(1)}, u32[]{:S(2)}, u32[]{:S(2)}) %collective-permute-start.3) | collective-permute-done | bytes 131104 | tf_op jit(solution)/shard_map/ppermute | solution.py:229
  34.2 3.9 %collective-permute-done.5 = bf16[1,2,128,256]{3,2,1,0:T(8,128)(2,1)S(1)} collective-permute-done((bf16[1,2,128,256]{3,2,1,0:T(8,128)(2,1)S(1)}, bf16[1,2,128,256]{3,2,1,0:T(8,128)(2,1)S(1)}, u32[]{:S(2)}, u32[]{:S(2)}) %collective-permute-start.5) | collective-permute-done | bytes 131104 | tf_op jit(solution)/shard_map/ppermute | solution.py:229
  38.1 0.1 pad_maximum_fusion
  38.3 0.0 copy-start.1
  38.3 0.1 collective-permute-start.6
  38.3 0.7 iota_add_fusion
  39.0 0.6 slice.67.page_ok_ref
  39.6 0.4 collective-permute-start.7
  40.0 1.0 %collective-permute-start.8 = (bf16[2,2,128,256]{3,2,1,0:T(8,128)(2,1)S(1)}, bf16[2,2,128,256]{3,2,1,0:T(8,128)(2,1)S(1)}, u32[]{:S(2)}, u32[]{:S(2)}) collective-permute-start(bf16[2,2,128,256]{3,2,1,0:T(8,128)(2,1)S(1)} %pad_maximum_fusion.3.page_ref), channel_id=1, source_target_pairs={{0,12},{4,0},{8,4},{12,8},{1,13},{5,1},{9,5},{13,9},{2,14},{6,2},{... | collective-permute-start | bytes 786440 | tf_op jit(solution)/shard_map/ppermute | solution.py:249
  41.0 0.0 copy-done
  41.0 0.6 fusion.6
  42.3 0.9 %pad_maximum_fusion.1.new_ref = bf16[4,2,128,256]{3,2,1,0:T(8,128)(2,1)} fusion(bf16[1,2,128,256]{3,2,1,0:T(8,128)(2,1)S(1)} %bitcast.41, bf16[1,2,128,256]{3,2,1,0:T(8,128)(2,1)S(1)} %bitcast.40, bf16[1,2,128,256]{3,2,1,0:T(8,128)(2,1)S(1)} %bitcast.39, bf16[1,2,128,256]{3,2,1,0:T(8,128)(2,1)S(1)} %bitcast.38), kind=kLoop, calls=%fused_computation.3 | loop fusion | flops 786432 | bytes 1048576 | tf_op jit(solution)/shard_map/stack | solution.py:225
  43.2 0.0 copy-done.1
  43.2 5.5 %shard_map.55 = (f32[128,2048]{1,0:T(8,128)}, f32[2,128,8]{2,1,0:T(8,128)}, f32[2,128,8]{2,1,0:T(8,128)}) custom-call(s32[1]{0:T(128)} %bitcast.18.query_start, bf16[128,2048]{1,0:T(8,128)(2,1)} %q_ref.5, bf16[4,2,128,256]{3,2,1,0:T(8,128)(2,1)} %pad_maximum_fusion.1.new_ref, bf16[2,2,128,256]{3,2,1,0:T(8,128)(2,1)} %copy-done.1, s32[1,512]{1,0:T(1,128)} %bitcast.47, ...), custom_call_target="tpu_custom_call" | custom-call | tf_op jit(solution)/shard_map/pallas_call | solution.py:169
  48.7 0.0 collective-permute-done.6.page_ref
  48.7 0.0 copy-start.2
  48.7 0.7 %copy-done.2 = bf16[2,2,128,256]{3,2,1,0:T(8,128)(2,1)} copy-done((bf16[2,2,128,256]{3,2,1,0:T(8,128)(2,1)}, bf16[2,2,128,256]{3,2,1,0:T(8,128)(2,1)S(1)}, u32[]{:S(2)}) %copy-start.2) | copy-done | bytes 262168
  49.4 7.2 %shard_map.56 = (f32[128,2048]{1,0:T(8,128)}, f32[2,128,8]{2,1,0:T(8,128)}, f32[2,128,8]{2,1,0:T(8,128)}) custom-call(bf16[128,2048]{1,0:T(8,128)(2,1)} %q_ref.5, bf16[2,2,128,256]{3,2,1,0:T(8,128)(2,1)} %copy-done.2, s32[1,256]{1,0:T(1,128)} %get-tuple-element.51.page_ok_ref, f32[128,2048]{1,0:T(8,128)} %get-tuple-element.26.acc_ref, ...), custom_call_target="tpu_custom_call" | custom-call | flops 268435456 | bytes 2883584 | tf_op jit(solution)/shard_map/pallas_call | solution.py:141
  56.7 3.9 %collective-permute-done.7 = bf16[2,2,128,256]{3,2,1,0:T(8,128)(2,1)S(1)} collective-permute-done((bf16[2,2,128,256]{3,2,1,0:T(8,128)(2,1)S(1)}, bf16[2,2,128,256]{3,2,1,0:T(8,128)(2,1)S(1)}, u32[]{:S(2)}, u32[]{:S(2)}) %collective-permute-start.7) | collective-permute-done | bytes 262176 | tf_op jit(solution)/shard_map/ppermute | solution.py:249
  60.6 1.9 %collective-permute-done.8 = bf16[2,2,128,256]{3,2,1,0:T(8,128)(2,1)S(1)} collective-permute-done((bf16[2,2,128,256]{3,2,1,0:T(8,128)(2,1)S(1)}, bf16[2,2,128,256]{3,2,1,0:T(8,128)(2,1)S(1)}, u32[]{:S(2)}, u32[]{:S(2)}) %collective-permute-start.8) | collective-permute-done | bytes 262176 | tf_op jit(solution)/shard_map/ppermute | solution.py:249
  62.4 0.8 %pad_maximum_fusion.2.page_ref = bf16[4,2,128,256]{3,2,1,0:T(8,128)(2,1)} fusion(bf16[2,2,128,256]{3,2,1,0:T(8,128)(2,1)S(1)} %collective-permute-done.8, bf16[2,2,128,256]{3,2,1,0:T(8,128)(2,1)S(1)} %collective-permute-done.7), kind=kLoop, calls=%fused_computation.4 | loop fusion | flops 262144 | bytes 1048576 | tf_op jit(solution)/shard_map/concatenate | solution.py:278
  63.3 5.6 %shard_map.57 = bf16[128,2048]{1,0:T(8,128)(2,1)} custom-call(bf16[128,2048]{1,0:T(8,128)(2,1)} %q_ref.5, bf16[4,2,128,256]{3,2,1,0:T(8,128)(2,1)} %pad_maximum_fusion.2.page_ref, s32[1,512]{1,0:T(1,128)} %slice.67.page_ok_ref, f32[128,2048]{1,0:T(8,128)} %get-tuple-element.34.acc_ref, f32[2,128,8]{2,1,0:T(8,128)} %get-tuple-element.35.top_ref, ...), custom_call_target="tpu_custom_call" | custom-call | flops 536870912 | bytes 3145728 | tf_op jit(solution)/shard_map/pallas_call | solution.py:141
  (10 shorter events, 0.1 us)
Async XLA Ops:
  0.0 41.0 %copy-start = (s32[4]{0:T(128)S(1)}, s32[4]{0:T(128)}, u32[]{:S(2)}) copy-start(s32[4]{0:T(128)} %param.9) | copy-start | bytes 52
  0.9 22.5 %collective-permute-start = (bf16[2,128,256]{2,1,0:T(8,128)(2,1)S(1)}, bf16[2,128,256]{2,1,0:T(8,128)(2,1)S(1)}, u32[]{:S(2)}, u32[]{:S(2)}) collective-permute-start(bf16[2,128,256]{2,1,0:T(8,128)(2,1)S(1)} %bitcast.35), channel_id=1, source_target_pairs={{0,4},{4,8},{8,12},{12,0},{1,5},{5,9},{9,13},{13,1},{2,6},{6,10},{... | collective-permute-start | bytes 393224 | tf_op jit(solution)/shard_map/ppermute | solution.py:203
  2.3 21.2 %collective-permute-start.1 = (bf16[2,128,256]{2,1,0:T(8,128)(2,1)S(1)}, bf16[2,128,256]{2,1,0:T(8,128)(2,1)S(1)}, u32[]{:S(2)}, u32[]{:S(2)}) collective-permute-start(bf16[2,128,256]{2,1,0:T(8,128)(2,1)S(1)} %bitcast.36), channel_id=1, source_target_pairs={{0,8},{4,12},{8,0},{12,4},{1,9},{5,13},{9,1},{13,5},{2,10},{6,14},... | collective-permute-start | bytes 393224 | tf_op jit(solution)/shard_map/ppermute | solution.py:203
  3.4 20.1 %collective-permute-start.2 = (bf16[2,128,256]{2,1,0:T(8,128)(2,1)S(1)}, bf16[2,128,256]{2,1,0:T(8,128)(2,1)S(1)}, u32[]{:S(2)}, u32[]{:S(2)}) collective-permute-start(bf16[2,128,256]{2,1,0:T(8,128)(2,1)S(1)} %bitcast.37), channel_id=1, source_target_pairs={{0,12},{4,0},{8,4},{12,8},{1,13},{5,1},{9,5},{13,9},{2,14},{6,2},{... | collective-permute-start | bytes 393224 | tf_op jit(solution)/shard_map/ppermute | solution.py:203
  23.5 4.9 %collective-permute-start.4 = (bf16[1,2,128,256]{3,2,1,0:T(8,128)(2,1)S(1)}, bf16[1,2,128,256]{3,2,1,0:T(8,128)(2,1)S(1)}, u32[]{:S(2)}, u32[]{:S(2)}) collective-permute-start(bf16[1,2,128,256]{3,2,1,0:T(8,128)(2,1)S(1)} %get-tuple-element.48), channel_id=1, source_target_pairs={{0,8},{4,12},{8,0},{12,4},{1,9},{5,13},{9,1},{13,5},{2,10},{6,14},... | collective-permute-start | bytes 393224 | tf_op jit(solution)/shard_map/ppermute | solution.py:229
  23.7 10.5 %collective-permute-start.3 = (bf16[1,2,128,256]{3,2,1,0:T(8,128)(2,1)S(1)}, bf16[1,2,128,256]{3,2,1,0:T(8,128)(2,1)S(1)}, u32[]{:S(2)}, u32[]{:S(2)}) collective-permute-start(bf16[1,2,128,256]{3,2,1,0:T(8,128)(2,1)S(1)} %get-tuple-element.49), channel_id=1, source_target_pairs={{0,4},{4,8},{8,12},{12,0},{1,5},{5,9},{9,13},{13,1},{2,6},{6,10},{... | collective-permute-start | bytes 393224 | tf_op jit(solution)/shard_map/ppermute | solution.py:229
  25.9 12.3 %collective-permute-start.5 = (bf16[1,2,128,256]{3,2,1,0:T(8,128)(2,1)S(1)}, bf16[1,2,128,256]{3,2,1,0:T(8,128)(2,1)S(1)}, u32[]{:S(2)}, u32[]{:S(2)}) collective-permute-start(bf16[1,2,128,256]{3,2,1,0:T(8,128)(2,1)S(1)} %slice_bitcast_fusion.2), channel_id=1, source_target_pairs={{0,12},{4,0},{8,4},{12,8},{1,13},{5,1},{9,5},{13,9},{2,14},{6,2},{... | collective-permute-start | bytes 393224 | tf_op jit(solution)/shard_map/ppermute | solution.py:229
  38.3 4.9 %copy-start.1 = (bf16[2,2,128,256]{3,2,1,0:T(8,128)(2,1)}, bf16[2,2,128,256]{3,2,1,0:T(8,128)(2,1)S(1)}, u32[]{:S(2)}) copy-start(bf16[2,2,128,256]{3,2,1,0:T(8,128)(2,1)S(1)} %pad_maximum_fusion.3.page_ref) | copy-start | bytes 786436
  38.3 10.5 %collective-permute-start.6 = (bf16[2,2,128,256]{3,2,1,0:T(8,128)(2,1)S(1)}, bf16[2,2,128,256]{3,2,1,0:T(8,128)(2,1)S(1)}, u32[]{:S(2)}, u32[]{:S(2)}) collective-permute-start(bf16[2,2,128,256]{3,2,1,0:T(8,128)(2,1)S(1)} %pad_maximum_fusion.3.page_ref), channel_id=1, source_target_pairs={{0,4},{4,8},{8,12},{12,0},{1,5},{5,9},{9,13},{13,1},{2,6},{6,10},{... | collective-permute-start | bytes 786440 | tf_op jit(solution)/shard_map/ppermute | solution.py:249
  39.6 21.0 %collective-permute-start.7 = (bf16[2,2,128,256]{3,2,1,0:T(8,128)(2,1)S(1)}, bf16[2,2,128,256]{3,2,1,0:T(8,128)(2,1)S(1)}, u32[]{:S(2)}, u32[]{:S(2)}) collective-permute-start(bf16[2,2,128,256]{3,2,1,0:T(8,128)(2,1)S(1)} %pad_maximum_fusion.3.page_ref), channel_id=1, source_target_pairs={{0,8},{4,12},{8,0},{12,4},{1,9},{5,13},{9,1},{13,5},{2,10},{6,14},... | collective-permute-start | bytes 786440 | tf_op jit(solution)/shard_map/ppermute | solution.py:249
  40.0 22.4 %collective-permute-start.8 = (bf16[2,2,128,256]{3,2,1,0:T(8,128)(2,1)S(1)}, bf16[2,2,128,256]{3,2,1,0:T(8,128)(2,1)S(1)}, u32[]{:S(2)}, u32[]{:S(2)}) collective-permute-start(bf16[2,2,128,256]{3,2,1,0:T(8,128)(2,1)S(1)} %pad_maximum_fusion.3.page_ref), channel_id=1, source_target_pairs={{0,12},{4,0},{8,4},{12,8},{1,13},{5,1},{9,5},{13,9},{2,14},{6,2},{... | collective-permute-start | bytes 786440 | tf_op jit(solution)/shard_map/ppermute | solution.py:249
  48.7 0.7 %copy-start.2 = (bf16[2,2,128,256]{3,2,1,0:T(8,128)(2,1)}, bf16[2,2,128,256]{3,2,1,0:T(8,128)(2,1)S(1)}, u32[]{:S(2)}) copy-start(bf16[2,2,128,256]{3,2,1,0:T(8,128)(2,1)S(1)} %collective-permute-done.6.page_ref) | copy-start | bytes 786436

commit v17 on v15

--- a/solution.py
+++ b/solution.py
@@ -79,7 +79,7 @@
     page_visible = page_ok_ref[...] > 0
     dims = (((1,), (1,)), ((), ()))
     pv = (((1,), (0,)), ((), ()))
-    stack = 2 if group_size % 2 == 0 else 1
+    stack = math.gcd(group_size, 4)
     for c in range(group_size // stack):
         heads = range(c * stack, (c + 1) * stack)
         queries = jnp.concatenate(

time: 61.9 us -> 63.1 us (1.019)
  Pallas kernels: 18.4 us -> 19.1 us
    pallas_call x2, Pallas kernels: 12.9 us -> 13.6 us  [prefix_part(): pl.pallas_call(kernel, out_shape=out_shape, cost_estimate=cost, grid=(kv_...]
  transfers between devices with their start and end apart: 9 -> 9, of which waited for: 6 -> 6; matrix products, arithmetic and copies ran while one was open for 20% -> 20% of each run, Pallas kernels for 21% -> 20%
where the time goes in v17:
time: 63.1 us; the launch traced here: 62.8 us
  waiting for transfers between devices  19.7 us (31%)
  Pallas kernels  19.1 us (30%)
  local copies, waits for them, and re-layouts  8.92 us (14%)
  starting transfers between devices  7.53 us (12%)
  other arithmetic  6.8 us (11%)
  between operations  0.79 us (1%)
    pallas_call x2, Pallas kernels, prefix_part(): pl.pallas_call(kernel, out_shape=out_shape, cost_estimate=cost, grid=(kv_...  13.6 us
    ppermute x3, waiting for transfers between devices, local(): lax.ppermute(sent[k], 'blk', [(i, (i + k) % blocks) for i in range(blocks)])  12.4 us
    ppermute x3, waiting for transfers between devices, local(): lax.ppermute(own, 'blk', [(i, (i + k) % blocks) for i in range(blocks)])  6.23 us
    pallas_call x1, Pallas kernels, attention(): pl.pallas_call(kernel, out_shape=(jax.ShapeDtypeStruct(q_new.shape, jnp.f...  5.55 us
    ppermute x3, starting transfers between devices, local(): lax.ppermute(own_rows, 'blk', [(i, (i + k) % blocks) for i in range(block...  3.83 us
    gather x1, local copies, waits for them, and re-layouts, local(): sent = kv_cache[by_shift].reshape((blocks, per_peer) + kv_cache.shape[1:])  2.77 us
    ppermute x3, starting transfers between devices, local(): lax.ppermute(sent[k], 'blk', [(i, (i + k) % blocks) for i in range(blocks)])  2.2 us
    unnamed x7, local copies, waits for them, and re-layouts  1.64 us
  transfers between devices with their start and end apart: 9, of which 6 were waited for; matrix products, arithmetic and copies ran while one was open for 20% of the time, Pallas kernels for 20%

profile of v17, /device:TPU:13, one launch (start us, length us, event | category | flops | bytes accessed | tf_op | source)
XLA Modules:
  0.0 62.8 jit_solution(14943016378025382765)
XLA Ops:
  0.0 0.0 copy-start
  0.0 0.9 %copy.19 = bf16[128,2,256]{2,0,1:T(8,128)(2,1)S(1)} copy(bf16[128,2,256]{2,1,0:T(2,128)(2,1)} %param.6) | data formatting | bytes 262144 | tf_op args[1]
  0.9 1.3 %collective-permute-start = (bf16[2,128,256]{2,1,0:T(8,128)(2,1)S(1)}, bf16[2,128,256]{2,1,0:T(8,128)(2,1)S(1)}, u32[]{:S(2)}, u32[]{:S(2)}) collective-permute-start(bf16[2,128,256]{2,1,0:T(8,128)(2,1)S(1)} %bitcast.53), channel_id=1, source_target_pairs={{0,4},{4,8},{8,12},{12,0},{1,5},{5,9},{9,13},{13,1},{2,6},{6,10},{... | collective-permute-start | bytes 393224 | tf_op jit(solution)/shard_map/ppermute | solution.py:203
  2.3 1.1 %collective-permute-start.1 = (bf16[2,128,256]{2,1,0:T(8,128)(2,1)S(1)}, bf16[2,128,256]{2,1,0:T(8,128)(2,1)S(1)}, u32[]{:S(2)}, u32[]{:S(2)}) collective-permute-start(bf16[2,128,256]{2,1,0:T(8,128)(2,1)S(1)} %bitcast.54), channel_id=1, source_target_pairs={{0,8},{4,12},{8,0},{12,4},{1,9},{5,13},{9,1},{13,5},{2,10},{6,14},... | collective-permute-start | bytes 393224 | tf_op jit(solution)/shard_map/ppermute | solution.py:203
  3.4 1.4 %collective-permute-start.2 = (bf16[2,128,256]{2,1,0:T(8,128)(2,1)S(1)}, bf16[2,128,256]{2,1,0:T(8,128)(2,1)S(1)}, u32[]{:S(2)}, u32[]{:S(2)}) collective-permute-start(bf16[2,128,256]{2,1,0:T(8,128)(2,1)S(1)} %bitcast.55), channel_id=1, source_target_pairs={{0,12},{4,0},{8,4},{12,8},{1,13},{5,1},{9,5},{13,9},{2,14},{6,2},{... | collective-permute-start | bytes 393224 | tf_op jit(solution)/shard_map/ppermute | solution.py:203
  4.8 0.7 %and_select_fusion.5 = s32[8]{0:T(128)S(1)} fusion(s32[8]{0:T(128)} %param.8), kind=kLoop, calls=%fused_computation.42 | loop fusion | flops 88 | bytes 64 | tf_op jit(solution)/shard_map/jit(remainder)/select_n | solution.py:210
  5.4 0.7 %convert_bitcast_fusion.1 = (s32[8,1]{0,1:T(1,128)S(1)}, pred[8]{0:T(512)(128)(4,1)S(1)}, s32[8]{0:T(128)S(1)}) fusion(s32[]{:T(128)S(6)} %axis_index.15, s32[8]{0:T(128)} %param.8), kind=kLoop, calls=%fused_computation.64 | loop fusion | flops 136 | bytes 108 | tf_op jit(solution)/shard_map/convert
  6.1 0.1 convert_reduce_fusion
  6.2 0.2 reduce-window.22
  6.4 0.6 %and_select_fusion = (s32[4]{0:T(128)S(1)}, s32[]{:T(128)}) fusion(s32[]{:T(128)S(6)} %axis_index.15, s32[4]{0:T(128)S(1)} %convert_reduce_fusion, s32[4,1]{0,1:T(1,128)S(1)} %reduce-window.22), kind=kLoop, calls=%fused_computation.36 | loop fusion | flops 63 | bytes 56 | tf_op jit(solution)/shard_map/jit(remainder)/select_n | solution.py:230
  7.1 0.7 %and_select_fusion.6 = s32[4]{0:T(128)S(1)} fusion(s32[]{:T(128)} %get-tuple-element.46), kind=kLoop, calls=%fused_computation.43 | loop fusion | flops 48 | bytes 20 | tf_op jit(solution)/shard_map/jit(remainder)/select_n | solution.py:216
  7.7 0.2 reduce-window.21
  7.9 0.2 select_reduce_fusion
  8.1 0.6 %gather_fusion = s32[4]{0:T(128)S(1)} fusion(s32[4]{0:T(128)S(1)} %select_reduce_fusion, s32[1024]{0:T(1024)S(1)} %pad_clamp_fusion.3), kind=kCustom, calls=%fused_computation | custom fusion | bytes 48 | tf_op jit(solution)/shard_map/gather | solution.py:219
  8.8 0.6 %gather_fusion.2 = pred[4]{0:T(512)(128)(4,1)S(1)} fusion(pred[4]{0:T(512)(128)(4,1)S(1)} %compare_bitcast_fusion, s32[1024]{0:T(1024)S(1)} %pad_clamp_fusion.1), kind=kCustom, calls=%fused_computation.2 | custom fusion | bytes 24 | tf_op jit(solution)/shard_map/gather | solution.py:230
  9.4 0.2 reduce-window.23
  9.6 0.1 fusion.1
  9.7 0.1 fusion
  9.8 0.1 reshape.427
  9.9 0.1 broadcast_in_dim.38
  10.0 0.6 fusion.14
  10.6 1.3 %gather_fusion.4 = s32[4]{0:T(128)S(1)} fusion(s32[4]{0:T(128)} %param.9, s32[1024]{0:T(1024)S(1)} %pad_clamp_fusion.1), kind=kCustom, calls=%fused_computation.4 | custom fusion | bytes 48 | tf_op jit(solution)/shard_map/gather | solution.py:205
  11.9 2.8 %gather_fusion.1 = bf16[4,2,128,256]{3,2,1,0:T(8,128)(2,1)S(1)} fusion(bf16[32,2,128,256]{3,2,1,0:T(8,128)(2,1)} %param.7, s32[1024]{0:T(1024)S(1)} %pad_clamp_fusion.2), kind=kCustom, calls=%fused_computation.1 | custom fusion | bytes 1048592 | tf_op jit(solution)/shard_map/gather | solution.py:220
  14.6 0.0 collective-permute-done
  14.7 0.0 collective-permute-done.1
  14.7 1.0 %collective-permute-done.2 = bf16[2,128,256]{2,1,0:T(8,128)(2,1)S(1)} collective-permute-done((bf16[2,128,256]{2,1,0:T(8,128)(2,1)S(1)}, bf16[2,128,256]{2,1,0:T(8,128)(2,1)S(1)}, u32[]{:S(2)}, u32[]{:S(2)}) %collective-permute-start.2) | collective-permute-done | bytes 131104 | tf_op jit(solution)/shard_map/ppermute | solution.py:203
  15.7 0.1 collective-permute-start.3
  15.8 2.1 %collective-permute-start.4 = (bf16[1,2,128,256]{3,2,1,0:T(8,128)(2,1)S(1)}, bf16[1,2,128,256]{3,2,1,0:T(8,128)(2,1)S(1)}, u32[]{:S(2)}, u32[]{:S(2)}) collective-permute-start(bf16[1,2,128,256]{3,2,1,0:T(8,128)(2,1)S(1)} %get-tuple-element.41), channel_id=1, source_target_pairs={{0,8},{4,12},{8,0},{12,4},{1,9},{5,13},{9,1},{13,5},{2,10},{6,14},... | collective-permute-start | bytes 393224 | tf_op jit(solution)/shard_map/ppermute | solution.py:226
  17.9 0.0 collective-permute-start.5
  18.0 2.4 %collective-permute-done.3 = bf16[1,2,128,256]{3,2,1,0:T(8,128)(2,1)S(1)} collective-permute-done((bf16[1,2,128,256]{3,2,1,0:T(8,128)(2,1)S(1)}, bf16[1,2,128,256]{3,2,1,0:T(8,128)(2,1)S(1)}, u32[]{:S(2)}, u32[]{:S(2)}) %collective-permute-start.3) | collective-permute-done | bytes 131104 | tf_op jit(solution)/shard_map/ppermute | solution.py:226
  20.3 6.1 %collective-permute-done.4 = bf16[1,2,128,256]{3,2,1,0:T(8,128)(2,1)S(1)} collective-permute-done((bf16[1,2,128,256]{3,2,1,0:T(8,128)(2,1)S(1)}, bf16[1,2,128,256]{3,2,1,0:T(8,128)(2,1)S(1)}, u32[]{:S(2)}, u32[]{:S(2)}) %collective-permute-start.4) | collective-permute-done | bytes 131104 | tf_op jit(solution)/shard_map/ppermute | solution.py:226
  26.4 3.9 %collective-permute-done.5 = bf16[1,2,128,256]{3,2,1,0:T(8,128)(2,1)S(1)} collective-permute-done((bf16[1,2,128,256]{3,2,1,0:T(8,128)(2,1)S(1)}, bf16[1,2,128,256]{3,2,1,0:T(8,128)(2,1)S(1)}, u32[]{:S(2)}, u32[]{:S(2)}) %collective-permute-start.5) | collective-permute-done | bytes 131104 | tf_op jit(solution)/shard_map/ppermute | solution.py:226
  30.4 0.1 maximum_bitcast_fusion
  30.4 0.6 gather_fusion.3
  31.0 0.0 copy-start.1
  31.0 0.1 collective-permute-start.6
  31.1 0.7 %iota_add_fusion = s32[4,128]{1,0:T(4,128)} fusion(s32[4]{0:T(128)S(1)} %broadcast_multiply_fusion), kind=kLoop, calls=%fused_computation.30 | loop fusion | flops 512 | bytes 2064 | tf_op jit(solution)/shard_map/add | solution.py:248
  31.7 0.6 slice.43.page_ok_ref
  32.3 0.4 collective-permute-start.7
  32.8 1.0 %collective-permute-start.8 = (bf16[2,2,128,256]{3,2,1,0:T(8,128)(2,1)S(1)}, bf16[2,2,128,256]{3,2,1,0:T(8,128)(2,1)S(1)}, u32[]{:S(2)}, u32[]{:S(2)}) collective-permute-start(bf16[2,2,128,256]{3,2,1,0:T(8,128)(2,1)S(1)} %gather_fusion.3), channel_id=1, source_target_pairs={{0,12},{4,0},{8,4},{12,8},{1,13},{5,1},{9,5},{13,9},{2,14},{6,2},{... | collective-permute-start | bytes 786440 | tf_op jit(solution)/shard_map/ppermute | solution.py:240
  33.8 0.0 copy-done
  33.8 0.6 %fusion.3 = s32[]{:T(128)} fusion(s32[4]{0:T(128)S(1)} %copy-done, s32[]{:T(128)S(6)} %axis_index.15), kind=kLoop, calls=%fused_computation.52 | loop fusion | flops 11 | bytes 24 | tf_op jit(solution)/shard_map/reduce_sum | solution.py:197
  35.1 0.9 %pad_maximum_fusion.new_ref = bf16[4,2,128,256]{3,2,1,0:T(8,128)(2,1)} fusion(bf16[1,2,128,256]{3,2,1,0:T(8,128)(2,1)S(1)} %bitcast.59, bf16[1,2,128,256]{3,2,1,0:T(8,128)(2,1)S(1)} %bitcast.58, bf16[1,2,128,256]{3,2,1,0:T(8,128)(2,1)S(1)} %bitcast.57, bf16[1,2,128,256]{3,2,1,0:T(8,128)(2,1)S(1)} %bitcast.56), kind=kLoop, calls=%fused_computation.6 | loop fusion | flops 786432 | bytes 1048576 | tf_op jit(solution)/shard_map/stack | solution.py:222
  35.9 0.0 copy-done.1
  35.9 5.5 %shard_map.55 = (f32[128,2048]{1,0:T(8,128)}, f32[2,128,8]{2,1,0:T(8,128)}, f32[2,128,8]{2,1,0:T(8,128)}) custom-call(s32[1]{0:T(128)} %bitcast.24.query_start, bf16[128,2048]{1,0:T(8,128)(2,1)} %q_ref.5, bf16[4,2,128,256]{3,2,1,0:T(8,128)(2,1)} %pad_maximum_fusion.new_ref, bf16[2,2,128,256]{3,2,1,0:T(8,128)(2,1)} %copy-done.1, s32[1,512]{1,0:T(1,128)} %bitcast.65, ...), custom_call_target="tpu_custom_call" | custom-call | tf_op jit(solution)/shard_map/pallas_call | solution.py:169
  41.5 0.0 collective-permute-done.6.page_ref
  41.5 0.0 copy-start.2
  41.5 0.7 %copy-done.2 = bf16[2,2,128,256]{3,2,1,0:T(8,128)(2,1)} copy-done((bf16[2,2,128,256]{3,2,1,0:T(8,128)(2,1)}, bf16[2,2,128,256]{3,2,1,0:T(8,128)(2,1)S(1)}, u32[]{:S(2)}) %copy-start.2) | copy-done | bytes 262168
  42.2 6.8 %shard_map.56 = (f32[128,2048]{1,0:T(8,128)}, f32[2,128,8]{2,1,0:T(8,128)}, f32[2,128,8]{2,1,0:T(8,128)}) custom-call(bf16[128,2048]{1,0:T(8,128)(2,1)} %q_ref.5, bf16[2,2,128,256]{3,2,1,0:T(8,128)(2,1)} %copy-done.2, s32[1,256]{1,0:T(1,128)} %get-tuple-element.44.page_ok_ref, f32[128,2048]{1,0:T(8,128)} %get-tuple-element.26.acc_ref, ...), custom_call_target="tpu_custom_call" | custom-call | flops 268435456 | bytes 2883584 | tf_op jit(solution)/shard_map/pallas_call | solution.py:141
  49.0 4.5 %collective-permute-done.7 = bf16[2,2,128,256]{3,2,1,0:T(8,128)(2,1)S(1)} collective-permute-done((bf16[2,2,128,256]{3,2,1,0:T(8,128)(2,1)S(1)}, bf16[2,2,128,256]{3,2,1,0:T(8,128)(2,1)S(1)}, u32[]{:S(2)}, u32[]{:S(2)}) %collective-permute-start.7) | collective-permute-done | bytes 262176 | tf_op jit(solution)/shard_map/ppermute | solution.py:240
  53.4 1.8 %collective-permute-done.8 = bf16[2,2,128,256]{3,2,1,0:T(8,128)(2,1)S(1)} collective-permute-done((bf16[2,2,128,256]{3,2,1,0:T(8,128)(2,1)S(1)}, bf16[2,2,128,256]{3,2,1,0:T(8,128)(2,1)S(1)}, u32[]{:S(2)}, u32[]{:S(2)}) %collective-permute-start.8) | collective-permute-done | bytes 262176 | tf_op jit(solution)/shard_map/ppermute | solution.py:240
  55.2 0.8 %pad_maximum_fusion.1.page_ref = bf16[4,2,128,256]{3,2,1,0:T(8,128)(2,1)} fusion(bf16[2,2,128,256]{3,2,1,0:T(8,128)(2,1)S(1)} %collective-permute-done.8, bf16[2,2,128,256]{3,2,1,0:T(8,128)(2,1)S(1)} %collective-permute-done.7), kind=kLoop, calls=%fused_computation.7 | loop fusion | flops 262144 | bytes 1048576 | tf_op jit(solution)/shard_map/concatenate | solution.py:269
  56.0 6.8 %shard_map.57 = bf16[128,2048]{1,0:T(8,128)(2,1)} custom-call(bf16[128,2048]{1,0:T(8,128)(2,1)} %q_ref.5, bf16[4,2,128,256]{3,2,1,0:T(8,128)(2,1)} %pad_maximum_fusion.1.page_ref, s32[1,512]{1,0:T(1,128)} %slice.43.page_ok_ref, f32[128,2048]{1,0:T(8,128)} %get-tuple-element.34.acc_ref, f32[2,128,8]{2,1,0:T(8,128)} %get-tuple-element.35.top_ref, ...), custom_call_target="tpu_custom_call" | custom-call | flops 536870912 | bytes 3145728 | tf_op jit(solution)/shard_map/pallas_call | solution.py:141
  (15 shorter events, 0.1 us)
Async XLA Ops:
  0.0 33.8 %copy-start = (s32[4]{0:T(128)S(1)}, s32[4]{0:T(128)}, u32[]{:S(2)}) copy-start(s32[4]{0:T(128)} %param.9) | copy-start | bytes 52
  0.9 13.7 %collective-permute-start = (bf16[2,128,256]{2,1,0:T(8,128)(2,1)S(1)}, bf16[2,128,256]{2,1,0:T(8,128)(2,1)S(1)}, u32[]{:S(2)}, u32[]{:S(2)}) collective-permute-start(bf16[2,128,256]{2,1,0:T(8,128)(2,1)S(1)} %bitcast.53), channel_id=1, source_target_pairs={{0,4},{4,8},{8,12},{12,0},{1,5},{5,9},{9,13},{13,1},{2,6},{6,10},{... | collective-permute-start | bytes 393224 | tf_op jit(solution)/shard_map/ppermute | solution.py:203
  2.3 12.4 %collective-permute-start.1 = (bf16[2,128,256]{2,1,0:T(8,128)(2,1)S(1)}, bf16[2,128,256]{2,1,0:T(8,128)(2,1)S(1)}, u32[]{:S(2)}, u32[]{:S(2)}) collective-permute-start(bf16[2,128,256]{2,1,0:T(8,128)(2,1)S(1)} %bitcast.54), channel_id=1, source_target_pairs={{0,8},{4,12},{8,0},{12,4},{1,9},{5,13},{9,1},{13,5},{2,10},{6,14},... | collective-permute-start | bytes 393224 | tf_op jit(solution)/shard_map/ppermute | solution.py:203
  3.4 12.3 %collective-permute-start.2 = (bf16[2,128,256]{2,1,0:T(8,128)(2,1)S(1)}, bf16[2,128,256]{2,1,0:T(8,128)(2,1)S(1)}, u32[]{:S(2)}, u32[]{:S(2)}) collective-permute-start(bf16[2,128,256]{2,1,0:T(8,128)(2,1)S(1)} %bitcast.55), channel_id=1, source_target_pairs={{0,12},{4,0},{8,4},{12,8},{1,13},{5,1},{9,5},{13,9},{2,14},{6,2},{... | collective-permute-start | bytes 393224 | tf_op jit(solution)/shard_map/ppermute | solution.py:203
  15.7 4.6 %collective-permute-start.3 = (bf16[1,2,128,256]{3,2,1,0:T(8,128)(2,1)S(1)}, bf16[1,2,128,256]{3,2,1,0:T(8,128)(2,1)S(1)}, u32[]{:S(2)}, u32[]{:S(2)}) collective-permute-start(bf16[1,2,128,256]{3,2,1,0:T(8,128)(2,1)S(1)} %get-tuple-element.42), channel_id=1, source_target_pairs={{0,4},{4,8},{8,12},{12,0},{1,5},{5,9},{9,13},{13,1},{2,6},{6,10},{... | collective-permute-start | bytes 393224 | tf_op jit(solution)/shard_map/ppermute | solution.py:226
  15.8 10.6 %collective-permute-start.4 = (bf16[1,2,128,256]{3,2,1,0:T(8,128)(2,1)S(1)}, bf16[1,2,128,256]{3,2,1,0:T(8,128)(2,1)S(1)}, u32[]{:S(2)}, u32[]{:S(2)}) collective-permute-start(bf16[1,2,128,256]{3,2,1,0:T(8,128)(2,1)S(1)} %get-tuple-element.41), channel_id=1, source_target_pairs={{0,8},{4,12},{8,0},{12,4},{1,9},{5,13},{9,1},{13,5},{2,10},{6,14},... | collective-permute-start | bytes 393224 | tf_op jit(solution)/shard_map/ppermute | solution.py:226
  17.9 12.4 %collective-permute-start.5 = (bf16[1,2,128,256]{3,2,1,0:T(8,128)(2,1)S(1)}, bf16[1,2,128,256]{3,2,1,0:T(8,128)(2,1)S(1)}, u32[]{:S(2)}, u32[]{:S(2)}) collective-permute-start(bf16[1,2,128,256]{3,2,1,0:T(8,128)(2,1)S(1)} %slice_bitcast_fusion.2), channel_id=1, source_target_pairs={{0,12},{4,0},{8,4},{12,8},{1,13},{5,1},{9,5},{13,9},{2,14},{6,2},{... | collective-permute-start | bytes 393224 | tf_op jit(solution)/shard_map/ppermute | solution.py:226
  31.0 4.9 %copy-start.1 = (bf16[2,2,128,256]{3,2,1,0:T(8,128)(2,1)}, bf16[2,2,128,256]{3,2,1,0:T(8,128)(2,1)S(1)}, u32[]{:S(2)}) copy-start(bf16[2,2,128,256]{3,2,1,0:T(8,128)(2,1)S(1)} %gather_fusion.3) | copy-start | bytes 786436
  31.0 10.5 %collective-permute-start.6 = (bf16[2,2,128,256]{3,2,1,0:T(8,128)(2,1)S(1)}, bf16[2,2,128,256]{3,2,1,0:T(8,128)(2,1)S(1)}, u32[]{:S(2)}, u32[]{:S(2)}) collective-permute-start(bf16[2,2,128,256]{3,2,1,0:T(8,128)(2,1)S(1)} %gather_fusion.3), channel_id=1, source_target_pairs={{0,4},{4,8},{8,12},{12,0},{1,5},{5,9},{9,13},{13,1},{2,6},{6,10},{... | collective-permute-start | bytes 786440 | tf_op jit(solution)/shard_map/ppermute | solution.py:240
  32.3 21.1 %collective-permute-start.7 = (bf16[2,2,128,256]{3,2,1,0:T(8,128)(2,1)S(1)}, bf16[2,2,128,256]{3,2,1,0:T(8,128)(2,1)S(1)}, u32[]{:S(2)}, u32[]{:S(2)}) collective-permute-start(bf16[2,2,128,256]{3,2,1,0:T(8,128)(2,1)S(1)} %gather_fusion.3), channel_id=1, source_target_pairs={{0,8},{4,12},{8,0},{12,4},{1,9},{5,13},{9,1},{13,5},{2,10},{6,14},... | collective-permute-start | bytes 786440 | tf_op jit(solution)/shard_map/ppermute | solution.py:240
  32.8 22.4 %collective-permute-start.8 = (bf16[2,2,128,256]{3,2,1,0:T(8,128)(2,1)S(1)}, bf16[2,2,128,256]{3,2,1,0:T(8,128)(2,1)S(1)}, u32[]{:S(2)}, u32[]{:S(2)}) collective-permute-start(bf16[2,2,128,256]{3,2,1,0:T(8,128)(2,1)S(1)} %gather_fusion.3), channel_id=1, source_target_pairs={{0,12},{4,0},{8,4},{12,8},{1,13},{5,1},{9,5},{13,9},{2,14},{6,2},{... | collective-permute-start | bytes 786440 | tf_op jit(solution)/shard_map/ppermute | solution.py:240
  41.5 0.7 %copy-start.2 = (bf16[2,2,128,256]{3,2,1,0:T(8,128)(2,1)}, bf16[2,2,128,256]{3,2,1,0:T(8,128)(2,1)S(1)}, u32[]{:S(2)}) copy-start(bf16[2,2,128,256]{3,2,1,0:T(8,128)(2,1)S(1)} %collective-permute-done.6.page_ref) | copy-start | bytes 786436

commit v18 on v15

--- a/solution.py
+++ b/solution.py
@@ -217,7 +217,11 @@
     picked = owned[None, None, :] & (page_rank[None, None, :] == wanted[..., None])
     chosen = jnp.sum(jnp.where(picked, local_slot[None, None, :], 0), axis=2).reshape(-1)
     by_shift = chosen.reshape(blocks, per_peer)[(myself + block_ids) % blocks].reshape(-1)
-    sent = kv_cache[by_shift].reshape((blocks, per_peer) + kv_cache.shape[1:])
+    sent = [
+        lax.dynamic_slice_in_dim(kv_cache, by_shift[k * per_peer], per_peer)
+        if per_peer == 1 else kv_cache[by_shift[k * per_peer : (k + 1) * per_peer]]
+        for k in range(blocks)
+    ]
     sent, new_all = lax.optimization_barrier((sent, new_all))
     new_all = jnp.stack(new_all)
     arrived = [sent[0]]

time: 61.9 us -> 67.7 us (1.094)
  the two profiles are of different devices: /device:TPU:13 before, /device:TPU:11 now
where the time goes in v18:
time: 67.7 us; the launch traced here: 67.4 us
  Pallas kernels  18.4 us (27%)
  waiting for transfers between devices  17.2 us (25%)
  starting transfers between devices  8.55 us (13%)
  between operations  8.49 us (13%)
  local copies, waits for them, and re-layouts  8.03 us (12%)
  other arithmetic  6.79 us (10%)
    pallas_call x2, Pallas kernels, prefix_part(): pl.pallas_call(kernel, out_shape=out_shape, cost_estimate=cost, grid=(kv_...  12.9 us
    ppermute x3, waiting for transfers between devices, local(): lax.ppermute(sent[k], 'blk', [(i, (i + k) % blocks) for i in range(blocks)])  11.6 us
    ppermute x3, waiting for transfers between devices, local(): lax.ppermute(own, 'blk', [(i, (i + k) % blocks) for i in range(blocks)])  5.59 us
    pallas_call x1, Pallas kernels, attention(): pl.pallas_call(kernel, out_shape=(jax.ShapeDtypeStruct(q_new.shape, jnp.f...  5.54 us
    ppermute x3, starting transfers between devices, local(): lax.ppermute(own_rows, 'blk', [(i, (i + k) % blocks) for i in range(block...  3.83 us
    ppermute x3, starting transfers between devices, local(): lax.ppermute(sent[k], 'blk', [(i, (i + k) % blocks) for i in range(blocks)])  3.09 us
    ppermute x3, starting transfers between devices, local(): lax.ppermute(own, 'blk', [(i, (i + k) % blocks) for i in range(blocks)])  1.64 us
    unnamed x7, local copies, waits for them, and re-layouts  1.64 us
  transfers between devices with their start and end apart: 9, of which 5 were waited for; matrix products, arithmetic and copies ran while one was open for 17% of the time, Pallas kernels for 19%

profile of v18, /device:TPU:11, one launch (start us, length us, event | category | flops | bytes accessed | tf_op | source)
XLA Modules:
  0.0 67.4 jit_solution(10502661278016748721)
XLA Ops:
  0.0 0.0 copy-start
  0.0 0.9 %copy.10 = bf16[128,2,256]{2,0,1:T(8,128)(2,1)S(1)} copy(bf16[128,2,256]{2,1,0:T(2,128)(2,1)} %param.6) | data formatting | bytes 262144 | tf_op args[1]
  0.9 1.3 %collective-permute-start = (bf16[2,128,256]{2,1,0:T(8,128)(2,1)S(1)}, bf16[2,128,256]{2,1,0:T(8,128)(2,1)S(1)}, u32[]{:S(2)}, u32[]{:S(2)}) collective-permute-start(bf16[2,128,256]{2,1,0:T(8,128)(2,1)S(1)} %bitcast.44), channel_id=1, source_target_pairs={{0,4},{4,8},{8,12},{12,0},{1,5},{5,9},{9,13},{13,1},{2,6},{6,10},{... | collective-permute-start | bytes 393224 | tf_op jit(solution)/shard_map/ppermute | solution.py:203
  2.3 1.1 %collective-permute-start.1 = (bf16[2,128,256]{2,1,0:T(8,128)(2,1)S(1)}, bf16[2,128,256]{2,1,0:T(8,128)(2,1)S(1)}, u32[]{:S(2)}, u32[]{:S(2)}) collective-permute-start(bf16[2,128,256]{2,1,0:T(8,128)(2,1)S(1)} %bitcast.45), channel_id=1, source_target_pairs={{0,8},{4,12},{8,0},{12,4},{1,9},{5,13},{9,1},{13,5},{2,10},{6,14},... | collective-permute-start | bytes 393224 | tf_op jit(solution)/shard_map/ppermute | solution.py:203
  3.4 1.4 %collective-permute-start.2 = (bf16[2,128,256]{2,1,0:T(8,128)(2,1)S(1)}, bf16[2,128,256]{2,1,0:T(8,128)(2,1)S(1)}, u32[]{:S(2)}, u32[]{:S(2)}) collective-permute-start(bf16[2,128,256]{2,1,0:T(8,128)(2,1)S(1)} %bitcast.46), channel_id=1, source_target_pairs={{0,12},{4,0},{8,4},{12,8},{1,13},{5,1},{9,5},{13,9},{2,14},{6,2},{... | collective-permute-start | bytes 393224 | tf_op jit(solution)/shard_map/ppermute | solution.py:203
  4.8 0.7 and_select_fusion.5
  5.4 0.7 convert_bitcast_fusion.1
  6.1 0.1 convert_reduce_fusion
  6.2 0.2 reduce-window.22
  6.4 0.6 fusion.2
  7.1 0.7 and_select_fusion
  7.7 0.2 reduce-window.21
  7.9 0.6 gather_fusion.1
  8.6 0.2 reduce-window.23
  8.8 0.1 fusion.1
  8.9 0.1 fusion
  9.0 0.1 reshape.413
  9.1 0.1 broadcast_in_dim.58
  9.1 0.6 fusion.12
  9.7 0.2 select_reduce_fusion
  9.9 0.6 gather_fusion
  10.6 0.7 fusion.13
  16.4 1.3 %gather_fusion.3 = s32[4]{0:T(128)S(1)} fusion(s32[4]{0:T(128)} %param.9, s32[1024]{0:T(1024)S(1)} %pad_clamp_fusion.1), kind=kCustom, calls=%fused_computation.3 | custom fusion | bytes 48 | tf_op jit(solution)/shard_map/gather | solution.py:205
  20.2 1.3 %constant_dynamic-slice_fusion = (bf16[1,2,128,256]{3,2,1,0:T(8,128)(2,1)S(1)}, bf16[1,2,128,256]{3,2,1,0:T(8,128)(2,1)S(1)}, bf16[1,2,128,256]{3,2,1,0:T(8,128)(2,1)S(1)}, bf16[1,2,128,256]{3,2,1,0:T(8,128)(2,1)S(1)}) fusion(bf16[32,2,128,256]{3,2,1,0:T(8,128)(2,1)} %param.7, s32[]{:T(128)S(6)} %select_n.145, s32[]{:T(128)S(6)} %select_n.143, ...), kind=kLoop, calls=%fused_computation.45 | loop fusion | bytes 1048592 | tf_op jit(solution)/shard_map/dynamic_slice | solution.py:221
  21.5 0.0 collective-permute-done
  21.5 0.0 collective-permute-done.1
  21.5 0.0 collective-permute-done.2
  21.5 0.1 collective-permute-start.3
  21.6 3.0 %collective-permute-start.4 = (bf16[1,2,128,256]{3,2,1,0:T(8,128)(2,1)S(1)}, bf16[1,2,128,256]{3,2,1,0:T(8,128)(2,1)S(1)}, u32[]{:S(2)}, u32[]{:S(2)}) collective-permute-start(bf16[1,2,128,256]{3,2,1,0:T(8,128)(2,1)S(1)} %get-tuple-element.26), channel_id=1, source_target_pairs={{0,8},{4,12},{8,0},{12,4},{1,9},{5,13},{9,1},{13,5},{2,10},{6,14},... | collective-permute-start | bytes 393224 | tf_op jit(solution)/shard_map/ppermute | solution.py:230
  24.6 0.0 collective-permute-start.5
  24.6 0.8 %collective-permute-done.3 = bf16[1,2,128,256]{3,2,1,0:T(8,128)(2,1)S(1)} collective-permute-done((bf16[1,2,128,256]{3,2,1,0:T(8,128)(2,1)S(1)}, bf16[1,2,128,256]{3,2,1,0:T(8,128)(2,1)S(1)}, u32[]{:S(2)}, u32[]{:S(2)}) %collective-permute-start.3) | collective-permute-done | bytes 131104 | tf_op jit(solution)/shard_map/ppermute | solution.py:230
  25.4 7.8 %collective-permute-done.4 = bf16[1,2,128,256]{3,2,1,0:T(8,128)(2,1)S(1)} collective-permute-done((bf16[1,2,128,256]{3,2,1,0:T(8,128)(2,1)S(1)}, bf16[1,2,128,256]{3,2,1,0:T(8,128)(2,1)S(1)}, u32[]{:S(2)}, u32[]{:S(2)}) %collective-permute-start.4) | collective-permute-done | bytes 131104 | tf_op jit(solution)/shard_map/ppermute | solution.py:230
  33.2 3.0 %collective-permute-done.5 = bf16[1,2,128,256]{3,2,1,0:T(8,128)(2,1)S(1)} collective-permute-done((bf16[1,2,128,256]{3,2,1,0:T(8,128)(2,1)S(1)}, bf16[1,2,128,256]{3,2,1,0:T(8,128)(2,1)S(1)}, u32[]{:S(2)}, u32[]{:S(2)}) %collective-permute-start.5) | collective-permute-done | bytes 131104 | tf_op jit(solution)/shard_map/ppermute | solution.py:230
  36.2 0.1 maximum_bitcast_fusion
  36.3 0.6 gather_fusion.2
  36.8 0.0 copy-start.1
  36.8 0.1 collective-permute-start.6
  36.9 0.7 iota_add_fusion
  37.6 0.6 slice.46.page_ok_ref
  38.2 0.4 collective-permute-start.7
  38.6 1.1 %collective-permute-start.8 = (bf16[2,2,128,256]{3,2,1,0:T(8,128)(2,1)S(1)}, bf16[2,2,128,256]{3,2,1,0:T(8,128)(2,1)S(1)}, u32[]{:S(2)}, u32[]{:S(2)}) collective-permute-start(bf16[2,2,128,256]{3,2,1,0:T(8,128)(2,1)S(1)} %gather_fusion.2), channel_id=1, source_target_pairs={{0,12},{4,0},{8,4},{12,8},{1,13},{5,1},{9,5},{13,9},{2,14},{6,2},{... | collective-permute-start | bytes 786440 | tf_op jit(solution)/shard_map/ppermute | solution.py:244
  39.7 0.0 copy-done
  39.7 0.6 fusion.3
  41.0 0.9 %pad_maximum_fusion.new_ref = bf16[4,2,128,256]{3,2,1,0:T(8,128)(2,1)} fusion(bf16[1,2,128,256]{3,2,1,0:T(8,128)(2,1)S(1)} %bitcast.51, bf16[1,2,128,256]{3,2,1,0:T(8,128)(2,1)S(1)} %bitcast.50, bf16[1,2,128,256]{3,2,1,0:T(8,128)(2,1)S(1)} %bitcast.49, bf16[1,2,128,256]{3,2,1,0:T(8,128)(2,1)S(1)} %bitcast.47), kind=kLoop, calls=%fused_computation.5 | loop fusion | flops 786432 | bytes 1048576 | tf_op jit(solution)/shard_map/stack | solution.py:226
  41.9 0.0 copy-done.1
  41.9 5.5 %shard_map.55 = (f32[128,2048]{1,0:T(8,128)}, f32[2,128,8]{2,1,0:T(8,128)}, f32[2,128,8]{2,1,0:T(8,128)}) custom-call(s32[1]{0:T(128)} %bitcast.22.query_start, bf16[128,2048]{1,0:T(8,128)(2,1)} %q_ref.5, bf16[4,2,128,256]{3,2,1,0:T(8,128)(2,1)} %pad_maximum_fusion.new_ref, bf16[2,2,128,256]{3,2,1,0:T(8,128)(2,1)} %copy-done.1, s32[1,512]{1,0:T(1,128)} %bitcast.57, ...), custom_call_target="tpu_custom_call" | custom-call | tf_op jit(solution)/shard_map/pallas_call | solution.py:169
  47.4 0.0 collective-permute-done.6.page_ref
  47.4 0.0 copy-start.2
  47.4 0.7 %copy-done.2 = bf16[2,2,128,256]{3,2,1,0:T(8,128)(2,1)} copy-done((bf16[2,2,128,256]{3,2,1,0:T(8,128)(2,1)}, bf16[2,2,128,256]{3,2,1,0:T(8,128)(2,1)S(1)}, u32[]{:S(2)}) %copy-start.2) | copy-done | bytes 262168
  48.1 7.2 %shard_map.56 = (f32[128,2048]{1,0:T(8,128)}, f32[2,128,8]{2,1,0:T(8,128)}, f32[2,128,8]{2,1,0:T(8,128)}) custom-call(bf16[128,2048]{1,0:T(8,128)(2,1)} %q_ref.5, bf16[2,2,128,256]{3,2,1,0:T(8,128)(2,1)} %copy-done.2, s32[1,256]{1,0:T(1,128)} %get-tuple-element.51.page_ok_ref, f32[128,2048]{1,0:T(8,128)} %get-tuple-element.32.acc_ref, ...), custom_call_target="tpu_custom_call" | custom-call | flops 268435456 | bytes 2883584 | tf_op jit(solution)/shard_map/pallas_call | solution.py:141
  55.4 3.3 %collective-permute-done.7 = bf16[2,2,128,256]{3,2,1,0:T(8,128)(2,1)S(1)} collective-permute-done((bf16[2,2,128,256]{3,2,1,0:T(8,128)(2,1)S(1)}, bf16[2,2,128,256]{3,2,1,0:T(8,128)(2,1)S(1)}, u32[]{:S(2)}, u32[]{:S(2)}) %collective-permute-start.7) | collective-permute-done | bytes 262176 | tf_op jit(solution)/shard_map/ppermute | solution.py:244
  58.7 2.2 %collective-permute-done.8 = bf16[2,2,128,256]{3,2,1,0:T(8,128)(2,1)S(1)} collective-permute-done((bf16[2,2,128,256]{3,2,1,0:T(8,128)(2,1)S(1)}, bf16[2,2,128,256]{3,2,1,0:T(8,128)(2,1)S(1)}, u32[]{:S(2)}, u32[]{:S(2)}) %collective-permute-start.8) | collective-permute-done | bytes 262176 | tf_op jit(solution)/shard_map/ppermute | solution.py:244
  61.0 0.8 %pad_maximum_fusion.1.page_ref = bf16[4,2,128,256]{3,2,1,0:T(8,128)(2,1)} fusion(bf16[2,2,128,256]{3,2,1,0:T(8,128)(2,1)S(1)} %collective-permute-done.8, bf16[2,2,128,256]{3,2,1,0:T(8,128)(2,1)S(1)} %collective-permute-done.7), kind=kLoop, calls=%fused_computation.6 | loop fusion | flops 262144 | bytes 1048576 | tf_op jit(solution)/shard_map/concatenate | solution.py:273
  61.8 5.6 %shard_map.57 = bf16[128,2048]{1,0:T(8,128)(2,1)} custom-call(bf16[128,2048]{1,0:T(8,128)(2,1)} %q_ref.5, bf16[4,2,128,256]{3,2,1,0:T(8,128)(2,1)} %pad_maximum_fusion.1.page_ref, s32[1,512]{1,0:T(1,128)} %slice.46.page_ok_ref, f32[128,2048]{1,0:T(8,128)} %get-tuple-element.40.acc_ref, f32[2,128,8]{2,1,0:T(8,128)} %get-tuple-element.41.top_ref, ...), custom_call_target="tpu_custom_call" | custom-call | flops 536870912 | bytes 3145728 | tf_op jit(solution)/shard_map/pallas_call | solution.py:141
  (11 shorter events, 0.1 us)
Async XLA Ops:
  0.0 39.7 %copy-start = (s32[4]{0:T(128)S(1)}, s32[4]{0:T(128)}, u32[]{:S(2)}) copy-start(s32[4]{0:T(128)} %param.9) | copy-start | bytes 52
  0.9 20.6 %collective-permute-start = (bf16[2,128,256]{2,1,0:T(8,128)(2,1)S(1)}, bf16[2,128,256]{2,1,0:T(8,128)(2,1)S(1)}, u32[]{:S(2)}, u32[]{:S(2)}) collective-permute-start(bf16[2,128,256]{2,1,0:T(8,128)(2,1)S(1)} %bitcast.44), channel_id=1, source_target_pairs={{0,4},{4,8},{8,12},{12,0},{1,5},{5,9},{9,13},{13,1},{2,6},{6,10},{... | collective-permute-start | bytes 393224 | tf_op jit(solution)/shard_map/ppermute | solution.py:203
  2.3 19.2 %collective-permute-start.1 = (bf16[2,128,256]{2,1,0:T(8,128)(2,1)S(1)}, bf16[2,128,256]{2,1,0:T(8,128)(2,1)S(1)}, u32[]{:S(2)}, u32[]{:S(2)}) collective-permute-start(bf16[2,128,256]{2,1,0:T(8,128)(2,1)S(1)} %bitcast.45), channel_id=1, source_target_pairs={{0,8},{4,12},{8,0},{12,4},{1,9},{5,13},{9,1},{13,5},{2,10},{6,14},... | collective-permute-start | bytes 393224 | tf_op jit(solution)/shard_map/ppermute | solution.py:203
  3.4 18.1 %collective-permute-start.2 = (bf16[2,128,256]{2,1,0:T(8,128)(2,1)S(1)}, bf16[2,128,256]{2,1,0:T(8,128)(2,1)S(1)}, u32[]{:S(2)}, u32[]{:S(2)}) collective-permute-start(bf16[2,128,256]{2,1,0:T(8,128)(2,1)S(1)} %bitcast.46), channel_id=1, source_target_pairs={{0,12},{4,0},{8,4},{12,8},{1,13},{5,1},{9,5},{13,9},{2,14},{6,2},{... | collective-permute-start | bytes 393224 | tf_op jit(solution)/shard_map/ppermute | solution.py:203
  21.5 3.9 %collective-permute-start.3 = (bf16[1,2,128,256]{3,2,1,0:T(8,128)(2,1)S(1)}, bf16[1,2,128,256]{3,2,1,0:T(8,128)(2,1)S(1)}, u32[]{:S(2)}, u32[]{:S(2)}) collective-permute-start(bf16[1,2,128,256]{3,2,1,0:T(8,128)(2,1)S(1)} %get-tuple-element.25), channel_id=1, source_target_pairs={{0,4},{4,8},{8,12},{12,0},{1,5},{5,9},{9,13},{13,1},{2,6},{6,10},{... | collective-permute-start | bytes 393224 | tf_op jit(solution)/shard_map/ppermute | solution.py:230
  21.6 11.6 %collective-permute-start.4 = (bf16[1,2,128,256]{3,2,1,0:T(8,128)(2,1)S(1)}, bf16[1,2,128,256]{3,2,1,0:T(8,128)(2,1)S(1)}, u32[]{:S(2)}, u32[]{:S(2)}) collective-permute-start(bf16[1,2,128,256]{3,2,1,0:T(8,128)(2,1)S(1)} %get-tuple-element.26), channel_id=1, source_target_pairs={{0,8},{4,12},{8,0},{12,4},{1,9},{5,13},{9,1},{13,5},{2,10},{6,14},... | collective-permute-start | bytes 393224 | tf_op jit(solution)/shard_map/ppermute | solution.py:230
  24.6 11.6 %collective-permute-start.5 = (bf16[1,2,128,256]{3,2,1,0:T(8,128)(2,1)S(1)}, bf16[1,2,128,256]{3,2,1,0:T(8,128)(2,1)S(1)}, u32[]{:S(2)}, u32[]{:S(2)}) collective-permute-start(bf16[1,2,128,256]{3,2,1,0:T(8,128)(2,1)S(1)} %get-tuple-element.27), channel_id=1, source_target_pairs={{0,12},{4,0},{8,4},{12,8},{1,13},{5,1},{9,5},{13,9},{2,14},{6,2},{... | collective-permute-start | bytes 393224 | tf_op jit(solution)/shard_map/ppermute | solution.py:230
  36.8 5.1 %copy-start.1 = (bf16[2,2,128,256]{3,2,1,0:T(8,128)(2,1)}, bf16[2,2,128,256]{3,2,1,0:T(8,128)(2,1)S(1)}, u32[]{:S(2)}) copy-start(bf16[2,2,128,256]{3,2,1,0:T(8,128)(2,1)S(1)} %gather_fusion.2) | copy-start | bytes 786436
  36.8 10.6 %collective-permute-start.6 = (bf16[2,2,128,256]{3,2,1,0:T(8,128)(2,1)S(1)}, bf16[2,2,128,256]{3,2,1,0:T(8,128)(2,1)S(1)}, u32[]{:S(2)}, u32[]{:S(2)}) collective-permute-start(bf16[2,2,128,256]{3,2,1,0:T(8,128)(2,1)S(1)} %gather_fusion.2), channel_id=1, source_target_pairs={{0,4},{4,8},{8,12},{12,0},{1,5},{5,9},{9,13},{13,1},{2,6},{6,10},{... | collective-permute-start | bytes 786440 | tf_op jit(solution)/shard_map/ppermute | solution.py:244
  38.2 20.6 %collective-permute-start.7 = (bf16[2,2,128,256]{3,2,1,0:T(8,128)(2,1)S(1)}, bf16[2,2,128,256]{3,2,1,0:T(8,128)(2,1)S(1)}, u32[]{:S(2)}, u32[]{:S(2)}) collective-permute-start(bf16[2,2,128,256]{3,2,1,0:T(8,128)(2,1)S(1)} %gather_fusion.2), channel_id=1, source_target_pairs={{0,8},{4,12},{8,0},{12,4},{1,9},{5,13},{9,1},{13,5},{2,10},{6,14},... | collective-permute-start | bytes 786440 | tf_op jit(solution)/shard_map/ppermute | solution.py:244
  38.6 22.4 %collective-permute-start.8 = (bf16[2,2,128,256]{3,2,1,0:T(8,128)(2,1)S(1)}, bf16[2,2,128,256]{3,2,1,0:T(8,128)(2,1)S(1)}, u32[]{:S(2)}, u32[]{:S(2)}) collective-permute-start(bf16[2,2,128,256]{3,2,1,0:T(8,128)(2,1)S(1)} %gather_fusion.2), channel_id=1, source_target_pairs={{0,12},{4,0},{8,4},{12,8},{1,13},{5,1},{9,5},{13,9},{2,14},{6,2},{... | collective-permute-start | bytes 786440 | tf_op jit(solution)/shard_map/ppermute | solution.py:244
  47.4 0.7 %copy-start.2 = (bf16[2,2,128,256]{3,2,1,0:T(8,128)(2,1)}, bf16[2,2,128,256]{3,2,1,0:T(8,128)(2,1)S(1)}, u32[]{:S(2)}) copy-start(bf16[2,2,128,256]{3,2,1,0:T(8,128)(2,1)S(1)} %collective-permute-done.6.page_ref) | copy-start | bytes 786436

commit v19 on v15

--- a/solution.py
+++ b/solution.py
@@ -68,12 +68,16 @@
 
 
 def prefix_kernel(
-    q_ref, page_ref, page_ok_ref, acc_ref, top_ref, total_ref, *out_refs,
-    head_size, group_size, mask_pages, final,
+    q_ref, *refs, head_size, group_size, mask_pages, final, parts,
 ):
+    page_refs = refs[:parts]
+    page_ok_ref, acc_ref, top_ref, total_ref = refs[parts : parts + 4]
+    out_refs = refs[parts + 4 :]
     scale = 1.0 / math.sqrt(head_size)
     q_rows = q_ref.shape[0]
-    page_kv = page_ref[:, 0].reshape(-1, page_ref.shape[-1])
+    page_kv = jnp.concatenate(
+        [r[:, 0].reshape(-1, r.shape[-1]) for r in page_refs], axis=0
+    )
     page_keys = page_kv[:, :head_size]
     page_values = page_kv[:, head_size:]
     page_visible = page_ok_ref[...] > 0
@@ -113,13 +117,14 @@
                 out_refs[2][0, :, h : h + 1] = row_total[rows]
 
 
-def prefix_part(page_ok, q_new, pages, acc, top, total, group_size, head_size, mask_pages,
+def prefix_part(page_ok, q_new, page_list, acc, top, total, group_size, head_size, mask_pages,
                 final=True):
     q_rows = q_new.shape[0]
-    npage, kv_heads, page_len, width = pages.shape
+    part_pages, kv_heads, page_len, width = page_list[0].shape
+    npage = part_pages * len(page_list)
     kernel = functools.partial(
         prefix_kernel, head_size=head_size, group_size=group_size, mask_pages=mask_pages,
-        final=final,
+        final=final, parts=len(page_list),
     )
     span = group_size * head_size
     block = pl.BlockSpec((q_rows, span), lambda g: (0, g))
@@ -136,7 +141,7 @@
     cost = pl.CostEstimate(
         flops=4 * rows * keys * head_size,
         transcendentals=rows * keys,
-        bytes_accessed=q_new.size * 2 + pages.size * 2 + acc.size * 8,
+        bytes_accessed=q_new.size * 2 + npage * kv_heads * page_len * width * 2 + acc.size * 8,
     )
     return pl.pallas_call(
         kernel,
@@ -145,14 +150,15 @@
         grid=(kv_heads,),
         in_specs=[
             block,
-            pl.BlockSpec((npage, 1, page_len, width), lambda g: (0, g, 0, 0)),
+            *[pl.BlockSpec((part_pages, 1, page_len, width), lambda g: (0, g, 0, 0))]
+            * len(page_list),
             pl.BlockSpec((1, npage * page_len), lambda g: (0, 0)),
             block,
             stat_spec,
             stat_spec,
         ],
         out_specs=out_specs,
-    )(q_new, pages, page_ok, acc, top, total)
+    )(q_new, *page_list, page_ok, acc, top, total)
 
 
 def attention(query_start, key_pos, page_ok, q_new, new_all, pages, group_size, head_size,
@@ -260,14 +266,13 @@
     )
     if not later:
         return prefix_part(
-            first_ok, q_new, gathered[1], acc, top, total, group_size, head_size, ragged
+            first_ok, q_new, [gathered[1]], acc, top, total, group_size, head_size, ragged
         )
     acc, top, total = prefix_part(
-        first_ok, q_new, gathered[1], acc, top, total, group_size, head_size, ragged, False
+        first_ok, q_new, [gathered[1]], acc, top, total, group_size, head_size, ragged, False
     )
     acc, top, total, farther = lax.optimization_barrier((acc, top, total, gathered[2:]))
-    later = jnp.concatenate(farther)
-    return prefix_part(later_ok, q_new, later, acc, top, total, group_size, head_size, ragged)
+    return prefix_part(later_ok, q_new, list(farther), acc, top, total, group_size, head_size, ragged)
 
 
 def solution(mesh):

time: 61.9 us -> 61.8 us (level)
  the two profiles are of different devices: /device:TPU:13 before, /device:TPU:15 now
where the time goes in v19:
time: 61.8 us; the launch traced here: 61.5 us
  waiting for transfers between devices  19.2 us (31%)
  Pallas kernels  18.4 us (30%)
  local copies, waits for them, and re-layouts  9.62 us (16%)
  starting transfers between devices  7.53 us (12%)
  other arithmetic  5.97 us (10%)
  between operations  0.79 us (1%)
    pallas_call x2, Pallas kernels, prefix_part(): pl.pallas_call(kernel, out_shape=out_shape, cost_estimate=cost, grid=(kv_...  12.9 us
    ppermute x3, waiting for transfers between devices, local(): lax.ppermute(sent[k], 'blk', [(i, (i + k) % blocks) for i in range(blocks)])  12.4 us
    ppermute x3, waiting for transfers between devices, local(): lax.ppermute(own, 'blk', [(i, (i + k) % blocks) for i in range(blocks)])  5.76 us
    pallas_call x1, Pallas kernels, attention(): pl.pallas_call(kernel, out_shape=(jax.ShapeDtypeStruct(q_new.shape, jnp.f...  5.54 us
    ppermute x3, starting transfers between devices, local(): lax.ppermute(own_rows, 'blk', [(i, (i + k) % blocks) for i in range(block...  3.83 us
    gather x1, local copies, waits for them, and re-layouts, local(): sent = kv_cache[by_shift].reshape((blocks, per_peer) + kv_cache.shape[1:])  2.77 us
    unnamed x11, local copies, waits for them, and re-layouts  2.34 us
    ppermute x3, starting transfers between devices, local(): lax.ppermute(sent[k], 'blk', [(i, (i + k) % blocks) for i in range(blocks)])  2.2 us
  transfers between devices with their start and end apart: 9, of which 6 were waited for; matrix products, arithmetic and copies ran while one was open for 20% of the time, Pallas kernels for 21%

profile of v19, /device:TPU:15, one launch (start us, length us, event | category | flops | bytes accessed | tf_op | source)
XLA Modules:
  0.0 61.5 jit_solution(10053212659050990715)
XLA Ops:
  0.0 0.0 copy-start
  0.0 0.9 %copy.19 = bf16[128,2,256]{2,0,1:T(8,128)(2,1)S(1)} copy(bf16[128,2,256]{2,1,0:T(2,128)(2,1)} %param.6) | data formatting | bytes 262144 | tf_op args[1]
  0.9 1.3 %collective-permute-start = (bf16[2,128,256]{2,1,0:T(8,128)(2,1)S(1)}, bf16[2,128,256]{2,1,0:T(8,128)(2,1)S(1)}, u32[]{:S(2)}, u32[]{:S(2)}) collective-permute-start(bf16[2,128,256]{2,1,0:T(8,128)(2,1)S(1)} %bitcast.53), channel_id=1, source_target_pairs={{0,4},{4,8},{8,12},{12,0},{1,5},{5,9},{9,13},{13,1},{2,6},{6,10},{... | collective-permute-start | bytes 393224 | tf_op jit(solution)/shard_map/ppermute | solution.py:209
  2.3 1.1 %collective-permute-start.1 = (bf16[2,128,256]{2,1,0:T(8,128)(2,1)S(1)}, bf16[2,128,256]{2,1,0:T(8,128)(2,1)S(1)}, u32[]{:S(2)}, u32[]{:S(2)}) collective-permute-start(bf16[2,128,256]{2,1,0:T(8,128)(2,1)S(1)} %bitcast.54), channel_id=1, source_target_pairs={{0,8},{4,12},{8,0},{12,4},{1,9},{5,13},{9,1},{13,5},{2,10},{6,14},... | collective-permute-start | bytes 393224 | tf_op jit(solution)/shard_map/ppermute | solution.py:209
  3.4 1.4 %collective-permute-start.2 = (bf16[2,128,256]{2,1,0:T(8,128)(2,1)S(1)}, bf16[2,128,256]{2,1,0:T(8,128)(2,1)S(1)}, u32[]{:S(2)}, u32[]{:S(2)}) collective-permute-start(bf16[2,128,256]{2,1,0:T(8,128)(2,1)S(1)} %bitcast.55), channel_id=1, source_target_pairs={{0,12},{4,0},{8,4},{12,8},{1,13},{5,1},{9,5},{13,9},{2,14},{6,2},{... | collective-permute-start | bytes 393224 | tf_op jit(solution)/shard_map/ppermute | solution.py:209
  4.8 0.7 %and_select_fusion.5 = s32[8]{0:T(128)S(1)} fusion(s32[8]{0:T(128)} %param.8), kind=kLoop, calls=%fused_computation.41 | loop fusion | flops 88 | bytes 64 | tf_op jit(solution)/shard_map/jit(remainder)/select_n | solution.py:216
  5.4 0.7 %convert_bitcast_fusion.1 = (s32[8,1]{0,1:T(1,128)S(1)}, pred[8]{0:T(512)(128)(4,1)S(1)}, s32[8]{0:T(128)S(1)}) fusion(s32[]{:T(128)S(6)} %axis_index.15, s32[8]{0:T(128)} %param.8), kind=kLoop, calls=%fused_computation.63 | loop fusion | flops 136 | bytes 108 | tf_op jit(solution)/shard_map/convert
  6.1 0.1 convert_reduce_fusion
  6.2 0.2 reduce-window.22
  6.4 0.6 %and_select_fusion = (s32[4]{0:T(128)S(1)}, s32[]{:T(128)}) fusion(s32[]{:T(128)S(6)} %axis_index.15, s32[4]{0:T(128)S(1)} %convert_reduce_fusion, s32[4,1]{0,1:T(1,128)S(1)} %reduce-window.22), kind=kLoop, calls=%fused_computation.35 | loop fusion | flops 63 | bytes 56 | tf_op jit(solution)/shard_map/jit(remainder)/select_n | solution.py:236
  7.1 0.7 %and_select_fusion.6 = s32[4]{0:T(128)S(1)} fusion(s32[]{:T(128)} %get-tuple-element.46), kind=kLoop, calls=%fused_computation.42 | loop fusion | flops 48 | bytes 20 | tf_op jit(solution)/shard_map/jit(remainder)/select_n | solution.py:222
  7.7 0.2 reduce-window.21
  7.9 0.2 select_reduce_fusion
  8.1 0.6 %gather_fusion = s32[4]{0:T(128)S(1)} fusion(s32[4]{0:T(128)S(1)} %select_reduce_fusion, s32[1024]{0:T(1024)S(1)} %pad_clamp_fusion.3), kind=kCustom, calls=%fused_computation | custom fusion | bytes 48 | tf_op jit(solution)/shard_map/gather | solution.py:225
  8.8 0.6 %gather_fusion.2 = pred[4]{0:T(512)(128)(4,1)S(1)} fusion(pred[4]{0:T(512)(128)(4,1)S(1)} %compare_bitcast_fusion, s32[1024]{0:T(1024)S(1)} %pad_clamp_fusion.1), kind=kCustom, calls=%fused_computation.2 | custom fusion | bytes 24 | tf_op jit(solution)/shard_map/gather | solution.py:236
  9.4 0.2 reduce-window.23
  9.6 0.1 fusion.1
  9.7 0.1 fusion
  9.8 0.1 reshape.427
  9.9 0.1 broadcast_in_dim.38
  10.0 0.6 fusion.14
  10.6 1.3 %gather_fusion.4 = s32[4]{0:T(128)S(1)} fusion(s32[4]{0:T(128)} %param.9, s32[1024]{0:T(1024)S(1)} %pad_clamp_fusion.1), kind=kCustom, calls=%fused_computation.4 | custom fusion | bytes 48 | tf_op jit(solution)/shard_map/gather | solution.py:211
  11.9 2.8 %gather_fusion.1 = bf16[4,2,128,256]{3,2,1,0:T(8,128)(2,1)S(1)} fusion(bf16[32,2,128,256]{3,2,1,0:T(8,128)(2,1)} %param.7, s32[1024]{0:T(1024)S(1)} %pad_clamp_fusion.2), kind=kCustom, calls=%fused_computation.1 | custom fusion | bytes 1048592 | tf_op jit(solution)/shard_map/gather | solution.py:226
  14.6 0.0 collective-permute-done
  14.7 0.0 collective-permute-done.1
  14.7 1.0 %collective-permute-done.2 = bf16[2,128,256]{2,1,0:T(8,128)(2,1)S(1)} collective-permute-done((bf16[2,128,256]{2,1,0:T(8,128)(2,1)S(1)}, bf16[2,128,256]{2,1,0:T(8,128)(2,1)S(1)}, u32[]{:S(2)}, u32[]{:S(2)}) %collective-permute-start.2) | collective-permute-done | bytes 131104 | tf_op jit(solution)/shard_map/ppermute | solution.py:209
  15.7 0.1 collective-permute-start.3
  15.8 2.1 %collective-permute-start.4 = (bf16[1,2,128,256]{3,2,1,0:T(8,128)(2,1)S(1)}, bf16[1,2,128,256]{3,2,1,0:T(8,128)(2,1)S(1)}, u32[]{:S(2)}, u32[]{:S(2)}) collective-permute-start(bf16[1,2,128,256]{3,2,1,0:T(8,128)(2,1)S(1)} %get-tuple-element.41), channel_id=1, source_target_pairs={{0,8},{4,12},{8,0},{12,4},{1,9},{5,13},{9,1},{13,5},{2,10},{6,14},... | collective-permute-start | bytes 393224 | tf_op jit(solution)/shard_map/ppermute | solution.py:232
  17.9 0.0 collective-permute-start.5
  18.0 2.4 %collective-permute-done.3 = bf16[1,2,128,256]{3,2,1,0:T(8,128)(2,1)S(1)} collective-permute-done((bf16[1,2,128,256]{3,2,1,0:T(8,128)(2,1)S(1)}, bf16[1,2,128,256]{3,2,1,0:T(8,128)(2,1)S(1)}, u32[]{:S(2)}, u32[]{:S(2)}) %collective-permute-start.3) | collective-permute-done | bytes 131104 | tf_op jit(solution)/shard_map/ppermute | solution.py:232
  20.3 6.1 %collective-permute-done.4 = bf16[1,2,128,256]{3,2,1,0:T(8,128)(2,1)S(1)} collective-permute-done((bf16[1,2,128,256]{3,2,1,0:T(8,128)(2,1)S(1)}, bf16[1,2,128,256]{3,2,1,0:T(8,128)(2,1)S(1)}, u32[]{:S(2)}, u32[]{:S(2)}) %collective-permute-start.4) | collective-permute-done | bytes 131104 | tf_op jit(solution)/shard_map/ppermute | solution.py:232
  26.4 3.9 %collective-permute-done.5 = bf16[1,2,128,256]{3,2,1,0:T(8,128)(2,1)S(1)} collective-permute-done((bf16[1,2,128,256]{3,2,1,0:T(8,128)(2,1)S(1)}, bf16[1,2,128,256]{3,2,1,0:T(8,128)(2,1)S(1)}, u32[]{:S(2)}, u32[]{:S(2)}) %collective-permute-start.5) | collective-permute-done | bytes 131104 | tf_op jit(solution)/shard_map/ppermute | solution.py:232
  30.4 0.1 maximum_bitcast_fusion
  30.4 0.6 gather_fusion.3
  31.0 0.0 copy-start.1
  31.0 0.1 collective-permute-start.6
  31.1 0.7 %iota_add_fusion = s32[4,128]{1,0:T(4,128)} fusion(s32[4]{0:T(128)S(1)} %broadcast_multiply_fusion), kind=kLoop, calls=%fused_computation.29 | loop fusion | flops 512 | bytes 2064 | tf_op jit(solution)/shard_map/add | solution.py:254
  31.7 0.6 slice.43.refs_2_
  32.3 0.4 collective-permute-start.7
  32.8 1.0 %collective-permute-start.8 = (bf16[2,2,128,256]{3,2,1,0:T(8,128)(2,1)S(1)}, bf16[2,2,128,256]{3,2,1,0:T(8,128)(2,1)S(1)}, u32[]{:S(2)}, u32[]{:S(2)}) collective-permute-start(bf16[2,2,128,256]{3,2,1,0:T(8,128)(2,1)S(1)} %gather_fusion.3), channel_id=1, source_target_pairs={{0,12},{4,0},{8,4},{12,8},{1,13},{5,1},{9,5},{13,9},{2,14},{6,2},{... | collective-permute-start | bytes 786440 | tf_op jit(solution)/shard_map/ppermute | solution.py:246
  33.8 0.0 copy-done
  33.8 0.6 %fusion.3 = s32[]{:T(128)} fusion(s32[4]{0:T(128)S(1)} %copy-done, s32[]{:T(128)S(6)} %axis_index.15), kind=kLoop, calls=%fused_computation.51 | loop fusion | flops 11 | bytes 24 | tf_op jit(solution)/shard_map/reduce_sum | solution.py:203
  35.1 0.9 %pad_maximum_fusion.new_ref = bf16[4,2,128,256]{3,2,1,0:T(8,128)(2,1)} fusion(bf16[1,2,128,256]{3,2,1,0:T(8,128)(2,1)S(1)} %bitcast.59, bf16[1,2,128,256]{3,2,1,0:T(8,128)(2,1)S(1)} %bitcast.58, bf16[1,2,128,256]{3,2,1,0:T(8,128)(2,1)S(1)} %bitcast.57, bf16[1,2,128,256]{3,2,1,0:T(8,128)(2,1)S(1)} %bitcast.56), kind=kLoop, calls=%fused_computation.6 | loop fusion | flops 786432 | bytes 1048576 | tf_op jit(solution)/shard_map/stack | solution.py:228
  35.9 0.0 copy-done.1
  35.9 5.5 %shard_map.55 = (f32[128,2048]{1,0:T(8,128)}, f32[2,128,8]{2,1,0:T(8,128)}, f32[2,128,8]{2,1,0:T(8,128)}) custom-call(s32[1]{0:T(128)} %bitcast.24.query_start, bf16[128,2048]{1,0:T(8,128)(2,1)} %q_ref.5, bf16[4,2,128,256]{3,2,1,0:T(8,128)(2,1)} %pad_maximum_fusion.new_ref, bf16[2,2,128,256]{3,2,1,0:T(8,128)(2,1)} %copy-done.1, s32[1,512]{1,0:T(1,128)} %bitcast.65, ...), custom_call_target="tpu_custom_call" | custom-call | tf_op jit(solution)/shard_map/pallas_call | solution.py:175
  41.5 0.0 collective-permute-done.6.refs_0_
  41.5 0.0 copy-start.4
  41.5 0.7 %copy-done.4 = bf16[2,2,128,256]{3,2,1,0:T(8,128)(2,1)} copy-done((bf16[2,2,128,256]{3,2,1,0:T(8,128)(2,1)}, bf16[2,2,128,256]{3,2,1,0:T(8,128)(2,1)S(1)}, u32[]{:S(2)}) %copy-start.4) | copy-done | bytes 262168
  42.2 7.2 %shard_map.56 = (f32[128,2048]{1,0:T(8,128)}, f32[2,128,8]{2,1,0:T(8,128)}, f32[2,128,8]{2,1,0:T(8,128)}) custom-call(bf16[128,2048]{1,0:T(8,128)(2,1)} %q_ref.5, bf16[2,2,128,256]{3,2,1,0:T(8,128)(2,1)} %copy-done.4, s32[1,256]{1,0:T(1,128)} %get-tuple-element.44.refs_1_, f32[128,2048]{1,0:T(8,128)} %get-tuple-element.26.refs_2_, ...), custom_call_target="tpu_custom_call" | custom-call | flops 268435456 | bytes 2883584 | tf_op jit(solution)/shard_map/pallas_call | solution.py:146
  49.4 4.0 %collective-permute-done.7.refs_0_ = bf16[2,2,128,256]{3,2,1,0:T(8,128)(2,1)S(1)} collective-permute-done((bf16[2,2,128,256]{3,2,1,0:T(8,128)(2,1)S(1)}, bf16[2,2,128,256]{3,2,1,0:T(8,128)(2,1)S(1)}, u32[]{:S(2)}, u32[]{:S(2)}) %collective-permute-start.7) | collective-permute-done | bytes 262176 | tf_op jit(solution)/shard_map/ppermute | solution.py:246
  53.4 0.0 copy-start.2
  53.4 1.8 %collective-permute-done.8.refs_1_ = bf16[2,2,128,256]{3,2,1,0:T(8,128)(2,1)S(1)} collective-permute-done((bf16[2,2,128,256]{3,2,1,0:T(8,128)(2,1)S(1)}, bf16[2,2,128,256]{3,2,1,0:T(8,128)(2,1)S(1)}, u32[]{:S(2)}, u32[]{:S(2)}) %collective-permute-start.8) | collective-permute-done | bytes 262176 | tf_op jit(solution)/shard_map/ppermute | solution.py:246
  55.2 0.0 copy-start.3
  55.2 0.0 copy-done.2
  55.2 0.7 %copy-done.3 = bf16[2,2,128,256]{3,2,1,0:T(8,128)(2,1)} copy-done((bf16[2,2,128,256]{3,2,1,0:T(8,128)(2,1)}, bf16[2,2,128,256]{3,2,1,0:T(8,128)(2,1)S(1)}, u32[]{:S(2)}) %copy-start.3) | copy-done | bytes 262168
  55.9 5.7 %shard_map.57 = bf16[128,2048]{1,0:T(8,128)(2,1)} custom-call(bf16[128,2048]{1,0:T(8,128)(2,1)} %q_ref.5, bf16[2,2,128,256]{3,2,1,0:T(8,128)(2,1)} %copy-done.2, bf16[2,2,128,256]{3,2,1,0:T(8,128)(2,1)} %copy-done.3, s32[1,512]{1,0:T(1,128)} %slice.43.refs_2_, f32[128,2048]{1,0:T(8,128)} %get-tuple-element.34.refs_3_, ...), custom_call_target="tpu_custom_call" | custom-call | flops 536870912 | bytes 3145728 | tf_op jit(solution)/shard_map/pallas_call | solution.py:146
  (15 shorter events, 0.1 us)
Async XLA Ops:
  0.0 33.8 %copy-start = (s32[4]{0:T(128)S(1)}, s32[4]{0:T(128)}, u32[]{:S(2)}) copy-start(s32[4]{0:T(128)} %param.9) | copy-start | bytes 52
  0.9 13.7 %collective-permute-start = (bf16[2,128,256]{2,1,0:T(8,128)(2,1)S(1)}, bf16[2,128,256]{2,1,0:T(8,128)(2,1)S(1)}, u32[]{:S(2)}, u32[]{:S(2)}) collective-permute-start(bf16[2,128,256]{2,1,0:T(8,128)(2,1)S(1)} %bitcast.53), channel_id=1, source_target_pairs={{0,4},{4,8},{8,12},{12,0},{1,5},{5,9},{9,13},{13,1},{2,6},{6,10},{... | collective-permute-start | bytes 393224 | tf_op jit(solution)/shard_map/ppermute | solution.py:209
  2.3 12.4 %collective-permute-start.1 = (bf16[2,128,256]{2,1,0:T(8,128)(2,1)S(1)}, bf16[2,128,256]{2,1,0:T(8,128)(2,1)S(1)}, u32[]{:S(2)}, u32[]{:S(2)}) collective-permute-start(bf16[2,128,256]{2,1,0:T(8,128)(2,1)S(1)} %bitcast.54), channel_id=1, source_target_pairs={{0,8},{4,12},{8,0},{12,4},{1,9},{5,13},{9,1},{13,5},{2,10},{6,14},... | collective-permute-start | bytes 393224 | tf_op jit(solution)/shard_map/ppermute | solution.py:209
  3.4 12.3 %collective-permute-start.2 = (bf16[2,128,256]{2,1,0:T(8,128)(2,1)S(1)}, bf16[2,128,256]{2,1,0:T(8,128)(2,1)S(1)}, u32[]{:S(2)}, u32[]{:S(2)}) collective-permute-start(bf16[2,128,256]{2,1,0:T(8,128)(2,1)S(1)} %bitcast.55), channel_id=1, source_target_pairs={{0,12},{4,0},{8,4},{12,8},{1,13},{5,1},{9,5},{13,9},{2,14},{6,2},{... | collective-permute-start | bytes 393224 | tf_op jit(solution)/shard_map/ppermute | solution.py:209
  15.7 4.6 %collective-permute-start.3 = (bf16[1,2,128,256]{3,2,1,0:T(8,128)(2,1)S(1)}, bf16[1,2,128,256]{3,2,1,0:T(8,128)(2,1)S(1)}, u32[]{:S(2)}, u32[]{:S(2)}) collective-permute-start(bf16[1,2,128,256]{3,2,1,0:T(8,128)(2,1)S(1)} %get-tuple-element.42), channel_id=1, source_target_pairs={{0,4},{4,8},{8,12},{12,0},{1,5},{5,9},{9,13},{13,1},{2,6},{6,10},{... | collective-permute-start | bytes 393224 | tf_op jit(solution)/shard_map/ppermute | solution.py:232
  15.8 10.6 %collective-permute-start.4 = (bf16[1,2,128,256]{3,2,1,0:T(8,128)(2,1)S(1)}, bf16[1,2,128,256]{3,2,1,0:T(8,128)(2,1)S(1)}, u32[]{:S(2)}, u32[]{:S(2)}) collective-permute-start(bf16[1,2,128,256]{3,2,1,0:T(8,128)(2,1)S(1)} %get-tuple-element.41), channel_id=1, source_target_pairs={{0,8},{4,12},{8,0},{12,4},{1,9},{5,13},{9,1},{13,5},{2,10},{6,14},... | collective-permute-start | bytes 393224 | tf_op jit(solution)/shard_map/ppermute | solution.py:232
  17.9 12.4 %collective-permute-start.5 = (bf16[1,2,128,256]{3,2,1,0:T(8,128)(2,1)S(1)}, bf16[1,2,128,256]{3,2,1,0:T(8,128)(2,1)S(1)}, u32[]{:S(2)}, u32[]{:S(2)}) collective-permute-start(bf16[1,2,128,256]{3,2,1,0:T(8,128)(2,1)S(1)} %slice_bitcast_fusion.2), channel_id=1, source_target_pairs={{0,12},{4,0},{8,4},{12,8},{1,13},{5,1},{9,5},{13,9},{2,14},{6,2},{... | collective-permute-start | bytes 393224 | tf_op jit(solution)/shard_map/ppermute | solution.py:232
  31.0 4.9 %copy-start.1 = (bf16[2,2,128,256]{3,2,1,0:T(8,128)(2,1)}, bf16[2,2,128,256]{3,2,1,0:T(8,128)(2,1)S(1)}, u32[]{:S(2)}) copy-start(bf16[2,2,128,256]{3,2,1,0:T(8,128)(2,1)S(1)} %gather_fusion.3) | copy-start | bytes 786436
  31.0 10.5 %collective-permute-start.6 = (bf16[2,2,128,256]{3,2,1,0:T(8,128)(2,1)S(1)}, bf16[2,2,128,256]{3,2,1,0:T(8,128)(2,1)S(1)}, u32[]{:S(2)}, u32[]{:S(2)}) collective-permute-start(bf16[2,2,128,256]{3,2,1,0:T(8,128)(2,1)S(1)} %gather_fusion.3), channel_id=1, source_target_pairs={{0,4},{4,8},{8,12},{12,0},{1,5},{5,9},{9,13},{13,1},{2,6},{6,10},{... | collective-permute-start | bytes 786440 | tf_op jit(solution)/shard_map/ppermute | solution.py:246
  32.3 21.1 %collective-permute-start.7 = (bf16[2,2,128,256]{3,2,1,0:T(8,128)(2,1)S(1)}, bf16[2,2,128,256]{3,2,1,0:T(8,128)(2,1)S(1)}, u32[]{:S(2)}, u32[]{:S(2)}) collective-permute-start(bf16[2,2,128,256]{3,2,1,0:T(8,128)(2,1)S(1)} %gather_fusion.3), channel_id=1, source_target_pairs={{0,8},{4,12},{8,0},{12,4},{1,9},{5,13},{9,1},{13,5},{2,10},{6,14},... | collective-permute-start | bytes 786440 | tf_op jit(solution)/shard_map/ppermute | solution.py:246
  32.8 22.4 %collective-permute-start.8 = (bf16[2,2,128,256]{3,2,1,0:T(8,128)(2,1)S(1)}, bf16[2,2,128,256]{3,2,1,0:T(8,128)(2,1)S(1)}, u32[]{:S(2)}, u32[]{:S(2)}) collective-permute-start(bf16[2,2,128,256]{3,2,1,0:T(8,128)(2,1)S(1)} %gather_fusion.3), channel_id=1, source_target_pairs={{0,12},{4,0},{8,4},{12,8},{1,13},{5,1},{9,5},{13,9},{2,14},{6,2},{... | collective-permute-start | bytes 786440 | tf_op jit(solution)/shard_map/ppermute | solution.py:246
  41.5 0.7 %copy-start.4 = (bf16[2,2,128,256]{3,2,1,0:T(8,128)(2,1)}, bf16[2,2,128,256]{3,2,1,0:T(8,128)(2,1)S(1)}, u32[]{:S(2)}) copy-start(bf16[2,2,128,256]{3,2,1,0:T(8,128)(2,1)S(1)} %collective-permute-done.6.refs_0_) | copy-start | bytes 786436
  53.4 1.8 %copy-start.2 = (bf16[2,2,128,256]{3,2,1,0:T(8,128)(2,1)}, bf16[2,2,128,256]{3,2,1,0:T(8,128)(2,1)S(1)}, u32[]{:S(2)}) copy-start(bf16[2,2,128,256]{3,2,1,0:T(8,128)(2,1)S(1)} %collective-permute-done.7.refs_0_) | copy-start | bytes 786436
  55.2 0.7 %copy-start.3 = (bf16[2,2,128,256]{3,2,1,0:T(8,128)(2,1)}, bf16[2,2,128,256]{3,2,1,0:T(8,128)(2,1)S(1)}, u32[]{:S(2)}) copy-start(bf16[2,2,128,256]{3,2,1,0:T(8,128)(2,1)S(1)} %collective-permute-done.8.refs_1_) | copy-start | bytes 786436

commit v20 on v19

--- a/solution.py
+++ b/solution.py
@@ -264,15 +264,10 @@
     acc, top, total = attention(
         query_start, key_pos, own_ok, q_new, new_all, own, group_size, head_size, ragged
     )
-    if not later:
-        return prefix_part(
-            first_ok, q_new, [gathered[1]], acc, top, total, group_size, head_size, ragged
-        )
-    acc, top, total = prefix_part(
-        first_ok, q_new, [gathered[1]], acc, top, total, group_size, head_size, ragged, False
-    )
-    acc, top, total, farther = lax.optimization_barrier((acc, top, total, gathered[2:]))
-    return prefix_part(later_ok, q_new, list(farther), acc, top, total, group_size, head_size, ragged)
+    others_ok = page_ok[:, pg * page_len :]
+    return prefix_part(
+        others_ok, q_new, gathered[1:], acc, top, total, group_size, head_size, ragged
+    )
 
 
 def solution(mesh):

time: 61.8 us -> 62.3 us (level)
  the two profiles are of different devices: /device:TPU:15 before, /device:TPU:11 now
where the time goes in v20:
time: 62.3 us; the launch traced here: 62 us
  waiting for transfers between devices  25.7 us (41%)
  Pallas kernels  12.5 us (20%)
  local copies, waits for them, and re-layouts  8.87 us (14%)
  starting transfers between devices  7.61 us (12%)
  other arithmetic  6.61 us (11%)
  between operations  0.78 us (1%)
    ppermute x3, waiting for transfers between devices, local(): lax.ppermute(own, 'blk', [(i, (i + k) % blocks) for i in range(blocks)])  15.1 us
    ppermute x3, waiting for transfers between devices, local(): lax.ppermute(sent[k], 'blk', [(i, (i + k) % blocks) for i in range(blocks)])  8.73 us
    pallas_call x1, Pallas kernels, prefix_part(): pl.pallas_call(kernel, out_shape=out_shape, cost_estimate=cost, grid=(kv_...  6.94 us
    pallas_call x1, Pallas kernels, attention(): pl.pallas_call(kernel, out_shape=(jax.ShapeDtypeStruct(q_new.shape, jnp.f...  5.54 us
    ppermute x3, starting transfers between devices, local(): lax.ppermute(own_rows, 'blk', [(i, (i + k) % blocks) for i in range(block...  3.83 us
    gather x1, local copies, waits for them, and re-layouts, local(): sent = kv_cache[by_shift].reshape((blocks, per_peer) + kv_cache.shape[1:])  2.77 us
    ppermute x3, starting transfers between devices, local(): lax.ppermute(own, 'blk', [(i, (i + k) % blocks) for i in range(blocks)])  1.98 us
    ppermute x3, starting transfers between devices, local(): lax.ppermute(sent[k], 'blk', [(i, (i + k) % blocks) for i in range(blocks)])  1.81 us
  transfers between devices with their start and end apart: 9, of which 5 were waited for; matrix products, arithmetic and copies ran while one was open for 21% of the time, Pallas kernels for 9%

profile of v20, /device:TPU:11, one launch (start us, length us, event | category | flops | bytes accessed | tf_op | source)
XLA Modules:
  0.0 62.0 jit_solution(13893703307771123492)
XLA Ops:
  0.0 0.9 %copy.19 = bf16[128,2,256]{2,0,1:T(8,128)(2,1)S(1)} copy(bf16[128,2,256]{2,1,0:T(2,128)(2,1)} %param.6) | data formatting | bytes 262144 | tf_op args[1]
  0.9 1.3 %collective-permute-start = (bf16[2,128,256]{2,1,0:T(8,128)(2,1)S(1)}, bf16[2,128,256]{2,1,0:T(8,128)(2,1)S(1)}, u32[]{:S(2)}, u32[]{:S(2)}) collective-permute-start(bf16[2,128,256]{2,1,0:T(8,128)(2,1)S(1)} %bitcast.53), channel_id=1, source_target_pairs={{0,4},{4,8},{8,12},{12,0},{1,5},{5,9},{9,13},{13,1},{2,6},{6,10},{... | collective-permute-start | bytes 393224 | tf_op jit(solution)/shard_map/ppermute | solution.py:209
  2.3 1.1 %collective-permute-start.1 = (bf16[2,128,256]{2,1,0:T(8,128)(2,1)S(1)}, bf16[2,128,256]{2,1,0:T(8,128)(2,1)S(1)}, u32[]{:S(2)}, u32[]{:S(2)}) collective-permute-start(bf16[2,128,256]{2,1,0:T(8,128)(2,1)S(1)} %bitcast.54), channel_id=1, source_target_pairs={{0,8},{4,12},{8,0},{12,4},{1,9},{5,13},{9,1},{13,5},{2,10},{6,14},... | collective-permute-start | bytes 393224 | tf_op jit(solution)/shard_map/ppermute | solution.py:209
  3.4 1.4 %collective-permute-start.2 = (bf16[2,128,256]{2,1,0:T(8,128)(2,1)S(1)}, bf16[2,128,256]{2,1,0:T(8,128)(2,1)S(1)}, u32[]{:S(2)}, u32[]{:S(2)}) collective-permute-start(bf16[2,128,256]{2,1,0:T(8,128)(2,1)S(1)} %bitcast.55), channel_id=1, source_target_pairs={{0,12},{4,0},{8,4},{12,8},{1,13},{5,1},{9,5},{13,9},{2,14},{6,2},{... | collective-permute-start | bytes 393224 | tf_op jit(solution)/shard_map/ppermute | solution.py:209
  4.8 0.7 %and_select_fusion.5 = s32[8]{0:T(128)S(1)} fusion(s32[8]{0:T(128)} %param.8), kind=kLoop, calls=%fused_computation.41 | loop fusion | flops 88 | bytes 64 | tf_op jit(solution)/shard_map/jit(remainder)/select_n | solution.py:216
  5.4 0.7 %convert_bitcast_fusion.1 = (s32[8,1]{0,1:T(1,128)S(1)}, pred[8]{0:T(512)(128)(4,1)S(1)}, s32[8]{0:T(128)S(1)}) fusion(s32[]{:T(128)S(6)} %axis_index.15, s32[8]{0:T(128)} %param.8), kind=kLoop, calls=%fused_computation.63 | loop fusion | flops 136 | bytes 108 | tf_op jit(solution)/shard_map/convert
  6.1 0.1 convert_reduce_fusion
  6.2 0.2 reduce-window.22
  6.4 0.6 %and_select_fusion = (s32[4]{0:T(128)S(1)}, s32[]{:T(128)}) fusion(s32[]{:T(128)S(6)} %axis_index.15, s32[4]{0:T(128)S(1)} %convert_reduce_fusion, s32[4,1]{0,1:T(1,128)S(1)} %reduce-window.22), kind=kLoop, calls=%fused_computation.35 | loop fusion | flops 63 | bytes 56 | tf_op jit(solution)/shard_map/jit(remainder)/select_n | solution.py:236
  7.1 0.7 %and_select_fusion.6 = s32[4]{0:T(128)S(1)} fusion(s32[]{:T(128)} %get-tuple-element.28), kind=kLoop, calls=%fused_computation.42 | loop fusion | flops 48 | bytes 20 | tf_op jit(solution)/shard_map/jit(remainder)/select_n | solution.py:222
  7.7 0.2 reduce-window.21
  7.9 0.2 select_reduce_fusion
  8.1 0.6 %gather_fusion = s32[4]{0:T(128)S(1)} fusion(s32[4]{0:T(128)S(1)} %select_reduce_fusion, s32[1024]{0:T(1024)S(1)} %pad_clamp_fusion.3), kind=kCustom, calls=%fused_computation | custom fusion | bytes 48 | tf_op jit(solution)/shard_map/gather | solution.py:225
  8.8 0.6 %gather_fusion.2 = pred[4]{0:T(512)(128)(4,1)S(1)} fusion(pred[4]{0:T(512)(128)(4,1)S(1)} %compare_bitcast_fusion, s32[1024]{0:T(1024)S(1)} %pad_clamp_fusion.1), kind=kCustom, calls=%fused_computation.2 | custom fusion | bytes 24 | tf_op jit(solution)/shard_map/gather | solution.py:236
  9.4 0.2 reduce-window.23
  9.6 0.1 fusion.1
  9.7 1.3 %gather_fusion.4 = s32[4]{0:T(128)S(1)} fusion(s32[4]{0:T(128)} %param.9, s32[1024]{0:T(1024)S(1)} %pad_clamp_fusion.1), kind=kCustom, calls=%fused_computation.4 | custom fusion | bytes 48 | tf_op jit(solution)/shard_map/gather | solution.py:211
  11.0 2.8 %gather_fusion.1 = bf16[4,2,128,256]{3,2,1,0:T(8,128)(2,1)S(1)} fusion(bf16[32,2,128,256]{3,2,1,0:T(8,128)(2,1)} %param.7, s32[1024]{0:T(1024)S(1)} %pad_clamp_fusion.2), kind=kCustom, calls=%fused_computation.1 | custom fusion | bytes 1048592 | tf_op jit(solution)/shard_map/gather | solution.py:226
  13.8 0.1 fusion
  13.9 0.0 collective-permute-done
  13.9 0.0 collective-permute-done.1
  13.9 1.8 %collective-permute-done.2 = bf16[2,128,256]{2,1,0:T(8,128)(2,1)S(1)} collective-permute-done((bf16[2,128,256]{2,1,0:T(8,128)(2,1)S(1)}, bf16[2,128,256]{2,1,0:T(8,128)(2,1)S(1)}, u32[]{:S(2)}, u32[]{:S(2)}) %collective-permute-start.2) | collective-permute-done | bytes 131104 | tf_op jit(solution)/shard_map/ppermute | solution.py:209
  15.7 0.1 collective-permute-start.3
  15.8 1.4 %collective-permute-start.4 = (bf16[1,2,128,256]{3,2,1,0:T(8,128)(2,1)S(1)}, bf16[1,2,128,256]{3,2,1,0:T(8,128)(2,1)S(1)}, u32[]{:S(2)}, u32[]{:S(2)}) collective-permute-start(bf16[1,2,128,256]{3,2,1,0:T(8,128)(2,1)S(1)} %get-tuple-element.25), channel_id=1, source_target_pairs={{0,8},{4,12},{8,0},{12,4},{1,9},{5,13},{9,1},{13,5},{2,10},{6,14},... | collective-permute-start | bytes 393224 | tf_op jit(solution)/shard_map/ppermute | solution.py:232
  17.2 0.4 collective-permute-start.5
  17.5 1.3 %fusion.3 = s32[]{:T(128)} fusion(s32[4]{0:T(128)} %param.9, s32[]{:T(128)S(6)} %axis_index.15), kind=kLoop, calls=%fused_computation.51 | loop fusion | flops 11 | bytes 24 | tf_op jit(solution)/shard_map/reduce_sum | solution.py:203
  18.8 0.1 reshape.427
  18.9 0.1 broadcast_in_dim.38
  19.0 0.5 slice.38.page_ok_ref
  19.5 0.6 slice.37.refs_3_
  20.8 0.0 collective-permute-done.3
  20.8 6.1 %collective-permute-done.4 = bf16[1,2,128,256]{3,2,1,0:T(8,128)(2,1)S(1)} collective-permute-done((bf16[1,2,128,256]{3,2,1,0:T(8,128)(2,1)S(1)}, bf16[1,2,128,256]{3,2,1,0:T(8,128)(2,1)S(1)}, u32[]{:S(2)}, u32[]{:S(2)}) %collective-permute-start.4) | collective-permute-done | bytes 131104 | tf_op jit(solution)/shard_map/ppermute | solution.py:232
  26.9 2.6 %collective-permute-done.5 = bf16[1,2,128,256]{3,2,1,0:T(8,128)(2,1)S(1)} collective-permute-done((bf16[1,2,128,256]{3,2,1,0:T(8,128)(2,1)S(1)}, bf16[1,2,128,256]{3,2,1,0:T(8,128)(2,1)S(1)}, u32[]{:S(2)}, u32[]{:S(2)}) %collective-permute-start.5) | collective-permute-done | bytes 131104 | tf_op jit(solution)/shard_map/ppermute | solution.py:232
  29.5 0.1 maximum_bitcast_fusion
  29.6 0.6 gather_fusion.3
  30.2 0.0 copy-start
  30.2 0.1 collective-permute-start.6
  30.3 0.5 collective-permute-start.7
  30.8 1.4 %collective-permute-start.8 = (bf16[2,2,128,256]{3,2,1,0:T(8,128)(2,1)S(1)}, bf16[2,2,128,256]{3,2,1,0:T(8,128)(2,1)S(1)}, u32[]{:S(2)}, u32[]{:S(2)}) collective-permute-start(bf16[2,2,128,256]{3,2,1,0:T(8,128)(2,1)S(1)} %gather_fusion.3), channel_id=1, source_target_pairs={{0,12},{4,0},{8,4},{12,8},{1,13},{5,1},{9,5},{13,9},{2,14},{6,2},{... | collective-permute-start | bytes 786440 | tf_op jit(solution)/shard_map/ppermute | solution.py:246
  32.2 0.6 %iota_add_fusion = s32[4,128]{1,0:T(4,128)} fusion(s32[4]{0:T(128)S(1)} %broadcast_multiply_fusion), kind=kLoop, calls=%fused_computation.29 | loop fusion | flops 512 | bytes 2064 | tf_op jit(solution)/shard_map/add | solution.py:254
  32.8 0.9 %pad_maximum_fusion.new_ref = bf16[4,2,128,256]{3,2,1,0:T(8,128)(2,1)} fusion(bf16[1,2,128,256]{3,2,1,0:T(8,128)(2,1)S(1)} %bitcast.59, bf16[1,2,128,256]{3,2,1,0:T(8,128)(2,1)S(1)} %bitcast.58, bf16[1,2,128,256]{3,2,1,0:T(8,128)(2,1)S(1)} %bitcast.57, bf16[1,2,128,256]{3,2,1,0:T(8,128)(2,1)S(1)} %bitcast.56), kind=kLoop, calls=%fused_computation.6 | loop fusion | flops 786432 | bytes 1048576 | tf_op jit(solution)/shard_map/stack | solution.py:228
  33.7 0.0 copy-done
  33.7 5.5 %shard_map.55 = (f32[128,2048]{1,0:T(8,128)}, f32[2,128,8]{2,1,0:T(8,128)}, f32[2,128,8]{2,1,0:T(8,128)}) custom-call(s32[1]{0:T(128)} %bitcast.24.query_start, bf16[128,2048]{1,0:T(8,128)(2,1)} %q_ref.3, bf16[4,2,128,256]{3,2,1,0:T(8,128)(2,1)} %pad_maximum_fusion.new_ref, bf16[2,2,128,256]{3,2,1,0:T(8,128)(2,1)} %copy-done, s32[1,512]{1,0:T(1,128)} %bitcast.65, ...), custom_call_target="tpu_custom_call" | custom-call | tf_op jit(solution)/shard_map/pallas_call | solution.py:175
  39.2 0.0 collective-permute-done.6.refs_0_
  39.2 0.0 copy-start.1
  39.2 13.4 %collective-permute-done.7.refs_1_ = bf16[2,2,128,256]{3,2,1,0:T(8,128)(2,1)S(1)} collective-permute-done((bf16[2,2,128,256]{3,2,1,0:T(8,128)(2,1)S(1)}, bf16[2,2,128,256]{3,2,1,0:T(8,128)(2,1)S(1)}, u32[]{:S(2)}, u32[]{:S(2)}) %collective-permute-start.7) | collective-permute-done | bytes 262176 | tf_op jit(solution)/shard_map/ppermute | solution.py:246
  52.6 0.0 copy-start.2
  52.6 1.8 %collective-permute-done.8.refs_2_ = bf16[2,2,128,256]{3,2,1,0:T(8,128)(2,1)S(1)} collective-permute-done((bf16[2,2,128,256]{3,2,1,0:T(8,128)(2,1)S(1)}, bf16[2,2,128,256]{3,2,1,0:T(8,128)(2,1)S(1)}, u32[]{:S(2)}, u32[]{:S(2)}) %collective-permute-start.8) | collective-permute-done | bytes 262176 | tf_op jit(solution)/shard_map/ppermute | solution.py:246
  54.4 0.0 copy-start.3
  54.4 0.0 copy-done.1
  54.4 0.0 copy-done.2
  54.4 0.7 %copy-done.3 = bf16[2,2,128,256]{3,2,1,0:T(8,128)(2,1)} copy-done((bf16[2,2,128,256]{3,2,1,0:T(8,128)(2,1)}, bf16[2,2,128,256]{3,2,1,0:T(8,128)(2,1)S(1)}, u32[]{:S(2)}) %copy-start.3) | copy-done | bytes 262168
  55.1 6.9 %shard_map.56 = bf16[128,2048]{1,0:T(8,128)(2,1)} custom-call(bf16[128,2048]{1,0:T(8,128)(2,1)} %q_ref.3, bf16[2,2,128,256]{3,2,1,0:T(8,128)(2,1)} %copy-done.1, bf16[2,2,128,256]{3,2,1,0:T(8,128)(2,1)} %copy-done.2, bf16[2,2,128,256]{3,2,1,0:T(8,128)(2,1)} %copy-done.3, s32[1,768]{1,0:T(1,128)} %slice.37.refs_3_, f32[128,2048]{1,0:T(8,128)} %get-tuple-element.18.refs_4_, ...), custom_call_target="tpu_custom_call" | custom-call | flops 805306368 | bytes 3407872 | tf_op jit(solution)/shard_map/pallas_call | solution.py:146
  (15 shorter events, 0.1 us)
Async XLA Ops:
  0.9 13.0 %collective-permute-start = (bf16[2,128,256]{2,1,0:T(8,128)(2,1)S(1)}, bf16[2,128,256]{2,1,0:T(8,128)(2,1)S(1)}, u32[]{:S(2)}, u32[]{:S(2)}) collective-permute-start(bf16[2,128,256]{2,1,0:T(8,128)(2,1)S(1)} %bitcast.53), channel_id=1, source_target_pairs={{0,4},{4,8},{8,12},{12,0},{1,5},{5,9},{9,13},{13,1},{2,6},{6,10},{... | collective-permute-start | bytes 393224 | tf_op jit(solution)/shard_map/ppermute | solution.py:209
  2.3 11.6 %collective-permute-start.1 = (bf16[2,128,256]{2,1,0:T(8,128)(2,1)S(1)}, bf16[2,128,256]{2,1,0:T(8,128)(2,1)S(1)}, u32[]{:S(2)}, u32[]{:S(2)}) collective-permute-start(bf16[2,128,256]{2,1,0:T(8,128)(2,1)S(1)} %bitcast.54), channel_id=1, source_target_pairs={{0,8},{4,12},{8,0},{12,4},{1,9},{5,13},{9,1},{13,5},{2,10},{6,14},... | collective-permute-start | bytes 393224 | tf_op jit(solution)/shard_map/ppermute | solution.py:209
  3.4 12.3 %collective-permute-start.2 = (bf16[2,128,256]{2,1,0:T(8,128)(2,1)S(1)}, bf16[2,128,256]{2,1,0:T(8,128)(2,1)S(1)}, u32[]{:S(2)}, u32[]{:S(2)}) collective-permute-start(bf16[2,128,256]{2,1,0:T(8,128)(2,1)S(1)} %bitcast.55), channel_id=1, source_target_pairs={{0,12},{4,0},{8,4},{12,8},{1,13},{5,1},{9,5},{13,9},{2,14},{6,2},{... | collective-permute-start | bytes 393224 | tf_op jit(solution)/shard_map/ppermute | solution.py:209
  15.7 5.1 %collective-permute-start.3 = (bf16[1,2,128,256]{3,2,1,0:T(8,128)(2,1)S(1)}, bf16[1,2,128,256]{3,2,1,0:T(8,128)(2,1)S(1)}, u32[]{:S(2)}, u32[]{:S(2)}) collective-permute-start(bf16[1,2,128,256]{3,2,1,0:T(8,128)(2,1)S(1)} %get-tuple-element.26), channel_id=1, source_target_pairs={{0,4},{4,8},{8,12},{12,0},{1,5},{5,9},{9,13},{13,1},{2,6},{6,10},{... | collective-permute-start | bytes 393224 | tf_op jit(solution)/shard_map/ppermute | solution.py:232
  15.8 11.1 %collective-permute-start.4 = (bf16[1,2,128,256]{3,2,1,0:T(8,128)(2,1)S(1)}, bf16[1,2,128,256]{3,2,1,0:T(8,128)(2,1)S(1)}, u32[]{:S(2)}, u32[]{:S(2)}) collective-permute-start(bf16[1,2,128,256]{3,2,1,0:T(8,128)(2,1)S(1)} %get-tuple-element.25), channel_id=1, source_target_pairs={{0,8},{4,12},{8,0},{12,4},{1,9},{5,13},{9,1},{13,5},{2,10},{6,14},... | collective-permute-start | bytes 393224 | tf_op jit(solution)/shard_map/ppermute | solution.py:232
  17.2 12.4 %collective-permute-start.5 = (bf16[1,2,128,256]{3,2,1,0:T(8,128)(2,1)S(1)}, bf16[1,2,128,256]{3,2,1,0:T(8,128)(2,1)S(1)}, u32[]{:S(2)}, u32[]{:S(2)}) collective-permute-start(bf16[1,2,128,256]{3,2,1,0:T(8,128)(2,1)S(1)} %slice_bitcast_fusion.2), channel_id=1, source_target_pairs={{0,12},{4,0},{8,4},{12,8},{1,13},{5,1},{9,5},{13,9},{2,14},{6,2},{... | collective-permute-start | bytes 393224 | tf_op jit(solution)/shard_map/ppermute | solution.py:232
  30.2 3.5 %copy-start = (bf16[2,2,128,256]{3,2,1,0:T(8,128)(2,1)}, bf16[2,2,128,256]{3,2,1,0:T(8,128)(2,1)S(1)}, u32[]{:S(2)}) copy-start(bf16[2,2,128,256]{3,2,1,0:T(8,128)(2,1)S(1)} %gather_fusion.3) | copy-start | bytes 786436
  30.2 9.0 %collective-permute-start.6 = (bf16[2,2,128,256]{3,2,1,0:T(8,128)(2,1)S(1)}, bf16[2,2,128,256]{3,2,1,0:T(8,128)(2,1)S(1)}, u32[]{:S(2)}, u32[]{:S(2)}) collective-permute-start(bf16[2,2,128,256]{3,2,1,0:T(8,128)(2,1)S(1)} %gather_fusion.3), channel_id=1, source_target_pairs={{0,4},{4,8},{8,12},{12,0},{1,5},{5,9},{9,13},{13,1},{2,6},{6,10},{... | collective-permute-start | bytes 786440 | tf_op jit(solution)/shard_map/ppermute | solution.py:246
  30.3 22.3 %collective-permute-start.7 = (bf16[2,2,128,256]{3,2,1,0:T(8,128)(2,1)S(1)}, bf16[2,2,128,256]{3,2,1,0:T(8,128)(2,1)S(1)}, u32[]{:S(2)}, u32[]{:S(2)}) collective-permute-start(bf16[2,2,128,256]{3,2,1,0:T(8,128)(2,1)S(1)} %gather_fusion.3), channel_id=1, source_target_pairs={{0,8},{4,12},{8,0},{12,4},{1,9},{5,13},{9,1},{13,5},{2,10},{6,14},... | collective-permute-start | bytes 786440 | tf_op jit(solution)/shard_map/ppermute | solution.py:246
  30.8 23.6 %collective-permute-start.8 = (bf16[2,2,128,256]{3,2,1,0:T(8,128)(2,1)S(1)}, bf16[2,2,128,256]{3,2,1,0:T(8,128)(2,1)S(1)}, u32[]{:S(2)}, u32[]{:S(2)}) collective-permute-start(bf16[2,2,128,256]{3,2,1,0:T(8,128)(2,1)S(1)} %gather_fusion.3), channel_id=1, source_target_pairs={{0,12},{4,0},{8,4},{12,8},{1,13},{5,1},{9,5},{13,9},{2,14},{6,2},{... | collective-permute-start | bytes 786440 | tf_op jit(solution)/shard_map/ppermute | solution.py:246
  39.2 15.1 %copy-start.1 = (bf16[2,2,128,256]{3,2,1,0:T(8,128)(2,1)}, bf16[2,2,128,256]{3,2,1,0:T(8,128)(2,1)S(1)}, u32[]{:S(2)}) copy-start(bf16[2,2,128,256]{3,2,1,0:T(8,128)(2,1)S(1)} %collective-permute-done.6.refs_0_) | copy-start | bytes 786436
  52.6 1.8 %copy-start.2 = (bf16[2,2,128,256]{3,2,1,0:T(8,128)(2,1)}, bf16[2,2,128,256]{3,2,1,0:T(8,128)(2,1)S(1)}, u32[]{:S(2)}) copy-start(bf16[2,2,128,256]{3,2,1,0:T(8,128)(2,1)S(1)} %collective-permute-done.7.refs_1_) | copy-start | bytes 786436
  54.4 0.7 %copy-start.3 = (bf16[2,2,128,256]{3,2,1,0:T(8,128)(2,1)}, bf16[2,2,128,256]{3,2,1,0:T(8,128)(2,1)S(1)}, u32[]{:S(2)}) copy-start(bf16[2,2,128,256]{3,2,1,0:T(8,128)(2,1)S(1)} %collective-permute-done.8.refs_2_) | copy-start | bytes 786436

commit v21 on v19

--- a/solution.py
+++ b/solution.py
@@ -212,11 +212,14 @@
 
     page_owner = page_table // slots_dev
     owned = page_owner == myself
-    page_rank = jnp.cumsum(owned.astype(jnp.int32)) - 1
+    page_ids = jnp.arange(npages, dtype=jnp.int32)
+    page_rank = jnp.sum(
+        ((page_ids[None, :] < page_ids[:, None]) & owned[None, :]).astype(jnp.int32), axis=1
+    )
     local_slot = page_table % slots_dev
     counts = jnp.sum((page_owner[None, :] == block_ids[:, None]).astype(jnp.int32), axis=1)
     per_peer = (CAP + blocks - 1) // blocks
-    starts = jnp.cumsum(counts) - counts
+    starts = jnp.sum((page_owner[None, :] < block_ids[:, None]).astype(jnp.int32), axis=1)
     my_start = jnp.sum(jnp.where(block_ids == myself, starts, 0))
     peer_slots = jnp.arange(per_peer, dtype=jnp.int32)[None, :]
     wanted = (block_ids[:, None] - my_start) % blocks + peer_slots * blocks
@@ -234,7 +237,10 @@
     received = jnp.stack(arrived).reshape((blocks * per_peer,) + kv_cache.shape[1:])
     arriving = (myself - starts[:, None]) % blocks + peer_slots * blocks
     present = (arriving < counts[:, None])[(myself - block_ids) % blocks].reshape(-1)
-    order_rank = jnp.cumsum(present.astype(jnp.int32)) - 1
+    chunk_ids = jnp.arange(blocks * per_peer, dtype=jnp.int32)
+    order_rank = jnp.sum(
+        ((chunk_ids[None, :] < chunk_ids[:, None]) & present[None, :]).astype(jnp.int32), axis=1
+    )
     choose = present[None, :] & (order_rank[None, :] == jnp.arange(pg, dtype=jnp.int32)[:, None])
     positions = jnp.sum(
         jnp.where(choose, jnp.arange(blocks * per_peer, dtype=jnp.int32)[None, :], 0), axis=1

time: 61.8 us -> 61.5 us (level)
  the two profiles are of different devices: /device:TPU:15 before, /device:TPU:9 now
where the time goes in v21:
time: 61.5 us; the launch traced here: 61.2 us
  waiting for transfers between devices  19.4 us (32%)
  Pallas kernels  18.4 us (30%)
  local copies, waits for them, and re-layouts  9.62 us (16%)
  starting transfers between devices  7.25 us (12%)
  other arithmetic  5.67 us (9%)
  between operations  0.8 us (1%)
    pallas_call x2, Pallas kernels, prefix_part(): pl.pallas_call(kernel, out_shape=out_shape, cost_estimate=cost, grid=(kv_...  12.9 us
    ppermute x3, waiting for transfers between devices, local(): lax.ppermute(sent[k], 'blk', [(i, (i + k) % blocks) for i in range(blocks)])  12.4 us
    ppermute x3, waiting for transfers between devices, local(): lax.ppermute(own, 'blk', [(i, (i + k) % blocks) for i in range(blocks)])  5.76 us
    pallas_call x1, Pallas kernels, attention(): pl.pallas_call(kernel, out_shape=(jax.ShapeDtypeStruct(q_new.shape, jnp.f...  5.54 us
    ppermute x3, starting transfers between devices, local(): lax.ppermute(own_rows, 'blk', [(i, (i + k) % blocks) for i in range(block...  3.83 us
    gather x1, local copies, waits for them, and re-layouts, local(): sent = kv_cache[by_shift].reshape((blocks, per_peer) + kv_cache.shape[1:])  2.77 us
    unnamed x11, local copies, waits for them, and re-layouts  2.34 us
    ppermute x3, starting transfers between devices, local(): lax.ppermute(sent[k], 'blk', [(i, (i + k) % blocks) for i in range(blocks)])  1.91 us
  transfers between devices with their start and end apart: 9, of which 6 were waited for; matrix products, arithmetic and copies ran while one was open for 20% of the time, Pallas kernels for 21%

profile of v21, /device:TPU:9, one launch (start us, length us, event | category | flops | bytes accessed | tf_op | source)
XLA Modules:
  0.0 61.2 jit_solution(13352278541766638289)
XLA Ops:
  0.0 0.0 copy-start
  0.0 0.9 %copy.19 = bf16[128,2,256]{2,0,1:T(8,128)(2,1)S(1)} copy(bf16[128,2,256]{2,1,0:T(2,128)(2,1)} %param.6) | data formatting | bytes 262144 | tf_op args[1]
  0.9 1.3 %collective-permute-start = (bf16[2,128,256]{2,1,0:T(8,128)(2,1)S(1)}, bf16[2,128,256]{2,1,0:T(8,128)(2,1)S(1)}, u32[]{:S(2)}, u32[]{:S(2)}) collective-permute-start(bf16[2,128,256]{2,1,0:T(8,128)(2,1)S(1)} %bitcast.43), channel_id=1, source_target_pairs={{0,4},{4,8},{8,12},{12,0},{1,5},{5,9},{9,13},{13,1},{2,6},{6,10},{... | collective-permute-start | bytes 393224 | tf_op jit(solution)/shard_map/ppermute | solution.py:209
  2.3 1.1 %collective-permute-start.1 = (bf16[2,128,256]{2,1,0:T(8,128)(2,1)S(1)}, bf16[2,128,256]{2,1,0:T(8,128)(2,1)S(1)}, u32[]{:S(2)}, u32[]{:S(2)}) collective-permute-start(bf16[2,128,256]{2,1,0:T(8,128)(2,1)S(1)} %bitcast.44), channel_id=1, source_target_pairs={{0,8},{4,12},{8,0},{12,4},{1,9},{5,13},{9,1},{13,5},{2,10},{6,14},... | collective-permute-start | bytes 393224 | tf_op jit(solution)/shard_map/ppermute | solution.py:209
  3.4 1.4 %collective-permute-start.2 = (bf16[2,128,256]{2,1,0:T(8,128)(2,1)S(1)}, bf16[2,128,256]{2,1,0:T(8,128)(2,1)S(1)}, u32[]{:S(2)}, u32[]{:S(2)}) collective-permute-start(bf16[2,128,256]{2,1,0:T(8,128)(2,1)S(1)} %bitcast.45), channel_id=1, source_target_pairs={{0,12},{4,0},{8,4},{12,8},{1,13},{5,1},{9,5},{13,9},{2,14},{6,2},{... | collective-permute-start | bytes 393224 | tf_op jit(solution)/shard_map/ppermute | solution.py:209
  4.8 0.7 %and_select_fusion.5 = s32[8]{0:T(128)S(1)} fusion(s32[8]{0:T(128)} %param.8), kind=kLoop, calls=%fused_computation.49 | loop fusion | flops 88 | bytes 64 | tf_op jit(solution)/shard_map/jit(remainder)/select_n | solution.py:219
  5.4 0.7 %broadcast_compare_fusion = (pred[8]{0:T(512)(128)(4,1)S(1)}, s32[8]{0:T(128)S(1)}) fusion(s32[]{:T(128)S(6)} %axis_index.15, s32[8]{0:T(128)} %param.8), kind=kLoop, calls=%fused_computation.71 | loop fusion | flops 128 | bytes 76 | tf_op jit(solution)/shard_map/eq | solution.py:214
  6.1 0.1 convert_reduce_fusion.2
  6.3 0.6 %and_select_fusion = (s32[4]{0:T(128)S(1)}, s32[]{:T(128)}) fusion(s32[]{:T(128)S(6)} %axis_index.15, s32[4]{0:T(128)S(1)} %get-tuple-element.38), kind=kLoop, calls=%fused_computation.43 | loop fusion | flops 59 | bytes 40 | tf_op jit(solution)/shard_map/jit(remainder)/select_n | solution.py:239
  6.9 0.7 %and_select_fusion.6 = s32[4]{0:T(128)S(1)} fusion(s32[]{:T(128)} %get-tuple-element.47), kind=kLoop, calls=%fused_computation.50 | loop fusion | flops 48 | bytes 20 | tf_op jit(solution)/shard_map/jit(remainder)/select_n | solution.py:225
  7.6 0.1 convert_reduce_fusion
  7.7 0.2 select_reduce_fusion
  7.9 0.6 %gather_fusion = s32[4]{0:T(128)S(1)} fusion(s32[4]{0:T(128)S(1)} %select_reduce_fusion, s32[1024]{0:T(1024)S(1)} %pad_clamp_fusion.3), kind=kCustom, calls=%fused_computation | custom fusion | bytes 48 | tf_op jit(solution)/shard_map/gather | solution.py:228
  8.6 0.6 %gather_fusion.2 = pred[4]{0:T(512)(128)(4,1)S(1)} fusion(pred[4]{0:T(512)(128)(4,1)S(1)} %compare_bitcast_fusion, s32[1024]{0:T(1024)S(1)} %pad_clamp_fusion.1), kind=kCustom, calls=%fused_computation.2 | custom fusion | bytes 24 | tf_op jit(solution)/shard_map/gather | solution.py:239
  9.2 0.1 convert_reduce_fusion.1
  9.3 0.1 fusion.3
  9.4 0.1 fusion.1
  9.5 0.1 reshape.360
  9.6 0.1 broadcast_in_dim.34
  9.7 0.6 fusion.16
  10.3 1.3 %gather_fusion.4 = s32[4]{0:T(128)S(1)} fusion(s32[4]{0:T(128)} %param.9, s32[1024]{0:T(1024)S(1)} %pad_clamp_fusion.1), kind=kCustom, calls=%fused_computation.4 | custom fusion | bytes 48 | tf_op jit(solution)/shard_map/gather | solution.py:211
  11.6 2.8 %gather_fusion.1 = bf16[4,2,128,256]{3,2,1,0:T(8,128)(2,1)S(1)} fusion(bf16[32,2,128,256]{3,2,1,0:T(8,128)(2,1)} %param.7, s32[1024]{0:T(1024)S(1)} %pad_clamp_fusion.2), kind=kCustom, calls=%fused_computation.1 | custom fusion | bytes 1048592 | tf_op jit(solution)/shard_map/gather | solution.py:229
  14.4 0.0 collective-permute-done
  14.4 0.0 collective-permute-done.1
  14.4 1.3 %collective-permute-done.2 = bf16[2,128,256]{2,1,0:T(8,128)(2,1)S(1)} collective-permute-done((bf16[2,128,256]{2,1,0:T(8,128)(2,1)S(1)}, bf16[2,128,256]{2,1,0:T(8,128)(2,1)S(1)}, u32[]{:S(2)}, u32[]{:S(2)}) %collective-permute-start.2) | collective-permute-done | bytes 131104 | tf_op jit(solution)/shard_map/ppermute | solution.py:209
  15.7 0.1 collective-permute-start.3
  15.8 1.8 %collective-permute-start.4 = (bf16[1,2,128,256]{3,2,1,0:T(8,128)(2,1)S(1)}, bf16[1,2,128,256]{3,2,1,0:T(8,128)(2,1)S(1)}, u32[]{:S(2)}, u32[]{:S(2)}) collective-permute-start(bf16[1,2,128,256]{3,2,1,0:T(8,128)(2,1)S(1)} %get-tuple-element.42), channel_id=1, source_target_pairs={{0,8},{4,12},{8,0},{12,4},{1,9},{5,13},{9,1},{13,5},{2,10},{6,14},... | collective-permute-start | bytes 393224 | tf_op jit(solution)/shard_map/ppermute | solution.py:235
  17.6 0.0 collective-permute-start.5
  17.7 2.7 %collective-permute-done.3 = bf16[1,2,128,256]{3,2,1,0:T(8,128)(2,1)S(1)} collective-permute-done((bf16[1,2,128,256]{3,2,1,0:T(8,128)(2,1)S(1)}, bf16[1,2,128,256]{3,2,1,0:T(8,128)(2,1)S(1)}, u32[]{:S(2)}, u32[]{:S(2)}) %collective-permute-start.3) | collective-permute-done | bytes 131104 | tf_op jit(solution)/shard_map/ppermute | solution.py:235
  20.4 6.2 %collective-permute-done.4 = bf16[1,2,128,256]{3,2,1,0:T(8,128)(2,1)S(1)} collective-permute-done((bf16[1,2,128,256]{3,2,1,0:T(8,128)(2,1)S(1)}, bf16[1,2,128,256]{3,2,1,0:T(8,128)(2,1)S(1)}, u32[]{:S(2)}, u32[]{:S(2)}) %collective-permute-start.4) | collective-permute-done | bytes 131104 | tf_op jit(solution)/shard_map/ppermute | solution.py:235
  26.6 3.5 %collective-permute-done.5 = bf16[1,2,128,256]{3,2,1,0:T(8,128)(2,1)S(1)} collective-permute-done((bf16[1,2,128,256]{3,2,1,0:T(8,128)(2,1)S(1)}, bf16[1,2,128,256]{3,2,1,0:T(8,128)(2,1)S(1)}, u32[]{:S(2)}, u32[]{:S(2)}) %collective-permute-start.5) | collective-permute-done | bytes 131104 | tf_op jit(solution)/shard_map/ppermute | solution.py:235
  30.0 0.1 maximum_bitcast_fusion
  30.1 0.6 gather_fusion.3
  30.7 0.0 copy-start.1
  30.7 0.1 collective-permute-start.6
  30.7 0.7 %iota_add_fusion = s32[4,128]{1,0:T(4,128)} fusion(s32[4]{0:T(128)S(1)} %broadcast_multiply_fusion), kind=kLoop, calls=%fused_computation.32 | loop fusion | flops 512 | bytes 2064 | tf_op jit(solution)/shard_map/add | solution.py:260
  31.4 0.6 slice.43.refs_2_
  32.0 0.4 collective-permute-start.7
  32.4 1.0 %collective-permute-start.8 = (bf16[2,2,128,256]{3,2,1,0:T(8,128)(2,1)S(1)}, bf16[2,2,128,256]{3,2,1,0:T(8,128)(2,1)S(1)}, u32[]{:S(2)}, u32[]{:S(2)}) collective-permute-start(bf16[2,2,128,256]{3,2,1,0:T(8,128)(2,1)S(1)} %gather_fusion.3), channel_id=1, source_target_pairs={{0,12},{4,0},{8,4},{12,8},{1,13},{5,1},{9,5},{13,9},{2,14},{6,2},{... | collective-permute-start | bytes 786440 | tf_op jit(solution)/shard_map/ppermute | solution.py:252
  33.4 0.0 copy-done
  33.4 0.6 %fusion.5 = s32[]{:T(128)} fusion(s32[4]{0:T(128)S(1)} %copy-done, s32[]{:T(128)S(6)} %axis_index.15), kind=kLoop, calls=%fused_computation.59 | loop fusion | flops 11 | bytes 24 | tf_op jit(solution)/shard_map/reduce_sum | solution.py:203
  34.7 0.9 %pad_maximum_fusion.new_ref = bf16[4,2,128,256]{3,2,1,0:T(8,128)(2,1)} fusion(bf16[1,2,128,256]{3,2,1,0:T(8,128)(2,1)S(1)} %bitcast.49, bf16[1,2,128,256]{3,2,1,0:T(8,128)(2,1)S(1)} %bitcast.48, bf16[1,2,128,256]{3,2,1,0:T(8,128)(2,1)S(1)} %bitcast.47, bf16[1,2,128,256]{3,2,1,0:T(8,128)(2,1)S(1)} %bitcast.46), kind=kLoop, calls=%fused_computation.6 | loop fusion | flops 786432 | bytes 1048576 | tf_op jit(solution)/shard_map/stack | solution.py:231
  35.6 0.0 copy-done.1
  35.6 5.5 %shard_map.55 = (f32[128,2048]{1,0:T(8,128)}, f32[2,128,8]{2,1,0:T(8,128)}, f32[2,128,8]{2,1,0:T(8,128)}) custom-call(s32[1]{0:T(128)} %bitcast.20.query_start, bf16[128,2048]{1,0:T(8,128)(2,1)} %q_ref.5, bf16[4,2,128,256]{3,2,1,0:T(8,128)(2,1)} %pad_maximum_fusion.new_ref, bf16[2,2,128,256]{3,2,1,0:T(8,128)(2,1)} %copy-done.1, s32[1,512]{1,0:T(1,128)} %bitcast.55, ...), custom_call_target="tpu_custom_call" | custom-call | tf_op jit(solution)/shard_map/pallas_call | solution.py:175
  41.1 0.0 collective-permute-done.6.refs_0_
  41.1 0.0 copy-start.4
  41.2 0.7 %copy-done.4 = bf16[2,2,128,256]{3,2,1,0:T(8,128)(2,1)} copy-done((bf16[2,2,128,256]{3,2,1,0:T(8,128)(2,1)}, bf16[2,2,128,256]{3,2,1,0:T(8,128)(2,1)S(1)}, u32[]{:S(2)}) %copy-start.4) | copy-done | bytes 262168
  41.8 7.2 %shard_map.56 = (f32[128,2048]{1,0:T(8,128)}, f32[2,128,8]{2,1,0:T(8,128)}, f32[2,128,8]{2,1,0:T(8,128)}) custom-call(bf16[128,2048]{1,0:T(8,128)(2,1)} %q_ref.5, bf16[2,2,128,256]{3,2,1,0:T(8,128)(2,1)} %copy-done.4, s32[1,256]{1,0:T(1,128)} %get-tuple-element.45.refs_1_, f32[128,2048]{1,0:T(8,128)} %get-tuple-element.26.refs_2_, ...), custom_call_target="tpu_custom_call" | custom-call | flops 268435456 | bytes 2883584 | tf_op jit(solution)/shard_map/pallas_call | solution.py:146
  49.1 4.0 %collective-permute-done.7.refs_0_ = bf16[2,2,128,256]{3,2,1,0:T(8,128)(2,1)S(1)} collective-permute-done((bf16[2,2,128,256]{3,2,1,0:T(8,128)(2,1)S(1)}, bf16[2,2,128,256]{3,2,1,0:T(8,128)(2,1)S(1)}, u32[]{:S(2)}, u32[]{:S(2)}) %collective-permute-start.7) | collective-permute-done | bytes 262176 | tf_op jit(solution)/shard_map/ppermute | solution.py:252
  53.1 0.0 copy-start.2
  53.1 1.8 %collective-permute-done.8.refs_1_ = bf16[2,2,128,256]{3,2,1,0:T(8,128)(2,1)S(1)} collective-permute-done((bf16[2,2,128,256]{3,2,1,0:T(8,128)(2,1)S(1)}, bf16[2,2,128,256]{3,2,1,0:T(8,128)(2,1)S(1)}, u32[]{:S(2)}, u32[]{:S(2)}) %collective-permute-start.8) | collective-permute-done | bytes 262176 | tf_op jit(solution)/shard_map/ppermute | solution.py:252
  54.9 0.0 copy-start.3
  54.9 0.0 copy-done.2
  54.9 0.7 %copy-done.3 = bf16[2,2,128,256]{3,2,1,0:T(8,128)(2,1)} copy-done((bf16[2,2,128,256]{3,2,1,0:T(8,128)(2,1)}, bf16[2,2,128,256]{3,2,1,0:T(8,128)(2,1)S(1)}, u32[]{:S(2)}) %copy-start.3) | copy-done | bytes 262168
  55.6 5.6 %shard_map.57 = bf16[128,2048]{1,0:T(8,128)(2,1)} custom-call(bf16[128,2048]{1,0:T(8,128)(2,1)} %q_ref.5, bf16[2,2,128,256]{3,2,1,0:T(8,128)(2,1)} %copy-done.2, bf16[2,2,128,256]{3,2,1,0:T(8,128)(2,1)} %copy-done.3, s32[1,512]{1,0:T(1,128)} %slice.43.refs_2_, f32[128,2048]{1,0:T(8,128)} %get-tuple-element.34.refs_3_, ...), custom_call_target="tpu_custom_call" | custom-call | flops 536870912 | bytes 3145728 | tf_op jit(solution)/shard_map/pallas_call | solution.py:146
  (12 shorter events, 0.1 us)
Async XLA Ops:
  0.0 33.4 %copy-start = (s32[4]{0:T(128)S(1)}, s32[4]{0:T(128)}, u32[]{:S(2)}) copy-start(s32[4]{0:T(128)} %param.9) | copy-start | bytes 52
  0.9 13.4 %collective-permute-start = (bf16[2,128,256]{2,1,0:T(8,128)(2,1)S(1)}, bf16[2,128,256]{2,1,0:T(8,128)(2,1)S(1)}, u32[]{:S(2)}, u32[]{:S(2)}) collective-permute-start(bf16[2,128,256]{2,1,0:T(8,128)(2,1)S(1)} %bitcast.43), channel_id=1, source_target_pairs={{0,4},{4,8},{8,12},{12,0},{1,5},{5,9},{9,13},{13,1},{2,6},{6,10},{... | collective-permute-start | bytes 393224 | tf_op jit(solution)/shard_map/ppermute | solution.py:209
  2.3 12.1 %collective-permute-start.1 = (bf16[2,128,256]{2,1,0:T(8,128)(2,1)S(1)}, bf16[2,128,256]{2,1,0:T(8,128)(2,1)S(1)}, u32[]{:S(2)}, u32[]{:S(2)}) collective-permute-start(bf16[2,128,256]{2,1,0:T(8,128)(2,1)S(1)} %bitcast.44), channel_id=1, source_target_pairs={{0,8},{4,12},{8,0},{12,4},{1,9},{5,13},{9,1},{13,5},{2,10},{6,14},... | collective-permute-start | bytes 393224 | tf_op jit(solution)/shard_map/ppermute | solution.py:209
  3.4 12.3 %collective-permute-start.2 = (bf16[2,128,256]{2,1,0:T(8,128)(2,1)S(1)}, bf16[2,128,256]{2,1,0:T(8,128)(2,1)S(1)}, u32[]{:S(2)}, u32[]{:S(2)}) collective-permute-start(bf16[2,128,256]{2,1,0:T(8,128)(2,1)S(1)} %bitcast.45), channel_id=1, source_target_pairs={{0,12},{4,0},{8,4},{12,8},{1,13},{5,1},{9,5},{13,9},{2,14},{6,2},{... | collective-permute-start | bytes 393224 | tf_op jit(solution)/shard_map/ppermute | solution.py:209
  15.7 4.6 %collective-permute-start.3 = (bf16[1,2,128,256]{3,2,1,0:T(8,128)(2,1)S(1)}, bf16[1,2,128,256]{3,2,1,0:T(8,128)(2,1)S(1)}, u32[]{:S(2)}, u32[]{:S(2)}) collective-permute-start(bf16[1,2,128,256]{3,2,1,0:T(8,128)(2,1)S(1)} %get-tuple-element.43), channel_id=1, source_target_pairs={{0,4},{4,8},{8,12},{12,0},{1,5},{5,9},{9,13},{13,1},{2,6},{6,10},{... | collective-permute-start | bytes 393224 | tf_op jit(solution)/shard_map/ppermute | solution.py:235
  15.8 10.8 %collective-permute-start.4 = (bf16[1,2,128,256]{3,2,1,0:T(8,128)(2,1)S(1)}, bf16[1,2,128,256]{3,2,1,0:T(8,128)(2,1)S(1)}, u32[]{:S(2)}, u32[]{:S(2)}) collective-permute-start(bf16[1,2,128,256]{3,2,1,0:T(8,128)(2,1)S(1)} %get-tuple-element.42), channel_id=1, source_target_pairs={{0,8},{4,12},{8,0},{12,4},{1,9},{5,13},{9,1},{13,5},{2,10},{6,14},... | collective-permute-start | bytes 393224 | tf_op jit(solution)/shard_map/ppermute | solution.py:235
  17.6 12.4 %collective-permute-start.5 = (bf16[1,2,128,256]{3,2,1,0:T(8,128)(2,1)S(1)}, bf16[1,2,128,256]{3,2,1,0:T(8,128)(2,1)S(1)}, u32[]{:S(2)}, u32[]{:S(2)}) collective-permute-start(bf16[1,2,128,256]{3,2,1,0:T(8,128)(2,1)S(1)} %slice_bitcast_fusion.2), channel_id=1, source_target_pairs={{0,12},{4,0},{8,4},{12,8},{1,13},{5,1},{9,5},{13,9},{2,14},{6,2},{... | collective-permute-start | bytes 393224 | tf_op jit(solution)/shard_map/ppermute | solution.py:235
  30.7 4.9 %copy-start.1 = (bf16[2,2,128,256]{3,2,1,0:T(8,128)(2,1)}, bf16[2,2,128,256]{3,2,1,0:T(8,128)(2,1)S(1)}, u32[]{:S(2)}) copy-start(bf16[2,2,128,256]{3,2,1,0:T(8,128)(2,1)S(1)} %gather_fusion.3) | copy-start | bytes 786436
  30.7 10.5 %collective-permute-start.6 = (bf16[2,2,128,256]{3,2,1,0:T(8,128)(2,1)S(1)}, bf16[2,2,128,256]{3,2,1,0:T(8,128)(2,1)S(1)}, u32[]{:S(2)}, u32[]{:S(2)}) collective-permute-start(bf16[2,2,128,256]{3,2,1,0:T(8,128)(2,1)S(1)} %gather_fusion.3), channel_id=1, source_target_pairs={{0,4},{4,8},{8,12},{12,0},{1,5},{5,9},{9,13},{13,1},{2,6},{6,10},{... | collective-permute-start | bytes 786440 | tf_op jit(solution)/shard_map/ppermute | solution.py:252
  32.0 21.1 %collective-permute-start.7 = (bf16[2,2,128,256]{3,2,1,0:T(8,128)(2,1)S(1)}, bf16[2,2,128,256]{3,2,1,0:T(8,128)(2,1)S(1)}, u32[]{:S(2)}, u32[]{:S(2)}) collective-permute-start(bf16[2,2,128,256]{3,2,1,0:T(8,128)(2,1)S(1)} %gather_fusion.3), channel_id=1, source_target_pairs={{0,8},{4,12},{8,0},{12,4},{1,9},{5,13},{9,1},{13,5},{2,10},{6,14},... | collective-permute-start | bytes 786440 | tf_op jit(solution)/shard_map/ppermute | solution.py:252
  32.4 22.4 %collective-permute-start.8 = (bf16[2,2,128,256]{3,2,1,0:T(8,128)(2,1)S(1)}, bf16[2,2,128,256]{3,2,1,0:T(8,128)(2,1)S(1)}, u32[]{:S(2)}, u32[]{:S(2)}) collective-permute-start(bf16[2,2,128,256]{3,2,1,0:T(8,128)(2,1)S(1)} %gather_fusion.3), channel_id=1, source_target_pairs={{0,12},{4,0},{8,4},{12,8},{1,13},{5,1},{9,5},{13,9},{2,14},{6,2},{... | collective-permute-start | bytes 786440 | tf_op jit(solution)/shard_map/ppermute | solution.py:252
  41.1 0.7 %copy-start.4 = (bf16[2,2,128,256]{3,2,1,0:T(8,128)(2,1)}, bf16[2,2,128,256]{3,2,1,0:T(8,128)(2,1)S(1)}, u32[]{:S(2)}) copy-start(bf16[2,2,128,256]{3,2,1,0:T(8,128)(2,1)S(1)} %collective-permute-done.6.refs_0_) | copy-start | bytes 786436
  53.1 1.8 %copy-start.2 = (bf16[2,2,128,256]{3,2,1,0:T(8,128)(2,1)}, bf16[2,2,128,256]{3,2,1,0:T(8,128)(2,1)S(1)}, u32[]{:S(2)}) copy-start(bf16[2,2,128,256]{3,2,1,0:T(8,128)(2,1)S(1)} %collective-permute-done.7.refs_0_) | copy-start | bytes 786436
  54.9 0.7 %copy-start.3 = (bf16[2,2,128,256]{3,2,1,0:T(8,128)(2,1)}, bf16[2,2,128,256]{3,2,1,0:T(8,128)(2,1)S(1)}, u32[]{:S(2)}) copy-start(bf16[2,2,128,256]{3,2,1,0:T(8,128)(2,1)S(1)} %collective-permute-done.8.refs_1_) | copy-start | bytes 786436

commit v22 on v21

--- a/solution.py
+++ b/solution.py
@@ -84,13 +84,29 @@
     dims = (((1,), (1,)), ((), ()))
     pv = (((1,), (0,)), ((), ()))
     stack = 2 if group_size % 2 == 0 else 1
-    for c in range(group_size // stack):
+    pair_steps = final and q_ref.shape[1] == stack * head_size
+    for c in range(1 if pair_steps else group_size // stack):
         heads = range(c * stack, (c + 1) * stack)
+        if pair_steps:
+            first = pl.program_id(1) * stack
+            lane = lax.broadcasted_iota(jnp.int32, top_ref.shape[1:], 1)
+
+            def pick(ref, j):
+                return jnp.max(
+                    jnp.where(lane == first + j, ref[0], -jnp.inf), axis=1, keepdims=True
+                )
+
+            top_prev = jnp.concatenate([pick(top_ref, j) for j in range(stack)], axis=0)
+            total_prev = jnp.concatenate([pick(total_ref, j) for j in range(stack)], axis=0)
+            heads = range(stack)
         queries = jnp.concatenate(
             [q_ref[:, h * head_size : (h + 1) * head_size] for h in heads], axis=0
         )
-        top_prev = jnp.concatenate([top_ref[0, :, h : h + 1] for h in heads], axis=0)
-        total_prev = jnp.concatenate([total_ref[0, :, h : h + 1] for h in heads], axis=0)
+        if not pair_steps:
+            top_prev = jnp.concatenate([top_ref[0, :, h : h + 1] for h in heads], axis=0)
+            total_prev = jnp.concatenate(
+                [total_ref[0, :, h : h + 1] for h in heads], axis=0
+            )
         acc_prev = jnp.concatenate(
             [acc_ref[:, h * head_size : (h + 1) * head_size] for h in heads], axis=0
         )
@@ -143,6 +159,26 @@
         transcendentals=rows * keys,
         bytes_accessed=q_new.size * 2 + npage * kv_heads * page_len * width * 2 + acc.size * 8,
     )
+    stack = 2 if group_size % 2 == 0 else 1
+    if final:
+        pairs = group_size // stack
+        part = pl.BlockSpec((q_rows, stack * head_size), lambda g, c: (0, g * pairs + c))
+        return pl.pallas_call(
+            kernel,
+            out_shape=out_shape,
+            cost_estimate=cost,
+            grid=(kv_heads, pairs),
+            in_specs=[
+                part,
+                *[pl.BlockSpec((part_pages, 1, page_len, width), lambda g, c: (0, g, 0, 0))]
+                * len(page_list),
+                pl.BlockSpec((1, npage * page_len), lambda g, c: (0, 0)),
+                part,
+                pl.BlockSpec((1, q_rows, group_size), lambda g, c: (g, 0, 0)),
+                pl.BlockSpec((1, q_rows, group_size), lambda g, c: (g, 0, 0)),
+            ],
+            out_specs=part,
+        )(q_new, *page_list, page_ok, acc, top, total)
     return pl.pallas_call(
         kernel,
         out_shape=out_shape,

time: 61.5 us -> 63.8 us (1.037)
  the two profiles are of different devices: /device:TPU:9 before, /device:TPU:15 now
where the time goes in v22:
time: 63.8 us; the launch traced here: 63.4 us
  Pallas kernels  20.7 us (32%)
  waiting for transfers between devices  19.4 us (30%)
  local copies, waits for them, and re-layouts  9.62 us (15%)
  starting transfers between devices  7.25 us (11%)
  other arithmetic  5.67 us (9%)
  between operations  0.8 us (1%)
    pallas_call x2, Pallas kernels, prefix_part(): pl.pallas_call(kernel, out_shape=out_shape, cost_estimate=cost, grid=(kv_...  15.1 us
    ppermute x3, waiting for transfers between devices, local(): lax.ppermute(sent[k], 'blk', [(i, (i + k) % blocks) for i in range(blocks)])  12.4 us
    ppermute x3, waiting for transfers between devices, local(): lax.ppermute(own, 'blk', [(i, (i + k) % blocks) for i in range(blocks)])  5.75 us
    pallas_call x1, Pallas kernels, attention(): pl.pallas_call(kernel, out_shape=(jax.ShapeDtypeStruct(q_new.shape, jnp.f...  5.55 us
    ppermute x3, starting transfers between devices, local(): lax.ppermute(own_rows, 'blk', [(i, (i + k) % blocks) for i in range(block...  3.83 us
    gather x1, local copies, waits for them, and re-layouts, local(): sent = kv_cache[by_shift].reshape((blocks, per_peer) + kv_cache.shape[1:])  2.77 us
    unnamed x11, local copies, waits for them, and re-layouts  2.34 us
    ppermute x3, starting transfers between devices, local(): lax.ppermute(sent[k], 'blk', [(i, (i + k) % blocks) for i in range(blocks)])  1.91 us
  transfers between devices with their start and end apart: 9, of which 6 were waited for; matrix products, arithmetic and copies ran while one was open for 19% of the time, Pallas kernels for 20%

profile of v22, /device:TPU:15, one launch (start us, length us, event | category | flops | bytes accessed | tf_op | source)
XLA Modules:
  0.0 63.4 jit_solution(5188898693514353887)
XLA Ops:
  0.0 0.0 copy-start
  0.0 0.9 %copy.19 = bf16[128,2,256]{2,0,1:T(8,128)(2,1)S(1)} copy(bf16[128,2,256]{2,1,0:T(2,128)(2,1)} %param.6) | data formatting | bytes 262144 | tf_op args[1]
  0.9 1.3 %collective-permute-start = (bf16[2,128,256]{2,1,0:T(8,128)(2,1)S(1)}, bf16[2,128,256]{2,1,0:T(8,128)(2,1)S(1)}, u32[]{:S(2)}, u32[]{:S(2)}) collective-permute-start(bf16[2,128,256]{2,1,0:T(8,128)(2,1)S(1)} %bitcast.43), channel_id=1, source_target_pairs={{0,4},{4,8},{8,12},{12,0},{1,5},{5,9},{9,13},{13,1},{2,6},{6,10},{... | collective-permute-start | bytes 393224 | tf_op jit(solution)/shard_map/ppermute | solution.py:245
  2.3 1.1 %collective-permute-start.1 = (bf16[2,128,256]{2,1,0:T(8,128)(2,1)S(1)}, bf16[2,128,256]{2,1,0:T(8,128)(2,1)S(1)}, u32[]{:S(2)}, u32[]{:S(2)}) collective-permute-start(bf16[2,128,256]{2,1,0:T(8,128)(2,1)S(1)} %bitcast.44), channel_id=1, source_target_pairs={{0,8},{4,12},{8,0},{12,4},{1,9},{5,13},{9,1},{13,5},{2,10},{6,14},... | collective-permute-start | bytes 393224 | tf_op jit(solution)/shard_map/ppermute | solution.py:245
  3.4 1.4 %collective-permute-start.2 = (bf16[2,128,256]{2,1,0:T(8,128)(2,1)S(1)}, bf16[2,128,256]{2,1,0:T(8,128)(2,1)S(1)}, u32[]{:S(2)}, u32[]{:S(2)}) collective-permute-start(bf16[2,128,256]{2,1,0:T(8,128)(2,1)S(1)} %bitcast.45), channel_id=1, source_target_pairs={{0,12},{4,0},{8,4},{12,8},{1,13},{5,1},{9,5},{13,9},{2,14},{6,2},{... | collective-permute-start | bytes 393224 | tf_op jit(solution)/shard_map/ppermute | solution.py:245
  4.8 0.7 %and_select_fusion.5 = s32[8]{0:T(128)S(1)} fusion(s32[8]{0:T(128)} %param.8), kind=kLoop, calls=%fused_computation.49 | loop fusion | flops 88 | bytes 64 | tf_op jit(solution)/shard_map/jit(remainder)/select_n | solution.py:255
  5.4 0.7 %broadcast_compare_fusion = (pred[8]{0:T(512)(128)(4,1)S(1)}, s32[8]{0:T(128)S(1)}) fusion(s32[]{:T(128)S(6)} %axis_index.15, s32[8]{0:T(128)} %param.8), kind=kLoop, calls=%fused_computation.71 | loop fusion | flops 128 | bytes 76 | tf_op jit(solution)/shard_map/eq | solution.py:250
  6.1 0.1 convert_reduce_fusion.2
  6.3 0.6 %and_select_fusion = (s32[4]{0:T(128)S(1)}, s32[]{:T(128)}) fusion(s32[]{:T(128)S(6)} %axis_index.15, s32[4]{0:T(128)S(1)} %get-tuple-element.38), kind=kLoop, calls=%fused_computation.43 | loop fusion | flops 59 | bytes 40 | tf_op jit(solution)/shard_map/jit(remainder)/select_n | solution.py:275
  6.9 0.7 %and_select_fusion.6 = s32[4]{0:T(128)S(1)} fusion(s32[]{:T(128)} %get-tuple-element.47), kind=kLoop, calls=%fused_computation.50 | loop fusion | flops 48 | bytes 20 | tf_op jit(solution)/shard_map/jit(remainder)/select_n | solution.py:261
  7.6 0.1 convert_reduce_fusion
  7.7 0.2 select_reduce_fusion
  7.9 0.6 %gather_fusion = s32[4]{0:T(128)S(1)} fusion(s32[4]{0:T(128)S(1)} %select_reduce_fusion, s32[1024]{0:T(1024)S(1)} %pad_clamp_fusion.3), kind=kCustom, calls=%fused_computation | custom fusion | bytes 48 | tf_op jit(solution)/shard_map/gather | solution.py:264
  8.6 0.6 %gather_fusion.2 = pred[4]{0:T(512)(128)(4,1)S(1)} fusion(pred[4]{0:T(512)(128)(4,1)S(1)} %compare_bitcast_fusion, s32[1024]{0:T(1024)S(1)} %pad_clamp_fusion.1), kind=kCustom, calls=%fused_computation.2 | custom fusion | bytes 24 | tf_op jit(solution)/shard_map/gather | solution.py:275
  9.2 0.1 convert_reduce_fusion.1
  9.3 0.1 fusion.3
  9.4 0.1 fusion.1
  9.5 0.1 reshape.360
  9.6 0.1 broadcast_in_dim.34
  9.7 0.6 fusion.16
  10.3 1.3 %gather_fusion.4 = s32[4]{0:T(128)S(1)} fusion(s32[4]{0:T(128)} %param.9, s32[1024]{0:T(1024)S(1)} %pad_clamp_fusion.1), kind=kCustom, calls=%fused_computation.4 | custom fusion | bytes 48 | tf_op jit(solution)/shard_map/gather | solution.py:247
  11.6 2.8 %gather_fusion.1 = bf16[4,2,128,256]{3,2,1,0:T(8,128)(2,1)S(1)} fusion(bf16[32,2,128,256]{3,2,1,0:T(8,128)(2,1)} %param.7, s32[1024]{0:T(1024)S(1)} %pad_clamp_fusion.2), kind=kCustom, calls=%fused_computation.1 | custom fusion | bytes 1048592 | tf_op jit(solution)/shard_map/gather | solution.py:265
  14.4 0.0 collective-permute-done
  14.4 0.0 collective-permute-done.1
  14.4 1.3 %collective-permute-done.2 = bf16[2,128,256]{2,1,0:T(8,128)(2,1)S(1)} collective-permute-done((bf16[2,128,256]{2,1,0:T(8,128)(2,1)S(1)}, bf16[2,128,256]{2,1,0:T(8,128)(2,1)S(1)}, u32[]{:S(2)}, u32[]{:S(2)}) %collective-permute-start.2) | collective-permute-done | bytes 131104 | tf_op jit(solution)/shard_map/ppermute | solution.py:245
  15.7 0.1 collective-permute-start.3
  15.8 1.8 %collective-permute-start.4 = (bf16[1,2,128,256]{3,2,1,0:T(8,128)(2,1)S(1)}, bf16[1,2,128,256]{3,2,1,0:T(8,128)(2,1)S(1)}, u32[]{:S(2)}, u32[]{:S(2)}) collective-permute-start(bf16[1,2,128,256]{3,2,1,0:T(8,128)(2,1)S(1)} %get-tuple-element.42), channel_id=1, source_target_pairs={{0,8},{4,12},{8,0},{12,4},{1,9},{5,13},{9,1},{13,5},{2,10},{6,14},... | collective-permute-start | bytes 393224 | tf_op jit(solution)/shard_map/ppermute | solution.py:271
  17.6 0.0 collective-permute-start.5
  17.7 2.7 %collective-permute-done.3 = bf16[1,2,128,256]{3,2,1,0:T(8,128)(2,1)S(1)} collective-permute-done((bf16[1,2,128,256]{3,2,1,0:T(8,128)(2,1)S(1)}, bf16[1,2,128,256]{3,2,1,0:T(8,128)(2,1)S(1)}, u32[]{:S(2)}, u32[]{:S(2)}) %collective-permute-start.3) | collective-permute-done | bytes 131104 | tf_op jit(solution)/shard_map/ppermute | solution.py:271
  20.4 6.2 %collective-permute-done.4 = bf16[1,2,128,256]{3,2,1,0:T(8,128)(2,1)S(1)} collective-permute-done((bf16[1,2,128,256]{3,2,1,0:T(8,128)(2,1)S(1)}, bf16[1,2,128,256]{3,2,1,0:T(8,128)(2,1)S(1)}, u32[]{:S(2)}, u32[]{:S(2)}) %collective-permute-start.4) | collective-permute-done | bytes 131104 | tf_op jit(solution)/shard_map/ppermute | solution.py:271
  26.6 3.5 %collective-permute-done.5 = bf16[1,2,128,256]{3,2,1,0:T(8,128)(2,1)S(1)} collective-permute-done((bf16[1,2,128,256]{3,2,1,0:T(8,128)(2,1)S(1)}, bf16[1,2,128,256]{3,2,1,0:T(8,128)(2,1)S(1)}, u32[]{:S(2)}, u32[]{:S(2)}) %collective-permute-start.5) | collective-permute-done | bytes 131104 | tf_op jit(solution)/shard_map/ppermute | solution.py:271
  30.0 0.1 maximum_bitcast_fusion
  30.1 0.6 gather_fusion.3
  30.7 0.0 copy-start.1
  30.7 0.1 collective-permute-start.6
  30.7 0.7 %iota_add_fusion = s32[4,128]{1,0:T(4,128)} fusion(s32[4]{0:T(128)S(1)} %broadcast_multiply_fusion), kind=kLoop, calls=%fused_computation.32 | loop fusion | flops 512 | bytes 2064 | tf_op jit(solution)/shard_map/add | solution.py:296
  31.4 0.6 slice.43.refs_2_
  32.0 0.4 collective-permute-start.7
  32.4 1.0 %collective-permute-start.8 = (bf16[2,2,128,256]{3,2,1,0:T(8,128)(2,1)S(1)}, bf16[2,2,128,256]{3,2,1,0:T(8,128)(2,1)S(1)}, u32[]{:S(2)}, u32[]{:S(2)}) collective-permute-start(bf16[2,2,128,256]{3,2,1,0:T(8,128)(2,1)S(1)} %gather_fusion.3), channel_id=1, source_target_pairs={{0,12},{4,0},{8,4},{12,8},{1,13},{5,1},{9,5},{13,9},{2,14},{6,2},{... | collective-permute-start | bytes 786440 | tf_op jit(solution)/shard_map/ppermute | solution.py:288
  33.4 0.0 copy-done
  33.4 0.6 fusion.5
  34.7 0.9 %pad_maximum_fusion.new_ref = bf16[4,2,128,256]{3,2,1,0:T(8,128)(2,1)} fusion(bf16[1,2,128,256]{3,2,1,0:T(8,128)(2,1)S(1)} %bitcast.49, bf16[1,2,128,256]{3,2,1,0:T(8,128)(2,1)S(1)} %bitcast.48, bf16[1,2,128,256]{3,2,1,0:T(8,128)(2,1)S(1)} %bitcast.47, bf16[1,2,128,256]{3,2,1,0:T(8,128)(2,1)S(1)} %bitcast.46), kind=kLoop, calls=%fused_computation.6 | loop fusion | flops 786432 | bytes 1048576 | tf_op jit(solution)/shard_map/stack | solution.py:267
  35.6 0.0 copy-done.1
  35.6 5.5 %shard_map.55 = (f32[128,2048]{1,0:T(8,128)}, f32[2,128,8]{2,1,0:T(8,128)}, f32[2,128,8]{2,1,0:T(8,128)}) custom-call(s32[1]{0:T(128)} %bitcast.20.query_start, bf16[128,2048]{1,0:T(8,128)(2,1)} %q_ref.5, bf16[4,2,128,256]{3,2,1,0:T(8,128)(2,1)} %pad_maximum_fusion.new_ref, bf16[2,2,128,256]{3,2,1,0:T(8,128)(2,1)} %copy-done.1, s32[1,512]{1,0:T(1,128)} %bitcast.55, ...), custom_call_target="tpu_custom_call" | custom-call | tf_op jit(solution)/shard_map/pallas_call | solution.py:211
  41.1 0.0 collective-permute-done.6.refs_0_
  41.1 0.0 copy-start.4
  41.2 0.7 %copy-done.4 = bf16[2,2,128,256]{3,2,1,0:T(8,128)(2,1)} copy-done((bf16[2,2,128,256]{3,2,1,0:T(8,128)(2,1)}, bf16[2,2,128,256]{3,2,1,0:T(8,128)(2,1)S(1)}, u32[]{:S(2)}) %copy-start.4) | copy-done | bytes 262168
  41.9 7.2 %shard_map.56 = (f32[128,2048]{1,0:T(8,128)}, f32[2,128,8]{2,1,0:T(8,128)}, f32[2,128,8]{2,1,0:T(8,128)}) custom-call(bf16[128,2048]{1,0:T(8,128)(2,1)} %q_ref.5, bf16[2,2,128,256]{3,2,1,0:T(8,128)(2,1)} %copy-done.4, s32[1,256]{1,0:T(1,128)} %get-tuple-element.45.refs_1_, f32[128,2048]{1,0:T(8,128)} %get-tuple-element.26.refs_2_, ...), custom_call_target="tpu_custom_call" | custom-call | flops 268435456 | bytes 2883584 | tf_op jit(solution)/shard_map/pallas_call | solution.py:182
  49.1 4.0 %collective-permute-done.7.refs_0_ = bf16[2,2,128,256]{3,2,1,0:T(8,128)(2,1)S(1)} collective-permute-done((bf16[2,2,128,256]{3,2,1,0:T(8,128)(2,1)S(1)}, bf16[2,2,128,256]{3,2,1,0:T(8,128)(2,1)S(1)}, u32[]{:S(2)}, u32[]{:S(2)}) %collective-permute-start.7) | collective-permute-done | bytes 262176 | tf_op jit(solution)/shard_map/ppermute | solution.py:288
  53.1 0.0 copy-start.2
  53.1 1.8 %collective-permute-done.8.refs_1_ = bf16[2,2,128,256]{3,2,1,0:T(8,128)(2,1)S(1)} collective-permute-done((bf16[2,2,128,256]{3,2,1,0:T(8,128)(2,1)S(1)}, bf16[2,2,128,256]{3,2,1,0:T(8,128)(2,1)S(1)}, u32[]{:S(2)}, u32[]{:S(2)}) %collective-permute-start.8) | collective-permute-done | bytes 262176 | tf_op jit(solution)/shard_map/ppermute | solution.py:288
  54.9 0.0 copy-start.3
  54.9 0.0 copy-done.2
  54.9 0.7 %copy-done.3 = bf16[2,2,128,256]{3,2,1,0:T(8,128)(2,1)} copy-done((bf16[2,2,128,256]{3,2,1,0:T(8,128)(2,1)}, bf16[2,2,128,256]{3,2,1,0:T(8,128)(2,1)S(1)}, u32[]{:S(2)}) %copy-start.3) | copy-done | bytes 262168
  55.6 7.9 %shard_map.57 = bf16[128,2048]{1,0:T(8,128)(2,1)} custom-call(bf16[128,2048]{1,0:T(8,128)(2,1)} %q_ref.5, bf16[2,2,128,256]{3,2,1,0:T(8,128)(2,1)} %copy-done.2, bf16[2,2,128,256]{3,2,1,0:T(8,128)(2,1)} %copy-done.3, s32[1,512]{1,0:T(1,128)} %slice.43.refs_2_, f32[128,2048]{1,0:T(8,128)} %get-tuple-element.34.refs_3_, ...), custom_call_target="tpu_custom_call" | custom-call | flops 536870912 | bytes 3145728 | tf_op jit(solution)/shard_map/pallas_call | solution.py:166
  (12 shorter events, 0.1 us)
Async XLA Ops:
  0.0 33.4 %copy-start = (s32[4]{0:T(128)S(1)}, s32[4]{0:T(128)}, u32[]{:S(2)}) copy-start(s32[4]{0:T(128)} %param.9) | copy-start | bytes 52
  0.9 13.4 %collective-permute-start = (bf16[2,128,256]{2,1,0:T(8,128)(2,1)S(1)}, bf16[2,128,256]{2,1,0:T(8,128)(2,1)S(1)}, u32[]{:S(2)}, u32[]{:S(2)}) collective-permute-start(bf16[2,128,256]{2,1,0:T(8,128)(2,1)S(1)} %bitcast.43), channel_id=1, source_target_pairs={{0,4},{4,8},{8,12},{12,0},{1,5},{5,9},{9,13},{13,1},{2,6},{6,10},{... | collective-permute-start | bytes 393224 | tf_op jit(solution)/shard_map/ppermute | solution.py:245
  2.3 12.1 %collective-permute-start.1 = (bf16[2,128,256]{2,1,0:T(8,128)(2,1)S(1)}, bf16[2,128,256]{2,1,0:T(8,128)(2,1)S(1)}, u32[]{:S(2)}, u32[]{:S(2)}) collective-permute-start(bf16[2,128,256]{2,1,0:T(8,128)(2,1)S(1)} %bitcast.44), channel_id=1, source_target_pairs={{0,8},{4,12},{8,0},{12,4},{1,9},{5,13},{9,1},{13,5},{2,10},{6,14},... | collective-permute-start | bytes 393224 | tf_op jit(solution)/shard_map/ppermute | solution.py:245
  3.4 12.3 %collective-permute-start.2 = (bf16[2,128,256]{2,1,0:T(8,128)(2,1)S(1)}, bf16[2,128,256]{2,1,0:T(8,128)(2,1)S(1)}, u32[]{:S(2)}, u32[]{:S(2)}) collective-permute-start(bf16[2,128,256]{2,1,0:T(8,128)(2,1)S(1)} %bitcast.45), channel_id=1, source_target_pairs={{0,12},{4,0},{8,4},{12,8},{1,13},{5,1},{9,5},{13,9},{2,14},{6,2},{... | collective-permute-start | bytes 393224 | tf_op jit(solution)/shard_map/ppermute | solution.py:245
  15.7 4.6 %collective-permute-start.3 = (bf16[1,2,128,256]{3,2,1,0:T(8,128)(2,1)S(1)}, bf16[1,2,128,256]{3,2,1,0:T(8,128)(2,1)S(1)}, u32[]{:S(2)}, u32[]{:S(2)}) collective-permute-start(bf16[1,2,128,256]{3,2,1,0:T(8,128)(2,1)S(1)} %get-tuple-element.43), channel_id=1, source_target_pairs={{0,4},{4,8},{8,12},{12,0},{1,5},{5,9},{9,13},{13,1},{2,6},{6,10},{... | collective-permute-start | bytes 393224 | tf_op jit(solution)/shard_map/ppermute | solution.py:271
  15.8 10.8 %collective-permute-start.4 = (bf16[1,2,128,256]{3,2,1,0:T(8,128)(2,1)S(1)}, bf16[1,2,128,256]{3,2,1,0:T(8,128)(2,1)S(1)}, u32[]{:S(2)}, u32[]{:S(2)}) collective-permute-start(bf16[1,2,128,256]{3,2,1,0:T(8,128)(2,1)S(1)} %get-tuple-element.42), channel_id=1, source_target_pairs={{0,8},{4,12},{8,0},{12,4},{1,9},{5,13},{9,1},{13,5},{2,10},{6,14},... | collective-permute-start | bytes 393224 | tf_op jit(solution)/shard_map/ppermute | solution.py:271
  17.6 12.4 %collective-permute-start.5 = (bf16[1,2,128,256]{3,2,1,0:T(8,128)(2,1)S(1)}, bf16[1,2,128,256]{3,2,1,0:T(8,128)(2,1)S(1)}, u32[]{:S(2)}, u32[]{:S(2)}) collective-permute-start(bf16[1,2,128,256]{3,2,1,0:T(8,128)(2,1)S(1)} %slice_bitcast_fusion.2), channel_id=1, source_target_pairs={{0,12},{4,0},{8,4},{12,8},{1,13},{5,1},{9,5},{13,9},{2,14},{6,2},{... | collective-permute-start | bytes 393224 | tf_op jit(solution)/shard_map/ppermute | solution.py:271
  30.7 4.9 %copy-start.1 = (bf16[2,2,128,256]{3,2,1,0:T(8,128)(2,1)}, bf16[2,2,128,256]{3,2,1,0:T(8,128)(2,1)S(1)}, u32[]{:S(2)}) copy-start(bf16[2,2,128,256]{3,2,1,0:T(8,128)(2,1)S(1)} %gather_fusion.3) | copy-start | bytes 786436
  30.7 10.5 %collective-permute-start.6 = (bf16[2,2,128,256]{3,2,1,0:T(8,128)(2,1)S(1)}, bf16[2,2,128,256]{3,2,1,0:T(8,128)(2,1)S(1)}, u32[]{:S(2)}, u32[]{:S(2)}) collective-permute-start(bf16[2,2,128,256]{3,2,1,0:T(8,128)(2,1)S(1)} %gather_fusion.3), channel_id=1, source_target_pairs={{0,4},{4,8},{8,12},{12,0},{1,5},{5,9},{9,13},{13,1},{2,6},{6,10},{... | collective-permute-start | bytes 786440 | tf_op jit(solution)/shard_map/ppermute | solution.py:288
  32.0 21.1 %collective-permute-start.7 = (bf16[2,2,128,256]{3,2,1,0:T(8,128)(2,1)S(1)}, bf16[2,2,128,256]{3,2,1,0:T(8,128)(2,1)S(1)}, u32[]{:S(2)}, u32[]{:S(2)}) collective-permute-start(bf16[2,2,128,256]{3,2,1,0:T(8,128)(2,1)S(1)} %gather_fusion.3), channel_id=1, source_target_pairs={{0,8},{4,12},{8,0},{12,4},{1,9},{5,13},{9,1},{13,5},{2,10},{6,14},... | collective-permute-start | bytes 786440 | tf_op jit(solution)/shard_map/ppermute | solution.py:288
  32.4 22.4 %collective-permute-start.8 = (bf16[2,2,128,256]{3,2,1,0:T(8,128)(2,1)S(1)}, bf16[2,2,128,256]{3,2,1,0:T(8,128)(2,1)S(1)}, u32[]{:S(2)}, u32[]{:S(2)}) collective-permute-start(bf16[2,2,128,256]{3,2,1,0:T(8,128)(2,1)S(1)} %gather_fusion.3), channel_id=1, source_target_pairs={{0,12},{4,0},{8,4},{12,8},{1,13},{5,1},{9,5},{13,9},{2,14},{6,2},{... | collective-permute-start | bytes 786440 | tf_op jit(solution)/shard_map/ppermute | solution.py:288
  41.1 0.7 %copy-start.4 = (bf16[2,2,128,256]{3,2,1,0:T(8,128)(2,1)}, bf16[2,2,128,256]{3,2,1,0:T(8,128)(2,1)S(1)}, u32[]{:S(2)}) copy-start(bf16[2,2,128,256]{3,2,1,0:T(8,128)(2,1)S(1)} %collective-permute-done.6.refs_0_) | copy-start | bytes 786436
  53.1 1.8 %copy-start.2 = (bf16[2,2,128,256]{3,2,1,0:T(8,128)(2,1)}, bf16[2,2,128,256]{3,2,1,0:T(8,128)(2,1)S(1)}, u32[]{:S(2)}) copy-start(bf16[2,2,128,256]{3,2,1,0:T(8,128)(2,1)S(1)} %collective-permute-done.7.refs_0_) | copy-start | bytes 786436
  54.9 0.7 %copy-start.3 = (bf16[2,2,128,256]{3,2,1,0:T(8,128)(2,1)}, bf16[2,2,128,256]{3,2,1,0:T(8,128)(2,1)S(1)}, u32[]{:S(2)}) copy-start(bf16[2,2,128,256]{3,2,1,0:T(8,128)(2,1)S(1)} %collective-permute-done.8.refs_1_) | copy-start | bytes 786436
